TPU v7x, 512 devices: a whole 4x4x16 slice. The times are simulated.
512 devices in a mesh: seq: 64 (over z, y), tensor: 8 (over x, core).
Axes of the slice: x: 4, y: 4, z: 16, core: 2. Of those that a mesh axis runs over, the one named last changes fastest.
Arguments:
- queries: bfloat16 [9216, 4096], P('seq', 'tensor'), may hold values from -44 to 44
- keys_values: bfloat16 [9216, 2, 4096], P('seq', None, 'tensor'), may hold values from -16 to 16
- segment_ids: int32 [9216], P('seq'), may hold values from 0 to 8, never falling along the last dimension, each value on 1 to 2161 neighbouring positions
- out_weight: bfloat16 [4096, 7168], P('tensor', 'seq'), may hold values from -0.09375 to 0.09375
Outputs:
- hidden_states: bfloat16 [9216, 7168], P('seq', 'tensor')
- kv_cache: bfloat16 [2, 32, 9216, 128], P(None, 'tensor', 'seq')
Inputs may be any that keep to these rules, and one draw needn't show every extreme that they name: `segment_ids`: never falling along the tokens; each of the 9 prompts holds 1 to 2161 consecutive tokens, and one holds exactly 2161.
All inputs are finite; a program needn't handle non-finite values.
Results may differ from a plain program's by a relative error of at most 0.015.
Values may be sent and summed in bfloat16 or wider, within the bound.
No kernel may reach another device: no remote copies, remote signals or barrier semaphores. Data moves between devices by JAX's collectives and lax.ppermute only.
A program may use at most 64 MiB of HBM per device.

v0:
```python
import math

import jax
import jax.numpy as jnp
from jax import lax
from jax.sharding import PartitionSpec as P

HD = 128


def from_behind(value, axis, steps):
    count = lax.axis_size(axis)
    initial, last = (max(0, -steps), min(count, count - steps))
    return lax.ppermute(value, axis, [(source, source + steps) for source in range(initial, last)])


def local(queries, keys_values, segment_ids, out_weight):
    row_count = queries.shape[0]
    head_count = queries.shape[1] // HD
    span = min(16, lax.axis_size("seq") // 2)
    score_scale = 1.0 / math.sqrt(HD)
    seq_index = lax.axis_index("seq")
    offsets = jnp.arange(row_count, dtype=jnp.int32)
    query_pos = seq_index * row_count + offsets
    query_seg = segment_ids + 1
    query_heads = queries.reshape(row_count, head_count, HD)

    def attend(carried, pair_block, block_seg, distance):
        run_max, row_total, accumulated = carried
        key_pos = (seq_index - distance) * row_count + offsets
        key_rows = pair_block[:, 0].reshape(row_count, head_count, HD)
        value_rows = pair_block[:, 1].reshape(row_count, head_count, HD)
        scores = (
            jnp.einsum("qhd,khd->hqk", query_heads, key_rows, preferred_element_type=jnp.float32)
            * score_scale
        )
        allowed = (block_seg[None, :] == query_seg[:, None]) & (
            key_pos[None, :] <= query_pos[:, None]
        )
        masked = jnp.where(allowed[None], scores, -1e30)
        new_max = jnp.maximum(run_max, jnp.max(masked, axis=2))
        probs = jnp.where(allowed[None], jnp.exp(masked - new_max[..., None]), 0.0)
        factor = jnp.exp(run_max - new_max)
        row_total = row_total * factor + jnp.sum(probs, axis=2)
        accumulated = accumulated * factor[..., None] + jnp.einsum(
            "hqk,khd->hqd",
            probs.astype(jnp.bfloat16),
            value_rows,
            preferred_element_type=jnp.float32,
        )
        return (new_max, row_total, accumulated)

    def visit(carried, pair_block, block_seg, distance):
        return attend(carried, pair_block, block_seg, distance)

    start_state = (
        jnp.full((head_count, row_count), -1e30, jnp.float32),
        jnp.zeros((head_count, row_count), jnp.float32),
        jnp.zeros((head_count, row_count, HD), jnp.float32),
    )
    carried = visit(start_state, keys_values, query_seg, 0)

    def advance(distance, bundle):
        status, pair_block, block_seg = bundle
        pair_block, block_seg = from_behind((pair_block, block_seg), "seq", 1)
        status = visit(status, pair_block, block_seg, distance)
        return (status, pair_block, block_seg)

    carried, last_block, last_seg = lax.fori_loop(
        1, span, advance, (carried, keys_values, query_seg)
    )
    run_max, row_total, accumulated = carried
    attended = (accumulated / row_total[..., None]).astype(jnp.bfloat16)
    attended = attended.transpose(1, 0, 2).reshape(row_count, head_count * HD)
    partial_value = jnp.dot(
        attended,
        lax.all_gather(out_weight, "seq", axis=1, tiled=True),
        preferred_element_type=jnp.float32,
    )
    hidden_states = lax.psum_scatter(
        partial_value.astype(jnp.bfloat16), "tensor", scatter_dimension=1, tiled=True
    )
    head_major = keys_values.reshape(row_count, 2, head_count, HD).transpose(1, 2, 0, 3)
    return (hidden_states, head_major)


def solution(mesh):
    return jax.shard_map(
        local,
        mesh=mesh,
        in_specs=(P("seq", "tensor"), P("seq", None, "tensor"), P("seq"), P("tensor", "seq")),
        out_specs=(P("seq", "tensor"), P(None, "tensor", "seq", None)),
        check_vma=False,
    )
```

profile of v0, /device:TPU:1, one launch (start us, length us, event | category | flops | bytes accessed | tf_op | source)
XLA Modules:
  0.0 331.9 jit_solution(5841937601202774116)
XLA Ops:
  12.9 225.5 %while.22 = (s32[]{:T(128)}, f32[4,144]{1,0:T(4,128)S(1)}, f32[4,144]{1,0:T(4,128)S(1)}, f32[4,144,128]{2,1,0:T(8,128)S(1)}, bf16[144,2,512]{2,0,1:T(8,128)(2,1)...) while((s32[]{:T(128)}, f32[4,144]{1,0:T(4,128)S(1)}, ...), condition=%wide.region_5.6_spmd.clone, body=%wide.region_2.5_spmd.clone.sunk | while | flops 43424932 | bytes 5103589 | solution.py:69
  12.9 4.0 %collective-permute-start.1 = (s32[144]{0:T(256)S(1)}, s32[144]{0:T(256)S(1)}, u32[]{:S(2)}, u32[]{:S(2)}) collective-permute-start(s32[144]{0:T(256)S(1)} %get-tuple-element.367), channel_id=1, source_target_pairs={{0,8},{8,16},{16,24},{24,32},{32,40},{40,48},{48,56},{56,64},{64,7... | collective-permute-start | bytes 1736 | tf_op jit(solution)/shard_map/while/body/eval_jaxpr/ppermute | solution.py:14
  17.0 3.2 collective-permute-start
  20.4 4.2 %collective-permute-done = bf16[144,2,512]{2,0,1:T(8,128)(2,1)S(1)} collective-permute-done((bf16[144,2,512]{2,0,1:T(8,128)(2,1)S(1)}, bf16[144,2,512]{2,0,1:T(8,128)(2,1)S(1)}, u32[]{:S(2)}, u32[]{:S(2)}) %collective-permute-start) | collective-permute-done | bytes 294944 | tf_op jit(solution)/shard_map/while/body/eval_jaxpr/ppermute | solution.py:14
  25.5 4.1 %collective-permute-start.1 = (s32[144]{0:T(256)S(1)}, s32[144]{0:T(256)S(1)}, u32[]{:S(2)}, u32[]{:S(2)}) collective-permute-start(s32[144]{0:T(256)S(1)} %get-tuple-element.367), channel_id=1, source_target_pairs={{0,8},{8,16},{16,24},{24,32},{32,40},{40,48},{48,56},{56,64},{64,7... | collective-permute-start | bytes 1736 | tf_op jit(solution)/shard_map/while/body/eval_jaxpr/ppermute | solution.py:14
  29.7 3.9 %collective-permute-start = (bf16[144,2,512]{2,0,1:T(8,128)(2,1)S(1)}, bf16[144,2,512]{2,0,1:T(8,128)(2,1)S(1)}, u32[]{:S(2)}, u32[]{:S(2)}) collective-permute-start(bf16[144,2,512]{2,0,1:T(8,128)(2,1)S(1)} %get-tuple-element.366), channel_id=1, source_target_pairs={{0,8},{8,16},{16,24},{24,32},{32,40},{40,48},{48,56},{56,64},{64,7... | collective-permute-start | bytes 884744 | tf_op jit(solution)/shard_map/while/body/eval_jaxpr/ppermute | solution.py:14
  33.7 4.7 %collective-permute-done = bf16[144,2,512]{2,0,1:T(8,128)(2,1)S(1)} collective-permute-done((bf16[144,2,512]{2,0,1:T(8,128)(2,1)S(1)}, bf16[144,2,512]{2,0,1:T(8,128)(2,1)S(1)}, u32[]{:S(2)}, u32[]{:S(2)}) %collective-permute-start) | collective-permute-done | bytes 294944 | tf_op jit(solution)/shard_map/while/body/eval_jaxpr/ppermute | solution.py:14
  39.4 4.1 %collective-permute-start.1 = (s32[144]{0:T(256)S(1)}, s32[144]{0:T(256)S(1)}, u32[]{:S(2)}, u32[]{:S(2)}) collective-permute-start(s32[144]{0:T(256)S(1)} %get-tuple-element.367), channel_id=1, source_target_pairs={{0,8},{8,16},{16,24},{24,32},{32,40},{40,48},{48,56},{56,64},{64,7... | collective-permute-start | bytes 1736 | tf_op jit(solution)/shard_map/while/body/eval_jaxpr/ppermute | solution.py:14
  43.5 4.5 %collective-permute-start = (bf16[144,2,512]{2,0,1:T(8,128)(2,1)S(1)}, bf16[144,2,512]{2,0,1:T(8,128)(2,1)S(1)}, u32[]{:S(2)}, u32[]{:S(2)}) collective-permute-start(bf16[144,2,512]{2,0,1:T(8,128)(2,1)S(1)} %get-tuple-element.366), channel_id=1, source_target_pairs={{0,8},{8,16},{16,24},{24,32},{32,40},{40,48},{48,56},{56,64},{64,7... | collective-permute-start | bytes 884744 | tf_op jit(solution)/shard_map/while/body/eval_jaxpr/ppermute | solution.py:14
  48.1 3.7 %collective-permute-done = bf16[144,2,512]{2,0,1:T(8,128)(2,1)S(1)} collective-permute-done((bf16[144,2,512]{2,0,1:T(8,128)(2,1)S(1)}, bf16[144,2,512]{2,0,1:T(8,128)(2,1)S(1)}, u32[]{:S(2)}, u32[]{:S(2)}) %collective-permute-start) | collective-permute-done | bytes 294944 | tf_op jit(solution)/shard_map/while/body/eval_jaxpr/ppermute | solution.py:14
  52.8 4.3 %collective-permute-start.1 = (s32[144]{0:T(256)S(1)}, s32[144]{0:T(256)S(1)}, u32[]{:S(2)}, u32[]{:S(2)}) collective-permute-start(s32[144]{0:T(256)S(1)} %get-tuple-element.367), channel_id=1, source_target_pairs={{0,8},{8,16},{16,24},{24,32},{32,40},{40,48},{48,56},{56,64},{64,7... | collective-permute-start | bytes 1736 | tf_op jit(solution)/shard_map/while/body/eval_jaxpr/ppermute | solution.py:14
  57.1 3.9 %collective-permute-start = (bf16[144,2,512]{2,0,1:T(8,128)(2,1)S(1)}, bf16[144,2,512]{2,0,1:T(8,128)(2,1)S(1)}, u32[]{:S(2)}, u32[]{:S(2)}) collective-permute-start(bf16[144,2,512]{2,0,1:T(8,128)(2,1)S(1)} %get-tuple-element.366), channel_id=1, source_target_pairs={{0,8},{8,16},{16,24},{24,32},{32,40},{40,48},{48,56},{56,64},{64,7... | collective-permute-start | bytes 884744 | tf_op jit(solution)/shard_map/while/body/eval_jaxpr/ppermute | solution.py:14
  61.2 3.5 %collective-permute-done = bf16[144,2,512]{2,0,1:T(8,128)(2,1)S(1)} collective-permute-done((bf16[144,2,512]{2,0,1:T(8,128)(2,1)S(1)}, bf16[144,2,512]{2,0,1:T(8,128)(2,1)S(1)}, u32[]{:S(2)}, u32[]{:S(2)}) %collective-permute-start) | collective-permute-done | bytes 294944 | tf_op jit(solution)/shard_map/while/body/eval_jaxpr/ppermute | solution.py:14
  65.6 4.2 %collective-permute-start.1 = (s32[144]{0:T(256)S(1)}, s32[144]{0:T(256)S(1)}, u32[]{:S(2)}, u32[]{:S(2)}) collective-permute-start(s32[144]{0:T(256)S(1)} %get-tuple-element.367), channel_id=1, source_target_pairs={{0,8},{8,16},{16,24},{24,32},{32,40},{40,48},{48,56},{56,64},{64,7... | collective-permute-start | bytes 1736 | tf_op jit(solution)/shard_map/while/body/eval_jaxpr/ppermute | solution.py:14
  69.9 4.2 %collective-permute-start = (bf16[144,2,512]{2,0,1:T(8,128)(2,1)S(1)}, bf16[144,2,512]{2,0,1:T(8,128)(2,1)S(1)}, u32[]{:S(2)}, u32[]{:S(2)}) collective-permute-start(bf16[144,2,512]{2,0,1:T(8,128)(2,1)S(1)} %get-tuple-element.366), channel_id=1, source_target_pairs={{0,8},{8,16},{16,24},{24,32},{32,40},{40,48},{48,56},{56,64},{64,7... | collective-permute-start | bytes 884744 | tf_op jit(solution)/shard_map/while/body/eval_jaxpr/ppermute | solution.py:14
  74.2 3.5 %collective-permute-done = bf16[144,2,512]{2,0,1:T(8,128)(2,1)S(1)} collective-permute-done((bf16[144,2,512]{2,0,1:T(8,128)(2,1)S(1)}, bf16[144,2,512]{2,0,1:T(8,128)(2,1)S(1)}, u32[]{:S(2)}, u32[]{:S(2)}) %collective-permute-start) | collective-permute-done | bytes 294944 | tf_op jit(solution)/shard_map/while/body/eval_jaxpr/ppermute | solution.py:14
  78.7 4.1 %collective-permute-start.1 = (s32[144]{0:T(256)S(1)}, s32[144]{0:T(256)S(1)}, u32[]{:S(2)}, u32[]{:S(2)}) collective-permute-start(s32[144]{0:T(256)S(1)} %get-tuple-element.367), channel_id=1, source_target_pairs={{0,8},{8,16},{16,24},{24,32},{32,40},{40,48},{48,56},{56,64},{64,7... | collective-permute-start | bytes 1736 | tf_op jit(solution)/shard_map/while/body/eval_jaxpr/ppermute | solution.py:14
  82.9 4.3 %collective-permute-start = (bf16[144,2,512]{2,0,1:T(8,128)(2,1)S(1)}, bf16[144,2,512]{2,0,1:T(8,128)(2,1)S(1)}, u32[]{:S(2)}, u32[]{:S(2)}) collective-permute-start(bf16[144,2,512]{2,0,1:T(8,128)(2,1)S(1)} %get-tuple-element.366), channel_id=1, source_target_pairs={{0,8},{8,16},{16,24},{24,32},{32,40},{40,48},{48,56},{56,64},{64,7... | collective-permute-start | bytes 884744 | tf_op jit(solution)/shard_map/while/body/eval_jaxpr/ppermute | solution.py:14
  87.3 3.5 %collective-permute-done = bf16[144,2,512]{2,0,1:T(8,128)(2,1)S(1)} collective-permute-done((bf16[144,2,512]{2,0,1:T(8,128)(2,1)S(1)}, bf16[144,2,512]{2,0,1:T(8,128)(2,1)S(1)}, u32[]{:S(2)}, u32[]{:S(2)}) %collective-permute-start) | collective-permute-done | bytes 294944 | tf_op jit(solution)/shard_map/while/body/eval_jaxpr/ppermute | solution.py:14
  91.8 4.2 %collective-permute-start.1 = (s32[144]{0:T(256)S(1)}, s32[144]{0:T(256)S(1)}, u32[]{:S(2)}, u32[]{:S(2)}) collective-permute-start(s32[144]{0:T(256)S(1)} %get-tuple-element.367), channel_id=1, source_target_pairs={{0,8},{8,16},{16,24},{24,32},{32,40},{40,48},{48,56},{56,64},{64,7... | collective-permute-start | bytes 1736 | tf_op jit(solution)/shard_map/while/body/eval_jaxpr/ppermute | solution.py:14
  96.0 4.0 %collective-permute-start = (bf16[144,2,512]{2,0,1:T(8,128)(2,1)S(1)}, bf16[144,2,512]{2,0,1:T(8,128)(2,1)S(1)}, u32[]{:S(2)}, u32[]{:S(2)}) collective-permute-start(bf16[144,2,512]{2,0,1:T(8,128)(2,1)S(1)} %get-tuple-element.366), channel_id=1, source_target_pairs={{0,8},{8,16},{16,24},{24,32},{32,40},{40,48},{48,56},{56,64},{64,7... | collective-permute-start | bytes 884744 | tf_op jit(solution)/shard_map/while/body/eval_jaxpr/ppermute | solution.py:14
  100.2 4.3 %collective-permute-done = bf16[144,2,512]{2,0,1:T(8,128)(2,1)S(1)} collective-permute-done((bf16[144,2,512]{2,0,1:T(8,128)(2,1)S(1)}, bf16[144,2,512]{2,0,1:T(8,128)(2,1)S(1)}, u32[]{:S(2)}, u32[]{:S(2)}) %collective-permute-start) | collective-permute-done | bytes 294944 | tf_op jit(solution)/shard_map/while/body/eval_jaxpr/ppermute | solution.py:14
  105.5 5.6 %collective-permute-start.1 = (s32[144]{0:T(256)S(1)}, s32[144]{0:T(256)S(1)}, u32[]{:S(2)}, u32[]{:S(2)}) collective-permute-start(s32[144]{0:T(256)S(1)} %get-tuple-element.367), channel_id=1, source_target_pairs={{0,8},{8,16},{16,24},{24,32},{32,40},{40,48},{48,56},{56,64},{64,7... | collective-permute-start | bytes 1736 | tf_op jit(solution)/shard_map/while/body/eval_jaxpr/ppermute | solution.py:14
  111.1 6.0 %collective-permute-start = (bf16[144,2,512]{2,0,1:T(8,128)(2,1)S(1)}, bf16[144,2,512]{2,0,1:T(8,128)(2,1)S(1)}, u32[]{:S(2)}, u32[]{:S(2)}) collective-permute-start(bf16[144,2,512]{2,0,1:T(8,128)(2,1)S(1)} %get-tuple-element.366), channel_id=1, source_target_pairs={{0,8},{8,16},{16,24},{24,32},{32,40},{40,48},{48,56},{56,64},{64,7... | collective-permute-start | bytes 884744 | tf_op jit(solution)/shard_map/while/body/eval_jaxpr/ppermute | solution.py:14
  117.3 10.2 %collective-permute-done = bf16[144,2,512]{2,0,1:T(8,128)(2,1)S(1)} collective-permute-done((bf16[144,2,512]{2,0,1:T(8,128)(2,1)S(1)}, bf16[144,2,512]{2,0,1:T(8,128)(2,1)S(1)}, u32[]{:S(2)}, u32[]{:S(2)}) %collective-permute-start) | collective-permute-done | bytes 294944 | tf_op jit(solution)/shard_map/while/body/eval_jaxpr/ppermute | solution.py:14
  128.4 4.2 %collective-permute-start.1 = (s32[144]{0:T(256)S(1)}, s32[144]{0:T(256)S(1)}, u32[]{:S(2)}, u32[]{:S(2)}) collective-permute-start(s32[144]{0:T(256)S(1)} %get-tuple-element.367), channel_id=1, source_target_pairs={{0,8},{8,16},{16,24},{24,32},{32,40},{40,48},{48,56},{56,64},{64,7... | collective-permute-start | bytes 1736 | tf_op jit(solution)/shard_map/while/body/eval_jaxpr/ppermute | solution.py:14
  132.7 4.2 %collective-permute-start = (bf16[144,2,512]{2,0,1:T(8,128)(2,1)S(1)}, bf16[144,2,512]{2,0,1:T(8,128)(2,1)S(1)}, u32[]{:S(2)}, u32[]{:S(2)}) collective-permute-start(bf16[144,2,512]{2,0,1:T(8,128)(2,1)S(1)} %get-tuple-element.366), channel_id=1, source_target_pairs={{0,8},{8,16},{16,24},{24,32},{32,40},{40,48},{48,56},{56,64},{64,7... | collective-permute-start | bytes 884744 | tf_op jit(solution)/shard_map/while/body/eval_jaxpr/ppermute | solution.py:14
  137.0 9.1 %collective-permute-done = bf16[144,2,512]{2,0,1:T(8,128)(2,1)S(1)} collective-permute-done((bf16[144,2,512]{2,0,1:T(8,128)(2,1)S(1)}, bf16[144,2,512]{2,0,1:T(8,128)(2,1)S(1)}, u32[]{:S(2)}, u32[]{:S(2)}) %collective-permute-start) | collective-permute-done | bytes 294944 | tf_op jit(solution)/shard_map/while/body/eval_jaxpr/ppermute | solution.py:14
  147.1 4.2 %collective-permute-start.1 = (s32[144]{0:T(256)S(1)}, s32[144]{0:T(256)S(1)}, u32[]{:S(2)}, u32[]{:S(2)}) collective-permute-start(s32[144]{0:T(256)S(1)} %get-tuple-element.367), channel_id=1, source_target_pairs={{0,8},{8,16},{16,24},{24,32},{32,40},{40,48},{48,56},{56,64},{64,7... | collective-permute-start | bytes 1736 | tf_op jit(solution)/shard_map/while/body/eval_jaxpr/ppermute | solution.py:14
  151.3 3.6 %collective-permute-start = (bf16[144,2,512]{2,0,1:T(8,128)(2,1)S(1)}, bf16[144,2,512]{2,0,1:T(8,128)(2,1)S(1)}, u32[]{:S(2)}, u32[]{:S(2)}) collective-permute-start(bf16[144,2,512]{2,0,1:T(8,128)(2,1)S(1)} %get-tuple-element.366), channel_id=1, source_target_pairs={{0,8},{8,16},{16,24},{24,32},{32,40},{40,48},{48,56},{56,64},{64,7... | collective-permute-start | bytes 884744 | tf_op jit(solution)/shard_map/while/body/eval_jaxpr/ppermute | solution.py:14
  155.0 3.5 %collective-permute-done = bf16[144,2,512]{2,0,1:T(8,128)(2,1)S(1)} collective-permute-done((bf16[144,2,512]{2,0,1:T(8,128)(2,1)S(1)}, bf16[144,2,512]{2,0,1:T(8,128)(2,1)S(1)}, u32[]{:S(2)}, u32[]{:S(2)}) %collective-permute-start) | collective-permute-done | bytes 294944 | tf_op jit(solution)/shard_map/while/body/eval_jaxpr/ppermute | solution.py:14
  159.5 4.2 %collective-permute-start.1 = (s32[144]{0:T(256)S(1)}, s32[144]{0:T(256)S(1)}, u32[]{:S(2)}, u32[]{:S(2)}) collective-permute-start(s32[144]{0:T(256)S(1)} %get-tuple-element.367), channel_id=1, source_target_pairs={{0,8},{8,16},{16,24},{24,32},{32,40},{40,48},{48,56},{56,64},{64,7... | collective-permute-start | bytes 1736 | tf_op jit(solution)/shard_map/while/body/eval_jaxpr/ppermute | solution.py:14
  163.7 4.2 %collective-permute-start = (bf16[144,2,512]{2,0,1:T(8,128)(2,1)S(1)}, bf16[144,2,512]{2,0,1:T(8,128)(2,1)S(1)}, u32[]{:S(2)}, u32[]{:S(2)}) collective-permute-start(bf16[144,2,512]{2,0,1:T(8,128)(2,1)S(1)} %get-tuple-element.366), channel_id=1, source_target_pairs={{0,8},{8,16},{16,24},{24,32},{32,40},{40,48},{48,56},{56,64},{64,7... | collective-permute-start | bytes 884744 | tf_op jit(solution)/shard_map/while/body/eval_jaxpr/ppermute | solution.py:14
  168.1 3.5 %collective-permute-done = bf16[144,2,512]{2,0,1:T(8,128)(2,1)S(1)} collective-permute-done((bf16[144,2,512]{2,0,1:T(8,128)(2,1)S(1)}, bf16[144,2,512]{2,0,1:T(8,128)(2,1)S(1)}, u32[]{:S(2)}, u32[]{:S(2)}) %collective-permute-start) | collective-permute-done | bytes 294944 | tf_op jit(solution)/shard_map/while/body/eval_jaxpr/ppermute | solution.py:14
  172.6 8.1 %collective-permute-start.1 = (s32[144]{0:T(256)S(1)}, s32[144]{0:T(256)S(1)}, u32[]{:S(2)}, u32[]{:S(2)}) collective-permute-start(s32[144]{0:T(256)S(1)} %get-tuple-element.367), channel_id=1, source_target_pairs={{0,8},{8,16},{16,24},{24,32},{32,40},{40,48},{48,56},{56,64},{64,7... | collective-permute-start | bytes 1736 | tf_op jit(solution)/shard_map/while/body/eval_jaxpr/ppermute | solution.py:14
  180.7 6.0 %collective-permute-start = (bf16[144,2,512]{2,0,1:T(8,128)(2,1)S(1)}, bf16[144,2,512]{2,0,1:T(8,128)(2,1)S(1)}, u32[]{:S(2)}, u32[]{:S(2)}) collective-permute-start(bf16[144,2,512]{2,0,1:T(8,128)(2,1)S(1)} %get-tuple-element.366), channel_id=1, source_target_pairs={{0,8},{8,16},{16,24},{24,32},{32,40},{40,48},{48,56},{56,64},{64,7... | collective-permute-start | bytes 884744 | tf_op jit(solution)/shard_map/while/body/eval_jaxpr/ppermute | solution.py:14
  186.9 3.5 %collective-permute-done = bf16[144,2,512]{2,0,1:T(8,128)(2,1)S(1)} collective-permute-done((bf16[144,2,512]{2,0,1:T(8,128)(2,1)S(1)}, bf16[144,2,512]{2,0,1:T(8,128)(2,1)S(1)}, u32[]{:S(2)}, u32[]{:S(2)}) %collective-permute-start) | collective-permute-done | bytes 294944 | tf_op jit(solution)/shard_map/while/body/eval_jaxpr/ppermute | solution.py:14
  191.3 3.8 %collective-permute-start.1 = (s32[144]{0:T(256)S(1)}, s32[144]{0:T(256)S(1)}, u32[]{:S(2)}, u32[]{:S(2)}) collective-permute-start(s32[144]{0:T(256)S(1)} %get-tuple-element.367), channel_id=1, source_target_pairs={{0,8},{8,16},{16,24},{24,32},{32,40},{40,48},{48,56},{56,64},{64,7... | collective-permute-start | bytes 1736 | tf_op jit(solution)/shard_map/while/body/eval_jaxpr/ppermute | solution.py:14
  195.2 4.5 %collective-permute-start = (bf16[144,2,512]{2,0,1:T(8,128)(2,1)S(1)}, bf16[144,2,512]{2,0,1:T(8,128)(2,1)S(1)}, u32[]{:S(2)}, u32[]{:S(2)}) collective-permute-start(bf16[144,2,512]{2,0,1:T(8,128)(2,1)S(1)} %get-tuple-element.366), channel_id=1, source_target_pairs={{0,8},{8,16},{16,24},{24,32},{32,40},{40,48},{48,56},{56,64},{64,7... | collective-permute-start | bytes 884744 | tf_op jit(solution)/shard_map/while/body/eval_jaxpr/ppermute | solution.py:14
  199.8 5.0 %collective-permute-done = bf16[144,2,512]{2,0,1:T(8,128)(2,1)S(1)} collective-permute-done((bf16[144,2,512]{2,0,1:T(8,128)(2,1)S(1)}, bf16[144,2,512]{2,0,1:T(8,128)(2,1)S(1)}, u32[]{:S(2)}, u32[]{:S(2)}) %collective-permute-start) | collective-permute-done | bytes 294944 | tf_op jit(solution)/shard_map/while/body/eval_jaxpr/ppermute | solution.py:14
  205.7 7.5 %collective-permute-start.1 = (s32[144]{0:T(256)S(1)}, s32[144]{0:T(256)S(1)}, u32[]{:S(2)}, u32[]{:S(2)}) collective-permute-start(s32[144]{0:T(256)S(1)} %get-tuple-element.367), channel_id=1, source_target_pairs={{0,8},{8,16},{16,24},{24,32},{32,40},{40,48},{48,56},{56,64},{64,7... | collective-permute-start | bytes 1736 | tf_op jit(solution)/shard_map/while/body/eval_jaxpr/ppermute | solution.py:14
  213.2 6.2 %collective-permute-start = (bf16[144,2,512]{2,0,1:T(8,128)(2,1)S(1)}, bf16[144,2,512]{2,0,1:T(8,128)(2,1)S(1)}, u32[]{:S(2)}, u32[]{:S(2)}) collective-permute-start(bf16[144,2,512]{2,0,1:T(8,128)(2,1)S(1)} %get-tuple-element.366), channel_id=1, source_target_pairs={{0,8},{8,16},{16,24},{24,32},{32,40},{40,48},{48,56},{56,64},{64,7... | collective-permute-start | bytes 884744 | tf_op jit(solution)/shard_map/while/body/eval_jaxpr/ppermute | solution.py:14
  219.6 4.0 %collective-permute-done = bf16[144,2,512]{2,0,1:T(8,128)(2,1)S(1)} collective-permute-done((bf16[144,2,512]{2,0,1:T(8,128)(2,1)S(1)}, bf16[144,2,512]{2,0,1:T(8,128)(2,1)S(1)}, u32[]{:S(2)}, u32[]{:S(2)}) %collective-permute-start) | collective-permute-done | bytes 294944 | tf_op jit(solution)/shard_map/while/body/eval_jaxpr/ppermute | solution.py:14
  224.6 4.1 %collective-permute-start.1 = (s32[144]{0:T(256)S(1)}, s32[144]{0:T(256)S(1)}, u32[]{:S(2)}, u32[]{:S(2)}) collective-permute-start(s32[144]{0:T(256)S(1)} %get-tuple-element.367), channel_id=1, source_target_pairs={{0,8},{8,16},{16,24},{24,32},{32,40},{40,48},{48,56},{56,64},{64,7... | collective-permute-start | bytes 1736 | tf_op jit(solution)/shard_map/while/body/eval_jaxpr/ppermute | solution.py:14
  228.7 5.2 %collective-permute-start = (bf16[144,2,512]{2,0,1:T(8,128)(2,1)S(1)}, bf16[144,2,512]{2,0,1:T(8,128)(2,1)S(1)}, u32[]{:S(2)}, u32[]{:S(2)}) collective-permute-start(bf16[144,2,512]{2,0,1:T(8,128)(2,1)S(1)} %get-tuple-element.366), channel_id=1, source_target_pairs={{0,8},{8,16},{16,24},{24,32},{32,40},{40,48},{48,56},{56,64},{64,7... | collective-permute-start | bytes 884744 | tf_op jit(solution)/shard_map/while/body/eval_jaxpr/ppermute | solution.py:14
  234.0 3.5 %collective-permute-done = bf16[144,2,512]{2,0,1:T(8,128)(2,1)S(1)} collective-permute-done((bf16[144,2,512]{2,0,1:T(8,128)(2,1)S(1)}, bf16[144,2,512]{2,0,1:T(8,128)(2,1)S(1)}, u32[]{:S(2)}, u32[]{:S(2)}) %collective-permute-start) | collective-permute-done | bytes 294944 | tf_op jit(solution)/shard_map/while/body/eval_jaxpr/ppermute | solution.py:14
  238.5 5.7 %convolution_convert_fusion = bf16[144,7168]{1,0:T(8,128)(2,1)S(1)} fusion(bf16[512,7168]{0,1:T(8,128)(2,1)} %all-gather.2.cloned.1.call-done, f32[4,144,128]{2,1,0:T(8,128)S(1)} %get-tuple-element.187, f32[4,144]{1,0:T(4,128)S(1)} %get-tuple-element.188), kind=kOutput, calls=%fused_computation.19 | convolution fusion | flops 1058144256 | bytes 9701632 | tf_op jit(solution)/shard_map/dot_general | solution.py:75
  248.1 75.0 %reduce-scatter.4.cloned.1.call-done = bf16[896,144]{1,0:T(8,128)(2,1)} async-done(((bf16[7168,144]{1,0:T(8,128)(2,1)}), bf16[896,144]{1,0:T(8,128)(2,1)}) %reduce-scatter.4.cloned.1.call-update) | async-done | bytes 258064
  (234 shorter events, 27.2 us)
Async XLA Ops:
  7.2 5.0 %copy-start = (bf16[144,512]{1,0:T(8,128)(2,1)S(1)}, bf16[144,512]{1,0:T(8,128)(2,1)}, u32[]{:S(2)}) copy-start(bf16[144,512]{1,0:T(8,128)(2,1)} %param.6) | copy-start | bytes 442372
  7.2 231.3 %all-gather.2.cloned.1.call-start = ((), (), s32[]{:S(2)}) async-start(), calls=%async_computation.1 | async-start | bytes 7454720 | tf_op jit(solution)/shard_map/all_gather | solution.py:77
  7.9 315.3 %reduce-scatter.4.cloned.1.call-start = ((), (), s32[]{:S(2)}) async-start(), calls=%async_computation.2 | async-start | bytes 4128768
  12.9 7.3 %collective-permute-start.1 = (s32[144]{0:T(256)S(1)}, s32[144]{0:T(256)S(1)}, u32[]{:S(2)}, u32[]{:S(2)}) collective-permute-start(s32[144]{0:T(256)S(1)} %get-tuple-element.367), channel_id=1, source_target_pairs={{0,8},{8,16},{16,24},{24,32},{32,40},{40,48},{48,56},{56,64},{64,7... | collective-permute-start | bytes 1736 | tf_op jit(solution)/shard_map/while/body/eval_jaxpr/ppermute | solution.py:14
  17.0 7.6 %collective-permute-start = (bf16[144,2,512]{2,0,1:T(8,128)(2,1)S(1)}, bf16[144,2,512]{2,0,1:T(8,128)(2,1)S(1)}, u32[]{:S(2)}, u32[]{:S(2)}) collective-permute-start(bf16[144,2,512]{2,0,1:T(8,128)(2,1)S(1)} %get-tuple-element.366), channel_id=1, source_target_pairs={{0,8},{8,16},{16,24},{24,32},{32,40},{40,48},{48,56},{56,64},{64,7... | collective-permute-start | bytes 884744 | tf_op jit(solution)/shard_map/while/body/eval_jaxpr/ppermute | solution.py:14
  25.5 8.0 %collective-permute-start.1 = (s32[144]{0:T(256)S(1)}, s32[144]{0:T(256)S(1)}, u32[]{:S(2)}, u32[]{:S(2)}) collective-permute-start(s32[144]{0:T(256)S(1)} %get-tuple-element.367), channel_id=1, source_target_pairs={{0,8},{8,16},{16,24},{24,32},{32,40},{40,48},{48,56},{56,64},{64,7... | collective-permute-start | bytes 1736 | tf_op jit(solution)/shard_map/while/body/eval_jaxpr/ppermute | solution.py:14
  29.7 8.7 %collective-permute-start = (bf16[144,2,512]{2,0,1:T(8,128)(2,1)S(1)}, bf16[144,2,512]{2,0,1:T(8,128)(2,1)S(1)}, u32[]{:S(2)}, u32[]{:S(2)}) collective-permute-start(bf16[144,2,512]{2,0,1:T(8,128)(2,1)S(1)} %get-tuple-element.366), channel_id=1, source_target_pairs={{0,8},{8,16},{16,24},{24,32},{32,40},{40,48},{48,56},{56,64},{64,7... | collective-permute-start | bytes 884744 | tf_op jit(solution)/shard_map/while/body/eval_jaxpr/ppermute | solution.py:14
  39.4 8.6 %collective-permute-start.1 = (s32[144]{0:T(256)S(1)}, s32[144]{0:T(256)S(1)}, u32[]{:S(2)}, u32[]{:S(2)}) collective-permute-start(s32[144]{0:T(256)S(1)} %get-tuple-element.367), channel_id=1, source_target_pairs={{0,8},{8,16},{16,24},{24,32},{32,40},{40,48},{48,56},{56,64},{64,7... | collective-permute-start | bytes 1736 | tf_op jit(solution)/shard_map/while/body/eval_jaxpr/ppermute | solution.py:14
  43.5 8.4 %collective-permute-start = (bf16[144,2,512]{2,0,1:T(8,128)(2,1)S(1)}, bf16[144,2,512]{2,0,1:T(8,128)(2,1)S(1)}, u32[]{:S(2)}, u32[]{:S(2)}) collective-permute-start(bf16[144,2,512]{2,0,1:T(8,128)(2,1)S(1)} %get-tuple-element.366), channel_id=1, source_target_pairs={{0,8},{8,16},{16,24},{24,32},{32,40},{40,48},{48,56},{56,64},{64,7... | collective-permute-start | bytes 884744 | tf_op jit(solution)/shard_map/while/body/eval_jaxpr/ppermute | solution.py:14
  52.8 8.2 %collective-permute-start.1 = (s32[144]{0:T(256)S(1)}, s32[144]{0:T(256)S(1)}, u32[]{:S(2)}, u32[]{:S(2)}) collective-permute-start(s32[144]{0:T(256)S(1)} %get-tuple-element.367), channel_id=1, source_target_pairs={{0,8},{8,16},{16,24},{24,32},{32,40},{40,48},{48,56},{56,64},{64,7... | collective-permute-start | bytes 1736 | tf_op jit(solution)/shard_map/while/body/eval_jaxpr/ppermute | solution.py:14
  57.1 7.5 %collective-permute-start = (bf16[144,2,512]{2,0,1:T(8,128)(2,1)S(1)}, bf16[144,2,512]{2,0,1:T(8,128)(2,1)S(1)}, u32[]{:S(2)}, u32[]{:S(2)}) collective-permute-start(bf16[144,2,512]{2,0,1:T(8,128)(2,1)S(1)} %get-tuple-element.366), channel_id=1, source_target_pairs={{0,8},{8,16},{16,24},{24,32},{32,40},{40,48},{48,56},{56,64},{64,7... | collective-permute-start | bytes 884744 | tf_op jit(solution)/shard_map/while/body/eval_jaxpr/ppermute | solution.py:14
  65.6 8.5 %collective-permute-start.1 = (s32[144]{0:T(256)S(1)}, s32[144]{0:T(256)S(1)}, u32[]{:S(2)}, u32[]{:S(2)}) collective-permute-start(s32[144]{0:T(256)S(1)} %get-tuple-element.367), channel_id=1, source_target_pairs={{0,8},{8,16},{16,24},{24,32},{32,40},{40,48},{48,56},{56,64},{64,7... | collective-permute-start | bytes 1736 | tf_op jit(solution)/shard_map/while/body/eval_jaxpr/ppermute | solution.py:14
  69.9 7.8 %collective-permute-start = (bf16[144,2,512]{2,0,1:T(8,128)(2,1)S(1)}, bf16[144,2,512]{2,0,1:T(8,128)(2,1)S(1)}, u32[]{:S(2)}, u32[]{:S(2)}) collective-permute-start(bf16[144,2,512]{2,0,1:T(8,128)(2,1)S(1)} %get-tuple-element.366), channel_id=1, source_target_pairs={{0,8},{8,16},{16,24},{24,32},{32,40},{40,48},{48,56},{56,64},{64,7... | collective-permute-start | bytes 884744 | tf_op jit(solution)/shard_map/while/body/eval_jaxpr/ppermute | solution.py:14
  78.7 8.5 %collective-permute-start.1 = (s32[144]{0:T(256)S(1)}, s32[144]{0:T(256)S(1)}, u32[]{:S(2)}, u32[]{:S(2)}) collective-permute-start(s32[144]{0:T(256)S(1)} %get-tuple-element.367), channel_id=1, source_target_pairs={{0,8},{8,16},{16,24},{24,32},{32,40},{40,48},{48,56},{56,64},{64,7... | collective-permute-start | bytes 1736 | tf_op jit(solution)/shard_map/while/body/eval_jaxpr/ppermute | solution.py:14
  82.9 8.0 %collective-permute-start = (bf16[144,2,512]{2,0,1:T(8,128)(2,1)S(1)}, bf16[144,2,512]{2,0,1:T(8,128)(2,1)S(1)}, u32[]{:S(2)}, u32[]{:S(2)}) collective-permute-start(bf16[144,2,512]{2,0,1:T(8,128)(2,1)S(1)} %get-tuple-element.366), channel_id=1, source_target_pairs={{0,8},{8,16},{16,24},{24,32},{32,40},{40,48},{48,56},{56,64},{64,7... | collective-permute-start | bytes 884744 | tf_op jit(solution)/shard_map/while/body/eval_jaxpr/ppermute | solution.py:14
  91.8 8.3 %collective-permute-start.1 = (s32[144]{0:T(256)S(1)}, s32[144]{0:T(256)S(1)}, u32[]{:S(2)}, u32[]{:S(2)}) collective-permute-start(s32[144]{0:T(256)S(1)} %get-tuple-element.367), channel_id=1, source_target_pairs={{0,8},{8,16},{16,24},{24,32},{32,40},{40,48},{48,56},{56,64},{64,7... | collective-permute-start | bytes 1736 | tf_op jit(solution)/shard_map/while/body/eval_jaxpr/ppermute | solution.py:14
  96.0 8.5 %collective-permute-start = (bf16[144,2,512]{2,0,1:T(8,128)(2,1)S(1)}, bf16[144,2,512]{2,0,1:T(8,128)(2,1)S(1)}, u32[]{:S(2)}, u32[]{:S(2)}) collective-permute-start(bf16[144,2,512]{2,0,1:T(8,128)(2,1)S(1)} %get-tuple-element.366), channel_id=1, source_target_pairs={{0,8},{8,16},{16,24},{24,32},{32,40},{40,48},{48,56},{56,64},{64,7... | collective-permute-start | bytes 884744 | tf_op jit(solution)/shard_map/while/body/eval_jaxpr/ppermute | solution.py:14
  105.5 11.7 %collective-permute-start.1 = (s32[144]{0:T(256)S(1)}, s32[144]{0:T(256)S(1)}, u32[]{:S(2)}, u32[]{:S(2)}) collective-permute-start(s32[144]{0:T(256)S(1)} %get-tuple-element.367), channel_id=1, source_target_pairs={{0,8},{8,16},{16,24},{24,32},{32,40},{40,48},{48,56},{56,64},{64,7... | collective-permute-start | bytes 1736 | tf_op jit(solution)/shard_map/while/body/eval_jaxpr/ppermute | solution.py:14
  111.1 16.4 %collective-permute-start = (bf16[144,2,512]{2,0,1:T(8,128)(2,1)S(1)}, bf16[144,2,512]{2,0,1:T(8,128)(2,1)S(1)}, u32[]{:S(2)}, u32[]{:S(2)}) collective-permute-start(bf16[144,2,512]{2,0,1:T(8,128)(2,1)S(1)} %get-tuple-element.366), channel_id=1, source_target_pairs={{0,8},{8,16},{16,24},{24,32},{32,40},{40,48},{48,56},{56,64},{64,7... | collective-permute-start | bytes 884744 | tf_op jit(solution)/shard_map/while/body/eval_jaxpr/ppermute | solution.py:14
  128.4 8.4 %collective-permute-start.1 = (s32[144]{0:T(256)S(1)}, s32[144]{0:T(256)S(1)}, u32[]{:S(2)}, u32[]{:S(2)}) collective-permute-start(s32[144]{0:T(256)S(1)} %get-tuple-element.367), channel_id=1, source_target_pairs={{0,8},{8,16},{16,24},{24,32},{32,40},{40,48},{48,56},{56,64},{64,7... | collective-permute-start | bytes 1736 | tf_op jit(solution)/shard_map/while/body/eval_jaxpr/ppermute | solution.py:14
  132.7 13.4 %collective-permute-start = (bf16[144,2,512]{2,0,1:T(8,128)(2,1)S(1)}, bf16[144,2,512]{2,0,1:T(8,128)(2,1)S(1)}, u32[]{:S(2)}, u32[]{:S(2)}) collective-permute-start(bf16[144,2,512]{2,0,1:T(8,128)(2,1)S(1)} %get-tuple-element.366), channel_id=1, source_target_pairs={{0,8},{8,16},{16,24},{24,32},{32,40},{40,48},{48,56},{56,64},{64,7... | collective-permute-start | bytes 884744 | tf_op jit(solution)/shard_map/while/body/eval_jaxpr/ppermute | solution.py:14
  147.1 7.8 %collective-permute-start.1 = (s32[144]{0:T(256)S(1)}, s32[144]{0:T(256)S(1)}, u32[]{:S(2)}, u32[]{:S(2)}) collective-permute-start(s32[144]{0:T(256)S(1)} %get-tuple-element.367), channel_id=1, source_target_pairs={{0,8},{8,16},{16,24},{24,32},{32,40},{40,48},{48,56},{56,64},{64,7... | collective-permute-start | bytes 1736 | tf_op jit(solution)/shard_map/while/body/eval_jaxpr/ppermute | solution.py:14
  151.3 7.2 %collective-permute-start = (bf16[144,2,512]{2,0,1:T(8,128)(2,1)S(1)}, bf16[144,2,512]{2,0,1:T(8,128)(2,1)S(1)}, u32[]{:S(2)}, u32[]{:S(2)}) collective-permute-start(bf16[144,2,512]{2,0,1:T(8,128)(2,1)S(1)} %get-tuple-element.366), channel_id=1, source_target_pairs={{0,8},{8,16},{16,24},{24,32},{32,40},{40,48},{48,56},{56,64},{64,7... | collective-permute-start | bytes 884744 | tf_op jit(solution)/shard_map/while/body/eval_jaxpr/ppermute | solution.py:14
  159.5 8.5 %collective-permute-start.1 = (s32[144]{0:T(256)S(1)}, s32[144]{0:T(256)S(1)}, u32[]{:S(2)}, u32[]{:S(2)}) collective-permute-start(s32[144]{0:T(256)S(1)} %get-tuple-element.367), channel_id=1, source_target_pairs={{0,8},{8,16},{16,24},{24,32},{32,40},{40,48},{48,56},{56,64},{64,7... | collective-permute-start | bytes 1736 | tf_op jit(solution)/shard_map/while/body/eval_jaxpr/ppermute | solution.py:14
  163.7 7.9 %collective-permute-start = (bf16[144,2,512]{2,0,1:T(8,128)(2,1)S(1)}, bf16[144,2,512]{2,0,1:T(8,128)(2,1)S(1)}, u32[]{:S(2)}, u32[]{:S(2)}) collective-permute-start(bf16[144,2,512]{2,0,1:T(8,128)(2,1)S(1)} %get-tuple-element.366), channel_id=1, source_target_pairs={{0,8},{8,16},{16,24},{24,32},{32,40},{40,48},{48,56},{56,64},{64,7... | collective-permute-start | bytes 884744 | tf_op jit(solution)/shard_map/while/body/eval_jaxpr/ppermute | solution.py:14
  172.6 14.2 %collective-permute-start.1 = (s32[144]{0:T(256)S(1)}, s32[144]{0:T(256)S(1)}, u32[]{:S(2)}, u32[]{:S(2)}) collective-permute-start(s32[144]{0:T(256)S(1)} %get-tuple-element.367), channel_id=1, source_target_pairs={{0,8},{8,16},{16,24},{24,32},{32,40},{40,48},{48,56},{56,64},{64,7... | collective-permute-start | bytes 1736 | tf_op jit(solution)/shard_map/while/body/eval_jaxpr/ppermute | solution.py:14
  180.7 9.6 %collective-permute-start = (bf16[144,2,512]{2,0,1:T(8,128)(2,1)S(1)}, bf16[144,2,512]{2,0,1:T(8,128)(2,1)S(1)}, u32[]{:S(2)}, u32[]{:S(2)}) collective-permute-start(bf16[144,2,512]{2,0,1:T(8,128)(2,1)S(1)} %get-tuple-element.366), channel_id=1, source_target_pairs={{0,8},{8,16},{16,24},{24,32},{32,40},{40,48},{48,56},{56,64},{64,7... | collective-permute-start | bytes 884744 | tf_op jit(solution)/shard_map/while/body/eval_jaxpr/ppermute | solution.py:14
  191.3 8.3 %collective-permute-start.1 = (s32[144]{0:T(256)S(1)}, s32[144]{0:T(256)S(1)}, u32[]{:S(2)}, u32[]{:S(2)}) collective-permute-start(s32[144]{0:T(256)S(1)} %get-tuple-element.367), channel_id=1, source_target_pairs={{0,8},{8,16},{16,24},{24,32},{32,40},{40,48},{48,56},{56,64},{64,7... | collective-permute-start | bytes 1736 | tf_op jit(solution)/shard_map/while/body/eval_jaxpr/ppermute | solution.py:14
  195.2 9.6 %collective-permute-start = (bf16[144,2,512]{2,0,1:T(8,128)(2,1)S(1)}, bf16[144,2,512]{2,0,1:T(8,128)(2,1)S(1)}, u32[]{:S(2)}, u32[]{:S(2)}) collective-permute-start(bf16[144,2,512]{2,0,1:T(8,128)(2,1)S(1)} %get-tuple-element.366), channel_id=1, source_target_pairs={{0,8},{8,16},{16,24},{24,32},{32,40},{40,48},{48,56},{56,64},{64,7... | collective-permute-start | bytes 884744 | tf_op jit(solution)/shard_map/while/body/eval_jaxpr/ppermute | solution.py:14
  205.7 13.8 %collective-permute-start.1 = (s32[144]{0:T(256)S(1)}, s32[144]{0:T(256)S(1)}, u32[]{:S(2)}, u32[]{:S(2)}) collective-permute-start(s32[144]{0:T(256)S(1)} %get-tuple-element.367), channel_id=1, source_target_pairs={{0,8},{8,16},{16,24},{24,32},{32,40},{40,48},{48,56},{56,64},{64,7... | collective-permute-start | bytes 1736 | tf_op jit(solution)/shard_map/while/body/eval_jaxpr/ppermute | solution.py:14
  213.2 10.3 %collective-permute-start = (bf16[144,2,512]{2,0,1:T(8,128)(2,1)S(1)}, bf16[144,2,512]{2,0,1:T(8,128)(2,1)S(1)}, u32[]{:S(2)}, u32[]{:S(2)}) collective-permute-start(bf16[144,2,512]{2,0,1:T(8,128)(2,1)S(1)} %get-tuple-element.366), channel_id=1, source_target_pairs={{0,8},{8,16},{16,24},{24,32},{32,40},{40,48},{48,56},{56,64},{64,7... | collective-permute-start | bytes 884744 | tf_op jit(solution)/shard_map/while/body/eval_jaxpr/ppermute | solution.py:14
  224.6 9.3 %collective-permute-start.1 = (s32[144]{0:T(256)S(1)}, s32[144]{0:T(256)S(1)}, u32[]{:S(2)}, u32[]{:S(2)}) collective-permute-start(s32[144]{0:T(256)S(1)} %get-tuple-element.367), channel_id=1, source_target_pairs={{0,8},{8,16},{16,24},{24,32},{32,40},{40,48},{48,56},{56,64},{64,7... | collective-permute-start | bytes 1736 | tf_op jit(solution)/shard_map/while/body/eval_jaxpr/ppermute | solution.py:14
  228.7 8.8 %collective-permute-start = (bf16[144,2,512]{2,0,1:T(8,128)(2,1)S(1)}, bf16[144,2,512]{2,0,1:T(8,128)(2,1)S(1)}, u32[]{:S(2)}, u32[]{:S(2)}) collective-permute-start(bf16[144,2,512]{2,0,1:T(8,128)(2,1)S(1)} %get-tuple-element.366), channel_id=1, source_target_pairs={{0,8},{8,16},{16,24},{24,32},{32,40},{40,48},{48,56},{56,64},{64,7... | collective-permute-start | bytes 884744 | tf_op jit(solution)/shard_map/while/body/eval_jaxpr/ppermute | solution.py:14
  244.2 3.0 copy-start.1
Sparse Core Ops, SparseCore 0:
  11.0 162.0 all-gather.1
  247.3 75.8 reduce-scatter.3
where the time goes:
time: 334 us; the launch traced here: 332 us
  waiting for transfers between devices  145 us (43%)
  starting transfers between devices  139 us (42%)
  matrix products  16 us (5%)
  between operations  14.1 us (4%)
  local copies, waits for them, and re-layouts  11.1 us (3%)
  other arithmetic  5.01 us (2%)
    ppermute x30, starting transfers between devices, from_behind(): lax.ppermute(value, axis, [(source, source + steps) for source in range(i...  139 us
    unnamed x3, waiting for transfers between devices  75.7 us
    ppermute x30, waiting for transfers between devices, from_behind(): lax.ppermute(value, axis, [(source, source + steps) for source in range(i...  69.5 us
  transfers between devices with their start and end apart: 32, of which 16 were waited for; matrix products, arithmetic and copies ran while one was open for 6% of the time, Pallas kernels for 0%

commit v1 on v0

v1 whole, which is shorter than its diff:
```python
import math

import jax
import jax.numpy as jnp
from jax import lax
from jax.sharding import Mesh
from jax.sharding import PartitionSpec as P

HD = 128
NY = 4


def local(queries, keys_values, segment_ids, out_weight):
    rows = queries.shape[0]
    heads = queries.shape[1] // HD
    nz = lax.axis_size("z")
    z = lax.axis_index("z")
    level = NY * rows
    span = min(4, nz - 1)
    score_scale = 1.0 / math.sqrt(HD)

    packed = jnp.concatenate(
        [queries.reshape(rows, 1, heads, HD), keys_values.reshape(rows, 2, heads, HD)], axis=1
    ).reshape(rows, 3, NY, heads // NY, HD)
    packed = lax.all_to_all(packed, "y", 2, 0, tiled=True)
    hq = heads // NY
    query_rows = packed[:, 0, 0]
    pair = packed[:, 1:, 0]

    all_seg = lax.all_gather(segment_ids, ("z", "y"), tiled=True)
    offsets = jnp.arange(level, dtype=jnp.int32)
    query_pos = z * level + offsets
    query_seg = lax.dynamic_slice_in_dim(all_seg, z * level, level)

    def attend(carried, block, distance):
        run_max, row_total, accumulated = carried
        source = z - distance
        key_pos = source * level + offsets
        key_seg = lax.dynamic_slice_in_dim(all_seg, jnp.maximum(source, 0) * level, level)
        key_rows = block[:, 0]
        value_rows = block[:, 1]
        scores = (
            jnp.einsum("qhd,khd->hqk", query_rows, key_rows, preferred_element_type=jnp.float32)
            * score_scale
        )
        allowed = (
            (key_seg[None, :] == query_seg[:, None])
            & (key_pos[None, :] <= query_pos[:, None])
            & (source >= 0)
        )
        masked = jnp.where(allowed[None], scores, -1e30)
        new_max = jnp.maximum(run_max, jnp.max(masked, axis=2))
        probs = jnp.where(allowed[None], jnp.exp(masked - new_max[..., None]), 0.0)
        factor = jnp.exp(run_max - new_max)
        row_total = row_total * factor + jnp.sum(probs, axis=2)
        accumulated = accumulated * factor[..., None] + jnp.einsum(
            "hqk,khd->hqd",
            probs.astype(jnp.bfloat16),
            value_rows,
            preferred_element_type=jnp.float32,
        )
        return (new_max, row_total, accumulated)

    carried = (
        jnp.full((hq, level), -1e30, jnp.float32),
        jnp.zeros((hq, level), jnp.float32),
        jnp.zeros((hq, level, HD), jnp.float32),
    )
    carried = attend(carried, pair, 0)
    block = pair
    for distance in range(1, span + 1):
        block = lax.ppermute(block, "z", [(i, i + 1) for i in range(nz - 1)])
        carried = attend(carried, block, distance)
    run_max, row_total, accumulated = carried
    attended = (accumulated / row_total[..., None]).astype(jnp.bfloat16)
    attended = attended.transpose(1, 0, 2).reshape(level, hq * HD)

    level_attended = lax.all_gather(attended, "y", axis=1, tiled=True)
    weight_cols = lax.all_gather(out_weight, "z", axis=1, tiled=True)
    partial_value = jnp.dot(level_attended, weight_cols, preferred_element_type=jnp.float32)
    summed = lax.psum_scatter(
        partial_value.astype(jnp.bfloat16), "tensor", scatter_dimension=1, tiled=True
    )
    chunk = out_weight.shape[1]
    halves = summed.shape[1] // chunk
    summed = summed.reshape(NY, rows, halves, chunk)
    summed = lax.all_to_all(summed, "y", 0, 0, tiled=True)
    hidden_states = summed.transpose(1, 2, 0, 3).reshape(rows, halves * NY * chunk)

    head_major = keys_values.reshape(rows, 2, heads, HD).transpose(1, 2, 0, 3)
    return (hidden_states, head_major)


def solution(mesh):
    seq, tensor = mesh.shape["seq"], mesh.shape["tensor"]
    assert seq % NY == 0
    grid = Mesh(mesh.devices.reshape(seq // NY, NY, tensor), ("z", "y", "tensor"))
    s = ("z", "y")
    return jax.shard_map(
        local,
        mesh=grid,
        in_specs=(P(s, "tensor"), P(s, None, "tensor"), P(s), P("tensor", s)),
        out_specs=(P(s, "tensor"), P(None, "tensor", s, None)),
        check_vma=False,
    )
```

time: 334 us -> 426 us (1.28)
  blocking collectives: 0 us -> 248 us
  starting transfers between devices: 139 us -> 16.9 us
  waiting for transfers between devices: 145 us -> 121 us
  matrix products: 16 us -> 11.6 us
    unnamed x0 -> x1, blocking collectives: none -> 226 us
    ppermute x30 -> x4, starting transfers between devices: 139 us -> 13.4 us  [local(): block = lax.ppermute(block, 'z', [(i, i + 1) for i in range(nz - 1)])]
    reduce_scatter x0 -> x1, waiting for transfers between devices: none -> 107 us  [local(): lax.psum_scatter(partial_value.astype(jnp.bfloat16), 'tensor', scatter_di...]
    unnamed x3 -> x2, waiting for transfers between devices: 75.7 us -> 0.03 us
    ppermute x30 -> x4, waiting for transfers between devices: 69.5 us -> 8.32 us  [local(): block = lax.ppermute(block, 'z', [(i, i + 1) for i in range(nz - 1)])]
    all_to_all x0 -> x1, blocking collectives: none -> 11.3 us  [local(): packed = lax.all_to_all(packed, 'y', 2, 0, tiled=True)]
    all_gather x0 -> x1, blocking collectives: none -> 10.2 us  [local(): level_attended = lax.all_gather(attended, 'y', axis=1, tiled=True)]
    all_to_all x0 -> x1, waiting for transfers between devices: none -> 4.91 us  [local(): summed = lax.all_to_all(summed, 'y', 0, 0, tiled=True)]
  transfers between devices with their start and end apart: 32 -> 7, of which waited for: 16 -> 5; matrix products, arithmetic and copies ran while one was open for 6% -> 3% of each run, Pallas kernels for 0% -> 0%
where the time goes in v1:
time: 426 us; the launch traced here: 423 us
  blocking collectives  248 us (58%)
  waiting for transfers between devices  121 us (28%)
  starting transfers between devices  16.9 us (4%)
  between operations  14.9 us (3%)
  matrix products  11.6 us (3%)
  local copies, waits for them, and re-layouts  7.81 us (2%)
    unnamed x1, blocking collectives  226 us
    reduce_scatter x1, waiting for transfers between devices, local(): lax.psum_scatter(partial_value.astype(jnp.bfloat16), 'tensor', scatter_di...  107 us
    ppermute x4, starting transfers between devices, local(): block = lax.ppermute(block, 'z', [(i, i + 1) for i in range(nz - 1)])  13.4 us
    all_to_all x1, blocking collectives, local(): packed = lax.all_to_all(packed, 'y', 2, 0, tiled=True)  11.3 us
    all_gather x1, blocking collectives, local(): level_attended = lax.all_gather(attended, 'y', axis=1, tiled=True)  10.2 us
  transfers between devices with their start and end apart: 7, of which 5 were waited for; matrix products, arithmetic and copies ran while one was open for 3% of the time, Pallas kernels for 0%

profile of v1, /device:TPU:1, one launch (start us, length us, event | category | flops | bytes accessed | tf_op | source)
XLA Modules:
  0.0 423.3 jit_solution(16696719570066418822)
XLA Ops:
  7.2 0.0 all-gather.2.cloned.1.call-start
  7.2 1.2 reshape.400
  8.4 1.0 reshape.379
  9.3 0.2 maximum_bitcast_fusion
  9.5 0.1 copy.16
  9.6 0.0 copy-start
  9.6 11.3 %all_to_all.23 = bf16[144,3,4,1,128]{4,0,1,3,2:T(8,128)(2,1)S(1)} all-to-all(bf16[144,3,4,1,128]{4,0,1,3,2:T(8,128)(2,1)S(1)} %copy.16), channel_id=1, replica_groups=mesh['z'=16,'y'=4,'tensor'=8] {'y'}, dimensions={2} | all-to-all | bytes 884736 | tf_op jit(solution)/shard_map/all_to_all | solution.py:25
  21.0 4.5 %collective-permute-start = (bf16[576,2,1,128]{3,0,2,1:T(8,128)(2,1)S(1)}, bf16[576,2,1,128]{3,0,2,1:T(8,128)(2,1)S(1)}, u32[]{:S(2)}, u32[]{:S(2)}) collective-permute-start(bf16[576,2,1,128]{3,0,2,1:T(8,128)(2,1)S(1)} %slice_bitcast_fusion), channel_id=1, source_target_pairs={{0,32},{32,64},{64,96},{96,128},{128,160},{160,192},{192,224},{224... | collective-permute-start | bytes 884744 | tf_op jit(solution)/shard_map/ppermute | solution.py:72
  25.4 0.0 all-gather.2.cloned.1.call-update
  25.5 0.0 reduce-scatter.2.cloned.1.call-start
  25.5 1.3 dynamic-slice
  27.5 0.0 copy-done
  27.5 0.3 dynamic-update-slice
  27.8 226.4 %all-reduce = s32[9216]{0:T(1024)S(1)} all-reduce(s32[9216]{0:T(1024)S(1)} %dynamic-update-slice), channel_id=1, replica_groups=mesh['z'=16,'y'=4,'tensor'=8] {'z','y'}, use_global_device_ids=true, to_apply=%add | all-reduce | flops 9216 | bytes 73728
  254.1 0.0 collective-permute-done
  254.1 1.3 collective-permute-start.1
  255.5 0.1 fusion.39
  255.6 3.5 collective-permute-done.1
  259.1 3.8 collective-permute-start.2
  262.9 0.6 fusion.44
  263.5 0.6 fusion.43
  264.1 2.4 collective-permute-done.2
  266.6 3.8 collective-permute-start.3
  270.4 0.6 fusion.42
  271.0 0.6 fusion.41
  271.6 2.4 collective-permute-done.3
  274.0 0.6 fusion.40
  274.6 1.3 fusion.8
  275.9 1.9 fusion.6
  277.9 0.9 fusion
  278.8 0.8 fusion.1
  279.6 0.8 fusion.2
  280.4 0.8 fusion.3
  281.2 0.8 fusion.5
  282.0 10.2 %all_gather.10 = bf16[576,512]{1,0:T(8,128)(2,1)S(1)} all-gather(bf16[576,128]{1,0:T(8,128)(2,1)S(1)} %fusion.5), channel_id=1, replica_groups=mesh['z'=16,'y'=4,'tensor'=8] {'y'}, dimensions={1}, use_global_device_ids=true | all-gather | bytes 737280 | tf_op jit(solution)/shard_map/all_gather | solution.py:78
  292.2 0.0 all-gather.2.cloned.1.call-done
  292.2 4.5 %convolution_convert_fusion = bf16[576,1792]{0,1:T(8,128)(2,1)} fusion(bf16[576,512]{1,0:T(8,128)(2,1)S(1)} %all_gather.10, bf16[512,1792]{0,1:T(8,128)(2,1)} %all-gather.2.cloned.1.call-done), kind=kOutput, calls=%fused_computation | convolution fusion | flops 1057996800 | bytes 4489216 | tf_op jit(solution)/shard_map/dot_general | solution.py:80
  296.7 0.0 reduce-scatter.2.cloned.1.call-update
  296.7 107.4 %reduce-scatter.2.cloned.1.call-done = bf16[576,224]{0,1:T(8,128)(2,1)} async-done(((bf16[576,1792]{0,1:T(8,128)(2,1)}), bf16[576,224]{0,1:T(8,128)(2,1)}) %reduce-scatter.2.cloned.1.call-update) | async-done | bytes 258064 | tf_op jit(solution)/shard_map/reduce_scatter | solution.py:81
  404.1 1.1 copy.18
  405.2 0.9 reshape.393
  406.1 3.5 all-to-all-start.1
  409.6 0.8 copy.20
  410.3 4.9 %all-to-all-done.1 = bf16[4,144,2,112]{3,2,1,0:T(2,128)(2,1)S(1)} async-done(((bf16[4,144,2,112]{3,2,1,0:T(2,128)(2,1)}), bf16[4,144,2,112]{3,2,1,0:T(2,128)(2,1)S(1)}, u32[]{:S(2)}, u32[]{:S(2)}) %all-to-all-start.1) | async-done | bytes 258080 | tf_op jit(solution)/shard_map/all_to_all | solution.py:87
  415.2 0.2 copy.19
  415.5 0.9 reshape.394
  (9 shorter events, 0.1 us)
Async XLA Ops:
  7.2 285.0 %all-gather.2.cloned.1.call-start = ((), (), s32[]{:S(2)}) async-start(), calls=%async_computation.3 | async-start | bytes 1949696 | tf_op jit(solution)/shard_map/all_gather | solution.py:79
  9.6 17.9 %copy-start = (s32[144]{0:T(256)S(1)}, s32[144]{0:T(256)}, u32[]{:S(2)}) copy-start(s32[144]{0:T(256)} %param.6) | copy-start | bytes 1732
  21.0 233.2 %collective-permute-start = (bf16[576,2,1,128]{3,0,2,1:T(8,128)(2,1)S(1)}, bf16[576,2,1,128]{3,0,2,1:T(8,128)(2,1)S(1)}, u32[]{:S(2)}, u32[]{:S(2)}) collective-permute-start(bf16[576,2,1,128]{3,0,2,1:T(8,128)(2,1)S(1)} %slice_bitcast_fusion), channel_id=1, source_target_pairs={{0,32},{32,64},{64,96},{96,128},{128,160},{160,192},{192,224},{224... | collective-permute-start | bytes 884744 | tf_op jit(solution)/shard_map/ppermute | solution.py:72
  25.5 378.6 %reduce-scatter.2.cloned.1.call-start = ((), (), s32[]{:S(2)}) async-start(), calls=%async_computation.4 | async-start | bytes 2580480 | tf_op jit(solution)/shard_map/reduce_scatter | solution.py:81
  254.1 4.9 %collective-permute-start.1 = (bf16[576,2,1,128]{3,0,2,1:T(8,128)(2,1)S(1)}, bf16[576,2,1,128]{3,0,2,1:T(8,128)(2,1)S(1)}, u32[]{:S(2)}, u32[]{:S(2)}) collective-permute-start(bf16[576,2,1,128]{3,0,2,1:T(8,128)(2,1)S(1)} %collective-permute-done), channel_id=1, source_target_pairs={{0,32},{32,64},{64,96},{96,128},{128,160},{160,192},{192,224},{224... | collective-permute-start | bytes 884744 | tf_op jit(solution)/shard_map/ppermute | solution.py:72
  259.1 7.5 %collective-permute-start.2 = (bf16[576,2,1,128]{3,0,2,1:T(8,128)(2,1)S(1)}, bf16[576,2,1,128]{3,0,2,1:T(8,128)(2,1)S(1)}, u32[]{:S(2)}, u32[]{:S(2)}) collective-permute-start(bf16[576,2,1,128]{3,0,2,1:T(8,128)(2,1)S(1)} %collective-permute-done.1), channel_id=1, source_target_pairs={{0,32},{32,64},{64,96},{96,128},{128,160},{160,192},{192,224},{224... | collective-permute-start | bytes 884744 | tf_op jit(solution)/shard_map/ppermute | solution.py:72
  266.6 7.5 %collective-permute-start.3 = (bf16[576,2,1,128]{3,0,2,1:T(8,128)(2,1)S(1)}, bf16[576,2,1,128]{3,0,2,1:T(8,128)(2,1)S(1)}, u32[]{:S(2)}, u32[]{:S(2)}) collective-permute-start(bf16[576,2,1,128]{3,0,2,1:T(8,128)(2,1)S(1)} %collective-permute-done.2), channel_id=1, source_target_pairs={{0,32},{32,64},{64,96},{96,128},{128,160},{160,192},{192,224},{224... | collective-permute-start | bytes 884744 | tf_op jit(solution)/shard_map/ppermute | solution.py:72
  406.1 9.1 %all-to-all-start.1 = ((bf16[4,144,2,112]{3,2,1,0:T(2,128)(2,1)}), bf16[4,144,2,112]{3,2,1,0:T(2,128)(2,1)S(1)}, u32[]{:S(2)}, u32[]{:S(2)}) async-start(bf16[4,144,2,112]{3,2,1,0:T(2,128)(2,1)} %reshape.393), calls=%async_computation.2 | async-start | bytes 589824 | tf_op jit(solution)/shard_map/all_to_all | solution.py:87
Sparse Core Ops, SparseCore 0:
  25.6 66.9 all-gather.1
  296.9 107.2 reduce-scatter.1

commit v2 on v1

--- a/solution.py
+++ b/solution.py
@@ -19,26 +19,32 @@
     span = min(4, nz - 1)
     score_scale = 1.0 / math.sqrt(HD)
 
+    hq = heads // NY
     packed = jnp.concatenate(
         [queries.reshape(rows, 1, heads, HD), keys_values.reshape(rows, 2, heads, HD)], axis=1
-    ).reshape(rows, 3, NY, heads // NY, HD)
-    packed = lax.all_to_all(packed, "y", 2, 0, tiled=True)
-    hq = heads // NY
-    query_rows = packed[:, 0, 0]
-    pair = packed[:, 1:, 0]
+    ).reshape(rows, 3, NY, hq, HD)
+    seg_row = jnp.zeros((3 * hq * HD,), jnp.bfloat16).at[:rows].set(segment_ids.astype(jnp.bfloat16))
+    seg_row = jnp.broadcast_to(seg_row.reshape(1, 3, 1, hq, HD), (1, 3, NY, hq, HD))
+    packed = jnp.concatenate([packed, seg_row], axis=0)
+    packed = lax.all_to_all(packed, "y", 2, 0, tiled=True).reshape(NY, rows + 1, 3, hq, HD)
+    query_rows = packed[:, :rows, 0].reshape(level, hq, HD)
+    pair = packed[:, :rows, 1:].reshape(level, 2, hq, HD)
+    query_seg = packed[:, rows].reshape(NY, 3 * hq * HD)[:, :rows].reshape(level)
 
-    all_seg = lax.all_gather(segment_ids, ("z", "y"), tiled=True)
+    extra = -(-level // (2 * hq * HD))
+    seg_rows = jnp.zeros((extra * 2 * hq * HD,), jnp.bfloat16).at[:level].set(query_seg)
+    pair = jnp.concatenate([pair, seg_rows.reshape(extra, 2, hq, HD)], axis=0)
+    query_seg = query_seg.astype(jnp.int32)
     offsets = jnp.arange(level, dtype=jnp.int32)
     query_pos = z * level + offsets
-    query_seg = lax.dynamic_slice_in_dim(all_seg, z * level, level)
 
     def attend(carried, block, distance):
         run_max, row_total, accumulated = carried
         source = z - distance
         key_pos = source * level + offsets
-        key_seg = lax.dynamic_slice_in_dim(all_seg, jnp.maximum(source, 0) * level, level)
-        key_rows = block[:, 0]
-        value_rows = block[:, 1]
+        key_seg = block[level:].reshape(-1)[:level].astype(jnp.int32)
+        key_rows = block[:level, 0]
+        value_rows = block[:level, 1]
         scores = (
             jnp.einsum("qhd,khd->hqk", query_rows, key_rows, preferred_element_type=jnp.float32)
             * score_scale

time: 426 us -> 177 us (0.42)
  blocking collectives: 248 us -> 10.7 us
  waiting for transfers between devices: 121 us -> 78.4 us
  matrix products: 11.6 us -> 22.7 us
  starting transfers between devices: 16.9 us -> 27.1 us
  local copies, waits for them, and re-layouts: 7.81 us -> 13.5 us
    unnamed x1 -> x0, blocking collectives: 226 us -> none
    reduce_scatter x1, waiting for transfers between devices: 107 us -> 59.7 us  [local(): lax.psum_scatter(partial_value.astype(jnp.bfloat16), 'tensor', scatter_di...]
    all_to_all x1 -> x0, blocking collectives: 11.3 us -> none  [local(): packed = lax.all_to_all(packed, 'y', 2, 0, tiled=True)]
    dot_general x5, matrix products: 3.01 us -> 10.5 us  [attend(): jnp.einsum('qhd,khd->hqk', query_rows, key_rows, preferred_element_type=j...]
    ppermute x4, starting transfers between devices: 13.4 us -> 18.6 us  [local(): block = lax.ppermute(block, 'z', [(i, i + 1) for i in range(nz - 1)])]
    all_to_all x0 -> x1, starting transfers between devices: none -> 5.01 us  [local(): lax.all_to_all(packed, 'y', 2, 0, tiled=True)]
    all_to_all x0 -> x1, waiting for transfers between devices: none -> 4.66 us  [local(): lax.all_to_all(packed, 'y', 2, 0, tiled=True)]
  transfers between devices with their start and end apart: 7 -> 8, of which waited for: 5 -> 8; matrix products, arithmetic and copies ran while one was open for 3% -> 17% of each run, Pallas kernels for 0% -> 0%
where the time goes in v2:
time: 177 us; the launch traced here: 174 us
  waiting for transfers between devices  78.4 us (44%)
  starting transfers between devices  27.1 us (15%)
  matrix products  22.7 us (13%)
  between operations  14.4 us (8%)
  local copies, waits for them, and re-layouts  13.5 us (8%)
  blocking collectives  10.7 us (6%)
  other arithmetic  6.9 us (4%)
    reduce_scatter x1, waiting for transfers between devices, local(): lax.psum_scatter(partial_value.astype(jnp.bfloat16), 'tensor', scatter_di...  59.7 us
    ppermute x4, starting transfers between devices, local(): block = lax.ppermute(block, 'z', [(i, i + 1) for i in range(nz - 1)])  18.6 us
    all_gather x1, blocking collectives, local(): level_attended = lax.all_gather(attended, 'y', axis=1, tiled=True)  10.7 us
    dot_general x5, matrix products, attend(): jnp.einsum('qhd,khd->hqk', query_rows, key_rows, preferred_element_type=j...  10.5 us
    dot_general x5, matrix products, attend(): jnp.einsum('hqk,khd->hqd', probs.astype(jnp.bfloat16), value_rows, prefer...  7.63 us
    ppermute x4, waiting for transfers between devices, local(): block = lax.ppermute(block, 'z', [(i, i + 1) for i in range(nz - 1)])  7.49 us
    all_to_all x1, starting transfers between devices, local(): lax.all_to_all(packed, 'y', 2, 0, tiled=True)  5.01 us
    all_to_all x1, waiting for transfers between devices, local(): summed = lax.all_to_all(summed, 'y', 0, 0, tiled=True)  4.91 us
  transfers between devices with their start and end apart: 8, of which 8 were waited for; matrix products, arithmetic and copies ran while one was open for 17% of the time, Pallas kernels for 0%

profile of v2, /device:TPU:1, one launch (start us, length us, event | category | flops | bytes accessed | tf_op | source)
XLA Modules:
  0.0 173.7 jit_solution(7307379911061566046)
XLA Ops:
  7.2 1.2 reshape.474
  8.3 1.0 reshape.451
  9.3 0.7 convert_element_type.50
  10.4 0.9 copy.22
  11.2 5.0 %all-to-all-start = ((bf16[145,3,4,1,128]{4,0,1,3,2:T(8,128)(2,1)}), bf16[145,3,4,1,128]{4,0,1,3,2:T(8,128)(2,1)S(1)}, u32[]{:S(2)}, u32[]{:S(2)}) async-start(bf16[145,3,4,1,128]{4,0,1,3,2:T(8,128)(2,1)} %copy.22), calls=%async_computation | async-start | bytes 933888 | tf_op jit(solution)/shard_map/all_to_all | solution.py:29
  16.2 0.7 all-gather.2.cloned.1.call-update
  17.0 0.6 iota_add_fusion
  17.6 0.6 iota_add_fusion.1
  18.2 4.7 %all-to-all-done = bf16[145,3,4,1,128]{4,0,1,3,2:T(8,128)(2,1)S(1)} async-done(((bf16[145,3,4,1,128]{4,0,1,3,2:T(8,128)(2,1)}), bf16[145,3,4,1,128]{4,0,1,3,2:T(8,128)(2,1)S(1)}, u32[]{:S(2)}, u32[]{:S(2)}) %all-to-all-start) | async-done | bytes 445472 | tf_op jit(solution)/shard_map/all_to_all | solution.py:29
  23.1 4.6 %collective-permute-start = (bf16[579,2,1,128]{3,0,1,2:T(8,128)(2,1)S(1)}, bf16[579,2,1,128]{3,0,1,2:T(8,128)(2,1)S(1)}, u32[]{:S(2)}, u32[]{:S(2)}) collective-permute-start(bf16[579,2,1,128]{3,0,1,2:T(8,128)(2,1)S(1)} %pad_maximum_fusion.1), channel_id=1, source_target_pairs={{0,32},{32,64},{64,96},{96,128},{128,160},{160,192},{192,224},{224... | collective-permute-start | bytes 889352 | tf_op jit(solution)/shard_map/ppermute | solution.py:78
  27.8 2.3 %fusion.43 = (f32[576]{0:T(1024)}, f32[576,576]{0,1:T(8,128)}) fusion(bf16[576,128]{1,0:T(8,128)(2,1)S(1)} %bitcast.82, bf16[576,2,1,128]{3,0,1,2:T(8,128)(2,1)S(1)} %bitcast.79, pred[]{:T(512)S(6)} %ge.15, s32[576]{0:T(1024)S(1)} %get-tuple-element.59, s32[576]{0:T(1024)S(1)} %convert_element_type.51), kind=kOutput, calls=%fused_computation.90 | convolution fusion | flops 87256512 | bytes 1640705 | tf_op jit(solution)/shard_map/qhd,khd->hqk/dot_general | solution.py:49
  30.1 1.3 collective-permute-done
  31.4 4.8 %collective-permute-start.1 = (bf16[579,2,1,128]{3,0,1,2:T(8,128)(2,1)S(1)}, bf16[579,2,1,128]{3,0,1,2:T(8,128)(2,1)}, u32[]{:S(2)}, u32[]{:S(2)}) collective-permute-start(bf16[579,2,1,128]{3,0,1,2:T(8,128)(2,1)S(1)} %collective-permute-done), channel_id=1, source_target_pairs={{0,32},{32,64},{64,96},{96,128},{128,160},{160,192},{192,224},{224... | collective-permute-start | bytes 889352 | tf_op jit(solution)/shard_map/ppermute | solution.py:78
  36.3 1.2 fusion.42
  37.4 1.8 %collective-permute-done.1 = bf16[579,2,1,128]{3,0,1,2:T(8,128)(2,1)} collective-permute-done((bf16[579,2,1,128]{3,0,1,2:T(8,128)(2,1)S(1)}, bf16[579,2,1,128]{3,0,1,2:T(8,128)(2,1)}, u32[]{:S(2)}, u32[]{:S(2)}) %collective-permute-start.1) | collective-permute-done | bytes 296480 | tf_op jit(solution)/shard_map/ppermute | solution.py:78
  39.2 0.7 slice.123
  39.9 4.1 %collective-permute-start.2 = (bf16[579,2,1,128]{3,0,1,2:T(8,128)(2,1)}, bf16[579,2,1,128]{3,0,1,2:T(8,128)(2,1)S(1)}, u32[]{:S(2)}, u32[]{:S(2)}) collective-permute-start(bf16[579,2,1,128]{3,0,1,2:T(8,128)(2,1)} %collective-permute-done.1), channel_id=1, source_target_pairs={{0,32},{32,64},{64,96},{96,128},{128,160},{160,192},{192,224},{224... | collective-permute-start | bytes 889352 | tf_op jit(solution)/shard_map/ppermute | solution.py:78
  44.1 2.2 %fusion.41 = (f32[576]{0:T(1024)}, f32[576,576]{0,1:T(8,128)S(1)}) fusion(bf16[576,128]{1,0:T(8,128)(2,1)} %bitcast.84, bf16[579,2,1,128]{3,0,1,2:T(8,128)(2,1)} %collective-permute-done.1, pred[]{:T(512)S(6)} %ge.17, s32[576]{0:T(1024)S(1)} %get-tuple-element.59, s32[576]{0:T(1024)S(1)} %iota_add_fusion.2, s32[576]{0:T(1024)S(1)} %convert_element_type.51, ...), kind=kOutput, calls=%fused_computation.88 | convolution fusion | flops 87256512 | bytes 1633537 | tf_op jit(solution)/shard_map/qhd,khd->hqk/dot_general | solution.py:49
  46.2 3.2 %collective-permute-done.2 = bf16[579,2,1,128]{3,0,1,2:T(8,128)(2,1)S(1)} collective-permute-done((bf16[579,2,1,128]{3,0,1,2:T(8,128)(2,1)}, bf16[579,2,1,128]{3,0,1,2:T(8,128)(2,1)S(1)}, u32[]{:S(2)}, u32[]{:S(2)}) %collective-permute-start.2) | collective-permute-done | bytes 296480 | tf_op jit(solution)/shard_map/ppermute | solution.py:78
  49.4 0.7 copy-done.16
  50.1 0.6 copy.28
  50.7 1.3 reshape.466
  52.0 5.1 %collective-permute-start.3 = (bf16[579,2,1,128]{3,0,1,2:T(8,128)(2,1)}, bf16[579,2,1,128]{3,0,1,2:T(8,128)(2,1)S(1)}, u32[]{:S(2)}, u32[]{:S(2)}) collective-permute-start(bf16[579,2,1,128]{3,0,1,2:T(8,128)(2,1)} %copy-done.16), channel_id=1, source_target_pairs={{0,32},{32,64},{64,96},{96,128},{128,160},{160,192},{192,224},{224... | collective-permute-start | bytes 889352 | tf_op jit(solution)/shard_map/ppermute | solution.py:78
  57.1 0.7 slice_convert_fusion.1
  57.8 3.3 %fusion.40 = (f32[576]{0:T(1024)}, f32[576,576]{0,1:T(8,128)}) fusion(bf16[576,128]{1,0:T(8,128)(2,1)} %bitcast.85, bf16[579,2,1,128]{3,0,1,2:T(8,128)(2,1)} %copy-done.16, pred[]{:T(512)S(6)} %ge.18, s32[576]{0:T(1024)S(1)} %get-tuple-element.59, s32[576]{0:T(1024)} %get-tuple-element.58, s32[576]{0:T(1024)S(1)} %convert_element_type.51, ...), kind=kOutput, calls=%fused_computation.87 | convolution fusion | flops 87256512 | bytes 1635329 | tf_op jit(solution)/shard_map/qhd,khd->hqk/dot_general | solution.py:49
  61.1 1.3 collective-permute-done.3
  62.3 0.7 copy-done.17
  63.0 0.6 copy.29
  63.6 1.2 reshape.469
  64.9 0.7 slice_convert_fusion
  65.6 1.6 fusion.39
  67.3 1.3 fusion.8
  69.1 1.9 %fusion.6 = (f32[576]{0:T(1024)S(1)}, f32[576]{0:T(1024)S(1)}, f32[576]{0:T(1024)S(1)}) fusion(f32[576,576]{0,1:T(8,128)S(1)} %copy-done, f32[576]{0:T(1024)S(1)} %get-tuple-element.47, pred[]{:T(512)S(6)} %ge.15, s32[576]{0:T(1024)S(1)} %get-tuple-element.59, s32[576]{0:T(1024)S(1)} %convert_element_type.51, f32[576,576]{0,1:T(8,128)S(1)} %get-tuple-element.49, ...), kind=kLoop, calls=%fused_computation.27 | loop fusion | flops 6965568 | bytes 4008963 | tf_op jit(solution)/shard_map/reduce_sum | solution.py:61
  71.1 0.9 fusion
  71.9 1.7 fusion.1
  73.6 1.7 fusion.2
  75.3 1.7 fusion.3
  77.0 1.7 fusion.5
  78.7 10.7 %all_gather.6 = bf16[576,512]{1,0:T(8,128)(2,1)S(1)} all-gather(bf16[576,128]{1,0:T(8,128)(2,1)S(1)} %fusion.5), channel_id=1, replica_groups=mesh['z'=16,'y'=4,'tensor'=8] {'y'}, dimensions={1}, use_global_device_ids=true | all-gather | bytes 737280 | tf_op jit(solution)/shard_map/all_gather | solution.py:84
  89.4 0.9 all-gather.2.cloned.1.call-done
  90.3 4.5 %convolution_convert_fusion = bf16[576,1792]{0,1:T(8,128)(2,1)} fusion(bf16[576,512]{1,0:T(8,128)(2,1)S(1)} %all_gather.6, bf16[512,1792]{0,1:T(8,128)(2,1)} %all-gather.2.cloned.1.call-done), kind=kOutput, calls=%fused_computation | convolution fusion | flops 1057996800 | bytes 4489216 | tf_op jit(solution)/shard_map/dot_general | solution.py:86
  94.8 59.7 %reduce-scatter.2.cloned.1.call-done = bf16[576,224]{0,1:T(8,128)(2,1)} async-done(((bf16[576,1792]{0,1:T(8,128)(2,1)}), bf16[576,224]{0,1:T(8,128)(2,1)}) %reduce-scatter.2.cloned.1.call-update) | async-done | bytes 258064 | tf_op jit(solution)/shard_map/reduce_scatter | solution.py:87
  154.5 1.1 copy.30
  155.6 0.9 reshape.472
  156.5 3.5 %all-to-all-start.1 = ((bf16[4,144,2,112]{3,2,1,0:T(2,128)(2,1)}), bf16[4,144,2,112]{3,2,1,0:T(2,128)(2,1)S(1)}, u32[]{:S(2)}, u32[]{:S(2)}) async-start(bf16[4,144,2,112]{3,2,1,0:T(2,128)(2,1)} %reshape.472), calls=%async_computation.2 | async-start | bytes 589824 | tf_op jit(solution)/shard_map/all_to_all | solution.py:93
  160.0 0.8 copy.32
  160.7 4.9 %all-to-all-done.1 = bf16[4,144,2,112]{3,2,1,0:T(2,128)(2,1)S(1)} async-done(((bf16[4,144,2,112]{3,2,1,0:T(2,128)(2,1)}), bf16[4,144,2,112]{3,2,1,0:T(2,128)(2,1)S(1)}, u32[]{:S(2)}, u32[]{:S(2)}) %all-to-all-start.1) | async-done | bytes 258080 | tf_op jit(solution)/shard_map/all_to_all | solution.py:93
  165.9 0.9 reshape.473
  (67 shorter events, 1.6 us)
Async XLA Ops:
  11.2 11.6 %all-to-all-start = ((bf16[145,3,4,1,128]{4,0,1,3,2:T(8,128)(2,1)}), bf16[145,3,4,1,128]{4,0,1,3,2:T(8,128)(2,1)S(1)}, u32[]{:S(2)}, u32[]{:S(2)}) async-start(bf16[145,3,4,1,128]{4,0,1,3,2:T(8,128)(2,1)} %copy.22), calls=%async_computation | async-start | bytes 933888 | tf_op jit(solution)/shard_map/all_to_all | solution.py:29
  16.2 74.0 %all-gather.2.cloned.1.call-start = ((), (), s32[]{:S(2)}) async-start(), calls=%async_computation.3 | async-start | bytes 1949696 | tf_op jit(solution)/shard_map/all_gather | solution.py:85
  17.0 137.5 %reduce-scatter.2.cloned.1.call-start = ((), (), s32[]{:S(2)}) async-start(), calls=%async_computation.4 | async-start | bytes 2580480 | tf_op jit(solution)/shard_map/reduce_scatter | solution.py:87
  23.1 8.3 %collective-permute-start = (bf16[579,2,1,128]{3,0,1,2:T(8,128)(2,1)S(1)}, bf16[579,2,1,128]{3,0,1,2:T(8,128)(2,1)S(1)}, u32[]{:S(2)}, u32[]{:S(2)}) collective-permute-start(bf16[579,2,1,128]{3,0,1,2:T(8,128)(2,1)S(1)} %pad_maximum_fusion.1), channel_id=1, source_target_pairs={{0,32},{32,64},{64,96},{96,128},{128,160},{160,192},{192,224},{224... | collective-permute-start | bytes 889352 | tf_op jit(solution)/shard_map/ppermute | solution.py:78
  27.8 8.5 %copy-start.2 = (bf16[4,144,1,1,128]{4,1,0,3,2:T(8,128)(2,1)}, bf16[4,144,1,1,128]{4,1,0,3,2:T(8,128)(2,1)S(1)}, u32[]{:S(2)}) copy-start(bf16[4,144,1,1,128]{4,1,0,3,2:T(8,128)(2,1)S(1)} %slice.116) | copy-start | bytes 442372
  31.4 6.0 %copy-start.15 = (bf16[579,2,1,128]{3,0,1,2:T(8,128)(2,1)}, bf16[579,2,1,128]{3,0,1,2:T(8,128)(2,1)S(1)}, u32[]{:S(2)}) copy-start(bf16[579,2,1,128]{3,0,1,2:T(8,128)(2,1)S(1)} %collective-permute-done) | copy-start | bytes 889348
  31.4 7.8 %collective-permute-start.1 = (bf16[579,2,1,128]{3,0,1,2:T(8,128)(2,1)S(1)}, bf16[579,2,1,128]{3,0,1,2:T(8,128)(2,1)}, u32[]{:S(2)}, u32[]{:S(2)}) collective-permute-start(bf16[579,2,1,128]{3,0,1,2:T(8,128)(2,1)S(1)} %collective-permute-done), channel_id=1, source_target_pairs={{0,32},{32,64},{64,96},{96,128},{128,160},{160,192},{192,224},{224... | collective-permute-start | bytes 889352 | tf_op jit(solution)/shard_map/ppermute | solution.py:78
  36.3 1.2 copy-start.3
  39.9 9.5 %collective-permute-start.2 = (bf16[579,2,1,128]{3,0,1,2:T(8,128)(2,1)}, bf16[579,2,1,128]{3,0,1,2:T(8,128)(2,1)S(1)}, u32[]{:S(2)}, u32[]{:S(2)}) collective-permute-start(bf16[579,2,1,128]{3,0,1,2:T(8,128)(2,1)} %collective-permute-done.1), channel_id=1, source_target_pairs={{0,32},{32,64},{64,96},{96,128},{128,160},{160,192},{192,224},{224... | collective-permute-start | bytes 889352 | tf_op jit(solution)/shard_map/ppermute | solution.py:78
  44.0 2.2 %copy-start.5 = (s32[576]{0:T(1024)}, s32[576]{0:T(1024)S(1)}, u32[]{:S(2)}) copy-start(s32[576]{0:T(1024)S(1)} %slice_convert_fusion.2) | copy-start | bytes 6916
  49.4 0.7 copy-start.16
  52.0 10.3 %collective-permute-start.3 = (bf16[579,2,1,128]{3,0,1,2:T(8,128)(2,1)}, bf16[579,2,1,128]{3,0,1,2:T(8,128)(2,1)S(1)}, u32[]{:S(2)}, u32[]{:S(2)}) collective-permute-start(bf16[579,2,1,128]{3,0,1,2:T(8,128)(2,1)} %copy-done.16), channel_id=1, source_target_pairs={{0,32},{32,64},{64,96},{96,128},{128,160},{160,192},{192,224},{224... | collective-permute-start | bytes 889352 | tf_op jit(solution)/shard_map/ppermute | solution.py:78
  57.8 3.3 %copy-start.10 = (s32[576]{0:T(1024)}, s32[576]{0:T(1024)S(1)}, u32[]{:S(2)}) copy-start(s32[576]{0:T(1024)S(1)} %slice_convert_fusion.1) | copy-start | bytes 6916
  62.3 0.7 copy-start.17
  65.5 1.6 copy-start.7
  65.5 1.6 copy-start.12
  65.5 1.7 copy-start.13
  65.6 1.7 copy-start.14
  65.6 1.7 copy-start.4
  65.6 1.7 copy-start.6
  67.3 1.4 copy-start
  67.3 1.8 %copy-start.1 = (f32[576,576]{0,1:T(8,128)S(1)}, f32[576,576]{0,1:T(8,128)}, u32[]{:S(2)}) copy-start(f32[576,576]{0,1:T(8,128)} %get-tuple-element.51) | copy-start | bytes 3981316
  67.3 1.8 %copy-start.8 = (s32[576]{0:T(1024)S(1)}, s32[576]{0:T(1024)}, u32[]{:S(2)}) copy-start(s32[576]{0:T(1024)} %iota_add_fusion) | copy-start | bytes 6916
  67.3 1.8 %copy-start.9 = (s32[576]{0:T(1024)S(1)}, s32[576]{0:T(1024)}, u32[]{:S(2)}) copy-start(s32[576]{0:T(1024)} %get-tuple-element.58) | copy-start | bytes 6916
  67.3 1.8 %copy-start.11 = (s32[576]{0:T(1024)S(1)}, s32[576]{0:T(1024)}, u32[]{:S(2)}) copy-start(s32[576]{0:T(1024)} %copy-done.10) | copy-start | bytes 6916
  156.5 9.1 %all-to-all-start.1 = ((bf16[4,144,2,112]{3,2,1,0:T(2,128)(2,1)}), bf16[4,144,2,112]{3,2,1,0:T(2,128)(2,1)S(1)}, u32[]{:S(2)}, u32[]{:S(2)}) async-start(bf16[4,144,2,112]{3,2,1,0:T(2,128)(2,1)} %reshape.472), calls=%async_computation.2 | async-start | bytes 589824 | tf_op jit(solution)/shard_map/all_to_all | solution.py:93
Sparse Core Ops, SparseCore 0:
  19.1 71.0 all-gather.1
  94.9 59.5 reduce-scatter.1

commit v3 on v2

--- a/solution.py
+++ b/solution.py
@@ -81,17 +81,29 @@
     attended = (accumulated / row_total[..., None]).astype(jnp.bfloat16)
     attended = attended.transpose(1, 0, 2).reshape(level, hq * HD)
 
-    level_attended = lax.all_gather(attended, "y", axis=1, tiled=True)
+    c = lax.axis_index("c")
+    swap = [(0, 1), (1, 0)]
+    own_attended = lax.all_gather(attended, "y", axis=1, tiled=True)
+    other_attended = lax.ppermute(own_attended, "c", swap)
     weight_cols = lax.all_gather(out_weight, "z", axis=1, tiled=True)
-    partial_value = jnp.dot(level_attended, weight_cols, preferred_element_type=jnp.float32)
+    chunk = out_weight.shape[1]
+    weight_cols = weight_cols.reshape(weight_cols.shape[0], nz // 2, 2, chunk)
+    own_weight = lax.dynamic_index_in_dim(weight_cols, c, axis=2, keepdims=False)
+    other_weight = lax.ppermute(
+        lax.dynamic_index_in_dim(weight_cols, 1 - c, axis=2, keepdims=False), "c", swap
+    )
+    own_weight = own_weight.reshape(own_weight.shape[0], -1)
+    other_weight = other_weight.reshape(other_weight.shape[0], -1)
+    partial_value = jnp.dot(own_attended, own_weight, preferred_element_type=jnp.float32)
+    partial_value = partial_value + jnp.dot(
+        other_attended, other_weight, preferred_element_type=jnp.float32
+    )
     summed = lax.psum_scatter(
-        partial_value.astype(jnp.bfloat16), "tensor", scatter_dimension=1, tiled=True
+        partial_value.astype(jnp.bfloat16), "x", scatter_dimension=1, tiled=True
     )
-    chunk = out_weight.shape[1]
-    halves = summed.shape[1] // chunk
-    summed = summed.reshape(NY, rows, halves, chunk)
-    summed = lax.all_to_all(summed, "y", 0, 0, tiled=True)
-    hidden_states = summed.transpose(1, 2, 0, 3).reshape(rows, halves * NY * chunk)
+    summed = summed.reshape(NY, rows, 2, chunk).transpose(0, 2, 1, 3).reshape(2 * NY, rows, chunk)
+    summed = lax.all_to_all(summed, ("y", "c"), 0, 0, tiled=True)
+    hidden_states = summed.reshape(NY, 2, rows, chunk).transpose(2, 1, 0, 3).reshape(rows, 2 * NY * chunk)
 
     head_major = keys_values.reshape(rows, 2, heads, HD).transpose(1, 2, 0, 3)
     return (hidden_states, head_major)
@@ -99,13 +111,15 @@
 
 def solution(mesh):
     seq, tensor = mesh.shape["seq"], mesh.shape["tensor"]
-    assert seq % NY == 0
-    grid = Mesh(mesh.devices.reshape(seq // NY, NY, tensor), ("z", "y", "tensor"))
-    s = ("z", "y")
+    assert seq % NY == 0 and tensor % 2 == 0
+    grid = Mesh(
+        mesh.devices.reshape(seq // NY, NY, tensor // 2, 2), ("z", "y", "x", "c")
+    )
+    s, t = ("z", "y"), ("x", "c")
     return jax.shard_map(
         local,
         mesh=grid,
-        in_specs=(P(s, "tensor"), P(s, None, "tensor"), P(s), P("tensor", s)),
-        out_specs=(P(s, "tensor"), P(None, "tensor", s, None)),
+        in_specs=(P(s, t), P(s, None, t), P(s), P(t, s)),
+        out_specs=(P(s, t), P(None, t, s, None)),
         check_vma=False,
     )

time: 177 us -> 176 us (level); the launches traced: 174 us -> 175 us
  waiting for transfers between devices: 78.4 us -> 60.2 us
  starting transfers between devices: 27.1 us -> 44.4 us
  blocking collectives: 10.7 us -> 13.3 us
    reduce_scatter x1, waiting for transfers between devices: 59.7 us -> 27.3 us  [local(): lax.psum_scatter(partial_value.astype(jnp.bfloat16), 'x', scatter_dimensi...]
    ppermute x0 -> x2, starting transfers between devices: none -> 14.6 us  [the longest x1 10.9 us: local(): lax.ppermute(lax.dynamic_index_in_dim(weight_cols, 1 - c, axis=2, keepdim...]
    all_gather x1, waiting for transfers between devices: 0.89 us -> 12.5 us  [local(): weight_cols = lax.all_gather(out_weight, 'z', axis=1, tiled=True)]
    all_to_all x1, starting transfers between devices: 3.45 us -> 6.15 us  [local(): summed = lax.all_to_all(summed, ('y', 'c'), 0, 0, tiled=True)]
    all_gather x1, blocking collectives: 10.7 us -> 13.3 us  [local(): own_attended = lax.all_gather(attended, 'y', axis=1, tiled=True)]
    dot_general x1 -> x2, matrix products: 4.49 us -> 2.87 us  [the longest x1 1.96 us: local(): jnp.dot(other_attended, other_weight, preferred_element_type=jnp.float32)]
  transfers between devices with their start and end apart: 8 -> 10, of which waited for: 8 -> 9; matrix products, arithmetic and copies ran while one was open for 17% -> 17% of each run, Pallas kernels for 0% -> 0%
where the time goes in v3:
time: 176 us; the launch traced here: 175 us
  waiting for transfers between devices  60.2 us (34%)
  starting transfers between devices  44.4 us (25%)
  matrix products  21.1 us (12%)
  local copies, waits for them, and re-layouts  15.1 us (9%)
  between operations  14.6 us (8%)
  blocking collectives  13.3 us (8%)
  other arithmetic  6.88 us (4%)
    reduce_scatter x1, waiting for transfers between devices, local(): lax.psum_scatter(partial_value.astype(jnp.bfloat16), 'x', scatter_dimensi...  27.3 us
    ppermute x4, starting transfers between devices, local(): block = lax.ppermute(block, 'z', [(i, i + 1) for i in range(nz - 1)])  18.6 us
    all_gather x1, blocking collectives, local(): own_attended = lax.all_gather(attended, 'y', axis=1, tiled=True)  13.3 us
    all_gather x1, waiting for transfers between devices, local(): weight_cols = lax.all_gather(out_weight, 'z', axis=1, tiled=True)  12.5 us
    ppermute x1, starting transfers between devices, local(): lax.ppermute(lax.dynamic_index_in_dim(weight_cols, 1 - c, axis=2, keepdim...  10.9 us
    dot_general x5, matrix products, attend(): jnp.einsum('qhd,khd->hqk', query_rows, key_rows, preferred_element_type=j...  10.5 us
    ppermute x4, waiting for transfers between devices, local(): block = lax.ppermute(block, 'z', [(i, i + 1) for i in range(nz - 1)])  8.26 us
    dot_general x5, matrix products, attend(): jnp.einsum('hqk,khd->hqd', probs.astype(jnp.bfloat16), value_rows, prefer...  7.66 us
  transfers between devices with their start and end apart: 10, of which 9 were waited for; matrix products, arithmetic and copies ran while one was open for 17% of the time, Pallas kernels for 0%

profile of v3, /device:TPU:1, one launch (start us, length us, event | category | flops | bytes accessed | tf_op | source)
XLA Modules:
  0.0 175.4 jit_solution(12706220119201172626)
XLA Ops:
  7.2 1.2 reshape.495
  8.3 1.0 reshape.467
  9.3 0.7 convert_element_type.50
  10.4 0.8 copy.23
  11.2 5.0 %all-to-all-start = ((bf16[145,3,4,1,128]{4,0,1,3,2:T(8,128)(2,1)}), bf16[145,3,4,1,128]{4,0,1,3,2:T(8,128)(2,1)S(1)}, u32[]{:S(2)}, u32[]{:S(2)}) async-start(bf16[145,3,4,1,128]{4,0,1,3,2:T(8,128)(2,1)} %copy.23), calls=%async_computation | async-start | bytes 933888 | tf_op jit(solution)/shard_map/all_to_all | solution.py:29
  16.2 0.7 all-gather.2.cloned.1.call-update
  18.2 4.6 %all-to-all-done = bf16[145,3,4,1,128]{4,0,1,3,2:T(8,128)(2,1)S(1)} async-done(((bf16[145,3,4,1,128]{4,0,1,3,2:T(8,128)(2,1)}), bf16[145,3,4,1,128]{4,0,1,3,2:T(8,128)(2,1)S(1)}, u32[]{:S(2)}, u32[]{:S(2)}) %all-to-all-start) | async-done | bytes 445472 | tf_op jit(solution)/shard_map/all_to_all | solution.py:29
  23.1 4.6 %collective-permute-start = (bf16[579,2,1,128]{3,0,1,2:T(8,128)(2,1)S(1)}, bf16[579,2,1,128]{3,0,1,2:T(8,128)(2,1)S(1)}, u32[]{:S(2)}, u32[]{:S(2)}) collective-permute-start(bf16[579,2,1,128]{3,0,1,2:T(8,128)(2,1)S(1)} %pad_maximum_fusion.1), channel_id=1, source_target_pairs={{0,32},{32,64},{64,96},{96,128},{128,160},{160,192},{192,224},{224... | collective-permute-start | bytes 889352 | tf_op jit(solution)/shard_map/ppermute | solution.py:78
  27.8 2.3 %fusion.43 = (f32[576]{0:T(1024)}, f32[576,576]{0,1:T(8,128)}) fusion(bf16[576,128]{1,0:T(8,128)(2,1)S(1)} %bitcast.97, bf16[576,2,1,128]{3,0,1,2:T(8,128)(2,1)S(1)} %bitcast.92, pred[]{:T(512)S(6)} %ge.15, s32[576]{0:T(1024)S(1)} %get-tuple-element.61, s32[576]{0:T(1024)S(1)} %convert_element_type.51), kind=kOutput, calls=%fused_computation.92 | convolution fusion | flops 87256512 | bytes 1640705 | tf_op jit(solution)/shard_map/qhd,khd->hqk/dot_general | solution.py:49
  30.1 1.3 collective-permute-done
  31.4 4.8 %collective-permute-start.1 = (bf16[579,2,1,128]{3,0,1,2:T(8,128)(2,1)S(1)}, bf16[579,2,1,128]{3,0,1,2:T(8,128)(2,1)}, u32[]{:S(2)}, u32[]{:S(2)}) collective-permute-start(bf16[579,2,1,128]{3,0,1,2:T(8,128)(2,1)S(1)} %collective-permute-done), channel_id=1, source_target_pairs={{0,32},{32,64},{64,96},{96,128},{128,160},{160,192},{192,224},{224... | collective-permute-start | bytes 889352 | tf_op jit(solution)/shard_map/ppermute | solution.py:78
  36.2 1.2 fusion.42
  37.4 1.7 collective-permute-done.1
  39.2 0.7 slice.123
  39.9 4.1 %collective-permute-start.2 = (bf16[579,2,1,128]{3,0,1,2:T(8,128)(2,1)}, bf16[579,2,1,128]{3,0,1,2:T(8,128)(2,1)S(1)}, u32[]{:S(2)}, u32[]{:S(2)}) collective-permute-start(bf16[579,2,1,128]{3,0,1,2:T(8,128)(2,1)} %collective-permute-done.1), channel_id=1, source_target_pairs={{0,32},{32,64},{64,96},{96,128},{128,160},{160,192},{192,224},{224... | collective-permute-start | bytes 889352 | tf_op jit(solution)/shard_map/ppermute | solution.py:78
  44.0 2.2 %fusion.41 = (f32[576]{0:T(1024)}, f32[576,576]{0,1:T(8,128)S(1)}) fusion(bf16[576,128]{1,0:T(8,128)(2,1)} %bitcast.99, bf16[579,2,1,128]{3,0,1,2:T(8,128)(2,1)} %collective-permute-done.1, pred[]{:T(512)S(6)} %ge.17, s32[576]{0:T(1024)S(1)} %get-tuple-element.61, s32[576]{0:T(1024)S(1)} %iota_add_fusion.2, s32[576]{0:T(1024)S(1)} %convert_element_type.51, ...), kind=kOutput, calls=%fused_computation.90 | convolution fusion | flops 87256512 | bytes 1633537 | tf_op jit(solution)/shard_map/qhd,khd->hqk/dot_general | solution.py:49
  46.2 3.2 %collective-permute-done.2 = bf16[579,2,1,128]{3,0,1,2:T(8,128)(2,1)S(1)} collective-permute-done((bf16[579,2,1,128]{3,0,1,2:T(8,128)(2,1)}, bf16[579,2,1,128]{3,0,1,2:T(8,128)(2,1)S(1)}, u32[]{:S(2)}, u32[]{:S(2)}) %collective-permute-start.2) | collective-permute-done | bytes 296480 | tf_op jit(solution)/shard_map/ppermute | solution.py:78
  49.4 0.7 copy-done.26
  50.7 0.7 reshape.482
  51.4 5.1 %collective-permute-start.3 = (bf16[579,2,1,128]{3,0,1,2:T(8,128)(2,1)}, bf16[579,2,1,128]{3,0,1,2:T(8,128)(2,1)S(1)}, u32[]{:S(2)}, u32[]{:S(2)}) collective-permute-start(bf16[579,2,1,128]{3,0,1,2:T(8,128)(2,1)} %copy-done.26), channel_id=1, source_target_pairs={{0,32},{32,64},{64,96},{96,128},{128,160},{160,192},{192,224},{224... | collective-permute-start | bytes 889352 | tf_op jit(solution)/shard_map/ppermute | solution.py:78
  56.5 3.3 %fusion.40 = (f32[576]{0:T(1024)}, f32[576,576]{0,1:T(8,128)}) fusion(bf16[576,128]{1,0:T(8,128)(2,1)} %bitcast.100, bf16[579,2,1,128]{3,0,1,2:T(8,128)(2,1)} %copy-done.26, pred[]{:T(512)S(6)} %ge.18, s32[576]{0:T(1024)S(1)} %get-tuple-element.61, s32[576]{0:T(1024)} %get-tuple-element.60, s32[576]{0:T(1024)S(1)} %convert_element_type.51, ...), kind=kOutput, calls=%fused_computation.89 | convolution fusion | flops 87256512 | bytes 1635329 | tf_op jit(solution)/shard_map/qhd,khd->hqk/dot_general | solution.py:49
  59.8 2.0 %collective-permute-done.3 = bf16[579,2,1,128]{3,0,1,2:T(8,128)(2,1)S(1)} collective-permute-done((bf16[579,2,1,128]{3,0,1,2:T(8,128)(2,1)}, bf16[579,2,1,128]{3,0,1,2:T(8,128)(2,1)S(1)}, u32[]{:S(2)}, u32[]{:S(2)}) %collective-permute-start.3) | collective-permute-done | bytes 296480 | tf_op jit(solution)/shard_map/ppermute | solution.py:78
  61.8 0.7 copy-done.25
  63.1 1.3 reshape.485
  64.4 0.7 slice_convert_fusion
  65.2 1.6 fusion.39
  66.9 1.3 fusion.8
  69.2 2.0 %fusion.6 = (f32[576]{0:T(1024)S(1)}, f32[576]{0:T(1024)S(1)}, f32[576]{0:T(1024)S(1)}) fusion(f32[576,576]{0,1:T(8,128)S(1)} %copy-done, f32[576]{0:T(1024)S(1)} %get-tuple-element.49, pred[]{:T(512)S(6)} %ge.15, s32[576]{0:T(1024)S(1)} %get-tuple-element.61, s32[576]{0:T(1024)S(1)} %convert_element_type.51, f32[576,576]{0,1:T(8,128)S(1)} %get-tuple-element.51, ...), kind=kLoop, calls=%fused_computation.27 | loop fusion | flops 6965568 | bytes 4008963 | tf_op jit(solution)/shard_map/reduce_sum | solution.py:61
  71.8 0.9 fusion
  72.6 1.7 fusion.1
  74.3 1.7 fusion.2
  76.1 1.7 fusion.3
  77.8 12.5 %all-gather.2.cloned.1.call-done = bf16[512,1792]{0,1:T(8,128)(2,1)} async-done(((bf16[512,112]{0,1:T(8,128)(2,1)}), bf16[512,1792]{0,1:T(8,128)(2,1)}) %all-gather.2.cloned.1.call-update) | async-done | bytes 1835024 | tf_op jit(solution)/shard_map/all_gather | solution.py:88
  90.2 1.7 dynamic-slice_bitcast_fusion
  91.9 10.9 %collective-permute-start.5 = (bf16[512,8,112]{0,2,1:T(8,128)(2,1)S(1)}, bf16[512,8,112]{0,2,1:T(8,128)(2,1)S(1)}, u32[]{:S(2)}, u32[]{:S(2)}) collective-permute-start(bf16[512,8,112]{0,2,1:T(8,128)(2,1)S(1)} %get-tuple-element.46), channel_id=1, source_target_pairs={{0,1},{1,0},{2,3},{3,2},{4,5},{5,4},{6,7},{7,6},{8,9},{9,8},{10,11... | collective-permute-start | bytes 2752520 | tf_op jit(solution)/shard_map/ppermute | solution.py:92
  102.9 1.7 fusion.5
  104.6 13.3 %all_gather.6 = bf16[576,512]{1,0:T(8,128)(2,1)S(1)} all-gather(bf16[576,128]{1,0:T(8,128)(2,1)S(1)} %fusion.5), channel_id=1, replica_groups=mesh['z'=16,'y'=4,'x'=4,'c'=2] {'y'}, dimensions={1}, use_global_device_ids=true | all-gather | bytes 737280 | tf_op jit(solution)/shard_map/all_gather | solution.py:86
  117.8 3.7 %collective-permute-start.4 = (bf16[576,512]{1,0:T(8,128)(2,1)S(1)}, bf16[576,512]{1,0:T(8,128)(2,1)S(1)}, u32[]{:S(2)}, u32[]{:S(2)}) collective-permute-start(bf16[576,512]{1,0:T(8,128)(2,1)S(1)} %all_gather.6), channel_id=1, source_target_pairs={{0,1},{1,0},{2,3},{3,2},{4,5},{5,4},{6,7},{7,6},{8,9},{9,8},{10,11... | collective-permute-start | bytes 1769480 | tf_op jit(solution)/shard_map/ppermute | solution.py:87
  121.5 0.9 fusion.44
  122.4 0.7 collective-permute-done.4
  123.1 2.0 %add_convert_fusion = bf16[576,896]{0,1:T(8,128)(2,1)} fusion(f32[576,896]{0,1:T(8,128)S(1)} %fusion.44, bf16[576,512]{1,0:T(8,128)(2,1)S(1)} %collective-permute-done.4, bf16[512,896]{0,1:T(8,128)(2,1)S(1)} %bitcast.96), kind=kOutput, calls=%fused_computation | convolution fusion | flops 529514496 | bytes 4603904 | tf_op jit(solution)/shard_map/dot_general | solution.py:98
  125.1 27.3 %reduce-scatter.2.cloned.1.call-done = bf16[576,224]{0,1:T(8,128)(2,1)} async-done(((bf16[576,896]{0,1:T(8,128)(2,1)}), bf16[576,224]{0,1:T(8,128)(2,1)}) %reduce-scatter.2.cloned.1.call-update) | async-done | bytes 258064 | tf_op jit(solution)/shard_map/reduce_scatter | solution.py:101
  152.5 1.1 copy.31
  153.8 0.8 copy.32
  154.5 6.1 %all-to-all-start.1 = ((bf16[8,144,112]{2,1,0:T(8,128)(2,1)}), bf16[8,144,112]{2,1,0:T(8,128)(2,1)S(1)}, u32[]{:S(2)}, u32[]{:S(2)}) async-start(bf16[8,144,112]{2,1,0:T(8,128)(2,1)} %bitcast.25), calls=%async_computation.2 | async-start | bytes 589824 | tf_op jit(solution)/shard_map/all_to_all | solution.py:105
  160.7 0.8 copy.34
  161.4 6.1 %all-to-all-done.1 = bf16[8,144,112]{2,1,0:T(8,128)(2,1)S(1)} async-done(((bf16[8,144,112]{2,1,0:T(8,128)(2,1)}), bf16[8,144,112]{2,1,0:T(8,128)(2,1)S(1)}, u32[]{:S(2)}, u32[]{:S(2)}) %all-to-all-start.1) | async-done | bytes 258080 | tf_op jit(solution)/shard_map/all_to_all | solution.py:105
  167.6 0.9 reshape.494
  (92 shorter events, 5.1 us)
Async XLA Ops:
  11.2 11.6 %all-to-all-start = ((bf16[145,3,4,1,128]{4,0,1,3,2:T(8,128)(2,1)}), bf16[145,3,4,1,128]{4,0,1,3,2:T(8,128)(2,1)S(1)}, u32[]{:S(2)}, u32[]{:S(2)}) async-start(bf16[145,3,4,1,128]{4,0,1,3,2:T(8,128)(2,1)} %copy.23), calls=%async_computation | async-start | bytes 933888 | tf_op jit(solution)/shard_map/all_to_all | solution.py:29
  16.2 74.0 %all-gather.2.cloned.1.call-start = ((), (), s32[]{:S(2)}) async-start(), calls=%async_computation.3 | async-start | bytes 1949696 | tf_op jit(solution)/shard_map/all_gather | solution.py:88
  16.9 135.5 %reduce-scatter.2.cloned.1.call-start = ((), (), s32[]{:S(2)}) async-start(), calls=%async_computation.4 | async-start | bytes 1433600 | tf_op jit(solution)/shard_map/reduce_scatter | solution.py:101
  23.1 8.3 %collective-permute-start = (bf16[579,2,1,128]{3,0,1,2:T(8,128)(2,1)S(1)}, bf16[579,2,1,128]{3,0,1,2:T(8,128)(2,1)S(1)}, u32[]{:S(2)}, u32[]{:S(2)}) collective-permute-start(bf16[579,2,1,128]{3,0,1,2:T(8,128)(2,1)S(1)} %pad_maximum_fusion.1), channel_id=1, source_target_pairs={{0,32},{32,64},{64,96},{96,128},{128,160},{160,192},{192,224},{224... | collective-permute-start | bytes 889352 | tf_op jit(solution)/shard_map/ppermute | solution.py:78
  27.7 8.5 %copy-start.5 = (s32[576]{0:T(1024)}, s32[576]{0:T(1024)S(1)}, u32[]{:S(2)}) copy-start(s32[576]{0:T(1024)S(1)} %iota_add_fusion.3) | copy-start | bytes 6916
  27.8 8.4 %copy-start.4 = (bf16[4,144,1,1,128]{4,1,0,3,2:T(8,128)(2,1)}, bf16[4,144,1,1,128]{4,1,0,3,2:T(8,128)(2,1)S(1)}, u32[]{:S(2)}) copy-start(bf16[4,144,1,1,128]{4,1,0,3,2:T(8,128)(2,1)S(1)} %slice.116) | copy-start | bytes 442372
  31.4 6.0 %copy-start.24 = (bf16[579,2,1,128]{3,0,1,2:T(8,128)(2,1)}, bf16[579,2,1,128]{3,0,1,2:T(8,128)(2,1)S(1)}, u32[]{:S(2)}) copy-start(bf16[579,2,1,128]{3,0,1,2:T(8,128)(2,1)S(1)} %collective-permute-done) | copy-start | bytes 889348
  31.4 7.8 %collective-permute-start.1 = (bf16[579,2,1,128]{3,0,1,2:T(8,128)(2,1)S(1)}, bf16[579,2,1,128]{3,0,1,2:T(8,128)(2,1)}, u32[]{:S(2)}, u32[]{:S(2)}) collective-permute-start(bf16[579,2,1,128]{3,0,1,2:T(8,128)(2,1)S(1)} %collective-permute-done), channel_id=1, source_target_pairs={{0,32},{32,64},{64,96},{96,128},{128,160},{160,192},{192,224},{224... | collective-permute-start | bytes 889352 | tf_op jit(solution)/shard_map/ppermute | solution.py:78
  36.2 1.2 copy-start.7
  39.9 9.5 %collective-permute-start.2 = (bf16[579,2,1,128]{3,0,1,2:T(8,128)(2,1)}, bf16[579,2,1,128]{3,0,1,2:T(8,128)(2,1)S(1)}, u32[]{:S(2)}, u32[]{:S(2)}) collective-permute-start(bf16[579,2,1,128]{3,0,1,2:T(8,128)(2,1)} %collective-permute-done.1), channel_id=1, source_target_pairs={{0,32},{32,64},{64,96},{96,128},{128,160},{160,192},{192,224},{224... | collective-permute-start | bytes 889352 | tf_op jit(solution)/shard_map/ppermute | solution.py:78
  44.0 2.2 %copy-start.9 = (s32[576]{0:T(1024)}, s32[576]{0:T(1024)S(1)}, u32[]{:S(2)}) copy-start(s32[576]{0:T(1024)S(1)} %slice_convert_fusion.2) | copy-start | bytes 6916
  49.4 0.7 copy-start.26
  51.4 10.5 %collective-permute-start.3 = (bf16[579,2,1,128]{3,0,1,2:T(8,128)(2,1)}, bf16[579,2,1,128]{3,0,1,2:T(8,128)(2,1)S(1)}, u32[]{:S(2)}, u32[]{:S(2)}) collective-permute-start(bf16[579,2,1,128]{3,0,1,2:T(8,128)(2,1)} %copy-done.26), channel_id=1, source_target_pairs={{0,32},{32,64},{64,96},{96,128},{128,160},{160,192},{192,224},{224... | collective-permute-start | bytes 889352 | tf_op jit(solution)/shard_map/ppermute | solution.py:78
  56.5 3.3 %copy-start.18 = (s32[576]{0:T(1024)}, s32[576]{0:T(1024)S(1)}, u32[]{:S(2)}) copy-start(s32[576]{0:T(1024)S(1)} %slice_convert_fusion.1) | copy-start | bytes 6916
  56.5 8.6 %copy-start.12 = (s32[576]{0:T(1024)S(1)}, s32[576]{0:T(1024)}, u32[]{:S(2)}) copy-start(s32[576]{0:T(1024)} %iota_add_fusion) | copy-start | bytes 6916
  61.8 0.7 copy-start.25
  65.1 3.1 %copy-start.16 = (s32[576]{0:T(1024)}, s32[576]{0:T(1024)S(1)}, u32[]{:S(2)}) copy-start(s32[576]{0:T(1024)S(1)} %slice_convert_fusion) | copy-start | bytes 6916
  65.1 1.7 copy-start.11
  65.1 1.7 copy-start.20
  65.1 1.7 copy-start.21
  65.1 1.7 copy-start.22
  65.2 1.7 copy-start.6
  65.2 1.7 copy-start.8
  65.2 1.7 copy-start.10
  66.8 1.5 copy-start.1
  66.9 1.8 %copy-start = (f32[576,576]{0,1:T(8,128)S(1)}, f32[576,576]{0,1:T(8,128)}, u32[]{:S(2)}) copy-start(f32[576,576]{0,1:T(8,128)} %get-tuple-element.59) | copy-start | bytes 3981316
  66.9 2.3 %copy-start.3 = (f32[576,576]{0,1:T(8,128)S(1)}, f32[576,576]{0,1:T(8,128)}, u32[]{:S(2)}) copy-start(f32[576,576]{0,1:T(8,128)} %get-tuple-element.53) | copy-start | bytes 3981316
  66.9 2.3 %copy-start.13 = (s32[576]{0:T(1024)S(1)}, s32[576]{0:T(1024)}, u32[]{:S(2)}) copy-start(s32[576]{0:T(1024)} %iota_add_fusion) | copy-start | bytes 6916
  66.9 2.3 %copy-start.15 = (s32[576]{0:T(1024)S(1)}, s32[576]{0:T(1024)}, u32[]{:S(2)}) copy-start(s32[576]{0:T(1024)} %get-tuple-element.60) | copy-start | bytes 6916
  66.9 2.3 %copy-start.19 = (s32[576]{0:T(1024)S(1)}, s32[576]{0:T(1024)}, u32[]{:S(2)}) copy-start(s32[576]{0:T(1024)} %copy-done.18) | copy-start | bytes 6916
  90.2 12.6 %copy-start.2 = (f32[576,576]{0,1:T(8,128)S(1)}, f32[576,576]{0,1:T(8,128)}, u32[]{:S(2)}) copy-start(f32[576,576]{0,1:T(8,128)} %copy-done.1) | copy-start | bytes 3981316
  90.2 12.6 %copy-start.14 = (s32[576]{0:T(1024)S(1)}, s32[576]{0:T(1024)}, u32[]{:S(2)}) copy-start(s32[576]{0:T(1024)} %iota_add_fusion) | copy-start | bytes 6916
  90.2 12.6 %copy-start.17 = (s32[576]{0:T(1024)S(1)}, s32[576]{0:T(1024)}, u32[]{:S(2)}) copy-start(s32[576]{0:T(1024)} %copy-done.16) | copy-start | bytes 6916
  90.2 12.6 %copy-start.23 = (f32[576]{0:T(1024)S(1)}, f32[576]{0:T(1024)}, u32[]{:S(2)}) copy-start(f32[576]{0:T(1024)} %get-tuple-element.37) | copy-start | bytes 6916
  91.9 31.2 %collective-permute-start.5 = (bf16[512,8,112]{0,2,1:T(8,128)(2,1)S(1)}, bf16[512,8,112]{0,2,1:T(8,128)(2,1)S(1)}, u32[]{:S(2)}, u32[]{:S(2)}) collective-permute-start(bf16[512,8,112]{0,2,1:T(8,128)(2,1)S(1)} %get-tuple-element.46), channel_id=1, source_target_pairs={{0,1},{1,0},{2,3},{3,2},{4,5},{5,4},{6,7},{7,6},{8,9},{9,8},{10,11... | collective-permute-start | bytes 2752520 | tf_op jit(solution)/shard_map/ppermute | solution.py:92
  117.8 5.3 %collective-permute-start.4 = (bf16[576,512]{1,0:T(8,128)(2,1)S(1)}, bf16[576,512]{1,0:T(8,128)(2,1)S(1)}, u32[]{:S(2)}, u32[]{:S(2)}) collective-permute-start(bf16[576,512]{1,0:T(8,128)(2,1)S(1)} %all_gather.6), channel_id=1, source_target_pairs={{0,1},{1,0},{2,3},{3,2},{4,5},{5,4},{6,7},{7,6},{8,9},{9,8},{10,11... | collective-permute-start | bytes 1769480 | tf_op jit(solution)/shard_map/ppermute | solution.py:87
  154.5 13.0 %all-to-all-start.1 = ((bf16[8,144,112]{2,1,0:T(8,128)(2,1)}), bf16[8,144,112]{2,1,0:T(8,128)(2,1)S(1)}, u32[]{:S(2)}, u32[]{:S(2)}) async-start(bf16[8,144,112]{2,1,0:T(8,128)(2,1)} %bitcast.25), calls=%async_computation.2 | async-start | bytes 589824 | tf_op jit(solution)/shard_map/all_to_all | solution.py:105
Sparse Core Ops, SparseCore 0:
  19.1 71.0 all-gather.1
  125.2 27.1 reduce-scatter.1

commit v4 on v3

--- a/solution.py
+++ b/solution.py
@@ -84,8 +84,9 @@
     c = lax.axis_index("c")
     swap = [(0, 1), (1, 0)]
     own_attended = lax.all_gather(attended, "y", axis=1, tiled=True)
+    weight_cols = lax.all_gather(out_weight, "z", axis=1, tiled=True)
+    weight_cols, own_attended = lax.optimization_barrier((weight_cols, own_attended))
     other_attended = lax.ppermute(own_attended, "c", swap)
-    weight_cols = lax.all_gather(out_weight, "z", axis=1, tiled=True)
     chunk = out_weight.shape[1]
     weight_cols = weight_cols.reshape(weight_cols.shape[0], nz // 2, 2, chunk)
     own_weight = lax.dynamic_index_in_dim(weight_cols, c, axis=2, keepdims=False)

time: 176 us -> 164 us (0.932)
  waiting for transfers between devices: 60.2 us -> 70.6 us
  matrix products: 21.1 us -> 13.2 us
  local copies, waits for them, and re-layouts: 15.1 us -> 10.1 us
  starting transfers between devices: 44.4 us -> 40 us
  other arithmetic: 6.88 us -> 4.37 us
  blocking collectives: 13.3 us -> 10.8 us
    ppermute x4, waiting for transfers between devices: 8.26 us -> 15 us  [local(): block = lax.ppermute(block, 'z', [(i, i + 1) for i in range(nz - 1)])]
    reduce_scatter x1, waiting for transfers between devices: 27.3 us -> 31.9 us  [local(): lax.psum_scatter(partial_value.astype(jnp.bfloat16), 'x', scatter_dimensi...]
    dot_general x5, matrix products: 10.5 us -> 6.37 us  [attend(): jnp.einsum('qhd,khd->hqk', query_rows, key_rows, preferred_element_type=j...]
    dot_general x5, matrix products: 7.66 us -> 3.99 us  [attend(): jnp.einsum('hqk,khd->hqd', probs.astype(jnp.bfloat16), value_rows, prefer...]
    all_gather x1, waiting for transfers between devices: 12.5 us -> 9.98 us  [local(): weight_cols = lax.all_gather(out_weight, 'z', axis=1, tiled=True)]
    all_gather x1, blocking collectives: 13.3 us -> 10.8 us  [local(): own_attended = lax.all_gather(attended, 'y', axis=1, tiled=True)]
    ppermute x4, starting transfers between devices: 18.6 us -> 16.6 us  [local(): block = lax.ppermute(block, 'z', [(i, i + 1) for i in range(nz - 1)])]
    reshape x4, local copies, waits for them, and re-layouts: 2 us -> 0.08 us  [attend(): key_seg = block[level:].reshape(-1)[:level].astype(jnp.int32)]
  transfers between devices with their start and end apart: 10 -> 10, of which waited for: 9 -> 9; matrix products, arithmetic and copies ran while one was open for 17% -> 10% of each run, Pallas kernels for 0% -> 0%
where the time goes in v4:
time: 164 us; the launch traced here: 163 us
  waiting for transfers between devices  70.6 us (43%)
  starting transfers between devices  40 us (24%)
  between operations  14.4 us (9%)
  matrix products  13.2 us (8%)
  blocking collectives  10.8 us (7%)
  local copies, waits for them, and re-layouts  10.1 us (6%)
  other arithmetic  4.37 us (3%)
    reduce_scatter x1, waiting for transfers between devices, local(): lax.psum_scatter(partial_value.astype(jnp.bfloat16), 'x', scatter_dimensi...  31.9 us
    ppermute x4, starting transfers between devices, local(): block = lax.ppermute(block, 'z', [(i, i + 1) for i in range(nz - 1)])  16.6 us
    ppermute x4, waiting for transfers between devices, local(): block = lax.ppermute(block, 'z', [(i, i + 1) for i in range(nz - 1)])  15 us
    all_gather x1, blocking collectives, local(): own_attended = lax.all_gather(attended, 'y', axis=1, tiled=True)  10.8 us
    ppermute x1, starting transfers between devices, local(): lax.ppermute(lax.dynamic_index_in_dim(weight_cols, 1 - c, axis=2, keepdim...  10.3 us
    all_gather x1, waiting for transfers between devices, local(): weight_cols = lax.all_gather(out_weight, 'z', axis=1, tiled=True)  9.98 us
    dot_general x5, matrix products, attend(): jnp.einsum('qhd,khd->hqk', query_rows, key_rows, preferred_element_type=j...  6.37 us
    all_to_all x1, starting transfers between devices, local(): summed = lax.all_to_all(summed, ('y', 'c'), 0, 0, tiled=True)  6.15 us
  transfers between devices with their start and end apart: 10, of which 9 were waited for; matrix products, arithmetic and copies ran while one was open for 10% of the time, Pallas kernels for 0%

profile of v4, /device:TPU:1, one launch (start us, length us, event | category | flops | bytes accessed | tf_op | source)
XLA Modules:
  0.0 163.4 jit_solution(10596388108575767997)
XLA Ops:
  7.2 1.2 reshape.495
  8.3 1.0 reshape.467
  9.3 0.7 convert_element_type.50
  10.0 0.2 maximum_bitcast_fusion
  10.2 0.2 pad_maximum_fusion
  10.4 0.8 copy.23
  11.2 5.0 %all-to-all-start = ((bf16[145,3,4,1,128]{4,0,1,3,2:T(8,128)(2,1)}), bf16[145,3,4,1,128]{4,0,1,3,2:T(8,128)(2,1)S(1)}, u32[]{:S(2)}, u32[]{:S(2)}) async-start(bf16[145,3,4,1,128]{4,0,1,3,2:T(8,128)(2,1)} %copy.23), calls=%async_computation | async-start | bytes 933888 | tf_op jit(solution)/shard_map/all_to_all | solution.py:29
  16.2 0.7 all-gather.2.cloned.1.call-update
  17.0 5.8 %all-to-all-done = bf16[145,3,4,1,128]{4,0,1,3,2:T(8,128)(2,1)S(1)} async-done(((bf16[145,3,4,1,128]{4,0,1,3,2:T(8,128)(2,1)}), bf16[145,3,4,1,128]{4,0,1,3,2:T(8,128)(2,1)S(1)}, u32[]{:S(2)}, u32[]{:S(2)}) %all-to-all-start) | async-done | bytes 445472 | tf_op jit(solution)/shard_map/all_to_all | solution.py:29
  23.1 4.6 %collective-permute-start = (bf16[579,2,1,128]{3,0,1,2:T(8,128)(2,1)S(1)}, bf16[579,2,1,128]{3,0,1,2:T(8,128)(2,1)S(1)}, u32[]{:S(2)}, u32[]{:S(2)}) collective-permute-start(bf16[579,2,1,128]{3,0,1,2:T(8,128)(2,1)S(1)} %pad_maximum_fusion.1), channel_id=1, source_target_pairs={{0,32},{32,64},{64,96},{96,128},{128,160},{160,192},{192,224},{224... | collective-permute-start | bytes 889352 | tf_op jit(solution)/shard_map/ppermute | solution.py:78
  27.8 1.7 %fusion.43 = (f32[576]{0:T(1024)S(1)}, f32[576,576]{0,1:T(8,128)}) fusion(bf16[576,128]{1,0:T(8,128)(2,1)S(1)} %bitcast.97, bf16[576,2,1,128]{3,0,1,2:T(8,128)(2,1)S(1)} %bitcast.92, pred[]{:T(512)S(6)} %ge.15, s32[576]{0:T(1024)S(1)} %get-tuple-element.65, s32[576]{0:T(1024)S(1)} %convert_element_type.51), kind=kOutput, calls=%fused_computation.92 | convolution fusion | flops 87256512 | bytes 1640705 | tf_op jit(solution)/shard_map/qhd,khd->hqk/dot_general | solution.py:49
  29.5 1.9 %collective-permute-done = bf16[579,2,1,128]{3,0,1,2:T(8,128)(2,1)S(1)} collective-permute-done((bf16[579,2,1,128]{3,0,1,2:T(8,128)(2,1)S(1)}, bf16[579,2,1,128]{3,0,1,2:T(8,128)(2,1)S(1)}, u32[]{:S(2)}, u32[]{:S(2)}) %collective-permute-start) | collective-permute-done | bytes 296480 | tf_op jit(solution)/shard_map/ppermute | solution.py:78
  31.4 4.1 %collective-permute-start.1 = (bf16[579,2,1,128]{3,0,1,2:T(8,128)(2,1)S(1)}, bf16[579,2,1,128]{3,0,1,2:T(8,128)(2,1)S(1)}, u32[]{:S(2)}, u32[]{:S(2)}) collective-permute-start(bf16[579,2,1,128]{3,0,1,2:T(8,128)(2,1)S(1)} %collective-permute-done), channel_id=1, source_target_pairs={{0,32},{32,64},{64,96},{96,128},{128,160},{160,192},{192,224},{224... | collective-permute-start | bytes 889352 | tf_op jit(solution)/shard_map/ppermute | solution.py:78
  35.5 0.6 fusion.42
  36.1 3.1 %collective-permute-done.1 = bf16[579,2,1,128]{3,0,1,2:T(8,128)(2,1)S(1)} collective-permute-done((bf16[579,2,1,128]{3,0,1,2:T(8,128)(2,1)S(1)}, bf16[579,2,1,128]{3,0,1,2:T(8,128)(2,1)S(1)}, u32[]{:S(2)}, u32[]{:S(2)}) %collective-permute-start.1) | collective-permute-done | bytes 296480 | tf_op jit(solution)/shard_map/ppermute | solution.py:78
  39.2 4.1 %collective-permute-start.2 = (bf16[579,2,1,128]{3,0,1,2:T(8,128)(2,1)S(1)}, bf16[579,2,1,128]{3,0,1,2:T(8,128)(2,1)S(1)}, u32[]{:S(2)}, u32[]{:S(2)}) collective-permute-start(bf16[579,2,1,128]{3,0,1,2:T(8,128)(2,1)S(1)} %collective-permute-done.1), channel_id=1, source_target_pairs={{0,32},{32,64},{64,96},{96,128},{128,160},{160,192},{192,224},{224... | collective-permute-start | bytes 889352 | tf_op jit(solution)/shard_map/ppermute | solution.py:78
  43.3 1.7 %fusion.41 = (f32[576]{0:T(1024)S(1)}, f32[576,576]{0,1:T(8,128)}) fusion(bf16[576,128]{1,0:T(8,128)(2,1)S(1)} %bitcast.99, bf16[579,2,1,128]{3,0,1,2:T(8,128)(2,1)S(1)} %collective-permute-done.1, pred[]{:T(512)S(6)} %ge.17, s32[576]{0:T(1024)S(1)} %get-tuple-element.65, s32[576]{0:T(1024)S(1)} %iota_add_fusion.2, s32[576]{0:T(1024)S(1)} %convert_element_type.51, ...), kind=kOutput, calls=%fused_computation.90 | convolution fusion | flops 87256512 | bytes 1640705 | tf_op jit(solution)/shard_map/qhd,khd->hqk/dot_general | solution.py:49
  45.1 4.2 %collective-permute-done.2 = bf16[579,2,1,128]{3,0,1,2:T(8,128)(2,1)S(1)} collective-permute-done((bf16[579,2,1,128]{3,0,1,2:T(8,128)(2,1)S(1)}, bf16[579,2,1,128]{3,0,1,2:T(8,128)(2,1)S(1)}, u32[]{:S(2)}, u32[]{:S(2)}) %collective-permute-start.2) | collective-permute-done | bytes 296480 | tf_op jit(solution)/shard_map/ppermute | solution.py:78
  49.3 3.8 %collective-permute-start.3 = (bf16[579,2,1,128]{3,0,1,2:T(8,128)(2,1)S(1)}, bf16[579,2,1,128]{3,0,1,2:T(8,128)(2,1)S(1)}, u32[]{:S(2)}, u32[]{:S(2)}) collective-permute-start(bf16[579,2,1,128]{3,0,1,2:T(8,128)(2,1)S(1)} %collective-permute-done.2), channel_id=1, source_target_pairs={{0,32},{32,64},{64,96},{96,128},{128,160},{160,192},{192,224},{224... | collective-permute-start | bytes 889352 | tf_op jit(solution)/shard_map/ppermute | solution.py:78
  53.1 1.7 %fusion.40 = (f32[576]{0:T(1024)S(1)}, f32[576,576]{0,1:T(8,128)}) fusion(bf16[576,128]{1,0:T(8,128)(2,1)S(1)} %bitcast.100, bf16[579,2,1,128]{3,0,1,2:T(8,128)(2,1)S(1)} %collective-permute-done.2, pred[]{:T(512)S(6)} %ge.18, s32[576]{0:T(1024)S(1)} %get-tuple-element.65, s32[576]{0:T(1024)S(1)} %get-tuple-element.64, s32[576]{0:T(1024)S(1)} %convert_element_type.51, ...), kind=kOutput, calls=%fused_computation.89 | convolution fusion | flops 87256512 | bytes 1640705 | tf_op jit(solution)/shard_map/qhd,khd->hqk/dot_general | solution.py:49
  54.8 5.9 %collective-permute-done.3 = bf16[579,2,1,128]{3,0,1,2:T(8,128)(2,1)S(1)} collective-permute-done((bf16[579,2,1,128]{3,0,1,2:T(8,128)(2,1)S(1)}, bf16[579,2,1,128]{3,0,1,2:T(8,128)(2,1)S(1)}, u32[]{:S(2)}, u32[]{:S(2)}) %collective-permute-start.3) | collective-permute-done | bytes 296480 | tf_op jit(solution)/shard_map/ppermute | solution.py:78
  60.8 0.6 fusion.39
  61.4 0.8 copy-done
  62.1 1.3 fusion.8
  63.5 0.5 copy-done.2
  64.0 1.9 %fusion.6 = (f32[576]{0:T(1024)S(1)}, f32[576]{0:T(1024)S(1)}, f32[576]{0:T(1024)S(1)}) fusion(f32[576,576]{0,1:T(8,128)S(1)} %copy-done.1, f32[576]{0:T(1024)S(1)} %get-tuple-element.53, pred[]{:T(512)S(6)} %ge.15, s32[576]{0:T(1024)S(1)} %get-tuple-element.65, s32[576]{0:T(1024)S(1)} %convert_element_type.51, f32[576,576]{0,1:T(8,128)S(1)} %get-tuple-element.55, ...), kind=kLoop, calls=%fused_computation.27 | loop fusion | flops 6965568 | bytes 4008963 | tf_op jit(solution)/shard_map/reduce_sum | solution.py:61
  65.9 0.8 fusion
  66.8 0.8 fusion.1
  67.6 0.8 fusion.2
  68.4 0.8 fusion.3
  69.2 0.8 fusion.5
  70.0 10.8 %all_gather.7 = bf16[576,512]{1,0:T(8,128)(2,1)S(1)} all-gather(bf16[576,128]{1,0:T(8,128)(2,1)S(1)} %fusion.5), channel_id=1, replica_groups=mesh['z'=16,'y'=4,'x'=4,'c'=2] {'y'}, dimensions={1}, use_global_device_ids=true | all-gather | bytes 737280 | tf_op jit(solution)/shard_map/all_gather | solution.py:86
  80.8 10.0 %all-gather.2.cloned.1.call-done = bf16[512,1792]{0,1:T(8,128)(2,1)} async-done(((bf16[512,112]{0,1:T(8,128)(2,1)}), bf16[512,1792]{0,1:T(8,128)(2,1)}) %all-gather.2.cloned.1.call-update) | async-done | bytes 1835024 | tf_op jit(solution)/shard_map/all_gather | solution.py:87
  90.7 1.6 dynamic-slice_bitcast_fusion
  92.3 10.3 %collective-permute-start.5 = (bf16[512,8,112]{0,2,1:T(8,128)(2,1)S(1)}, bf16[512,8,112]{0,2,1:T(8,128)(2,1)S(1)}, u32[]{:S(2)}, u32[]{:S(2)}) collective-permute-start(bf16[512,8,112]{0,2,1:T(8,128)(2,1)S(1)} %get-tuple-element.50), channel_id=1, source_target_pairs={{0,1},{1,0},{2,3},{3,2},{4,5},{5,4},{6,7},{7,6},{8,9},{9,8},{10,11... | collective-permute-start | bytes 2752520 | tf_op jit(solution)/shard_map/ppermute | solution.py:93
  102.7 1.9 %collective-permute-start.4 = (bf16[576,512]{1,0:T(8,128)(2,1)S(1)}, bf16[576,512]{1,0:T(8,128)(2,1)S(1)}, u32[]{:S(2)}, u32[]{:S(2)}) collective-permute-start(bf16[576,512]{1,0:T(8,128)(2,1)S(1)} %all_gather.7), channel_id=1, source_target_pairs={{0,1},{1,0},{2,3},{3,2},{4,5},{5,4},{6,7},{7,6},{8,9},{9,8},{10,11... | collective-permute-start | bytes 1769480 | tf_op jit(solution)/shard_map/ppermute | solution.py:89
  104.6 0.9 fusion.44
  105.5 1.1 collective-permute-done.4
  106.6 1.9 %add_convert_fusion = bf16[576,896]{0,1:T(8,128)(2,1)} fusion(f32[576,896]{0,1:T(8,128)S(1)} %fusion.44, bf16[576,512]{1,0:T(8,128)(2,1)S(1)} %collective-permute-done.4, bf16[512,896]{0,1:T(8,128)(2,1)S(1)} %bitcast.96), kind=kOutput, calls=%fused_computation | convolution fusion | flops 529514496 | bytes 4603904 | tf_op jit(solution)/shard_map/dot_general | solution.py:99
  108.5 31.9 %reduce-scatter.2.cloned.1.call-done = bf16[576,224]{0,1:T(8,128)(2,1)} async-done(((bf16[576,896]{0,1:T(8,128)(2,1)}), bf16[576,224]{0,1:T(8,128)(2,1)}) %reduce-scatter.2.cloned.1.call-update) | async-done | bytes 258064 | tf_op jit(solution)/shard_map/reduce_scatter | solution.py:102
  140.4 1.1 copy.31
  141.6 0.2 reshape.491
  141.7 0.7 copy.32
  142.5 6.1 %all-to-all-start.1 = ((bf16[8,144,112]{2,1,0:T(8,128)(2,1)}), bf16[8,144,112]{2,1,0:T(8,128)(2,1)S(1)}, u32[]{:S(2)}, u32[]{:S(2)}) async-start(bf16[8,144,112]{2,1,0:T(8,128)(2,1)} %bitcast.25), calls=%async_computation.2 | async-start | bytes 589824 | tf_op jit(solution)/shard_map/all_to_all | solution.py:106
  148.6 0.8 copy.34
  149.4 6.1 %all-to-all-done.1 = bf16[8,144,112]{2,1,0:T(8,128)(2,1)S(1)} async-done(((bf16[8,144,112]{2,1,0:T(8,128)(2,1)}), bf16[8,144,112]{2,1,0:T(8,128)(2,1)S(1)}, u32[]{:S(2)}, u32[]{:S(2)}) %all-to-all-start.1) | async-done | bytes 258080 | tf_op jit(solution)/shard_map/all_to_all | solution.py:106
  155.5 0.2 copy.33
  155.6 0.9 reshape.494
  (44 shorter events, 0.6 us)
Async XLA Ops:
  11.2 11.6 %all-to-all-start = ((bf16[145,3,4,1,128]{4,0,1,3,2:T(8,128)(2,1)}), bf16[145,3,4,1,128]{4,0,1,3,2:T(8,128)(2,1)S(1)}, u32[]{:S(2)}, u32[]{:S(2)}) async-start(bf16[145,3,4,1,128]{4,0,1,3,2:T(8,128)(2,1)} %copy.23), calls=%async_computation | async-start | bytes 933888 | tf_op jit(solution)/shard_map/all_to_all | solution.py:29
  16.2 74.5 %all-gather.2.cloned.1.call-start = ((), (), s32[]{:S(2)}) async-start(), calls=%async_computation.3 | async-start | bytes 1949696 | tf_op jit(solution)/shard_map/all_gather | solution.py:87
  16.9 123.5 %reduce-scatter.2.cloned.1.call-start = ((), (), s32[]{:S(2)}) async-start(), calls=%async_computation.4 | async-start | bytes 1433600 | tf_op jit(solution)/shard_map/reduce_scatter | solution.py:102
  23.1 8.3 %collective-permute-start = (bf16[579,2,1,128]{3,0,1,2:T(8,128)(2,1)S(1)}, bf16[579,2,1,128]{3,0,1,2:T(8,128)(2,1)S(1)}, u32[]{:S(2)}, u32[]{:S(2)}) collective-permute-start(bf16[579,2,1,128]{3,0,1,2:T(8,128)(2,1)S(1)} %pad_maximum_fusion.1), channel_id=1, source_target_pairs={{0,32},{32,64},{64,96},{96,128},{128,160},{160,192},{192,224},{224... | collective-permute-start | bytes 889352 | tf_op jit(solution)/shard_map/ppermute | solution.py:78
  31.4 7.7 %collective-permute-start.1 = (bf16[579,2,1,128]{3,0,1,2:T(8,128)(2,1)S(1)}, bf16[579,2,1,128]{3,0,1,2:T(8,128)(2,1)S(1)}, u32[]{:S(2)}, u32[]{:S(2)}) collective-permute-start(bf16[579,2,1,128]{3,0,1,2:T(8,128)(2,1)S(1)} %collective-permute-done), channel_id=1, source_target_pairs={{0,32},{32,64},{64,96},{96,128},{128,160},{160,192},{192,224},{224... | collective-permute-start | bytes 889352 | tf_op jit(solution)/shard_map/ppermute | solution.py:78
  39.2 10.0 %collective-permute-start.2 = (bf16[579,2,1,128]{3,0,1,2:T(8,128)(2,1)S(1)}, bf16[579,2,1,128]{3,0,1,2:T(8,128)(2,1)S(1)}, u32[]{:S(2)}, u32[]{:S(2)}) collective-permute-start(bf16[579,2,1,128]{3,0,1,2:T(8,128)(2,1)S(1)} %collective-permute-done.1), channel_id=1, source_target_pairs={{0,32},{32,64},{64,96},{96,128},{128,160},{160,192},{192,224},{224... | collective-permute-start | bytes 889352 | tf_op jit(solution)/shard_map/ppermute | solution.py:78
  49.3 11.4 %collective-permute-start.3 = (bf16[579,2,1,128]{3,0,1,2:T(8,128)(2,1)S(1)}, bf16[579,2,1,128]{3,0,1,2:T(8,128)(2,1)S(1)}, u32[]{:S(2)}, u32[]{:S(2)}) collective-permute-start(bf16[579,2,1,128]{3,0,1,2:T(8,128)(2,1)S(1)} %collective-permute-done.2), channel_id=1, source_target_pairs={{0,32},{32,64},{64,96},{96,128},{128,160},{160,192},{192,224},{224... | collective-permute-start | bytes 889352 | tf_op jit(solution)/shard_map/ppermute | solution.py:78
  60.8 1.4 copy-start
  62.1 1.4 copy-start.1
  62.1 1.8 %copy-start.2 = (f32[576,576]{0,1:T(8,128)S(1)}, f32[576,576]{0,1:T(8,128)}, u32[]{:S(2)}) copy-start(f32[576,576]{0,1:T(8,128)} %get-tuple-element.57) | copy-start | bytes 3981316
  92.3 14.2 %collective-permute-start.5 = (bf16[512,8,112]{0,2,1:T(8,128)(2,1)S(1)}, bf16[512,8,112]{0,2,1:T(8,128)(2,1)S(1)}, u32[]{:S(2)}, u32[]{:S(2)}) collective-permute-start(bf16[512,8,112]{0,2,1:T(8,128)(2,1)S(1)} %get-tuple-element.50), channel_id=1, source_target_pairs={{0,1},{1,0},{2,3},{3,2},{4,5},{5,4},{6,7},{7,6},{8,9},{9,8},{10,11... | collective-permute-start | bytes 2752520 | tf_op jit(solution)/shard_map/ppermute | solution.py:93
  102.7 3.9 %collective-permute-start.4 = (bf16[576,512]{1,0:T(8,128)(2,1)S(1)}, bf16[576,512]{1,0:T(8,128)(2,1)S(1)}, u32[]{:S(2)}, u32[]{:S(2)}) collective-permute-start(bf16[576,512]{1,0:T(8,128)(2,1)S(1)} %all_gather.7), channel_id=1, source_target_pairs={{0,1},{1,0},{2,3},{3,2},{4,5},{5,4},{6,7},{7,6},{8,9},{9,8},{10,11... | collective-permute-start | bytes 1769480 | tf_op jit(solution)/shard_map/ppermute | solution.py:89
  142.5 13.0 %all-to-all-start.1 = ((bf16[8,144,112]{2,1,0:T(8,128)(2,1)}), bf16[8,144,112]{2,1,0:T(8,128)(2,1)S(1)}, u32[]{:S(2)}, u32[]{:S(2)}) async-start(bf16[8,144,112]{2,1,0:T(8,128)(2,1)} %bitcast.25), calls=%async_computation.2 | async-start | bytes 589824 | tf_op jit(solution)/shard_map/all_to_all | solution.py:106
Sparse Core Ops, SparseCore 0:
  19.1 71.5 all-gather.1
  108.6 31.7 reduce-scatter.1

commit v5 on v4

--- a/solution.py
+++ b/solution.py
@@ -99,9 +99,15 @@
     partial_value = partial_value + jnp.dot(
         other_attended, other_weight, preferred_element_type=jnp.float32
     )
-    summed = lax.psum_scatter(
-        partial_value.astype(jnp.bfloat16), "x", scatter_dimension=1, tiled=True
-    )
+    nx = lax.axis_size("x")
+    x = lax.axis_index("x")
+    quarters = partial_value.astype(jnp.bfloat16).reshape(level, nx, -1)
+    summed = lax.dynamic_index_in_dim(quarters, x, axis=1, keepdims=False).astype(jnp.float32)
+    for shift in range(1, nx):
+        part = lax.dynamic_index_in_dim(quarters, (x + shift) % nx, axis=1, keepdims=False)
+        part = lax.ppermute(part, "x", [(i, (i + shift) % nx) for i in range(nx)])
+        summed = summed + part.astype(jnp.float32)
+    summed = summed.astype(jnp.bfloat16)
     summed = summed.reshape(NY, rows, 2, chunk).transpose(0, 2, 1, 3).reshape(2 * NY, rows, chunk)
     summed = lax.all_to_all(summed, ("y", "c"), 0, 0, tiled=True)
     hidden_states = summed.reshape(NY, 2, rows, chunk).transpose(2, 1, 0, 3).reshape(rows, 2 * NY * chunk)

time: 164 us -> 161 us (0.982)
  the two profiles are of different devices: /device:TPU:1 before, /device:TPU:130 now
where the time goes in v5:
time: 161 us; the launch traced here: 160 us
  waiting for transfers between devices  54.9 us (34%)
  starting transfers between devices  33.5 us (21%)
  matrix products  20.9 us (13%)
  local copies, waits for them, and re-layouts  15.4 us (10%)
  between operations  14.6 us (9%)
  blocking collectives  13.6 us (8%)
  other arithmetic  7.05 us (4%)
    ppermute x4, waiting for transfers between devices, local(): block = lax.ppermute(block, 'z', [(i, i + 1) for i in range(nz - 1)])  28.5 us
    all_gather x1, blocking collectives, local(): own_attended = lax.all_gather(attended, 'y', axis=1, tiled=True)  13.6 us
    ppermute x3, waiting for transfers between devices, local(): part = lax.ppermute(part, 'x', [(i, (i + shift) % nx) for i in range(nx)])  11.1 us
    ppermute x3, starting transfers between devices, local(): part = lax.ppermute(part, 'x', [(i, (i + shift) % nx) for i in range(nx)])  10.8 us
    dot_general x5, matrix products, attend(): jnp.einsum('qhd,khd->hqk', query_rows, key_rows, preferred_element_type=j...  10.5 us
    ppermute x4, starting transfers between devices, local(): block = lax.ppermute(block, 'z', [(i, i + 1) for i in range(nz - 1)])  10.3 us
    dot_general x5, matrix products, attend(): jnp.einsum('hqk,khd->hqd', probs.astype(jnp.bfloat16), value_rows, prefer...  7.58 us
    all_to_all x1, waiting for transfers between devices, local(): summed = lax.all_to_all(summed, ('y', 'c'), 0, 0, tiled=True)  7.05 us
  transfers between devices with their start and end apart: 12, of which 10 were waited for; matrix products, arithmetic and copies ran while one was open for 19% of the time, Pallas kernels for 0%

profile of v5, /device:TPU:130, one launch (start us, length us, event | category | flops | bytes accessed | tf_op | source)
XLA Modules:
  0.0 159.8 jit_solution(9190665354555996111)
XLA Ops:
  7.2 1.2 reshape.502
  8.3 1.0 reshape.472
  10.4 0.8 copy.25
  11.2 4.5 %all-to-all-start = ((bf16[145,3,4,1,128]{4,0,1,3,2:T(8,128)(2,1)}), bf16[145,3,4,1,128]{4,0,1,3,2:T(8,128)(2,1)S(1)}, u32[]{:S(2)}, u32[]{:S(2)}) async-start(bf16[145,3,4,1,128]{4,0,1,3,2:T(8,128)(2,1)} %copy.25), calls=%async_computation | async-start | bytes 933888 | tf_op jit(solution)/shard_map/all_to_all | solution.py:29
  15.7 0.7 all-gather.2.cloned.1.call-update
  17.6 6.9 %all-to-all-done = bf16[145,3,4,1,128]{4,0,1,3,2:T(8,128)(2,1)S(1)} async-done(((bf16[145,3,4,1,128]{4,0,1,3,2:T(8,128)(2,1)}), bf16[145,3,4,1,128]{4,0,1,3,2:T(8,128)(2,1)S(1)}, u32[]{:S(2)}, u32[]{:S(2)}) %all-to-all-start) | async-done | bytes 445472 | tf_op jit(solution)/shard_map/all_to_all | solution.py:29
  24.8 3.8 %collective-permute-start = (bf16[579,2,1,128]{3,0,1,2:T(8,128)(2,1)S(1)}, bf16[579,2,1,128]{3,0,1,2:T(8,128)(2,1)S(1)}, u32[]{:S(2)}, u32[]{:S(2)}) collective-permute-start(bf16[579,2,1,128]{3,0,1,2:T(8,128)(2,1)S(1)} %pad_maximum_fusion.1), channel_id=1, source_target_pairs={{0,32},{32,64},{64,96},{96,128},{128,160},{160,192},{192,224},{224... | collective-permute-start | bytes 889352 | tf_op jit(solution)/shard_map/ppermute | solution.py:78
  28.7 2.3 %fusion.46 = (f32[576]{0:T(1024)}, f32[576,576]{0,1:T(8,128)}) fusion(bf16[576,128]{1,0:T(8,128)(2,1)S(1)} %bitcast.108, bf16[576,2,1,128]{3,0,1,2:T(8,128)(2,1)S(1)} %bitcast.104, pred[]{:T(512)S(6)} %ge.15, s32[576]{0:T(1024)S(1)} %get-tuple-element.68, s32[576]{0:T(1024)S(1)} %convert_element_type.69), kind=kOutput, calls=%fused_computation.99 | convolution fusion | flops 87256512 | bytes 1640705 | tf_op jit(solution)/shard_map/qhd,khd->hqk/dot_general | solution.py:49
  31.0 4.3 %collective-permute-done = bf16[579,2,1,128]{3,0,1,2:T(8,128)(2,1)S(1)} collective-permute-done((bf16[579,2,1,128]{3,0,1,2:T(8,128)(2,1)S(1)}, bf16[579,2,1,128]{3,0,1,2:T(8,128)(2,1)S(1)}, u32[]{:S(2)}, u32[]{:S(2)}) %collective-permute-start) | collective-permute-done | bytes 296480 | tf_op jit(solution)/shard_map/ppermute | solution.py:78
  35.3 2.6 %collective-permute-start.1 = (bf16[579,2,1,128]{3,0,1,2:T(8,128)(2,1)S(1)}, bf16[579,2,1,128]{3,0,1,2:T(8,128)(2,1)}, u32[]{:S(2)}, u32[]{:S(2)}) collective-permute-start(bf16[579,2,1,128]{3,0,1,2:T(8,128)(2,1)S(1)} %collective-permute-done), channel_id=1, source_target_pairs={{0,32},{32,64},{64,96},{96,128},{128,160},{160,192},{192,224},{224... | collective-permute-start | bytes 889352 | tf_op jit(solution)/shard_map/ppermute | solution.py:78
  37.9 1.2 fusion.45
  39.1 9.4 %collective-permute-done.1 = bf16[579,2,1,128]{3,0,1,2:T(8,128)(2,1)} collective-permute-done((bf16[579,2,1,128]{3,0,1,2:T(8,128)(2,1)S(1)}, bf16[579,2,1,128]{3,0,1,2:T(8,128)(2,1)}, u32[]{:S(2)}, u32[]{:S(2)}) %collective-permute-start.1) | collective-permute-done | bytes 296480 | tf_op jit(solution)/shard_map/ppermute | solution.py:78
  49.2 1.9 %collective-permute-start.2 = (bf16[579,2,1,128]{3,0,1,2:T(8,128)(2,1)}, bf16[579,2,1,128]{3,0,1,2:T(8,128)(2,1)S(1)}, u32[]{:S(2)}, u32[]{:S(2)}) collective-permute-start(bf16[579,2,1,128]{3,0,1,2:T(8,128)(2,1)} %collective-permute-done.1), channel_id=1, source_target_pairs={{0,32},{32,64},{64,96},{96,128},{128,160},{160,192},{192,224},{224... | collective-permute-start | bytes 889352 | tf_op jit(solution)/shard_map/ppermute | solution.py:78
  51.1 2.1 %fusion.44 = (f32[576]{0:T(1024)}, f32[576,576]{0,1:T(8,128)S(1)}) fusion(bf16[576,128]{1,0:T(8,128)(2,1)} %bitcast.110, bf16[579,2,1,128]{3,0,1,2:T(8,128)(2,1)} %collective-permute-done.1, pred[]{:T(512)S(6)} %ge.17, s32[576]{0:T(1024)S(1)} %get-tuple-element.68, s32[576]{0:T(1024)S(1)} %iota_add_fusion.2, s32[576]{0:T(1024)S(1)} %convert_element_type.69, ...), kind=kOutput, calls=%fused_computation.97 | convolution fusion | flops 87256512 | bytes 1633537 | tf_op jit(solution)/shard_map/qhd,khd->hqk/dot_general | solution.py:49
  53.3 8.6 %collective-permute-done.2 = bf16[579,2,1,128]{3,0,1,2:T(8,128)(2,1)S(1)} collective-permute-done((bf16[579,2,1,128]{3,0,1,2:T(8,128)(2,1)}, bf16[579,2,1,128]{3,0,1,2:T(8,128)(2,1)S(1)}, u32[]{:S(2)}, u32[]{:S(2)}) %collective-permute-start.2) | collective-permute-done | bytes 296480 | tf_op jit(solution)/shard_map/ppermute | solution.py:78
  61.9 0.7 copy-done.16
  63.2 1.3 reshape.487
  64.4 1.9 %collective-permute-start.3 = (bf16[579,2,1,128]{3,0,1,2:T(8,128)(2,1)}, bf16[579,2,1,128]{3,0,1,2:T(8,128)(2,1)S(1)}, u32[]{:S(2)}, u32[]{:S(2)}) collective-permute-start(bf16[579,2,1,128]{3,0,1,2:T(8,128)(2,1)} %copy-done.16), channel_id=1, source_target_pairs={{0,32},{32,64},{64,96},{96,128},{128,160},{160,192},{192,224},{224... | collective-permute-start | bytes 889352 | tf_op jit(solution)/shard_map/ppermute | solution.py:78
  67.0 3.3 %fusion.43 = (f32[576]{0:T(1024)}, f32[576,576]{0,1:T(8,128)}) fusion(bf16[576,128]{1,0:T(8,128)(2,1)} %bitcast.111, bf16[579,2,1,128]{3,0,1,2:T(8,128)(2,1)} %copy-done.16, pred[]{:T(512)S(6)} %ge.18, s32[576]{0:T(1024)S(1)} %get-tuple-element.68, s32[576]{0:T(1024)} %get-tuple-element.67, s32[576]{0:T(1024)S(1)} %convert_element_type.69, ...), kind=kOutput, calls=%fused_computation.96 | convolution fusion | flops 87256512 | bytes 1635329 | tf_op jit(solution)/shard_map/qhd,khd->hqk/dot_general | solution.py:49
  70.3 6.3 %collective-permute-done.3 = bf16[579,2,1,128]{3,0,1,2:T(8,128)(2,1)S(1)} collective-permute-done((bf16[579,2,1,128]{3,0,1,2:T(8,128)(2,1)}, bf16[579,2,1,128]{3,0,1,2:T(8,128)(2,1)S(1)}, u32[]{:S(2)}, u32[]{:S(2)}) %collective-permute-start.3) | collective-permute-done | bytes 296480 | tf_op jit(solution)/shard_map/ppermute | solution.py:78
  76.6 0.7 copy-done.17
  77.9 1.3 reshape.490
  79.9 1.6 fusion.42
  81.6 1.3 fusion.8
  83.4 1.9 %fusion.6 = (f32[576]{0:T(1024)S(1)}, f32[576]{0:T(1024)S(1)}, f32[576]{0:T(1024)S(1)}) fusion(f32[576,576]{0,1:T(8,128)S(1)} %copy-done, f32[576]{0:T(1024)S(1)} %get-tuple-element.56, pred[]{:T(512)S(6)} %ge.15, s32[576]{0:T(1024)S(1)} %get-tuple-element.68, s32[576]{0:T(1024)S(1)} %convert_element_type.69, f32[576,576]{0,1:T(8,128)S(1)} %get-tuple-element.58, ...), kind=kLoop, calls=%fused_computation.27 | loop fusion | flops 6965568 | bytes 4008963 | tf_op jit(solution)/shard_map/reduce_sum | solution.py:61
  85.4 0.8 fusion
  86.2 1.7 %fusion.1 = f32[576,128]{1,0:T(8,128)S(1)} fusion(f32[576,128]{1,0:T(8,128)S(1)} %fusion, f32[576,576]{0,1:T(8,128)S(1)} %get-tuple-element.64, f32[576]{0:T(1024)S(1)} %get-tuple-element.49, bf16[579,2,1,128]{3,0,1,2:T(8,128)(2,1)} %copy-done.15, f32[576]{0:T(1024)S(1)} %get-tuple-element.44, s32[576]{0:T(1024)S(1)} %get-tuple-element.68, ...), kind=kOutput, calls=%fused_computation.22 | convolution fusion | flops 87404544 | bytes 2078209 | tf_op jit(solution)/shard_map/hqk,khd->hqd/dot_general | solution.py:62
  87.9 1.7 %fusion.2 = f32[576,128]{1,0:T(8,128)S(1)} fusion(f32[576,128]{1,0:T(8,128)S(1)} %fusion.1, f32[576,576]{0,1:T(8,128)S(1)} %get-tuple-element.62, f32[576]{0:T(1024)S(1)} %get-tuple-element.48, bf16[579,2,1,128]{3,0,1,2:T(8,128)(2,1)} %collective-permute-done.1, f32[576]{0:T(1024)S(1)} %get-tuple-element.43, s32[576]{0:T(1024)S(1)} %get-tuple-element.68, ...), kind=kOutput, calls=%fused_computation.23 | convolution fusion | flops 87404544 | bytes 2078209 | tf_op jit(solution)/shard_map/hqk,khd->hqd/dot_general | solution.py:62
  89.6 1.7 %fusion.3 = f32[576,128]{1,0:T(8,128)S(1)} fusion(f32[576,128]{1,0:T(8,128)S(1)} %fusion.2, f32[576,576]{0,1:T(8,128)S(1)} %copy-done.1, f32[576]{0:T(1024)S(1)} %get-tuple-element.47, bf16[579,2,1,128]{3,0,1,2:T(8,128)(2,1)} %copy-done.16, f32[576]{0:T(1024)S(1)} %get-tuple-element.42, s32[576]{0:T(1024)S(1)} %get-tuple-element.68, ...), kind=kOutput, calls=%fused_computation.24 | convolution fusion | flops 87404544 | bytes 2078209 | tf_op jit(solution)/shard_map/hqk,khd->hqd/dot_general | solution.py:62
  91.3 1.7 %fusion.5 = bf16[576,128]{1,0:T(8,128)(2,1)S(1)} fusion(f32[576,128]{1,0:T(8,128)S(1)} %fusion.3, f32[576,576]{0,1:T(8,128)S(1)} %get-tuple-element.58, f32[576]{0:T(1024)S(1)} %get-tuple-element.46, bf16[579,2,1,128]{3,0,1,2:T(8,128)(2,1)} %copy-done.17, f32[576]{0:T(1024)S(1)} %get-tuple-element.41, s32[576]{0:T(1024)S(1)} %get-tuple-element.68, ...), kind=kOutput, calls=%fused_computation.26 | convolution fusion | flops 87478272 | bytes 1930753 | tf_op jit(solution)/shard_map/hqk,khd->hqd/dot_general | solution.py:62
  93.0 13.6 %all_gather.7 = bf16[576,512]{1,0:T(8,128)(2,1)S(1)} all-gather(bf16[576,128]{1,0:T(8,128)(2,1)S(1)} %fusion.5), channel_id=1, replica_groups=mesh['z'=16,'y'=4,'x'=4,'c'=2] {'y'}, dimensions={1}, use_global_device_ids=true | all-gather | bytes 737280 | tf_op jit(solution)/shard_map/all_gather | solution.py:86
  106.5 1.6 dynamic-slice_bitcast_fusion
  108.1 1.9 %collective-permute-start.5 = (bf16[512,8,112]{0,2,1:T(8,128)(2,1)S(1)}, bf16[512,8,112]{0,2,1:T(8,128)(2,1)}, u32[]{:S(2)}, u32[]{:S(2)}) collective-permute-start(bf16[512,8,112]{0,2,1:T(8,128)(2,1)S(1)} %get-tuple-element.50), channel_id=1, source_target_pairs={{0,1},{1,0},{2,3},{3,2},{4,5},{5,4},{6,7},{7,6},{8,9},{9,8},{10,11... | collective-permute-start | bytes 2752520 | tf_op jit(solution)/shard_map/ppermute | solution.py:93
  110.1 2.6 %collective-permute-start.4 = (bf16[576,512]{1,0:T(8,128)(2,1)S(1)}, bf16[576,512]{1,0:T(8,128)(2,1)S(1)}, u32[]{:S(2)}, u32[]{:S(2)}) collective-permute-start(bf16[576,512]{1,0:T(8,128)(2,1)S(1)} %all_gather.7), channel_id=1, source_target_pairs={{0,1},{1,0},{2,3},{3,2},{4,5},{5,4},{6,7},{7,6},{8,9},{9,8},{10,11... | collective-permute-start | bytes 1769480 | tf_op jit(solution)/shard_map/ppermute | solution.py:89
  112.7 0.8 fusion.47
  114.1 2.0 %add_convert_fusion = bf16[576,896]{1,0:T(8,128)(2,1)S(1)} fusion(f32[576,896]{1,0:T(8,128)S(1)} %fusion.47, bf16[576,512]{1,0:T(8,128)(2,1)S(1)} %collective-permute-done.4, bf16[512,896]{0,1:T(8,128)(2,1)} %bitcast.23), kind=kOutput, calls=%fused_computation | convolution fusion | flops 529514496 | bytes 4603904 | tf_op jit(solution)/shard_map/dot_general | solution.py:99
  116.1 1.1 copy.33
  117.3 3.6 %collective-permute-start.6 = (bf16[576,224]{0,1:T(8,128)(2,1)S(1)}, bf16[576,224]{0,1:T(8,128)(2,1)S(1)}, u32[]{:S(2)}, u32[]{:S(2)}) collective-permute-start(bf16[576,224]{0,1:T(8,128)(2,1)S(1)} %get-tuple-element.52), channel_id=1, source_target_pairs={{0,2},{2,4},{4,6},{6,0},{1,3},{3,5},{5,7},{7,1},{8,10},{10,12},{12... | collective-permute-start | bytes 774152 | tf_op jit(solution)/shard_map/ppermute | solution.py:108
  121.0 2.7 %collective-permute-start.7 = (bf16[576,224]{0,1:T(8,128)(2,1)S(1)}, bf16[576,224]{0,1:T(8,128)(2,1)S(1)}, u32[]{:S(2)}, u32[]{:S(2)}) collective-permute-start(bf16[576,224]{0,1:T(8,128)(2,1)S(1)} %get-tuple-element.54), channel_id=1, source_target_pairs={{0,4},{2,6},{4,0},{6,2},{1,5},{3,7},{5,1},{7,3},{8,12},{10,14},{12... | collective-permute-start | bytes 774152 | tf_op jit(solution)/shard_map/ppermute | solution.py:108
  123.7 4.5 %collective-permute-start.8 = (bf16[576,224]{0,1:T(8,128)(2,1)S(1)}, bf16[576,224]{0,1:T(8,128)(2,1)S(1)}, u32[]{:S(2)}, u32[]{:S(2)}) collective-permute-start(bf16[576,224]{0,1:T(8,128)(2,1)S(1)} %get-tuple-element.53), channel_id=1, source_target_pairs={{0,6},{2,0},{4,2},{6,4},{1,7},{3,1},{5,3},{7,5},{8,14},{10,8},{12,... | collective-permute-start | bytes 774152 | tf_op jit(solution)/shard_map/ppermute | solution.py:108
  128.2 0.7 collective-permute-done.6
  128.9 5.2 %collective-permute-done.7 = bf16[576,224]{0,1:T(8,128)(2,1)S(1)} collective-permute-done((bf16[576,224]{0,1:T(8,128)(2,1)S(1)}, bf16[576,224]{0,1:T(8,128)(2,1)S(1)}, u32[]{:S(2)}, u32[]{:S(2)}) %collective-permute-start.7) | collective-permute-done | bytes 258080 | tf_op jit(solution)/shard_map/ppermute | solution.py:108
  134.1 5.2 %collective-permute-done.8 = bf16[576,224]{0,1:T(8,128)(2,1)S(1)} collective-permute-done((bf16[576,224]{0,1:T(8,128)(2,1)S(1)}, bf16[576,224]{0,1:T(8,128)(2,1)S(1)}, u32[]{:S(2)}, u32[]{:S(2)}) %collective-permute-start.8) | collective-permute-done | bytes 258080 | tf_op jit(solution)/shard_map/ppermute | solution.py:108
  139.8 0.8 copy.35
  140.6 3.4 %all-to-all-start.1 = ((bf16[8,144,112]{2,1,0:T(8,128)(2,1)}), bf16[8,144,112]{2,1,0:T(8,128)(2,1)S(1)}, u32[]{:S(2)}, u32[]{:S(2)}) async-start(bf16[8,144,112]{2,1,0:T(8,128)(2,1)} %bitcast.30), calls=%async_computation.1 | async-start | bytes 589824 | tf_op jit(solution)/shard_map/all_to_all | solution.py:112
  144.0 0.8 copy.37
  144.8 7.1 %all-to-all-done.1 = bf16[8,144,112]{2,1,0:T(8,128)(2,1)S(1)} async-done(((bf16[8,144,112]{2,1,0:T(8,128)(2,1)}), bf16[8,144,112]{2,1,0:T(8,128)(2,1)S(1)}, u32[]{:S(2)}, u32[]{:S(2)}) %all-to-all-start.1) | async-done | bytes 258080 | tf_op jit(solution)/shard_map/all_to_all | solution.py:112
  152.0 0.9 reshape.500
  (80 shorter events, 7.7 us)
Async XLA Ops:
  11.2 13.3 %all-to-all-start = ((bf16[145,3,4,1,128]{4,0,1,3,2:T(8,128)(2,1)}), bf16[145,3,4,1,128]{4,0,1,3,2:T(8,128)(2,1)S(1)}, u32[]{:S(2)}, u32[]{:S(2)}) async-start(bf16[145,3,4,1,128]{4,0,1,3,2:T(8,128)(2,1)} %copy.25), calls=%async_computation | async-start | bytes 933888 | tf_op jit(solution)/shard_map/all_to_all | solution.py:29
  15.7 90.9 %all-gather.2.cloned.1.call-start = ((), (), s32[]{:S(2)}) async-start(), calls=%async_computation.2 | async-start | bytes 1949696 | tf_op jit(solution)/shard_map/all_gather | solution.py:87
  24.8 10.5 %collective-permute-start = (bf16[579,2,1,128]{3,0,1,2:T(8,128)(2,1)S(1)}, bf16[579,2,1,128]{3,0,1,2:T(8,128)(2,1)S(1)}, u32[]{:S(2)}, u32[]{:S(2)}) collective-permute-start(bf16[579,2,1,128]{3,0,1,2:T(8,128)(2,1)S(1)} %pad_maximum_fusion.1), channel_id=1, source_target_pairs={{0,32},{32,64},{64,96},{96,128},{128,160},{160,192},{192,224},{224... | collective-permute-start | bytes 889352 | tf_op jit(solution)/shard_map/ppermute | solution.py:78
  28.7 9.2 %copy-start.2 = (bf16[4,144,1,1,128]{4,1,0,3,2:T(8,128)(2,1)}, bf16[4,144,1,1,128]{4,1,0,3,2:T(8,128)(2,1)S(1)}, u32[]{:S(2)}) copy-start(bf16[4,144,1,1,128]{4,1,0,3,2:T(8,128)(2,1)S(1)} %slice.116) | copy-start | bytes 442372
  35.3 3.9 %copy-start.15 = (bf16[579,2,1,128]{3,0,1,2:T(8,128)(2,1)}, bf16[579,2,1,128]{3,0,1,2:T(8,128)(2,1)S(1)}, u32[]{:S(2)}) copy-start(bf16[579,2,1,128]{3,0,1,2:T(8,128)(2,1)S(1)} %collective-permute-done) | copy-start | bytes 889348
  35.3 13.2 %collective-permute-start.1 = (bf16[579,2,1,128]{3,0,1,2:T(8,128)(2,1)S(1)}, bf16[579,2,1,128]{3,0,1,2:T(8,128)(2,1)}, u32[]{:S(2)}, u32[]{:S(2)}) collective-permute-start(bf16[579,2,1,128]{3,0,1,2:T(8,128)(2,1)S(1)} %collective-permute-done), channel_id=1, source_target_pairs={{0,32},{32,64},{64,96},{96,128},{128,160},{160,192},{192,224},{224... | collective-permute-start | bytes 889352 | tf_op jit(solution)/shard_map/ppermute | solution.py:78
  37.9 1.2 copy-start.3
  49.2 12.7 %collective-permute-start.2 = (bf16[579,2,1,128]{3,0,1,2:T(8,128)(2,1)}, bf16[579,2,1,128]{3,0,1,2:T(8,128)(2,1)S(1)}, u32[]{:S(2)}, u32[]{:S(2)}) collective-permute-start(bf16[579,2,1,128]{3,0,1,2:T(8,128)(2,1)} %collective-permute-done.1), channel_id=1, source_target_pairs={{0,32},{32,64},{64,96},{96,128},{128,160},{160,192},{192,224},{224... | collective-permute-start | bytes 889352 | tf_op jit(solution)/shard_map/ppermute | solution.py:78
  51.1 2.2 %copy-start.5 = (s32[576]{0:T(1024)}, s32[576]{0:T(1024)S(1)}, u32[]{:S(2)}) copy-start(s32[576]{0:T(1024)S(1)} %slice_convert_fusion.2) | copy-start | bytes 6916
  61.9 0.7 copy-start.16
  64.4 12.2 %collective-permute-start.3 = (bf16[579,2,1,128]{3,0,1,2:T(8,128)(2,1)}, bf16[579,2,1,128]{3,0,1,2:T(8,128)(2,1)S(1)}, u32[]{:S(2)}, u32[]{:S(2)}) collective-permute-start(bf16[579,2,1,128]{3,0,1,2:T(8,128)(2,1)} %copy-done.16), channel_id=1, source_target_pairs={{0,32},{32,64},{64,96},{96,128},{128,160},{160,192},{192,224},{224... | collective-permute-start | bytes 889352 | tf_op jit(solution)/shard_map/ppermute | solution.py:78
  67.0 3.3 %copy-start.10 = (s32[576]{0:T(1024)}, s32[576]{0:T(1024)S(1)}, u32[]{:S(2)}) copy-start(s32[576]{0:T(1024)S(1)} %slice_convert_fusion.1) | copy-start | bytes 6916
  76.6 0.7 copy-start.17
  79.9 1.6 %copy-start.7 = (f32[576]{0:T(1024)S(1)}, f32[576]{0:T(1024)}, u32[]{:S(2)}) copy-start(f32[576]{0:T(1024)} %get-tuple-element.65) | copy-start | bytes 6916
  79.9 1.6 %copy-start.12 = (f32[576]{0:T(1024)S(1)}, f32[576]{0:T(1024)}, u32[]{:S(2)}) copy-start(f32[576]{0:T(1024)} %get-tuple-element.63) | copy-start | bytes 6916
  79.9 1.6 %copy-start.13 = (f32[576]{0:T(1024)S(1)}, f32[576]{0:T(1024)}, u32[]{:S(2)}) copy-start(f32[576]{0:T(1024)} %get-tuple-element.61) | copy-start | bytes 6916
  79.9 1.6 %copy-start.14 = (f32[576]{0:T(1024)S(1)}, f32[576]{0:T(1024)}, u32[]{:S(2)}) copy-start(f32[576]{0:T(1024)} %get-tuple-element.59) | copy-start | bytes 6916
  79.9 1.7 %copy-start.4 = (s32[576]{0:T(1024)S(1)}, s32[576]{0:T(1024)}, u32[]{:S(2)}) copy-start(s32[576]{0:T(1024)} %copy-done.3) | copy-start | bytes 6916
  79.9 1.7 %copy-start.6 = (s32[576]{0:T(1024)S(1)}, s32[576]{0:T(1024)}, u32[]{:S(2)}) copy-start(s32[576]{0:T(1024)} %copy-done.5) | copy-start | bytes 6916
  81.6 1.4 copy-start
  81.6 1.8 %copy-start.1 = (f32[576,576]{0,1:T(8,128)S(1)}, f32[576,576]{0,1:T(8,128)}, u32[]{:S(2)}) copy-start(f32[576,576]{0,1:T(8,128)} %get-tuple-element.60) | copy-start | bytes 3981316
  81.6 1.8 %copy-start.8 = (s32[576]{0:T(1024)S(1)}, s32[576]{0:T(1024)}, u32[]{:S(2)}) copy-start(s32[576]{0:T(1024)} %iota_add_fusion) | copy-start | bytes 6916
  81.6 1.8 %copy-start.9 = (s32[576]{0:T(1024)S(1)}, s32[576]{0:T(1024)}, u32[]{:S(2)}) copy-start(s32[576]{0:T(1024)} %get-tuple-element.67) | copy-start | bytes 6916
  81.6 1.8 %copy-start.11 = (s32[576]{0:T(1024)S(1)}, s32[576]{0:T(1024)}, u32[]{:S(2)}) copy-start(s32[576]{0:T(1024)} %copy-done.10) | copy-start | bytes 6916
  108.1 6.0 %collective-permute-start.5 = (bf16[512,8,112]{0,2,1:T(8,128)(2,1)S(1)}, bf16[512,8,112]{0,2,1:T(8,128)(2,1)}, u32[]{:S(2)}, u32[]{:S(2)}) collective-permute-start(bf16[512,8,112]{0,2,1:T(8,128)(2,1)S(1)} %get-tuple-element.50), channel_id=1, source_target_pairs={{0,1},{1,0},{2,3},{3,2},{4,5},{5,4},{6,7},{7,6},{8,9},{9,8},{10,11... | collective-permute-start | bytes 2752520 | tf_op jit(solution)/shard_map/ppermute | solution.py:93
  110.1 4.0 %collective-permute-start.4 = (bf16[576,512]{1,0:T(8,128)(2,1)S(1)}, bf16[576,512]{1,0:T(8,128)(2,1)S(1)}, u32[]{:S(2)}, u32[]{:S(2)}) collective-permute-start(bf16[576,512]{1,0:T(8,128)(2,1)S(1)} %all_gather.7), channel_id=1, source_target_pairs={{0,1},{1,0},{2,3},{3,2},{4,5},{5,4},{6,7},{7,6},{8,9},{9,8},{10,11... | collective-permute-start | bytes 1769480 | tf_op jit(solution)/shard_map/ppermute | solution.py:89
  117.3 11.6 %collective-permute-start.6 = (bf16[576,224]{0,1:T(8,128)(2,1)S(1)}, bf16[576,224]{0,1:T(8,128)(2,1)S(1)}, u32[]{:S(2)}, u32[]{:S(2)}) collective-permute-start(bf16[576,224]{0,1:T(8,128)(2,1)S(1)} %get-tuple-element.52), channel_id=1, source_target_pairs={{0,2},{2,4},{4,6},{6,0},{1,3},{3,5},{5,7},{7,1},{8,10},{10,12},{12... | collective-permute-start | bytes 774152 | tf_op jit(solution)/shard_map/ppermute | solution.py:108
  121.0 13.1 %collective-permute-start.7 = (bf16[576,224]{0,1:T(8,128)(2,1)S(1)}, bf16[576,224]{0,1:T(8,128)(2,1)S(1)}, u32[]{:S(2)}, u32[]{:S(2)}) collective-permute-start(bf16[576,224]{0,1:T(8,128)(2,1)S(1)} %get-tuple-element.54), channel_id=1, source_target_pairs={{0,4},{2,6},{4,0},{6,2},{1,5},{3,7},{5,1},{7,3},{8,12},{10,14},{12... | collective-permute-start | bytes 774152 | tf_op jit(solution)/shard_map/ppermute | solution.py:108
  123.7 15.7 %collective-permute-start.8 = (bf16[576,224]{0,1:T(8,128)(2,1)S(1)}, bf16[576,224]{0,1:T(8,128)(2,1)S(1)}, u32[]{:S(2)}, u32[]{:S(2)}) collective-permute-start(bf16[576,224]{0,1:T(8,128)(2,1)S(1)} %get-tuple-element.53), channel_id=1, source_target_pairs={{0,6},{2,0},{4,2},{6,4},{1,7},{3,1},{5,3},{7,5},{8,14},{10,8},{12,... | collective-permute-start | bytes 774152 | tf_op jit(solution)/shard_map/ppermute | solution.py:108
  140.6 11.2 %all-to-all-start.1 = ((bf16[8,144,112]{2,1,0:T(8,128)(2,1)}), bf16[8,144,112]{2,1,0:T(8,128)(2,1)S(1)}, u32[]{:S(2)}, u32[]{:S(2)}) async-start(bf16[8,144,112]{2,1,0:T(8,128)(2,1)} %bitcast.30), calls=%async_computation.1 | async-start | bytes 589824 | tf_op jit(solution)/shard_map/all_to_all | solution.py:112
Sparse Core Ops, SparseCore 0:
  18.6 74.5 all-gather.1

commit v6 on v5

--- a/solution.py
+++ b/solution.py
@@ -36,12 +36,10 @@
     pair = jnp.concatenate([pair, seg_rows.reshape(extra, 2, hq, HD)], axis=0)
     query_seg = query_seg.astype(jnp.int32)
     offsets = jnp.arange(level, dtype=jnp.int32)
-    query_pos = z * level + offsets
 
     def attend(carried, block, distance):
         run_max, row_total, accumulated = carried
         source = z - distance
-        key_pos = source * level + offsets
         key_seg = block[level:].reshape(-1)[:level].astype(jnp.int32)
         key_rows = block[:level, 0]
         value_rows = block[:level, 1]
@@ -49,11 +47,11 @@
             jnp.einsum("qhd,khd->hqk", query_rows, key_rows, preferred_element_type=jnp.float32)
             * score_scale
         )
-        allowed = (
-            (key_seg[None, :] == query_seg[:, None])
-            & (key_pos[None, :] <= query_pos[:, None])
-            & (source >= 0)
-        )
+        allowed = key_seg[None, :] == query_seg[:, None]
+        if distance == 0:
+            allowed = allowed & (offsets[None, :] <= offsets[:, None])
+        else:
+            allowed = allowed & (source >= 0)
         masked = jnp.where(allowed[None], scores, -1e30)
         new_max = jnp.maximum(run_max, jnp.max(masked, axis=2))
         probs = jnp.where(allowed[None], jnp.exp(masked - new_max[..., None]), 0.0)

time: 161 us -> 158 us (0.981)
  the two profiles are of different devices: /device:TPU:130 before, /device:TPU:1 now
where the time goes in v6:
time: 158 us; the launch traced here: 157 us
  starting transfers between devices  48.1 us (30%)
  waiting for transfers between devices  29.6 us (19%)
  blocking collectives  23.6 us (15%)
  matrix products  20.8 us (13%)
  between operations  14.5 us (9%)
  local copies, waits for them, and re-layouts  13.6 us (9%)
  other arithmetic  6.58 us (4%)
    ppermute x4, starting transfers between devices, local(): block = lax.ppermute(block, 'z', [(i, i + 1) for i in range(nz - 1)])  18.8 us
    all_gather x1, blocking collectives, local(): own_attended = lax.all_gather(attended, 'y', axis=1, tiled=True)  12.2 us
    all_to_all x1, blocking collectives, local(): lax.all_to_all(packed, 'y', 2, 0, tiled=True)  11.4 us
    ppermute x3, starting transfers between devices, local(): part = lax.ppermute(part, 'x', [(i, (i + shift) % nx) for i in range(nx)])  11.1 us
    dot_general x5, matrix products, attend(): jnp.einsum('qhd,khd->hqk', query_rows, key_rows, preferred_element_type=j...  11 us
    ppermute x1, starting transfers between devices, local(): lax.ppermute(lax.dynamic_index_in_dim(weight_cols, 1 - c, axis=2, keepdim...  10.7 us
    ppermute x4, waiting for transfers between devices, local(): block = lax.ppermute(block, 'z', [(i, i + 1) for i in range(nz - 1)])  9.42 us
    ppermute x3, waiting for transfers between devices, local(): part = lax.ppermute(part, 'x', [(i, (i + shift) % nx) for i in range(nx)])  9.09 us
  transfers between devices with their start and end apart: 11, of which 10 were waited for; matrix products, arithmetic and copies ran while one was open for 18% of the time, Pallas kernels for 0%

profile of v6, /device:TPU:1, one launch (start us, length us, event | category | flops | bytes accessed | tf_op | source)
XLA Modules:
  0.0 156.7 jit_solution(2143625168149722334)
XLA Ops:
  7.2 1.2 reshape.478
  8.4 1.0 reshape.448
  10.5 11.4 %all_to_all.20 = bf16[145,3,4,1,128]{4,0,1,3,2:T(8,128)(2,1)S(1)} all-to-all(bf16[145,3,4,1,128]{4,0,1,3,2:T(8,128)(2,1)S(1)} %copy.25), channel_id=1, replica_groups=mesh['z'=16,'y'=4,'x'=4,'c'=2] {'y'}, dimensions={2} | all-to-all | bytes 890880 | tf_op jit(solution)/shard_map/all_to_all | solution.py:29
  22.2 5.3 %collective-permute-start = (bf16[579,2,1,128]{3,0,1,2:T(8,128)(2,1)S(1)}, bf16[579,2,1,128]{3,0,1,2:T(8,128)(2,1)}, u32[]{:S(2)}, u32[]{:S(2)}) collective-permute-start(bf16[579,2,1,128]{3,0,1,2:T(8,128)(2,1)S(1)} %pad_maximum_fusion.1), channel_id=1, source_target_pairs={{0,32},{32,64},{64,96},{96,128},{128,160},{160,192},{192,224},{224... | collective-permute-start | bytes 889352 | tf_op jit(solution)/shard_map/ppermute | solution.py:76
  27.6 1.1 fusion.61
  28.7 2.3 %collective-permute-done = bf16[579,2,1,128]{3,0,1,2:T(8,128)(2,1)} collective-permute-done((bf16[579,2,1,128]{3,0,1,2:T(8,128)(2,1)S(1)}, bf16[579,2,1,128]{3,0,1,2:T(8,128)(2,1)}, u32[]{:S(2)}, u32[]{:S(2)}) %collective-permute-start) | collective-permute-done | bytes 296480 | tf_op jit(solution)/shard_map/ppermute | solution.py:76
  31.0 0.7 slice.120
  31.7 4.2 %collective-permute-start.1 = (bf16[579,2,1,128]{3,0,1,2:T(8,128)(2,1)}, bf16[579,2,1,128]{3,0,1,2:T(8,128)(2,1)S(1)}, u32[]{:S(2)}, u32[]{:S(2)}) collective-permute-start(bf16[579,2,1,128]{3,0,1,2:T(8,128)(2,1)} %collective-permute-done), channel_id=1, source_target_pairs={{0,32},{32,64},{64,96},{96,128},{128,160},{160,192},{192,224},{224... | collective-permute-start | bytes 889352 | tf_op jit(solution)/shard_map/ppermute | solution.py:76
  35.9 2.1 %fusion.60 = (f32[576]{0:T(1024)}, f32[576,576]{0,1:T(8,128)S(1)}) fusion(bf16[576,128]{1,0:T(8,128)(2,1)} %bitcast.109, bf16[579,2,1,128]{3,0,1,2:T(8,128)(2,1)} %collective-permute-done, pred[]{:T(512)S(6)} %ge.12, s32[576]{0:T(1024)S(1)} %convert_element_type.69, s32[576]{0:T(1024)S(1)} %slice_convert_fusion.3), kind=kOutput, calls=%fused_computation.108 | convolution fusion | flops 86592960 | bytes 1628929 | tf_op jit(solution)/shard_map/qhd,khd->hqk/dot_general | solution.py:47
  38.0 1.9 %collective-permute-done.1 = bf16[579,2,1,128]{3,0,1,2:T(8,128)(2,1)S(1)} collective-permute-done((bf16[579,2,1,128]{3,0,1,2:T(8,128)(2,1)}, bf16[579,2,1,128]{3,0,1,2:T(8,128)(2,1)S(1)}, u32[]{:S(2)}, u32[]{:S(2)}) %collective-permute-start.1) | collective-permute-done | bytes 296480 | tf_op jit(solution)/shard_map/ppermute | solution.py:76
  39.9 0.7 copy-done.7
  40.7 3.7 %collective-permute-start.2 = (bf16[579,2,1,128]{3,0,1,2:T(8,128)(2,1)}, bf16[579,2,1,128]{3,0,1,2:T(8,128)(2,1)S(1)}, u32[]{:S(2)}, u32[]{:S(2)}) collective-permute-start(bf16[579,2,1,128]{3,0,1,2:T(8,128)(2,1)} %copy-done.7), channel_id=1, source_target_pairs={{0,32},{32,64},{64,96},{96,128},{128,160},{160,192},{192,224},{224... | collective-permute-start | bytes 889352 | tf_op jit(solution)/shard_map/ppermute | solution.py:76
  44.4 3.2 %fusion.59 = (f32[576]{0:T(1024)}, f32[576,576]{0,1:T(8,128)}) fusion(bf16[576,128]{1,0:T(8,128)(2,1)} %bitcast.110, bf16[579,2,1,128]{3,0,1,2:T(8,128)(2,1)} %copy-done.7, pred[]{:T(512)S(6)} %ge.13, s32[576]{0:T(1024)S(1)} %convert_element_type.69, s32[576]{0:T(1024)S(1)} %slice_convert_fusion.2), kind=kOutput, calls=%fused_computation.107 | convolution fusion | flops 86592960 | bytes 1628929 | tf_op jit(solution)/shard_map/qhd,khd->hqk/dot_general | solution.py:47
  47.6 2.1 %collective-permute-done.2 = bf16[579,2,1,128]{3,0,1,2:T(8,128)(2,1)S(1)} collective-permute-done((bf16[579,2,1,128]{3,0,1,2:T(8,128)(2,1)}, bf16[579,2,1,128]{3,0,1,2:T(8,128)(2,1)S(1)}, u32[]{:S(2)}, u32[]{:S(2)}) %collective-permute-start.2) | collective-permute-done | bytes 296480 | tf_op jit(solution)/shard_map/ppermute | solution.py:76
  49.6 0.7 copy-done.8
  51.0 5.5 %collective-permute-start.3 = (bf16[579,2,1,128]{3,0,1,2:T(8,128)(2,1)}, bf16[579,2,1,128]{3,0,1,2:T(8,128)(2,1)S(1)}, u32[]{:S(2)}, u32[]{:S(2)}) collective-permute-start(bf16[579,2,1,128]{3,0,1,2:T(8,128)(2,1)} %copy-done.8), channel_id=1, source_target_pairs={{0,32},{32,64},{64,96},{96,128},{128,160},{160,192},{192,224},{224... | collective-permute-start | bytes 889352 | tf_op jit(solution)/shard_map/ppermute | solution.py:76
  56.5 0.7 slice_convert_fusion.1
  57.2 3.2 %fusion.58 = (f32[576]{0:T(1024)}, f32[576,576]{0,1:T(8,128)}) fusion(bf16[576,128]{1,0:T(8,128)(2,1)} %bitcast.111, bf16[579,2,1,128]{3,0,1,2:T(8,128)(2,1)} %copy-done.8, pred[]{:T(512)S(6)} %ge.14, s32[576]{0:T(1024)S(1)} %convert_element_type.69, s32[576]{0:T(1024)S(1)} %slice_convert_fusion.1), kind=kOutput, calls=%fused_computation.106 | convolution fusion | flops 86592960 | bytes 1628929 | tf_op jit(solution)/shard_map/qhd,khd->hqk/dot_general | solution.py:47
  60.4 3.1 %collective-permute-done.3 = bf16[579,2,1,128]{3,0,1,2:T(8,128)(2,1)S(1)} collective-permute-done((bf16[579,2,1,128]{3,0,1,2:T(8,128)(2,1)}, bf16[579,2,1,128]{3,0,1,2:T(8,128)(2,1)S(1)}, u32[]{:S(2)}, u32[]{:S(2)}) %collective-permute-start.3) | collective-permute-done | bytes 296480 | tf_op jit(solution)/shard_map/ppermute | solution.py:76
  63.6 0.7 copy-done.9
  64.9 1.3 reshape.466
  66.2 0.8 slice_convert_fusion
  67.0 1.5 fusion.57
  68.6 3.8 %fusion.15 = (f32[576]{0:T(1024)S(1)}, f32[576]{0:T(1024)S(1)}, f32[576]{0:T(1024)S(1)}, f32[576]{0:T(1024)S(1)}, f32[576]{0:T(1024)S(1)}) fusion(f32[576,576]{0,1:T(8,128)S(1)} %get-tuple-element.66, f32[576]{0:T(1024)S(1)} %get-tuple-element.56, s32[576]{0:T(1024)S(1)} %convert_element_type.69, f32[576,576]{0,1:T(8,128)S(1)} %get-tuple-element.64, ...), kind=kLoop, calls=%fused_computation.36 | loop fusion | flops 8623296 | bytes 6670084 | tf_op jit(solution)/shard_map/reduce_sum | solution.py:59
  73.0 1.6 fusion.2
  74.6 1.7 %fusion.3 = f32[576,128]{1,0:T(8,128)S(1)} fusion(f32[576,128]{1,0:T(8,128)S(1)} %fusion.2, f32[576,576]{0,1:T(8,128)S(1)} %copy-done, f32[576]{0:T(1024)S(1)} %get-tuple-element.48, s32[576]{0:T(1024)S(1)} %convert_element_type.69, s32[576]{0:T(1024)S(1)} %slice_convert_fusion.2, pred[]{:T(512)S(6)} %ge.13, bf16[579,2,1,128]{3,0,1,2:T(8,128)(2,1)} %copy-done.7, ...), kind=kOutput, calls=%fused_computation.24 | convolution fusion | flops 86740992 | bytes 2073601 | tf_op jit(solution)/shard_map/hqk,khd->hqd/dot_general | solution.py:60
  76.3 1.6 fusion.4
  77.8 1.5 fusion.6
  79.4 12.2 %all_gather.7 = bf16[576,512]{1,0:T(8,128)(2,1)S(1)} all-gather(bf16[576,128]{1,0:T(8,128)(2,1)S(1)} %fusion.6), channel_id=1, replica_groups=mesh['z'=16,'y'=4,'x'=4,'c'=2] {'y'}, dimensions={1}, use_global_device_ids=true | all-gather | bytes 737280 | tf_op jit(solution)/shard_map/all_gather | solution.py:84
  91.6 3.9 %all-gather.2.cloned.1.call-done = bf16[512,1792]{0,1:T(8,128)(2,1)} async-done(((bf16[512,112]{0,1:T(8,128)(2,1)}), bf16[512,1792]{0,1:T(8,128)(2,1)}) %all-gather.2.cloned.1.call-update) | async-done | bytes 1835024 | tf_op jit(solution)/shard_map/all_gather | solution.py:85
  95.4 1.6 %dynamic-slice_bitcast_fusion = (bf16[512,8,112]{0,2,1:T(8,128)(2,1)S(1)}, bf16[512,8,1,112]{0,3,2,1:T(8,128)(2,1)S(1)}) fusion(bf16[512,8,2,112]{0,3,2,1:T(8,128)(2,1)} %bitcast.99, s32[]{:T(128)S(6)} %select_n.87, s32[]{:T(128)S(6)} %select_n.86), kind=kLoop, calls=%fused_computation.38 | loop fusion | bytes 3670024 | tf_op jit(solution)/shard_map/jit(dynamic_index_in_dim)/squeeze | solution.py:92
  97.0 10.7 %collective-permute-start.5 = (bf16[512,8,112]{0,2,1:T(8,128)(2,1)S(1)}, bf16[512,8,112]{0,2,1:T(8,128)(2,1)}, u32[]{:S(2)}, u32[]{:S(2)}) collective-permute-start(bf16[512,8,112]{0,2,1:T(8,128)(2,1)S(1)} %get-tuple-element.50), channel_id=1, source_target_pairs={{0,1},{1,0},{2,3},{3,2},{4,5},{5,4},{6,7},{7,6},{8,9},{9,8},{10,11... | collective-permute-start | bytes 2752520 | tf_op jit(solution)/shard_map/ppermute | solution.py:91
  107.7 1.9 %collective-permute-start.4 = (bf16[576,512]{1,0:T(8,128)(2,1)S(1)}, bf16[576,512]{1,0:T(8,128)(2,1)S(1)}, u32[]{:S(2)}, u32[]{:S(2)}) collective-permute-start(bf16[576,512]{1,0:T(8,128)(2,1)S(1)} %all_gather.7), channel_id=1, source_target_pairs={{0,1},{1,0},{2,3},{3,2},{4,5},{5,4},{6,7},{7,6},{8,9},{9,8},{10,11... | collective-permute-start | bytes 1769480 | tf_op jit(solution)/shard_map/ppermute | solution.py:87
  109.7 0.8 fusion.62
  110.5 1.1 collective-permute-done.4
  111.6 2.0 %add_convert_fusion = bf16[576,896]{1,0:T(8,128)(2,1)S(1)} fusion(f32[576,896]{1,0:T(8,128)S(1)} %fusion.62, bf16[576,512]{1,0:T(8,128)(2,1)S(1)} %collective-permute-done.4, bf16[512,896]{0,1:T(8,128)(2,1)} %bitcast.23), kind=kOutput, calls=%fused_computation | convolution fusion | flops 529514496 | bytes 4603904 | tf_op jit(solution)/shard_map/dot_general | solution.py:97
  113.6 1.1 copy.33
  114.8 3.7 %collective-permute-start.6 = (bf16[576,224]{0,1:T(8,128)(2,1)S(1)}, bf16[576,224]{0,1:T(8,128)(2,1)S(1)}, u32[]{:S(2)}, u32[]{:S(2)}) collective-permute-start(bf16[576,224]{0,1:T(8,128)(2,1)S(1)} %get-tuple-element.52), channel_id=1, source_target_pairs={{0,2},{2,4},{4,6},{6,0},{1,3},{3,5},{5,7},{7,1},{8,10},{10,12},{12... | collective-permute-start | bytes 774152 | tf_op jit(solution)/shard_map/ppermute | solution.py:106
  118.5 4.2 %collective-permute-start.7 = (bf16[576,224]{0,1:T(8,128)(2,1)S(1)}, bf16[576,224]{0,1:T(8,128)(2,1)S(1)}, u32[]{:S(2)}, u32[]{:S(2)}) collective-permute-start(bf16[576,224]{0,1:T(8,128)(2,1)S(1)} %get-tuple-element.54), channel_id=1, source_target_pairs={{0,4},{2,6},{4,0},{6,2},{1,5},{3,7},{5,1},{7,3},{8,12},{10,14},{12... | collective-permute-start | bytes 774152 | tf_op jit(solution)/shard_map/ppermute | solution.py:106
  122.8 3.2 %collective-permute-start.8 = (bf16[576,224]{0,1:T(8,128)(2,1)S(1)}, bf16[576,224]{0,1:T(8,128)(2,1)S(1)}, u32[]{:S(2)}, u32[]{:S(2)}) collective-permute-start(bf16[576,224]{0,1:T(8,128)(2,1)S(1)} %get-tuple-element.53), channel_id=1, source_target_pairs={{0,6},{2,0},{4,2},{6,4},{1,7},{3,1},{5,3},{7,5},{8,14},{10,8},{12,... | collective-permute-start | bytes 774152 | tf_op jit(solution)/shard_map/ppermute | solution.py:106
  126.0 0.8 collective-permute-done.6
  126.8 7.0 %collective-permute-done.7 = bf16[576,224]{0,1:T(8,128)(2,1)S(1)} collective-permute-done((bf16[576,224]{0,1:T(8,128)(2,1)S(1)}, bf16[576,224]{0,1:T(8,128)(2,1)S(1)}, u32[]{:S(2)}, u32[]{:S(2)}) %collective-permute-start.7) | collective-permute-done | bytes 258080 | tf_op jit(solution)/shard_map/ppermute | solution.py:106
  133.8 1.3 collective-permute-done.8
  135.6 0.8 copy.35
  136.3 5.6 %all-to-all-start.1 = ((bf16[8,144,112]{2,1,0:T(8,128)(2,1)}), bf16[8,144,112]{2,1,0:T(8,128)(2,1)S(1)}, u32[]{:S(2)}, u32[]{:S(2)}) async-start(bf16[8,144,112]{2,1,0:T(8,128)(2,1)} %bitcast.30), calls=%async_computation.1 | async-start | bytes 589824 | tf_op jit(solution)/shard_map/all_to_all | solution.py:110
  142.0 0.8 copy.37
  142.7 6.1 %all-to-all-done.1 = bf16[8,144,112]{2,1,0:T(8,128)(2,1)S(1)} async-done(((bf16[8,144,112]{2,1,0:T(8,128)(2,1)}), bf16[8,144,112]{2,1,0:T(8,128)(2,1)S(1)}, u32[]{:S(2)}, u32[]{:S(2)}) %all-to-all-start.1) | async-done | bytes 258080 | tf_op jit(solution)/shard_map/all_to_all | solution.py:110
  148.9 0.9 reshape.476
  (58 shorter events, 4.2 us)
Async XLA Ops:
  7.2 88.3 %all-gather.2.cloned.1.call-start = ((), (), s32[]{:S(2)}) async-start(), calls=%async_computation.2 | async-start | bytes 1949696 | tf_op jit(solution)/shard_map/all_gather | solution.py:85
  22.2 8.8 %collective-permute-start = (bf16[579,2,1,128]{3,0,1,2:T(8,128)(2,1)S(1)}, bf16[579,2,1,128]{3,0,1,2:T(8,128)(2,1)}, u32[]{:S(2)}, u32[]{:S(2)}) collective-permute-start(bf16[579,2,1,128]{3,0,1,2:T(8,128)(2,1)S(1)} %pad_maximum_fusion.1), channel_id=1, source_target_pairs={{0,32},{32,64},{64,96},{96,128},{128,160},{160,192},{192,224},{224... | collective-permute-start | bytes 889352 | tf_op jit(solution)/shard_map/ppermute | solution.py:76
  27.6 3.4 %copy-start.2 = (bf16[4,144,1,1,128]{4,1,0,3,2:T(8,128)(2,1)}, bf16[4,144,1,1,128]{4,1,0,3,2:T(8,128)(2,1)S(1)}, u32[]{:S(2)}) copy-start(bf16[4,144,1,1,128]{4,1,0,3,2:T(8,128)(2,1)S(1)} %slice.116) | copy-start | bytes 442372
  31.7 8.2 %collective-permute-start.1 = (bf16[579,2,1,128]{3,0,1,2:T(8,128)(2,1)}, bf16[579,2,1,128]{3,0,1,2:T(8,128)(2,1)S(1)}, u32[]{:S(2)}, u32[]{:S(2)}) collective-permute-start(bf16[579,2,1,128]{3,0,1,2:T(8,128)(2,1)} %collective-permute-done), channel_id=1, source_target_pairs={{0,32},{32,64},{64,96},{96,128},{128,160},{160,192},{192,224},{224... | collective-permute-start | bytes 889352 | tf_op jit(solution)/shard_map/ppermute | solution.py:76
  39.9 0.7 copy-start.7
  40.7 9.0 %collective-permute-start.2 = (bf16[579,2,1,128]{3,0,1,2:T(8,128)(2,1)}, bf16[579,2,1,128]{3,0,1,2:T(8,128)(2,1)S(1)}, u32[]{:S(2)}, u32[]{:S(2)}) collective-permute-start(bf16[579,2,1,128]{3,0,1,2:T(8,128)(2,1)} %copy-done.7), channel_id=1, source_target_pairs={{0,32},{32,64},{64,96},{96,128},{128,160},{160,192},{192,224},{224... | collective-permute-start | bytes 889352 | tf_op jit(solution)/shard_map/ppermute | solution.py:76
  49.6 0.7 copy-start.8
  51.0 12.6 %collective-permute-start.3 = (bf16[579,2,1,128]{3,0,1,2:T(8,128)(2,1)}, bf16[579,2,1,128]{3,0,1,2:T(8,128)(2,1)S(1)}, u32[]{:S(2)}, u32[]{:S(2)}) collective-permute-start(bf16[579,2,1,128]{3,0,1,2:T(8,128)(2,1)} %copy-done.8), channel_id=1, source_target_pairs={{0,32},{32,64},{64,96},{96,128},{128,160},{160,192},{192,224},{224... | collective-permute-start | bytes 889352 | tf_op jit(solution)/shard_map/ppermute | solution.py:76
  63.6 0.7 copy-start.9
  66.2 2.3 %copy-start.3 = (f32[576]{0:T(1024)S(1)}, f32[576]{0:T(1024)}, u32[]{:S(2)}) copy-start(f32[576]{0:T(1024)} %get-tuple-element.65) | copy-start | bytes 6916
  66.2 2.3 %copy-start.4 = (f32[576]{0:T(1024)S(1)}, f32[576]{0:T(1024)}, u32[]{:S(2)}) copy-start(f32[576]{0:T(1024)} %get-tuple-element.63) | copy-start | bytes 6916
  66.2 2.3 %copy-start.5 = (f32[576]{0:T(1024)S(1)}, f32[576]{0:T(1024)}, u32[]{:S(2)}) copy-start(f32[576]{0:T(1024)} %get-tuple-element.61) | copy-start | bytes 6916
  66.2 2.3 %copy-start.6 = (f32[576]{0:T(1024)S(1)}, f32[576]{0:T(1024)}, u32[]{:S(2)}) copy-start(f32[576]{0:T(1024)} %get-tuple-element.59) | copy-start | bytes 6916
  66.2 2.4 %copy-start = (f32[576,576]{0,1:T(8,128)S(1)}, f32[576,576]{0,1:T(8,128)}, u32[]{:S(2)}) copy-start(f32[576,576]{0,1:T(8,128)} %get-tuple-element.62) | copy-start | bytes 3981316
  74.6 1.7 %copy-start.1 = (f32[576,576]{0,1:T(8,128)S(1)}, f32[576,576]{0,1:T(8,128)}, u32[]{:S(2)}) copy-start(f32[576,576]{0,1:T(8,128)} %get-tuple-element.60) | copy-start | bytes 3981316
  97.0 14.6 %collective-permute-start.5 = (bf16[512,8,112]{0,2,1:T(8,128)(2,1)S(1)}, bf16[512,8,112]{0,2,1:T(8,128)(2,1)}, u32[]{:S(2)}, u32[]{:S(2)}) collective-permute-start(bf16[512,8,112]{0,2,1:T(8,128)(2,1)S(1)} %get-tuple-element.50), channel_id=1, source_target_pairs={{0,1},{1,0},{2,3},{3,2},{4,5},{5,4},{6,7},{7,6},{8,9},{9,8},{10,11... | collective-permute-start | bytes 2752520 | tf_op jit(solution)/shard_map/ppermute | solution.py:91
  107.7 3.9 %collective-permute-start.4 = (bf16[576,512]{1,0:T(8,128)(2,1)S(1)}, bf16[576,512]{1,0:T(8,128)(2,1)S(1)}, u32[]{:S(2)}, u32[]{:S(2)}) collective-permute-start(bf16[576,512]{1,0:T(8,128)(2,1)S(1)} %all_gather.7), channel_id=1, source_target_pairs={{0,1},{1,0},{2,3},{3,2},{4,5},{5,4},{6,7},{7,6},{8,9},{9,8},{10,11... | collective-permute-start | bytes 1769480 | tf_op jit(solution)/shard_map/ppermute | solution.py:87
  114.8 11.9 %collective-permute-start.6 = (bf16[576,224]{0,1:T(8,128)(2,1)S(1)}, bf16[576,224]{0,1:T(8,128)(2,1)S(1)}, u32[]{:S(2)}, u32[]{:S(2)}) collective-permute-start(bf16[576,224]{0,1:T(8,128)(2,1)S(1)} %get-tuple-element.52), channel_id=1, source_target_pairs={{0,2},{2,4},{4,6},{6,0},{1,3},{3,5},{5,7},{7,1},{8,10},{10,12},{12... | collective-permute-start | bytes 774152 | tf_op jit(solution)/shard_map/ppermute | solution.py:106
  118.5 15.3 %collective-permute-start.7 = (bf16[576,224]{0,1:T(8,128)(2,1)S(1)}, bf16[576,224]{0,1:T(8,128)(2,1)S(1)}, u32[]{:S(2)}, u32[]{:S(2)}) collective-permute-start(bf16[576,224]{0,1:T(8,128)(2,1)S(1)} %get-tuple-element.54), channel_id=1, source_target_pairs={{0,4},{2,6},{4,0},{6,2},{1,5},{3,7},{5,1},{7,3},{8,12},{10,14},{12... | collective-permute-start | bytes 774152 | tf_op jit(solution)/shard_map/ppermute | solution.py:106
  122.8 12.3 %collective-permute-start.8 = (bf16[576,224]{0,1:T(8,128)(2,1)S(1)}, bf16[576,224]{0,1:T(8,128)(2,1)S(1)}, u32[]{:S(2)}, u32[]{:S(2)}) collective-permute-start(bf16[576,224]{0,1:T(8,128)(2,1)S(1)} %get-tuple-element.53), channel_id=1, source_target_pairs={{0,6},{2,0},{4,2},{6,4},{1,7},{3,1},{5,3},{7,5},{8,14},{10,8},{12,... | collective-permute-start | bytes 774152 | tf_op jit(solution)/shard_map/ppermute | solution.py:106
  136.3 12.4 %all-to-all-start.1 = ((bf16[8,144,112]{2,1,0:T(8,128)(2,1)}), bf16[8,144,112]{2,1,0:T(8,128)(2,1)S(1)}, u32[]{:S(2)}, u32[]{:S(2)}) async-start(bf16[8,144,112]{2,1,0:T(8,128)(2,1)} %bitcast.30), calls=%async_computation.1 | async-start | bytes 589824 | tf_op jit(solution)/shard_map/all_to_all | solution.py:110
Sparse Core Ops, SparseCore 0:
  27.6 67.7 all-gather.1

commit v7 on v6

--- a/solution.py
+++ b/solution.py
@@ -8,6 +8,20 @@
 
 HD = 128
 NY = 4
+
+
+def by_source(pieces, me):
+    n = len(pieces)
+    stacked = jnp.stack(pieces)
+    return jnp.take(stacked, (me - jnp.arange(n)) % n, axis=0)
+
+
+def from_all_y(value, me, piece=None):
+    pieces = [value if piece is None else piece(me)]
+    for shift in range(1, NY):
+        out = value if piece is None else piece((me + shift) % NY)
+        pieces.append(lax.ppermute(out, "y", [(i, (i + shift) % NY) for i in range(NY)]))
+    return by_source(pieces, me)
 
 
 def local(queries, keys_values, segment_ids, out_weight):
@@ -26,7 +40,10 @@
     seg_row = jnp.zeros((3 * hq * HD,), jnp.bfloat16).at[:rows].set(segment_ids.astype(jnp.bfloat16))
     seg_row = jnp.broadcast_to(seg_row.reshape(1, 3, 1, hq, HD), (1, 3, NY, hq, HD))
     packed = jnp.concatenate([packed, seg_row], axis=0)
-    packed = lax.all_to_all(packed, "y", 2, 0, tiled=True).reshape(NY, rows + 1, 3, hq, HD)
+    y = lax.axis_index("y")
+    packed = from_all_y(
+        packed, y, lambda dest: lax.dynamic_index_in_dim(packed, dest, axis=2, keepdims=False)
+    )
     query_rows = packed[:, :rows, 0].reshape(level, hq, HD)
     pair = packed[:, :rows, 1:].reshape(level, 2, hq, HD)
     query_seg = packed[:, rows].reshape(NY, 3 * hq * HD)[:, :rows].reshape(level)
@@ -81,7 +98,7 @@
 
     c = lax.axis_index("c")
     swap = [(0, 1), (1, 0)]
-    own_attended = lax.all_gather(attended, "y", axis=1, tiled=True)
+    own_attended = from_all_y(attended, y).transpose(1, 0, 2).reshape(level, NY * hq * HD)
     weight_cols = lax.all_gather(out_weight, "z", axis=1, tiled=True)
     weight_cols, own_attended = lax.optimization_barrier((weight_cols, own_attended))
     other_attended = lax.ppermute(own_attended, "c", swap)

time: 158 us -> 165 us (1.044)
  starting transfers between devices: 48.1 us -> 73.4 us
  blocking collectives: 23.6 us -> 0 us
    ppermute x0 -> x6, starting transfers between devices: none -> 26.9 us  [from_all_y(): lax.ppermute(out, 'y', [(i, (i + shift) % NY) for i in range(NY)])]
    all_gather x1 -> x0, blocking collectives: 12.2 us -> none  [local(): own_attended = lax.all_gather(attended, 'y', axis=1, tiled=True)]
    all_to_all x1 -> x0, blocking collectives: 11.4 us -> none  [local(): lax.all_to_all(packed, 'y', 2, 0, tiled=True)]
    ppermute x0 -> x6, waiting for transfers between devices: none -> 6.22 us  [from_all_y(): lax.ppermute(out, 'y', [(i, (i + shift) % NY) for i in range(NY)])]
    all_gather x1, waiting for transfers between devices: 3.87 us -> 1.07 us  [local(): weight_cols = lax.all_gather(out_weight, 'z', axis=1, tiled=True)]
    ppermute x4, waiting for transfers between devices: 9.42 us -> 6.79 us  [local(): block = lax.ppermute(block, 'z', [(i, i + 1) for i in range(nz - 1)])]
    ppermute x4, starting transfers between devices: 18.8 us -> 16.9 us  [local(): block = lax.ppermute(block, 'z', [(i, i + 1) for i in range(nz - 1)])]
  transfers between devices with their start and end apart: 11 -> 17, of which waited for: 10 -> 13; matrix products, arithmetic and copies ran while one was open for 18% -> 18% of each run, Pallas kernels for 0% -> 0%
where the time goes in v7:
time: 165 us; the launch traced here: 163 us
  starting transfers between devices  73.4 us (44%)
  waiting for transfers between devices  30.8 us (19%)
  matrix products  20.7 us (13%)
  local copies, waits for them, and re-layouts  15 us (9%)
  between operations  14.7 us (9%)
  other arithmetic  8.01 us (5%)
    ppermute x6, starting transfers between devices, from_all_y(): lax.ppermute(out, 'y', [(i, (i + shift) % NY) for i in range(NY)])  26.9 us
    ppermute x4, starting transfers between devices, local(): block = lax.ppermute(block, 'z', [(i, i + 1) for i in range(nz - 1)])  16.9 us
    ppermute x1, starting transfers between devices, local(): lax.ppermute(lax.dynamic_index_in_dim(weight_cols, 1 - c, axis=2, keepdim...  11.5 us
    dot_general x5, matrix products, attend(): jnp.einsum('qhd,khd->hqk', query_rows, key_rows, preferred_element_type=j...  11 us
    ppermute x3, starting transfers between devices, local(): part = lax.ppermute(part, 'x', [(i, (i + shift) % nx) for i in range(nx)])  10.1 us
    ppermute x3, waiting for transfers between devices, local(): part = lax.ppermute(part, 'x', [(i, (i + shift) % nx) for i in range(nx)])  9.65 us
    dot_general x5, matrix products, attend(): jnp.einsum('hqk,khd->hqd', probs.astype(jnp.bfloat16), value_rows, prefer...  6.93 us
    ppermute x4, waiting for transfers between devices, local(): block = lax.ppermute(block, 'z', [(i, i + 1) for i in range(nz - 1)])  6.79 us
  transfers between devices with their start and end apart: 17, of which 13 were waited for; matrix products, arithmetic and copies ran while one was open for 18% of the time, Pallas kernels for 0%

profile of v7, /device:TPU:1, one launch (start us, length us, event | category | flops | bytes accessed | tf_op | source)
XLA Modules:
  0.0 162.6 jit_solution(18411872958203830692)
XLA Ops:
  7.3 1.2 reshape.558
  8.4 1.0 reshape.510
  10.3 1.2 fusion.50
  11.5 4.0 %collective-permute-start = (bf16[145,3,1,128]{3,0,1,2:T(8,128)(2,1)S(1)}, bf16[145,3,1,128]{3,0,1,2:T(8,128)(2,1)S(1)}, u32[]{:S(2)}, u32[]{:S(2)}) collective-permute-start(bf16[145,3,1,128]{3,0,1,2:T(8,128)(2,1)S(1)} %bitcast.151), channel_id=1, source_target_pairs={{0,8},{8,16},{16,24},{24,0},{1,9},{9,17},{17,25},{25,1},{2,10},{10... | collective-permute-start | bytes 334088 | tf_op jit(solution)/shard_map/ppermute | solution.py:23
  15.5 4.5 %collective-permute-start.1 = (bf16[145,3,1,128]{3,0,1,2:T(8,128)(2,1)S(1)}, bf16[145,3,1,128]{3,0,1,2:T(8,128)(2,1)S(1)}, u32[]{:S(2)}, u32[]{:S(2)}) collective-permute-start(bf16[145,3,1,128]{3,0,1,2:T(8,128)(2,1)S(1)} %bitcast.152), channel_id=1, source_target_pairs={{0,16},{8,24},{16,0},{24,8},{1,17},{9,25},{17,1},{25,9},{2,18},{10... | collective-permute-start | bytes 334088 | tf_op jit(solution)/shard_map/ppermute | solution.py:23
  20.1 3.0 %collective-permute-start.2 = (bf16[145,3,1,128]{3,0,1,2:T(8,128)(2,1)S(1)}, bf16[145,3,1,128]{3,0,1,2:T(8,128)(2,1)S(1)}, u32[]{:S(2)}, u32[]{:S(2)}) collective-permute-start(bf16[145,3,1,128]{3,0,1,2:T(8,128)(2,1)S(1)} %bitcast.153), channel_id=1, source_target_pairs={{0,24},{8,0},{16,8},{24,16},{1,25},{9,1},{17,9},{25,17},{2,26},{10... | collective-permute-start | bytes 334088 | tf_op jit(solution)/shard_map/ppermute | solution.py:23
  23.2 2.7 %collective-permute-done.2 = bf16[145,3,1,128]{3,0,1,2:T(8,128)(2,1)S(1)} collective-permute-done((bf16[145,3,1,128]{3,0,1,2:T(8,128)(2,1)S(1)}, bf16[145,3,1,128]{3,0,1,2:T(8,128)(2,1)S(1)}, u32[]{:S(2)}, u32[]{:S(2)}) %collective-permute-start.2) | collective-permute-done | bytes 111392 | tf_op jit(solution)/shard_map/ppermute | solution.py:23
  27.0 4.1 %collective-permute-start.3 = (bf16[579,2,1,128]{3,0,1,2:T(8,128)(2,1)S(1)}, bf16[579,2,1,128]{3,0,1,2:T(8,128)(2,1)}, u32[]{:S(2)}, u32[]{:S(2)}) collective-permute-start(bf16[579,2,1,128]{3,0,1,2:T(8,128)(2,1)S(1)} %pad_maximum_fusion.1), channel_id=1, source_target_pairs={{0,32},{32,64},{64,96},{96,128},{128,160},{160,192},{192,224},{224... | collective-permute-start | bytes 889352 | tf_op jit(solution)/shard_map/ppermute | solution.py:93
  31.1 1.1 fusion.68
  32.2 1.8 %collective-permute-done.3 = bf16[579,2,1,128]{3,0,1,2:T(8,128)(2,1)} collective-permute-done((bf16[579,2,1,128]{3,0,1,2:T(8,128)(2,1)S(1)}, bf16[579,2,1,128]{3,0,1,2:T(8,128)(2,1)}, u32[]{:S(2)}, u32[]{:S(2)}) %collective-permute-start.3) | collective-permute-done | bytes 296480 | tf_op jit(solution)/shard_map/ppermute | solution.py:93
  34.7 3.9 %collective-permute-start.4 = (bf16[579,2,1,128]{3,0,1,2:T(8,128)(2,1)}, bf16[579,2,1,128]{3,0,1,2:T(8,128)(2,1)S(1)}, u32[]{:S(2)}, u32[]{:S(2)}) collective-permute-start(bf16[579,2,1,128]{3,0,1,2:T(8,128)(2,1)} %collective-permute-done.3), channel_id=1, source_target_pairs={{0,32},{32,64},{64,96},{96,128},{128,160},{160,192},{192,224},{224... | collective-permute-start | bytes 889352 | tf_op jit(solution)/shard_map/ppermute | solution.py:93
  38.7 2.1 %fusion.67 = (f32[576]{0:T(1024)}, f32[576,576]{0,1:T(8,128)S(1)}) fusion(bf16[576,128]{1,0:T(8,128)(2,1)} %bitcast.144, bf16[579,2,1,128]{3,0,1,2:T(8,128)(2,1)} %collective-permute-done.3, pred[]{:T(512)S(6)} %ge.22, s32[576]{0:T(1024)S(1)} %convert_element_type.71, s32[576]{0:T(1024)S(1)} %slice_convert_fusion.3), kind=kOutput, calls=%fused_computation.139 | convolution fusion | flops 86592960 | bytes 1628929 | tf_op jit(solution)/shard_map/qhd,khd->hqk/dot_general | solution.py:64
  40.7 1.9 %collective-permute-done.4 = bf16[579,2,1,128]{3,0,1,2:T(8,128)(2,1)S(1)} collective-permute-done((bf16[579,2,1,128]{3,0,1,2:T(8,128)(2,1)}, bf16[579,2,1,128]{3,0,1,2:T(8,128)(2,1)S(1)}, u32[]{:S(2)}, u32[]{:S(2)}) %collective-permute-start.4) | collective-permute-done | bytes 296480 | tf_op jit(solution)/shard_map/ppermute | solution.py:93
  43.4 4.1 %collective-permute-start.5 = (bf16[579,2,1,128]{3,0,1,2:T(8,128)(2,1)}, bf16[579,2,1,128]{3,0,1,2:T(8,128)(2,1)S(1)}, u32[]{:S(2)}, u32[]{:S(2)}) collective-permute-start(bf16[579,2,1,128]{3,0,1,2:T(8,128)(2,1)} %copy-done.10), channel_id=1, source_target_pairs={{0,32},{32,64},{64,96},{96,128},{128,160},{160,192},{192,224},{224... | collective-permute-start | bytes 889352 | tf_op jit(solution)/shard_map/ppermute | solution.py:93
  47.5 3.2 %fusion.66 = (f32[576]{0:T(1024)}, f32[576,576]{0,1:T(8,128)}) fusion(bf16[576,128]{1,0:T(8,128)(2,1)} %bitcast.145, bf16[579,2,1,128]{3,0,1,2:T(8,128)(2,1)} %copy-done.10, pred[]{:T(512)S(6)} %ge.23, s32[576]{0:T(1024)S(1)} %convert_element_type.71, s32[576]{0:T(1024)S(1)} %slice_convert_fusion.2), kind=kOutput, calls=%fused_computation.138 | convolution fusion | flops 86592960 | bytes 1628929 | tf_op jit(solution)/shard_map/qhd,khd->hqk/dot_general | solution.py:64
  50.7 0.8 collective-permute-done.5
  52.8 4.7 %collective-permute-start.6 = (bf16[579,2,1,128]{3,0,1,2:T(8,128)(2,1)}, bf16[579,2,1,128]{3,0,1,2:T(8,128)(2,1)S(1)}, u32[]{:S(2)}, u32[]{:S(2)}) collective-permute-start(bf16[579,2,1,128]{3,0,1,2:T(8,128)(2,1)} %copy-done.11), channel_id=1, source_target_pairs={{0,32},{32,64},{64,96},{96,128},{128,160},{160,192},{192,224},{224... | collective-permute-start | bytes 889352 | tf_op jit(solution)/shard_map/ppermute | solution.py:93
  58.3 3.2 %fusion.65 = (f32[576]{0:T(1024)}, f32[576,576]{0,1:T(8,128)}) fusion(bf16[576,128]{1,0:T(8,128)(2,1)} %bitcast.146, bf16[579,2,1,128]{3,0,1,2:T(8,128)(2,1)} %copy-done.11, pred[]{:T(512)S(6)} %ge.24, s32[576]{0:T(1024)S(1)} %convert_element_type.71, s32[576]{0:T(1024)S(1)} %slice_convert_fusion.1), kind=kOutput, calls=%fused_computation.137 | convolution fusion | flops 86592960 | bytes 1628929 | tf_op jit(solution)/shard_map/qhd,khd->hqk/dot_general | solution.py:64
  61.5 2.3 %collective-permute-done.6 = bf16[579,2,1,128]{3,0,1,2:T(8,128)(2,1)S(1)} collective-permute-done((bf16[579,2,1,128]{3,0,1,2:T(8,128)(2,1)}, bf16[579,2,1,128]{3,0,1,2:T(8,128)(2,1)S(1)}, u32[]{:S(2)}, u32[]{:S(2)}) %collective-permute-start.6) | collective-permute-done | bytes 296480 | tf_op jit(solution)/shard_map/ppermute | solution.py:93
  65.1 1.3 reshape.527
  67.2 1.5 fusion.64
  68.7 3.8 %fusion.15 = (f32[576]{0:T(1024)S(1)}, f32[576]{0:T(1024)S(1)}, f32[576]{0:T(1024)S(1)}, f32[576]{0:T(1024)S(1)}, f32[576]{0:T(1024)S(1)}) fusion(f32[576,576]{0,1:T(8,128)S(1)} %get-tuple-element.68, f32[576]{0:T(1024)S(1)} %get-tuple-element.58, s32[576]{0:T(1024)S(1)} %convert_element_type.71, f32[576,576]{0,1:T(8,128)S(1)} %get-tuple-element.66, ...), kind=kLoop, calls=%fused_computation.38 | loop fusion | flops 8623296 | bytes 6670084 | tf_op jit(solution)/shard_map/reduce_sum | solution.py:76
  73.1 1.6 fusion.2
  74.7 1.7 %fusion.3 = f32[576,128]{1,0:T(8,128)S(1)} fusion(f32[576,128]{1,0:T(8,128)S(1)} %fusion.2, f32[576,576]{0,1:T(8,128)S(1)} %copy-done, f32[576]{0:T(1024)S(1)} %get-tuple-element.46, s32[576]{0:T(1024)S(1)} %convert_element_type.71, s32[576]{0:T(1024)S(1)} %slice_convert_fusion.2, pred[]{:T(512)S(6)} %ge.23, bf16[579,2,1,128]{3,0,1,2:T(8,128)(2,1)} %copy-done.10, ...), kind=kOutput, calls=%fused_computation.26 | convolution fusion | flops 86740992 | bytes 2073601 | tf_op jit(solution)/shard_map/hqk,khd->hqd/dot_general | solution.py:77
  76.4 1.6 fusion.4
  77.9 1.6 fusion.6
  79.5 8.9 %collective-permute-start.7 = (bf16[576,128]{1,0:T(8,128)(2,1)S(1)}, bf16[576,128]{1,0:T(8,128)(2,1)S(1)}, u32[]{:S(2)}, u32[]{:S(2)}) collective-permute-start(bf16[576,128]{1,0:T(8,128)(2,1)S(1)} %fusion.6), channel_id=1, source_target_pairs={{0,8},{8,16},{16,24},{24,0},{1,9},{9,17},{17,25},{25,1},{2,10},{10... | collective-permute-start | bytes 442376 | tf_op jit(solution)/shard_map/ppermute | solution.py:23
  88.4 2.6 %collective-permute-start.8 = (bf16[576,128]{1,0:T(8,128)(2,1)S(1)}, bf16[576,128]{1,0:T(8,128)(2,1)S(1)}, u32[]{:S(2)}, u32[]{:S(2)}) collective-permute-start(bf16[576,128]{1,0:T(8,128)(2,1)S(1)} %fusion.6), channel_id=1, source_target_pairs={{0,16},{8,24},{16,0},{24,8},{1,17},{9,25},{17,1},{25,9},{2,18},{10... | collective-permute-start | bytes 442376 | tf_op jit(solution)/shard_map/ppermute | solution.py:23
  91.0 4.0 %collective-permute-start.9 = (bf16[576,128]{1,0:T(8,128)(2,1)S(1)}, bf16[576,128]{1,0:T(8,128)(2,1)S(1)}, u32[]{:S(2)}, u32[]{:S(2)}) collective-permute-start(bf16[576,128]{1,0:T(8,128)(2,1)S(1)} %fusion.6), channel_id=1, source_target_pairs={{0,24},{8,0},{16,8},{24,16},{1,25},{9,1},{17,9},{25,17},{2,26},{10... | collective-permute-start | bytes 442376 | tf_op jit(solution)/shard_map/ppermute | solution.py:23
  94.9 2.3 %collective-permute-done.8 = bf16[576,128]{1,0:T(8,128)(2,1)S(1)} collective-permute-done((bf16[576,128]{1,0:T(8,128)(2,1)S(1)}, bf16[576,128]{1,0:T(8,128)(2,1)S(1)}, u32[]{:S(2)}, u32[]{:S(2)}) %collective-permute-start.8) | collective-permute-done | bytes 147488 | tf_op jit(solution)/shard_map/ppermute | solution.py:23
  97.3 1.2 collective-permute-done.9
  99.6 1.1 all-gather.2.cloned.1.call-done
  100.6 1.6 dynamic-slice_bitcast_fusion
  102.2 11.5 %collective-permute-start.11 = (bf16[512,8,112]{0,2,1:T(8,128)(2,1)S(1)}, bf16[512,8,112]{0,2,1:T(8,128)(2,1)}, u32[]{:S(2)}, u32[]{:S(2)}) collective-permute-start(bf16[512,8,112]{0,2,1:T(8,128)(2,1)S(1)} %get-tuple-element.48), channel_id=1, source_target_pairs={{0,1},{1,0},{2,3},{3,2},{4,5},{5,4},{6,7},{7,6},{8,9},{9,8},{10,11... | collective-permute-start | bytes 2752520 | tf_op jit(solution)/shard_map/ppermute | solution.py:108
  113.7 2.1 %collective-permute-start.10 = (bf16[576,512]{1,0:T(8,128)(2,1)S(1)}, bf16[576,512]{1,0:T(8,128)(2,1)S(1)}, u32[]{:S(2)}, u32[]{:S(2)}) collective-permute-start(bf16[576,512]{1,0:T(8,128)(2,1)S(1)} %copy_bitcast_fusion), channel_id=1, source_target_pairs={{0,1},{1,0},{2,3},{3,2},{4,5},{5,4},{6,7},{7,6},{8,9},{9,8},{10,11... | collective-permute-start | bytes 1769480 | tf_op jit(solution)/shard_map/ppermute | solution.py:104
  115.9 0.8 fusion.69
  116.7 0.9 collective-permute-done.10
  117.6 2.0 %add_convert_fusion = bf16[576,896]{1,0:T(8,128)(2,1)S(1)} fusion(f32[576,896]{1,0:T(8,128)S(1)} %fusion.69, bf16[576,512]{1,0:T(8,128)(2,1)S(1)} %collective-permute-done.10, bf16[512,896]{0,1:T(8,128)(2,1)} %bitcast.32), kind=kOutput, calls=%fused_computation.2 | convolution fusion | flops 529514496 | bytes 4603904 | tf_op jit(solution)/shard_map/dot_general | solution.py:114
  119.6 1.1 copy.30
  120.9 3.0 %collective-permute-start.12 = (bf16[576,224]{0,1:T(8,128)(2,1)S(1)}, bf16[576,224]{0,1:T(8,128)(2,1)S(1)}, u32[]{:S(2)}, u32[]{:S(2)}) collective-permute-start(bf16[576,224]{0,1:T(8,128)(2,1)S(1)} %get-tuple-element.50), channel_id=1, source_target_pairs={{0,2},{2,4},{4,6},{6,0},{1,3},{3,5},{5,7},{7,1},{8,10},{10,12},{12... | collective-permute-start | bytes 774152 | tf_op jit(solution)/shard_map/ppermute | solution.py:123
  123.8 4.1 %collective-permute-start.13 = (bf16[576,224]{0,1:T(8,128)(2,1)S(1)}, bf16[576,224]{0,1:T(8,128)(2,1)S(1)}, u32[]{:S(2)}, u32[]{:S(2)}) collective-permute-start(bf16[576,224]{0,1:T(8,128)(2,1)S(1)} %get-tuple-element.52), channel_id=1, source_target_pairs={{0,4},{2,6},{4,0},{6,2},{1,5},{3,7},{5,1},{7,3},{8,12},{10,14},{12... | collective-permute-start | bytes 774152 | tf_op jit(solution)/shard_map/ppermute | solution.py:123
  127.9 3.1 %collective-permute-start.14 = (bf16[576,224]{0,1:T(8,128)(2,1)S(1)}, bf16[576,224]{0,1:T(8,128)(2,1)S(1)}, u32[]{:S(2)}, u32[]{:S(2)}) collective-permute-start(bf16[576,224]{0,1:T(8,128)(2,1)S(1)} %get-tuple-element.51), channel_id=1, source_target_pairs={{0,6},{2,0},{4,2},{6,4},{1,7},{3,1},{5,3},{7,5},{8,14},{10,8},{12,... | collective-permute-start | bytes 774152 | tf_op jit(solution)/shard_map/ppermute | solution.py:123
  131.0 1.3 collective-permute-done.12
  132.3 6.7 %collective-permute-done.13 = bf16[576,224]{0,1:T(8,128)(2,1)S(1)} collective-permute-done((bf16[576,224]{0,1:T(8,128)(2,1)S(1)}, bf16[576,224]{0,1:T(8,128)(2,1)S(1)}, u32[]{:S(2)}, u32[]{:S(2)}) %collective-permute-start.13) | collective-permute-done | bytes 258080 | tf_op jit(solution)/shard_map/ppermute | solution.py:123
  138.9 1.7 %collective-permute-done.14 = bf16[576,224]{0,1:T(8,128)(2,1)S(1)} collective-permute-done((bf16[576,224]{0,1:T(8,128)(2,1)S(1)}, bf16[576,224]{0,1:T(8,128)(2,1)S(1)}, u32[]{:S(2)}, u32[]{:S(2)}) %collective-permute-start.14) | collective-permute-done | bytes 258080 | tf_op jit(solution)/shard_map/ppermute | solution.py:123
  141.9 6.0 %all-to-all-start = ((bf16[8,144,112]{2,1,0:T(8,128)(2,1)}), bf16[8,144,112]{2,1,0:T(8,128)(2,1)S(1)}, u32[]{:S(2)}, u32[]{:S(2)}) async-start(bf16[8,144,112]{2,1,0:T(8,128)(2,1)} %bitcast.39), calls=%async_computation | async-start | bytes 589824 | tf_op jit(solution)/shard_map/all_to_all | solution.py:127
  148.6 6.1 %all-to-all-done = bf16[8,144,112]{2,1,0:T(8,128)(2,1)S(1)} async-done(((bf16[8,144,112]{2,1,0:T(8,128)(2,1)}), bf16[8,144,112]{2,1,0:T(8,128)(2,1)S(1)}, u32[]{:S(2)}, u32[]{:S(2)}) %all-to-all-start) | async-done | bytes 258080 | tf_op jit(solution)/shard_map/all_to_all | solution.py:127
  154.8 0.9 reshape.538
  (86 shorter events, 11.7 us)
Async XLA Ops:
  7.2 93.5 %all-gather.2.cloned.1.call-start = ((), (), s32[]{:S(2)}) async-start(), calls=%async_computation.1 | async-start | bytes 1949696 | tf_op jit(solution)/shard_map/all_gather | solution.py:102
  11.5 11.7 %collective-permute-start = (bf16[145,3,1,128]{3,0,1,2:T(8,128)(2,1)S(1)}, bf16[145,3,1,128]{3,0,1,2:T(8,128)(2,1)S(1)}, u32[]{:S(2)}, u32[]{:S(2)}) collective-permute-start(bf16[145,3,1,128]{3,0,1,2:T(8,128)(2,1)S(1)} %bitcast.151), channel_id=1, source_target_pairs={{0,8},{8,16},{16,24},{24,0},{1,9},{9,17},{17,25},{25,1},{2,10},{10... | collective-permute-start | bytes 334088 | tf_op jit(solution)/shard_map/ppermute | solution.py:23
  15.5 7.7 %collective-permute-start.1 = (bf16[145,3,1,128]{3,0,1,2:T(8,128)(2,1)S(1)}, bf16[145,3,1,128]{3,0,1,2:T(8,128)(2,1)S(1)}, u32[]{:S(2)}, u32[]{:S(2)}) collective-permute-start(bf16[145,3,1,128]{3,0,1,2:T(8,128)(2,1)S(1)} %bitcast.152), channel_id=1, source_target_pairs={{0,16},{8,24},{16,0},{24,8},{1,17},{9,25},{17,1},{25,9},{2,18},{10... | collective-permute-start | bytes 334088 | tf_op jit(solution)/shard_map/ppermute | solution.py:23
  20.1 5.8 %collective-permute-start.2 = (bf16[145,3,1,128]{3,0,1,2:T(8,128)(2,1)S(1)}, bf16[145,3,1,128]{3,0,1,2:T(8,128)(2,1)S(1)}, u32[]{:S(2)}, u32[]{:S(2)}) collective-permute-start(bf16[145,3,1,128]{3,0,1,2:T(8,128)(2,1)S(1)} %bitcast.153), channel_id=1, source_target_pairs={{0,24},{8,0},{16,8},{24,16},{1,25},{9,1},{17,9},{25,17},{2,26},{10... | collective-permute-start | bytes 334088 | tf_op jit(solution)/shard_map/ppermute | solution.py:23
  23.1 2.8 %copy-start.4 = (s32[1024]{0:T(1024)}, s32[1024]{0:T(1024)S(1)}, u32[]{:S(2)}) copy-start(s32[1024]{0:T(1024)S(1)} %pad_clamp_fusion) | copy-start | bytes 12292
  23.2 3.5 %copy-start.8 = (pred[4]{0:T(512)(128)(4,1)}, pred[4]{0:T(512)(128)(4,1)S(1)}, u32[]{:S(2)}) copy-start(pred[4]{0:T(512)(128)(4,1)S(1)} %compare_and_fusion.4) | copy-start | bytes 16
  27.0 7.0 %collective-permute-start.3 = (bf16[579,2,1,128]{3,0,1,2:T(8,128)(2,1)S(1)}, bf16[579,2,1,128]{3,0,1,2:T(8,128)(2,1)}, u32[]{:S(2)}, u32[]{:S(2)}) collective-permute-start(bf16[579,2,1,128]{3,0,1,2:T(8,128)(2,1)S(1)} %pad_maximum_fusion.1), channel_id=1, source_target_pairs={{0,32},{32,64},{64,96},{96,128},{128,160},{160,192},{192,224},{224... | collective-permute-start | bytes 889352 | tf_op jit(solution)/shard_map/ppermute | solution.py:93
  31.1 2.9 %copy-start.2 = (bf16[4,144,1,1,128]{4,1,2,0,3:T(8,128)(2,1)}, bf16[4,144,1,1,128]{4,1,2,0,3:T(8,128)(2,1)S(1)}, u32[]{:S(2)}) copy-start(bf16[4,144,1,1,128]{4,1,2,0,3:T(8,128)(2,1)S(1)} %slice.120) | copy-start | bytes 442372
  34.7 7.9 %collective-permute-start.4 = (bf16[579,2,1,128]{3,0,1,2:T(8,128)(2,1)}, bf16[579,2,1,128]{3,0,1,2:T(8,128)(2,1)S(1)}, u32[]{:S(2)}, u32[]{:S(2)}) collective-permute-start(bf16[579,2,1,128]{3,0,1,2:T(8,128)(2,1)} %collective-permute-done.3), channel_id=1, source_target_pairs={{0,32},{32,64},{64,96},{96,128},{128,160},{160,192},{192,224},{224... | collective-permute-start | bytes 889352 | tf_op jit(solution)/shard_map/ppermute | solution.py:93
  42.6 0.7 copy-start.10
  43.4 8.1 %collective-permute-start.5 = (bf16[579,2,1,128]{3,0,1,2:T(8,128)(2,1)}, bf16[579,2,1,128]{3,0,1,2:T(8,128)(2,1)S(1)}, u32[]{:S(2)}, u32[]{:S(2)}) collective-permute-start(bf16[579,2,1,128]{3,0,1,2:T(8,128)(2,1)} %copy-done.10), channel_id=1, source_target_pairs={{0,32},{32,64},{64,96},{96,128},{128,160},{160,192},{192,224},{224... | collective-permute-start | bytes 889352 | tf_op jit(solution)/shard_map/ppermute | solution.py:93
  51.5 0.7 copy-start.11
  52.8 10.9 %collective-permute-start.6 = (bf16[579,2,1,128]{3,0,1,2:T(8,128)(2,1)}, bf16[579,2,1,128]{3,0,1,2:T(8,128)(2,1)S(1)}, u32[]{:S(2)}, u32[]{:S(2)}) collective-permute-start(bf16[579,2,1,128]{3,0,1,2:T(8,128)(2,1)} %copy-done.11), channel_id=1, source_target_pairs={{0,32},{32,64},{64,96},{96,128},{128,160},{160,192},{192,224},{224... | collective-permute-start | bytes 889352 | tf_op jit(solution)/shard_map/ppermute | solution.py:93
  63.7 0.7 copy-start.12
  66.3 2.3 %copy-start.3 = (f32[576]{0:T(1024)S(1)}, f32[576]{0:T(1024)}, u32[]{:S(2)}) copy-start(f32[576]{0:T(1024)} %get-tuple-element.67) | copy-start | bytes 6916
  66.3 2.3 %copy-start.5 = (f32[576]{0:T(1024)S(1)}, f32[576]{0:T(1024)}, u32[]{:S(2)}) copy-start(f32[576]{0:T(1024)} %get-tuple-element.65) | copy-start | bytes 6916
  66.3 2.3 %copy-start.6 = (f32[576]{0:T(1024)S(1)}, f32[576]{0:T(1024)}, u32[]{:S(2)}) copy-start(f32[576]{0:T(1024)} %get-tuple-element.63) | copy-start | bytes 6916
  66.3 2.3 %copy-start.7 = (f32[576]{0:T(1024)S(1)}, f32[576]{0:T(1024)}, u32[]{:S(2)}) copy-start(f32[576]{0:T(1024)} %get-tuple-element.61) | copy-start | bytes 6916
  66.3 2.4 %copy-start = (f32[576,576]{0,1:T(8,128)S(1)}, f32[576,576]{0,1:T(8,128)}, u32[]{:S(2)}) copy-start(f32[576,576]{0,1:T(8,128)} %get-tuple-element.64) | copy-start | bytes 3981316
  74.7 1.7 %copy-start.1 = (f32[576,576]{0,1:T(8,128)S(1)}, f32[576,576]{0,1:T(8,128)}, u32[]{:S(2)}) copy-start(f32[576,576]{0,1:T(8,128)} %get-tuple-element.62) | copy-start | bytes 3981316
  79.5 19.9 %copy-start.9 = (pred[4]{0:T(512)(128)(4,1)S(1)}, pred[4]{0:T(512)(128)(4,1)}, u32[]{:S(2)}) copy-start(pred[4]{0:T(512)(128)(4,1)} %copy-done.8) | copy-start | bytes 16
  79.5 15.4 %collective-permute-start.7 = (bf16[576,128]{1,0:T(8,128)(2,1)S(1)}, bf16[576,128]{1,0:T(8,128)(2,1)S(1)}, u32[]{:S(2)}, u32[]{:S(2)}) collective-permute-start(bf16[576,128]{1,0:T(8,128)(2,1)S(1)} %fusion.6), channel_id=1, source_target_pairs={{0,8},{8,16},{16,24},{24,0},{1,9},{9,17},{17,25},{25,1},{2,10},{10... | collective-permute-start | bytes 442376 | tf_op jit(solution)/shard_map/ppermute | solution.py:23
  88.4 8.9 %collective-permute-start.8 = (bf16[576,128]{1,0:T(8,128)(2,1)S(1)}, bf16[576,128]{1,0:T(8,128)(2,1)S(1)}, u32[]{:S(2)}, u32[]{:S(2)}) collective-permute-start(bf16[576,128]{1,0:T(8,128)(2,1)S(1)} %fusion.6), channel_id=1, source_target_pairs={{0,16},{8,24},{16,0},{24,8},{1,17},{9,25},{17,1},{25,9},{2,18},{10... | collective-permute-start | bytes 442376 | tf_op jit(solution)/shard_map/ppermute | solution.py:23
  91.0 7.5 %collective-permute-start.9 = (bf16[576,128]{1,0:T(8,128)(2,1)S(1)}, bf16[576,128]{1,0:T(8,128)(2,1)S(1)}, u32[]{:S(2)}, u32[]{:S(2)}) collective-permute-start(bf16[576,128]{1,0:T(8,128)(2,1)S(1)} %fusion.6), channel_id=1, source_target_pairs={{0,24},{8,0},{16,8},{24,16},{1,25},{9,1},{17,9},{25,17},{2,26},{10... | collective-permute-start | bytes 442376 | tf_op jit(solution)/shard_map/ppermute | solution.py:23
  102.2 15.4 %collective-permute-start.11 = (bf16[512,8,112]{0,2,1:T(8,128)(2,1)S(1)}, bf16[512,8,112]{0,2,1:T(8,128)(2,1)}, u32[]{:S(2)}, u32[]{:S(2)}) collective-permute-start(bf16[512,8,112]{0,2,1:T(8,128)(2,1)S(1)} %get-tuple-element.48), channel_id=1, source_target_pairs={{0,1},{1,0},{2,3},{3,2},{4,5},{5,4},{6,7},{7,6},{8,9},{9,8},{10,11... | collective-permute-start | bytes 2752520 | tf_op jit(solution)/shard_map/ppermute | solution.py:108
  113.7 3.9 %collective-permute-start.10 = (bf16[576,512]{1,0:T(8,128)(2,1)S(1)}, bf16[576,512]{1,0:T(8,128)(2,1)S(1)}, u32[]{:S(2)}, u32[]{:S(2)}) collective-permute-start(bf16[576,512]{1,0:T(8,128)(2,1)S(1)} %copy_bitcast_fusion), channel_id=1, source_target_pairs={{0,1},{1,0},{2,3},{3,2},{4,5},{5,4},{6,7},{7,6},{8,9},{9,8},{10,11... | collective-permute-start | bytes 1769480 | tf_op jit(solution)/shard_map/ppermute | solution.py:104
  120.9 11.4 %collective-permute-start.12 = (bf16[576,224]{0,1:T(8,128)(2,1)S(1)}, bf16[576,224]{0,1:T(8,128)(2,1)S(1)}, u32[]{:S(2)}, u32[]{:S(2)}) collective-permute-start(bf16[576,224]{0,1:T(8,128)(2,1)S(1)} %get-tuple-element.50), channel_id=1, source_target_pairs={{0,2},{2,4},{4,6},{6,0},{1,3},{3,5},{5,7},{7,1},{8,10},{10,12},{12... | collective-permute-start | bytes 774152 | tf_op jit(solution)/shard_map/ppermute | solution.py:123
  123.8 15.1 %collective-permute-start.13 = (bf16[576,224]{0,1:T(8,128)(2,1)S(1)}, bf16[576,224]{0,1:T(8,128)(2,1)S(1)}, u32[]{:S(2)}, u32[]{:S(2)}) collective-permute-start(bf16[576,224]{0,1:T(8,128)(2,1)S(1)} %get-tuple-element.52), channel_id=1, source_target_pairs={{0,4},{2,6},{4,0},{6,2},{1,5},{3,7},{5,1},{7,3},{8,12},{10,14},{12... | collective-permute-start | bytes 774152 | tf_op jit(solution)/shard_map/ppermute | solution.py:123
  127.9 12.7 %collective-permute-start.14 = (bf16[576,224]{0,1:T(8,128)(2,1)S(1)}, bf16[576,224]{0,1:T(8,128)(2,1)S(1)}, u32[]{:S(2)}, u32[]{:S(2)}) collective-permute-start(bf16[576,224]{0,1:T(8,128)(2,1)S(1)} %get-tuple-element.51), channel_id=1, source_target_pairs={{0,6},{2,0},{4,2},{6,4},{1,7},{3,1},{5,3},{7,5},{8,14},{10,8},{12,... | collective-permute-start | bytes 774152 | tf_op jit(solution)/shard_map/ppermute | solution.py:123
  141.9 12.8 %all-to-all-start = ((bf16[8,144,112]{2,1,0:T(8,128)(2,1)}), bf16[8,144,112]{2,1,0:T(8,128)(2,1)S(1)}, u32[]{:S(2)}, u32[]{:S(2)}) async-start(bf16[8,144,112]{2,1,0:T(8,128)(2,1)} %bitcast.39), calls=%async_computation | async-start | bytes 589824 | tf_op jit(solution)/shard_map/all_to_all | solution.py:127
Sparse Core Ops, SparseCore 0:
  31.2 69.4 all-gather.1

commit v8 on v6

--- a/solution.py
+++ b/solution.py
@@ -70,11 +70,15 @@
         jnp.zeros((hq, level), jnp.float32),
         jnp.zeros((hq, level, HD), jnp.float32),
     )
+    relay = [(i, i + 1) for i in range(nz - 1)]
     carried = attend(carried, pair, 0)
-    block = pair
-    for distance in range(1, span + 1):
-        block = lax.ppermute(block, "z", [(i, i + 1) for i in range(nz - 1)])
-        carried = attend(carried, block, distance)
+    block = lax.ppermute(pair, "z", relay)
+    for distance in range(2, span + 1):
+        block, carried = lax.optimization_barrier((block, carried))
+        arriving = lax.ppermute(block, "z", relay)
+        carried = attend(carried, block, distance - 1)
+        block = arriving
+    carried = attend(carried, block, span)
     run_max, row_total, accumulated = carried
     attended = (accumulated / row_total[..., None]).astype(jnp.bfloat16)
     attended = attended.transpose(1, 0, 2).reshape(level, hq * HD)

time: 158 us -> 153 us (0.968)
  waiting for transfers between devices: 29.6 us -> 51.2 us
  blocking collectives: 23.6 us -> 10.6 us
  matrix products: 20.8 us -> 8.6 us
  starting transfers between devices: 48.1 us -> 53.8 us
  local copies, waits for them, and re-layouts: 13.6 us -> 9.03 us
  other arithmetic: 6.58 us -> 3.68 us
    all_to_all x1 -> x0, blocking collectives: 11.4 us -> none  [local(): lax.all_to_all(packed, 'y', 2, 0, tiled=True)]
    all_gather x1, waiting for transfers between devices: 3.87 us -> 15 us  [local(): weight_cols = lax.all_gather(out_weight, 'z', axis=1, tiled=True)]
    dot_general x5, matrix products: 11 us -> 2.56 us  [attend(): jnp.einsum('qhd,khd->hqk', query_rows, key_rows, preferred_element_type=j...]
    all_to_all x0 -> x1, waiting for transfers between devices: none -> 5.89 us  [local(): lax.all_to_all(packed, 'y', 2, 0, tiled=True)]
    all_to_all x0 -> x1, starting transfers between devices: none -> 5.01 us  [local(): lax.all_to_all(packed, 'y', 2, 0, tiled=True)]
    ppermute x4, waiting for transfers between devices: 9.42 us -> 13.4 us  [the longest x3 10.3 us: local(): arriving = lax.ppermute(block, 'z', relay)]
    dot_general x5, matrix products: 6.93 us -> 3.23 us  [attend(): jnp.einsum('hqk,khd->hqd', probs.astype(jnp.bfloat16), value_rows, prefer...]
    unnamed x21 -> x1, local copies, waits for them, and re-layouts: 2.94 us -> 0.75 us
  transfers between devices with their start and end apart: 11 -> 12, of which waited for: 10 -> 11; matrix products, arithmetic and copies ran while one was open for 18% -> 7% of each run, Pallas kernels for 0% -> 0%
where the time goes in v8:
time: 153 us; the launch traced here: 151 us
  starting transfers between devices  53.8 us (35%)
  waiting for transfers between devices  51.2 us (33%)
  between operations  14.5 us (9%)
  blocking collectives  10.6 us (7%)
  local copies, waits for them, and re-layouts  9.03 us (6%)
  matrix products  8.6 us (6%)
  other arithmetic  3.68 us (2%)
    ppermute x3, starting transfers between devices, local(): arriving = lax.ppermute(block, 'z', relay)  15.2 us
    all_gather x1, waiting for transfers between devices, local(): weight_cols = lax.all_gather(out_weight, 'z', axis=1, tiled=True)  15 us
    all_gather x1, blocking collectives, local(): own_attended = lax.all_gather(attended, 'y', axis=1, tiled=True)  10.6 us
    ppermute x1, starting transfers between devices, local(): lax.ppermute(lax.dynamic_index_in_dim(weight_cols, 1 - c, axis=2, keepdim...  10.5 us
    ppermute x3, starting transfers between devices, local(): part = lax.ppermute(part, 'x', [(i, (i + shift) % nx) for i in range(nx)])  10.5 us
    ppermute x3, waiting for transfers between devices, local(): arriving = lax.ppermute(block, 'z', relay)  10.3 us
    ppermute x3, waiting for transfers between devices, local(): part = lax.ppermute(part, 'x', [(i, (i + shift) % nx) for i in range(nx)])  9.24 us
    all_to_all x1, waiting for transfers between devices, local(): summed = lax.all_to_all(summed, ('y', 'c'), 0, 0, tiled=True)  6.06 us
  transfers between devices with their start and end apart: 12, of which 11 were waited for; matrix products, arithmetic and copies ran while one was open for 7% of the time, Pallas kernels for 0%

profile of v8, /device:TPU:1, one launch (start us, length us, event | category | flops | bytes accessed | tf_op | source)
XLA Modules:
  0.0 151.4 jit_solution(968892462842080332)
XLA Ops:
  7.2 1.2 reshape.339
  8.3 1.0 reshape.308
  9.3 0.7 convert_element_type.67
  10.4 0.8 copy.25
  11.2 5.0 %all-to-all-start = ((bf16[145,3,4,1,128]{4,0,1,3,2:T(8,128)(2,1)}), bf16[145,3,4,1,128]{4,0,1,3,2:T(8,128)(2,1)S(1)}, u32[]{:S(2)}, u32[]{:S(2)}) async-start(bf16[145,3,4,1,128]{4,0,1,3,2:T(8,128)(2,1)} %copy.25), calls=%async_computation | async-start | bytes 933888 | tf_op jit(solution)/shard_map/all_to_all | solution.py:29
  16.2 0.7 all-gather.3.cloned.1.call-update
  17.0 5.9 %all-to-all-done = bf16[145,3,4,1,128]{4,0,1,3,2:T(8,128)(2,1)S(1)} async-done(((bf16[145,3,4,1,128]{4,0,1,3,2:T(8,128)(2,1)}), bf16[145,3,4,1,128]{4,0,1,3,2:T(8,128)(2,1)S(1)}, u32[]{:S(2)}, u32[]{:S(2)}) %all-to-all-start) | async-done | bytes 445472 | tf_op jit(solution)/shard_map/all_to_all | solution.py:29
  23.1 0.5 fusion.78
  24.0 4.6 %collective-permute-start = (bf16[579,2,1,128]{3,0,1,2:T(8,128)(2,1)S(1)}, bf16[579,2,1,128]{3,0,1,2:T(8,128)(2,1)S(1)}, u32[]{:S(2)}, u32[]{:S(2)}) collective-permute-start(bf16[579,2,1,128]{3,0,1,2:T(8,128)(2,1)S(1)} %pad_maximum_fusion.1), channel_id=1, source_target_pairs={{0,32},{32,64},{64,96},{96,128},{128,160},{160,192},{192,224},{224... | collective-permute-start | bytes 889352 | tf_op jit(solution)/shard_map/ppermute | solution.py:75
  28.6 0.6 fusion.1
  29.2 3.1 %collective-permute-done = bf16[579,2,1,128]{3,0,1,2:T(8,128)(2,1)S(1)} collective-permute-done((bf16[579,2,1,128]{3,0,1,2:T(8,128)(2,1)S(1)}, bf16[579,2,1,128]{3,0,1,2:T(8,128)(2,1)S(1)}, u32[]{:S(2)}, u32[]{:S(2)}) %collective-permute-start) | collective-permute-done | bytes 296480 | tf_op jit(solution)/shard_map/ppermute | solution.py:75
  32.3 4.1 %collective-permute-start.1 = (bf16[579,2,1,128]{3,0,1,2:T(8,128)(2,1)S(1)}, bf16[579,2,1,128]{3,0,1,2:T(8,128)(2,1)S(1)}, u32[]{:S(2)}, u32[]{:S(2)}) collective-permute-start(bf16[579,2,1,128]{3,0,1,2:T(8,128)(2,1)S(1)} %collective-permute-done), channel_id=1, source_target_pairs={{0,32},{32,64},{64,96},{96,128},{128,160},{160,192},{192,224},{224... | collective-permute-start | bytes 889352 | tf_op jit(solution)/shard_map/ppermute | solution.py:78
  36.4 0.5 fusion.79
  37.0 0.5 fusion.6
  37.5 0.6 multiply_add_fusion.1
  38.1 1.9 %collective-permute-done.1 = bf16[579,2,1,128]{3,0,1,2:T(8,128)(2,1)S(1)} collective-permute-done((bf16[579,2,1,128]{3,0,1,2:T(8,128)(2,1)S(1)}, bf16[579,2,1,128]{3,0,1,2:T(8,128)(2,1)S(1)}, u32[]{:S(2)}, u32[]{:S(2)}) %collective-permute-start.1) | collective-permute-done | bytes 296480 | tf_op jit(solution)/shard_map/ppermute | solution.py:78
  40.0 4.1 %collective-permute-start.2 = (bf16[579,2,1,128]{3,0,1,2:T(8,128)(2,1)S(1)}, bf16[579,2,1,128]{3,0,1,2:T(8,128)(2,1)S(1)}, u32[]{:S(2)}, u32[]{:S(2)}) collective-permute-start(bf16[579,2,1,128]{3,0,1,2:T(8,128)(2,1)S(1)} %collective-permute-done.1), channel_id=1, source_target_pairs={{0,32},{32,64},{64,96},{96,128},{128,160},{160,192},{192,224},{224... | collective-permute-start | bytes 889352 | tf_op jit(solution)/shard_map/ppermute | solution.py:78
  44.2 0.5 fusion.80
  44.8 0.5 fusion.8
  45.3 0.6 multiply_add_fusion
  45.9 4.0 %collective-permute-done.2 = bf16[579,2,1,128]{3,0,1,2:T(8,128)(2,1)S(1)} collective-permute-done((bf16[579,2,1,128]{3,0,1,2:T(8,128)(2,1)S(1)}, bf16[579,2,1,128]{3,0,1,2:T(8,128)(2,1)S(1)}, u32[]{:S(2)}, u32[]{:S(2)}) %collective-permute-start.2) | collective-permute-done | bytes 296480 | tf_op jit(solution)/shard_map/ppermute | solution.py:78
  49.9 7.0 %collective-permute-start.3 = (bf16[579,2,1,128]{3,0,1,2:T(8,128)(2,1)S(1)}, bf16[579,2,1,128]{3,0,1,2:T(8,128)(2,1)S(1)}, u32[]{:S(2)}, u32[]{:S(2)}) collective-permute-start(bf16[579,2,1,128]{3,0,1,2:T(8,128)(2,1)S(1)} %collective-permute-done.2), channel_id=1, source_target_pairs={{0,32},{32,64},{64,96},{96,128},{128,160},{160,192},{192,224},{224... | collective-permute-start | bytes 889352 | tf_op jit(solution)/shard_map/ppermute | solution.py:78
  56.9 0.5 fusion.82
  57.4 4.3 %collective-permute-done.3 = bf16[579,2,1,128]{3,0,1,2:T(8,128)(2,1)S(1)} collective-permute-done((bf16[579,2,1,128]{3,0,1,2:T(8,128)(2,1)S(1)}, bf16[579,2,1,128]{3,0,1,2:T(8,128)(2,1)S(1)}, u32[]{:S(2)}, u32[]{:S(2)}) %collective-permute-start.3) | collective-permute-done | bytes 296480 | tf_op jit(solution)/shard_map/ppermute | solution.py:78
  61.8 0.5 fusion.81
  62.4 0.9 fusion.9
  63.4 0.6 convolution_bitcast_fusion.1
  64.0 0.8 fusion.4
  64.8 10.6 %all-gather = bf16[1,576,512]{2,1,0:T(8,128)(2,1)S(1)} all-gather(bf16[1,576,128]{2,1,0:T(8,128)(2,1)S(1)} %fusion.4), channel_id=2, replica_groups=mesh['z'=16,'y'=4,'x'=4,'c'=2] {'y'}, dimensions={2}, use_global_device_ids=true | all-gather | bytes 737280 | tf_op jit(solution)/shard_map/all_gather | solution.py:88
  75.4 15.0 %all-gather.3.cloned.1.call-done = bf16[512,1792]{0,1:T(8,128)(2,1)} async-done(((bf16[512,112]{0,1:T(8,128)(2,1)}), bf16[512,1792]{0,1:T(8,128)(2,1)}) %all-gather.3.cloned.1.call-update) | async-done | bytes 1835024 | tf_op jit(solution)/shard_map/all_gather | solution.py:89
  90.4 1.6 %dynamic-slice_bitcast_fusion = (bf16[512,8,112]{0,2,1:T(8,128)(2,1)S(1)}, bf16[512,8,1,112]{0,3,2,1:T(8,128)(2,1)S(1)}) fusion(bf16[512,8,2,112]{0,3,2,1:T(8,128)(2,1)} %bitcast.126, s32[]{:T(128)S(6)} %select_n.87, s32[]{:T(128)S(6)} %select_n.86), kind=kLoop, calls=%fused_computation.36 | loop fusion | bytes 3670024 | tf_op jit(solution)/shard_map/jit(dynamic_index_in_dim)/squeeze | solution.py:96
  92.0 10.5 %collective-permute-start.5 = (bf16[512,8,112]{0,2,1:T(8,128)(2,1)S(1)}, bf16[512,8,112]{0,2,1:T(8,128)(2,1)}, u32[]{:S(2)}, u32[]{:S(2)}) collective-permute-start(bf16[512,8,112]{0,2,1:T(8,128)(2,1)S(1)} %get-tuple-element.74), channel_id=1, source_target_pairs={{0,1},{1,0},{2,3},{3,2},{4,5},{5,4},{6,7},{7,6},{8,9},{9,8},{10,11... | collective-permute-start | bytes 2752520 | tf_op jit(solution)/shard_map/ppermute | solution.py:95
  102.5 2.1 %collective-permute-start.4 = (bf16[576,512]{1,0:T(8,128)(2,1)S(1)}, bf16[576,512]{1,0:T(8,128)(2,1)S(1)}, u32[]{:S(2)}, u32[]{:S(2)}) collective-permute-start(bf16[576,512]{1,0:T(8,128)(2,1)S(1)} %bitcast.124), channel_id=1, source_target_pairs={{0,1},{1,0},{2,3},{3,2},{4,5},{5,4},{6,7},{7,6},{8,9},{9,8},{10,11... | collective-permute-start | bytes 1769480 | tf_op jit(solution)/shard_map/ppermute | solution.py:91
  104.7 0.8 fusion.83
  105.5 0.9 collective-permute-done.4
  106.4 2.0 %add_convert_fusion = bf16[576,896]{1,0:T(8,128)(2,1)S(1)} fusion(f32[576,896]{1,0:T(8,128)S(1)} %fusion.83, bf16[576,512]{1,0:T(8,128)(2,1)S(1)} %collective-permute-done.4, bf16[512,896]{0,1:T(8,128)(2,1)} %bitcast.29), kind=kOutput, calls=%fused_computation | convolution fusion | flops 529514496 | bytes 4603904 | tf_op jit(solution)/shard_map/dot_general | solution.py:101
  108.5 1.1 copy.33
  109.7 3.1 %collective-permute-start.6 = (bf16[576,224]{0,1:T(8,128)(2,1)S(1)}, bf16[576,224]{0,1:T(8,128)(2,1)S(1)}, u32[]{:S(2)}, u32[]{:S(2)}) collective-permute-start(bf16[576,224]{0,1:T(8,128)(2,1)S(1)} %get-tuple-element.76), channel_id=1, source_target_pairs={{0,2},{2,4},{4,6},{6,0},{1,3},{3,5},{5,7},{7,1},{8,10},{10,12},{12... | collective-permute-start | bytes 774152 | tf_op jit(solution)/shard_map/ppermute | solution.py:110
  112.8 4.6 %collective-permute-start.7 = (bf16[576,224]{0,1:T(8,128)(2,1)S(1)}, bf16[576,224]{0,1:T(8,128)(2,1)S(1)}, u32[]{:S(2)}, u32[]{:S(2)}) collective-permute-start(bf16[576,224]{0,1:T(8,128)(2,1)S(1)} %get-tuple-element.78), channel_id=1, source_target_pairs={{0,4},{2,6},{4,0},{6,2},{1,5},{3,7},{5,1},{7,3},{8,12},{10,14},{12... | collective-permute-start | bytes 774152 | tf_op jit(solution)/shard_map/ppermute | solution.py:110
  117.3 2.8 %collective-permute-start.8 = (bf16[576,224]{0,1:T(8,128)(2,1)S(1)}, bf16[576,224]{0,1:T(8,128)(2,1)S(1)}, u32[]{:S(2)}, u32[]{:S(2)}) collective-permute-start(bf16[576,224]{0,1:T(8,128)(2,1)S(1)} %get-tuple-element.77), channel_id=1, source_target_pairs={{0,6},{2,0},{4,2},{6,4},{1,7},{3,1},{5,3},{7,5},{8,14},{10,8},{12,... | collective-permute-start | bytes 774152 | tf_op jit(solution)/shard_map/ppermute | solution.py:110
  120.2 0.9 collective-permute-done.6
  121.1 7.3 %collective-permute-done.7 = bf16[576,224]{0,1:T(8,128)(2,1)S(1)} collective-permute-done((bf16[576,224]{0,1:T(8,128)(2,1)S(1)}, bf16[576,224]{0,1:T(8,128)(2,1)S(1)}, u32[]{:S(2)}, u32[]{:S(2)}) %collective-permute-start.7) | collective-permute-done | bytes 258080 | tf_op jit(solution)/shard_map/ppermute | solution.py:110
  128.4 1.1 collective-permute-done.8
  129.9 0.7 copy.35
  130.7 5.9 %all-to-all-start.1 = ((bf16[8,144,112]{2,1,0:T(8,128)(2,1)}), bf16[8,144,112]{2,1,0:T(8,128)(2,1)S(1)}, u32[]{:S(2)}, u32[]{:S(2)}) async-start(bf16[8,144,112]{2,1,0:T(8,128)(2,1)} %bitcast.36), calls=%async_computation.1 | async-start | bytes 589824 | tf_op jit(solution)/shard_map/all_to_all | solution.py:114
  136.6 0.8 copy.37
  137.4 6.1 %all-to-all-done.1 = bf16[8,144,112]{2,1,0:T(8,128)(2,1)S(1)} async-done(((bf16[8,144,112]{2,1,0:T(8,128)(2,1)}), bf16[8,144,112]{2,1,0:T(8,128)(2,1)S(1)}, u32[]{:S(2)}, u32[]{:S(2)}) %all-to-all-start.1) | async-done | bytes 258080 | tf_op jit(solution)/shard_map/all_to_all | solution.py:114
  143.6 0.9 reshape.336
  (49 shorter events, 2.0 us)
Async XLA Ops:
  11.2 11.6 %all-to-all-start = ((bf16[145,3,4,1,128]{4,0,1,3,2:T(8,128)(2,1)}), bf16[145,3,4,1,128]{4,0,1,3,2:T(8,128)(2,1)S(1)}, u32[]{:S(2)}, u32[]{:S(2)}) async-start(bf16[145,3,4,1,128]{4,0,1,3,2:T(8,128)(2,1)} %copy.25), calls=%async_computation | async-start | bytes 933888 | tf_op jit(solution)/shard_map/all_to_all | solution.py:29
  16.2 74.2 %all-gather.3.cloned.1.call-start = ((), (), s32[]{:S(2)}) async-start(), calls=%async_computation.2 | async-start | bytes 1949696 | tf_op jit(solution)/shard_map/all_gather | solution.py:89
  24.0 8.3 %collective-permute-start = (bf16[579,2,1,128]{3,0,1,2:T(8,128)(2,1)S(1)}, bf16[579,2,1,128]{3,0,1,2:T(8,128)(2,1)S(1)}, u32[]{:S(2)}, u32[]{:S(2)}) collective-permute-start(bf16[579,2,1,128]{3,0,1,2:T(8,128)(2,1)S(1)} %pad_maximum_fusion.1), channel_id=1, source_target_pairs={{0,32},{32,64},{64,96},{96,128},{128,160},{160,192},{192,224},{224... | collective-permute-start | bytes 889352 | tf_op jit(solution)/shard_map/ppermute | solution.py:75
  32.3 7.8 %collective-permute-start.1 = (bf16[579,2,1,128]{3,0,1,2:T(8,128)(2,1)S(1)}, bf16[579,2,1,128]{3,0,1,2:T(8,128)(2,1)S(1)}, u32[]{:S(2)}, u32[]{:S(2)}) collective-permute-start(bf16[579,2,1,128]{3,0,1,2:T(8,128)(2,1)S(1)} %collective-permute-done), channel_id=1, source_target_pairs={{0,32},{32,64},{64,96},{96,128},{128,160},{160,192},{192,224},{224... | collective-permute-start | bytes 889352 | tf_op jit(solution)/shard_map/ppermute | solution.py:78
  40.0 9.9 %collective-permute-start.2 = (bf16[579,2,1,128]{3,0,1,2:T(8,128)(2,1)S(1)}, bf16[579,2,1,128]{3,0,1,2:T(8,128)(2,1)S(1)}, u32[]{:S(2)}, u32[]{:S(2)}) collective-permute-start(bf16[579,2,1,128]{3,0,1,2:T(8,128)(2,1)S(1)} %collective-permute-done.1), channel_id=1, source_target_pairs={{0,32},{32,64},{64,96},{96,128},{128,160},{160,192},{192,224},{224... | collective-permute-start | bytes 889352 | tf_op jit(solution)/shard_map/ppermute | solution.py:78
  49.9 11.9 %collective-permute-start.3 = (bf16[579,2,1,128]{3,0,1,2:T(8,128)(2,1)S(1)}, bf16[579,2,1,128]{3,0,1,2:T(8,128)(2,1)S(1)}, u32[]{:S(2)}, u32[]{:S(2)}) collective-permute-start(bf16[579,2,1,128]{3,0,1,2:T(8,128)(2,1)S(1)} %collective-permute-done.2), channel_id=1, source_target_pairs={{0,32},{32,64},{64,96},{96,128},{128,160},{160,192},{192,224},{224... | collective-permute-start | bytes 889352 | tf_op jit(solution)/shard_map/ppermute | solution.py:78
  92.0 14.5 %collective-permute-start.5 = (bf16[512,8,112]{0,2,1:T(8,128)(2,1)S(1)}, bf16[512,8,112]{0,2,1:T(8,128)(2,1)}, u32[]{:S(2)}, u32[]{:S(2)}) collective-permute-start(bf16[512,8,112]{0,2,1:T(8,128)(2,1)S(1)} %get-tuple-element.74), channel_id=1, source_target_pairs={{0,1},{1,0},{2,3},{3,2},{4,5},{5,4},{6,7},{7,6},{8,9},{9,8},{10,11... | collective-permute-start | bytes 2752520 | tf_op jit(solution)/shard_map/ppermute | solution.py:95
  102.5 3.9 %collective-permute-start.4 = (bf16[576,512]{1,0:T(8,128)(2,1)S(1)}, bf16[576,512]{1,0:T(8,128)(2,1)S(1)}, u32[]{:S(2)}, u32[]{:S(2)}) collective-permute-start(bf16[576,512]{1,0:T(8,128)(2,1)S(1)} %bitcast.124), channel_id=1, source_target_pairs={{0,1},{1,0},{2,3},{3,2},{4,5},{5,4},{6,7},{7,6},{8,9},{9,8},{10,11... | collective-permute-start | bytes 1769480 | tf_op jit(solution)/shard_map/ppermute | solution.py:91
  109.7 11.4 %collective-permute-start.6 = (bf16[576,224]{0,1:T(8,128)(2,1)S(1)}, bf16[576,224]{0,1:T(8,128)(2,1)S(1)}, u32[]{:S(2)}, u32[]{:S(2)}) collective-permute-start(bf16[576,224]{0,1:T(8,128)(2,1)S(1)} %get-tuple-element.76), channel_id=1, source_target_pairs={{0,2},{2,4},{4,6},{6,0},{1,3},{3,5},{5,7},{7,1},{8,10},{10,12},{12... | collective-permute-start | bytes 774152 | tf_op jit(solution)/shard_map/ppermute | solution.py:110
  112.8 15.6 %collective-permute-start.7 = (bf16[576,224]{0,1:T(8,128)(2,1)S(1)}, bf16[576,224]{0,1:T(8,128)(2,1)S(1)}, u32[]{:S(2)}, u32[]{:S(2)}) collective-permute-start(bf16[576,224]{0,1:T(8,128)(2,1)S(1)} %get-tuple-element.78), channel_id=1, source_target_pairs={{0,4},{2,6},{4,0},{6,2},{1,5},{3,7},{5,1},{7,3},{8,12},{10,14},{12... | collective-permute-start | bytes 774152 | tf_op jit(solution)/shard_map/ppermute | solution.py:110
  117.3 12.1 %collective-permute-start.8 = (bf16[576,224]{0,1:T(8,128)(2,1)S(1)}, bf16[576,224]{0,1:T(8,128)(2,1)S(1)}, u32[]{:S(2)}, u32[]{:S(2)}) collective-permute-start(bf16[576,224]{0,1:T(8,128)(2,1)S(1)} %get-tuple-element.77), channel_id=1, source_target_pairs={{0,6},{2,0},{4,2},{6,4},{1,7},{3,1},{5,3},{7,5},{8,14},{10,8},{12,... | collective-permute-start | bytes 774152 | tf_op jit(solution)/shard_map/ppermute | solution.py:110
  130.7 12.7 %all-to-all-start.1 = ((bf16[8,144,112]{2,1,0:T(8,128)(2,1)}), bf16[8,144,112]{2,1,0:T(8,128)(2,1)S(1)}, u32[]{:S(2)}, u32[]{:S(2)}) async-start(bf16[8,144,112]{2,1,0:T(8,128)(2,1)} %bitcast.36), calls=%async_computation.1 | async-start | bytes 589824 | tf_op jit(solution)/shard_map/all_to_all | solution.py:114
Sparse Core Ops, SparseCore 0:
  19.1 71.2 all-gather.2

commit v9 on v8

--- a/solution.py
+++ b/solution.py
@@ -13,8 +13,8 @@
 def local(queries, keys_values, segment_ids, out_weight):
     rows = queries.shape[0]
     heads = queries.shape[1] // HD
-    nz = lax.axis_size("z")
-    z = lax.axis_index("z")
+    nz = 2 * lax.axis_size("zh")
+    z = lax.axis_index("zh") * 2 + lax.axis_index("zl")
     level = NY * rows
     span = min(4, nz - 1)
     score_scale = 1.0 / math.sqrt(HD)
@@ -72,10 +72,10 @@
     )
     relay = [(i, i + 1) for i in range(nz - 1)]
     carried = attend(carried, pair, 0)
-    block = lax.ppermute(pair, "z", relay)
+    block = lax.ppermute(pair, ("zh", "zl"), relay)
     for distance in range(2, span + 1):
         block, carried = lax.optimization_barrier((block, carried))
-        arriving = lax.ppermute(block, "z", relay)
+        arriving = lax.ppermute(block, ("zh", "zl"), relay)
         carried = attend(carried, block, distance - 1)
         block = arriving
     carried = attend(carried, block, span)
@@ -86,9 +86,12 @@
     c = lax.axis_index("c")
     swap = [(0, 1), (1, 0)]
     own_attended = lax.all_gather(attended, "y", axis=1, tiled=True)
-    weight_cols = lax.all_gather(out_weight, "z", axis=1, tiled=True)
-    weight_cols, own_attended = lax.optimization_barrier((weight_cols, own_attended))
     other_attended = lax.ppermute(own_attended, "c", swap)
+    weight_cols = lax.all_gather(out_weight, "zl", axis=1, tiled=True)
+    weight_cols = lax.all_gather(weight_cols, "zh", axis=1, tiled=True)
+    weight_cols, own_attended, other_attended = lax.optimization_barrier(
+        (weight_cols, own_attended, other_attended)
+    )
     chunk = out_weight.shape[1]
     weight_cols = weight_cols.reshape(weight_cols.shape[0], nz // 2, 2, chunk)
     own_weight = lax.dynamic_index_in_dim(weight_cols, c, axis=2, keepdims=False)
@@ -121,10 +124,11 @@
 def solution(mesh):
     seq, tensor = mesh.shape["seq"], mesh.shape["tensor"]
     assert seq % NY == 0 and tensor % 2 == 0
+    assert (seq // NY) % 2 == 0
     grid = Mesh(
-        mesh.devices.reshape(seq // NY, NY, tensor // 2, 2), ("z", "y", "x", "c")
+        mesh.devices.reshape(seq // NY // 2, 2, NY, tensor // 2, 2), ("zh", "zl", "y", "x", "c")
     )
-    s, t = ("z", "y"), ("x", "c")
+    s, t = ("zh", "zl", "y"), ("x", "c")
     return jax.shard_map(
         local,
         mesh=grid,

time: 153 us -> 168 us (1.098)
  the two profiles are of different devices: /device:TPU:1 before, /device:TPU:130 now
where the time goes in v9:
time: 168 us
  waiting for transfers between devices  80.9 us (48%)
  starting transfers between devices  33.3 us (20%)
  blocking collectives  17.9 us (11%)
  between operations  14.5 us (9%)
  local copies, waits for them, and re-layouts  9.97 us (6%)
  matrix products  7.41 us (4%)
  other arithmetic  3.67 us (2%)
    ppermute x3, waiting for transfers between devices, local(): arriving = lax.ppermute(block, ('zh', 'zl'), relay)  49.3 us
    all_gather x1, blocking collectives, local(): own_attended = lax.all_gather(attended, 'y', axis=1, tiled=True)  12.3 us
    ppermute x3, waiting for transfers between devices, local(): part = lax.ppermute(part, 'x', [(i, (i + shift) % nx) for i in range(nx)])  10.9 us
    ppermute x3, starting transfers between devices, local(): part = lax.ppermute(part, 'x', [(i, (i + shift) % nx) for i in range(nx)])  10.7 us
    all_to_all x1, waiting for transfers between devices, local(): summed = lax.all_to_all(summed, ('y', 'c'), 0, 0, tiled=True)  7.14 us
    ppermute x3, starting transfers between devices, local(): arriving = lax.ppermute(block, ('zh', 'zl'), relay)  6.43 us
    ppermute x1, waiting for transfers between devices, local(): block = lax.ppermute(pair, ('zh', 'zl'), relay)  6.05 us
    all_gather x1, blocking collectives, local(): weight_cols = lax.all_gather(out_weight, 'zl', axis=1, tiled=True)  5.57 us
  transfers between devices with their start and end apart: 12, of which 11 were waited for; matrix products, arithmetic and copies ran while one was open for 6% of the time, Pallas kernels for 0%

profile of v9, /device:TPU:130, one launch (start us, length us, event | category | flops | bytes accessed | tf_op | source)
XLA Modules:
  0.0 167.6 jit_solution(14396724501877986005)
XLA Ops:
  7.2 1.2 reshape.339
  8.3 1.0 reshape.308
  9.3 0.7 convert_element_type.67
  10.4 0.8 copy.25
  11.2 4.5 %all-to-all-start = ((bf16[145,3,4,1,128]{4,0,1,3,2:T(8,128)(2,1)}), bf16[145,3,4,1,128]{4,0,1,3,2:T(8,128)(2,1)S(1)}, u32[]{:S(2)}, u32[]{:S(2)}) async-start(bf16[145,3,4,1,128]{4,0,1,3,2:T(8,128)(2,1)} %copy.25), calls=%async_computation | async-start | bytes 933888 | tf_op jit(solution)/shard_map/all_to_all | solution.py:29
  15.7 5.6 %all_gather.9 = bf16[512,224]{0,1:T(8,128)(2,1)} all-gather(bf16[512,112]{0,1:T(8,128)(2,1)S(1)} %copy-done), channel_id=1, replica_groups=mesh['zh'=8,'zl'=2,'y'=4,'x'=4,'c'=2] {'zl'}, dimensions={1}, use_global_device_ids=true | all-gather | bytes 344064 | tf_op jit(solution)/shard_map/all_gather | solution.py:90
  21.3 3.2 %all-to-all-done = bf16[145,3,4,1,128]{4,0,1,3,2:T(8,128)(2,1)S(1)} async-done(((bf16[145,3,4,1,128]{4,0,1,3,2:T(8,128)(2,1)}), bf16[145,3,4,1,128]{4,0,1,3,2:T(8,128)(2,1)S(1)}, u32[]{:S(2)}, u32[]{:S(2)}) %all-to-all-start) | async-done | bytes 445472 | tf_op jit(solution)/shard_map/all_to_all | solution.py:29
  24.8 0.5 fusion.78
  25.7 3.8 %collective-permute-start = (bf16[579,2,1,128]{3,0,1,2:T(8,128)(2,1)S(1)}, bf16[579,2,1,128]{3,0,1,2:T(8,128)(2,1)S(1)}, u32[]{:S(2)}, u32[]{:S(2)}) collective-permute-start(bf16[579,2,1,128]{3,0,1,2:T(8,128)(2,1)S(1)} %pad_maximum_fusion.1), channel_id=1, source_target_pairs={{0,32},{32,64},{64,96},{96,128},{128,160},{160,192},{192,224},{224... | collective-permute-start | bytes 889352 | tf_op jit(solution)/shard_map/ppermute | solution.py:75
  29.5 0.6 fusion.1
  30.1 6.0 %collective-permute-done = bf16[579,2,1,128]{3,0,1,2:T(8,128)(2,1)S(1)} collective-permute-done((bf16[579,2,1,128]{3,0,1,2:T(8,128)(2,1)S(1)}, bf16[579,2,1,128]{3,0,1,2:T(8,128)(2,1)S(1)}, u32[]{:S(2)}, u32[]{:S(2)}) %collective-permute-start) | collective-permute-done | bytes 296480 | tf_op jit(solution)/shard_map/ppermute | solution.py:75
  36.2 2.6 %collective-permute-start.1 = (bf16[579,2,1,128]{3,0,1,2:T(8,128)(2,1)S(1)}, bf16[579,2,1,128]{3,0,1,2:T(8,128)(2,1)S(1)}, u32[]{:S(2)}, u32[]{:S(2)}) collective-permute-start(bf16[579,2,1,128]{3,0,1,2:T(8,128)(2,1)S(1)} %collective-permute-done), channel_id=1, source_target_pairs={{0,32},{32,64},{64,96},{96,128},{128,160},{160,192},{192,224},{224... | collective-permute-start | bytes 889352 | tf_op jit(solution)/shard_map/ppermute | solution.py:78
  38.8 0.5 fusion.79
  39.4 0.5 fusion.6
  39.9 0.6 multiply_add_fusion.1
  40.5 20.4 %collective-permute-done.1 = bf16[579,2,1,128]{3,0,1,2:T(8,128)(2,1)S(1)} collective-permute-done((bf16[579,2,1,128]{3,0,1,2:T(8,128)(2,1)S(1)}, bf16[579,2,1,128]{3,0,1,2:T(8,128)(2,1)S(1)}, u32[]{:S(2)}, u32[]{:S(2)}) %collective-permute-start.1) | collective-permute-done | bytes 296480 | tf_op jit(solution)/shard_map/ppermute | solution.py:78
  60.9 1.9 %collective-permute-start.2 = (bf16[579,2,1,128]{3,0,1,2:T(8,128)(2,1)S(1)}, bf16[579,2,1,128]{3,0,1,2:T(8,128)(2,1)S(1)}, u32[]{:S(2)}, u32[]{:S(2)}) collective-permute-start(bf16[579,2,1,128]{3,0,1,2:T(8,128)(2,1)S(1)} %collective-permute-done.1), channel_id=1, source_target_pairs={{0,32},{32,64},{64,96},{96,128},{128,160},{160,192},{192,224},{224... | collective-permute-start | bytes 889352 | tf_op jit(solution)/shard_map/ppermute | solution.py:78
  62.9 0.5 fusion.80
  63.4 0.5 fusion.8
  63.9 0.6 multiply_add_fusion
  64.6 21.5 %collective-permute-done.2 = bf16[579,2,1,128]{3,0,1,2:T(8,128)(2,1)S(1)} collective-permute-done((bf16[579,2,1,128]{3,0,1,2:T(8,128)(2,1)S(1)}, bf16[579,2,1,128]{3,0,1,2:T(8,128)(2,1)S(1)}, u32[]{:S(2)}, u32[]{:S(2)}) %collective-permute-start.2) | collective-permute-done | bytes 296480 | tf_op jit(solution)/shard_map/ppermute | solution.py:78
  86.1 1.9 %collective-permute-start.3 = (bf16[579,2,1,128]{3,0,1,2:T(8,128)(2,1)S(1)}, bf16[579,2,1,128]{3,0,1,2:T(8,128)(2,1)S(1)}, u32[]{:S(2)}, u32[]{:S(2)}) collective-permute-start(bf16[579,2,1,128]{3,0,1,2:T(8,128)(2,1)S(1)} %collective-permute-done.2), channel_id=1, source_target_pairs={{0,32},{32,64},{64,96},{96,128},{128,160},{160,192},{192,224},{224... | collective-permute-start | bytes 889352 | tf_op jit(solution)/shard_map/ppermute | solution.py:78
  88.0 0.5 fusion.82
  88.6 7.4 %collective-permute-done.3 = bf16[579,2,1,128]{3,0,1,2:T(8,128)(2,1)S(1)} collective-permute-done((bf16[579,2,1,128]{3,0,1,2:T(8,128)(2,1)S(1)}, bf16[579,2,1,128]{3,0,1,2:T(8,128)(2,1)S(1)}, u32[]{:S(2)}, u32[]{:S(2)}) %collective-permute-start.3) | collective-permute-done | bytes 296480 | tf_op jit(solution)/shard_map/ppermute | solution.py:78
  96.0 0.5 fusion.81
  96.5 0.9 fusion.9
  97.5 0.6 convolution_bitcast_fusion.1
  98.2 0.8 fusion.4
  98.9 12.3 %all-gather = bf16[1,576,512]{2,1,0:T(8,128)(2,1)S(1)} all-gather(bf16[1,576,128]{2,1,0:T(8,128)(2,1)S(1)} %fusion.4), channel_id=2, replica_groups=mesh['zh'=8,'zl'=2,'y'=4,'x'=4,'c'=2] {'y'}, dimensions={2}, use_global_device_ids=true | all-gather | bytes 737280 | tf_op jit(solution)/shard_map/all_gather | solution.py:88
  111.2 1.9 %collective-permute-start.4 = (bf16[576,512]{1,0:T(8,128)(2,1)S(1)}, bf16[576,512]{1,0:T(8,128)(2,1)S(1)}, u32[]{:S(2)}, u32[]{:S(2)}) collective-permute-start(bf16[576,512]{1,0:T(8,128)(2,1)S(1)} %bitcast.124), channel_id=1, source_target_pairs={{0,1},{1,0},{2,3},{3,2},{4,5},{5,4},{6,7},{7,6},{8,9},{9,8},{10,11... | collective-permute-start | bytes 1769480 | tf_op jit(solution)/shard_map/ppermute | solution.py:89
  113.2 2.0 %collective-permute-done.4 = bf16[576,512]{1,0:T(8,128)(2,1)S(1)} collective-permute-done((bf16[576,512]{1,0:T(8,128)(2,1)S(1)}, bf16[576,512]{1,0:T(8,128)(2,1)S(1)}, u32[]{:S(2)}, u32[]{:S(2)}) %collective-permute-start.4) | collective-permute-done | bytes 589856 | tf_op jit(solution)/shard_map/ppermute | solution.py:89
  115.1 2.5 %constant_dynamic-slice_fusion = (bf16[512,8,1,112]{0,3,2,1:T(8,128)(2,1)S(1)}, bf16[512,8,112]{0,2,1:T(8,128)(2,1)}) fusion(bf16[512,8,2,112]{0,3,2,1:T(8,128)(2,1)} %bitcast.126, s32[]{:T(128)S(6)} %select_n.86, s32[]{:T(128)S(6)} %select_n.87), kind=kLoop, calls=%fused_computation.109 | loop fusion | bytes 3670024 | tf_op jit(solution)/shard_map/jit(dynamic_index_in_dim)/dynamic_slice | solution.py:97
  117.6 2.2 %collective-permute-start.5 = (bf16[512,8,112]{0,2,1:T(8,128)(2,1)}, bf16[512,8,112]{0,2,1:T(8,128)(2,1)S(1)}, u32[]{:S(2)}, u32[]{:S(2)}) collective-permute-start(bf16[512,8,112]{0,2,1:T(8,128)(2,1)} %get-tuple-element.77), channel_id=1, source_target_pairs={{0,1},{1,0},{2,3},{3,2},{4,5},{5,4},{6,7},{7,6},{8,9},{9,8},{10,11... | collective-permute-start | bytes 2752520 | tf_op jit(solution)/shard_map/ppermute | solution.py:98
  119.9 2.3 %collective-permute-done.5 = bf16[512,8,112]{0,2,1:T(8,128)(2,1)S(1)} collective-permute-done((bf16[512,8,112]{0,2,1:T(8,128)(2,1)}, bf16[512,8,112]{0,2,1:T(8,128)(2,1)S(1)}, u32[]{:S(2)}, u32[]{:S(2)}) %collective-permute-start.5) | collective-permute-done | bytes 917536 | tf_op jit(solution)/shard_map/ppermute | solution.py:98
  122.2 0.8 fusion.83
  123.0 0.8 add_convert_fusion
  123.8 1.1 copy.33
  125.1 3.5 %collective-permute-start.6 = (bf16[576,224]{0,1:T(8,128)(2,1)S(1)}, bf16[576,224]{0,1:T(8,128)(2,1)S(1)}, u32[]{:S(2)}, u32[]{:S(2)}) collective-permute-start(bf16[576,224]{0,1:T(8,128)(2,1)S(1)} %get-tuple-element.78), channel_id=1, source_target_pairs={{0,2},{2,4},{4,6},{6,0},{1,3},{3,5},{5,7},{7,1},{8,10},{10,12},{12... | collective-permute-start | bytes 774152 | tf_op jit(solution)/shard_map/ppermute | solution.py:113
  128.6 2.9 %collective-permute-start.7 = (bf16[576,224]{0,1:T(8,128)(2,1)S(1)}, bf16[576,224]{0,1:T(8,128)(2,1)S(1)}, u32[]{:S(2)}, u32[]{:S(2)}) collective-permute-start(bf16[576,224]{0,1:T(8,128)(2,1)S(1)} %get-tuple-element.80), channel_id=1, source_target_pairs={{0,4},{2,6},{4,0},{6,2},{1,5},{3,7},{5,1},{7,3},{8,12},{10,14},{12... | collective-permute-start | bytes 774152 | tf_op jit(solution)/shard_map/ppermute | solution.py:113
  131.5 4.3 %collective-permute-start.8 = (bf16[576,224]{0,1:T(8,128)(2,1)S(1)}, bf16[576,224]{0,1:T(8,128)(2,1)S(1)}, u32[]{:S(2)}, u32[]{:S(2)}) collective-permute-start(bf16[576,224]{0,1:T(8,128)(2,1)S(1)} %get-tuple-element.79), channel_id=1, source_target_pairs={{0,6},{2,0},{4,2},{6,4},{1,7},{3,1},{5,3},{7,5},{8,14},{10,8},{12,... | collective-permute-start | bytes 774152 | tf_op jit(solution)/shard_map/ppermute | solution.py:113
  135.8 0.9 collective-permute-done.6
  136.7 5.1 %collective-permute-done.7 = bf16[576,224]{0,1:T(8,128)(2,1)S(1)} collective-permute-done((bf16[576,224]{0,1:T(8,128)(2,1)S(1)}, bf16[576,224]{0,1:T(8,128)(2,1)S(1)}, u32[]{:S(2)}, u32[]{:S(2)}) %collective-permute-start.7) | collective-permute-done | bytes 258080 | tf_op jit(solution)/shard_map/ppermute | solution.py:113
  141.7 5.0 %collective-permute-done.8 = bf16[576,224]{0,1:T(8,128)(2,1)S(1)} collective-permute-done((bf16[576,224]{0,1:T(8,128)(2,1)S(1)}, bf16[576,224]{0,1:T(8,128)(2,1)S(1)}, u32[]{:S(2)}, u32[]{:S(2)}) %collective-permute-start.8) | collective-permute-done | bytes 258080 | tf_op jit(solution)/shard_map/ppermute | solution.py:113
  147.2 0.7 copy.35
  148.0 3.8 %all-to-all-start.1 = ((bf16[8,144,112]{2,1,0:T(8,128)(2,1)}), bf16[8,144,112]{2,1,0:T(8,128)(2,1)S(1)}, u32[]{:S(2)}, u32[]{:S(2)}) async-start(bf16[8,144,112]{2,1,0:T(8,128)(2,1)} %bitcast.36), calls=%async_computation.1 | async-start | bytes 589824 | tf_op jit(solution)/shard_map/all_to_all | solution.py:117
  151.8 0.8 copy.37
  152.5 7.1 %all-to-all-done.1 = bf16[8,144,112]{2,1,0:T(8,128)(2,1)S(1)} async-done(((bf16[8,144,112]{2,1,0:T(8,128)(2,1)}), bf16[8,144,112]{2,1,0:T(8,128)(2,1)S(1)}, u32[]{:S(2)}, u32[]{:S(2)}) %all-to-all-start.1) | async-done | bytes 258080 | tf_op jit(solution)/shard_map/all_to_all | solution.py:117
  159.8 0.9 reshape.336
  (52 shorter events, 2.0 us)
Async XLA Ops:
  10.2 5.5 %copy-start = (bf16[512,112]{0,1:T(8,128)(2,1)S(1)}, bf16[512,112]{0,1:T(8,128)(2,1)}, u32[]{:S(2)}) copy-start(bf16[512,112]{0,1:T(8,128)(2,1)} %param.11) | copy-start | bytes 344068
  11.2 13.3 %all-to-all-start = ((bf16[145,3,4,1,128]{4,0,1,3,2:T(8,128)(2,1)}), bf16[145,3,4,1,128]{4,0,1,3,2:T(8,128)(2,1)S(1)}, u32[]{:S(2)}, u32[]{:S(2)}) async-start(bf16[145,3,4,1,128]{4,0,1,3,2:T(8,128)(2,1)} %copy.25), calls=%async_computation | async-start | bytes 933888 | tf_op jit(solution)/shard_map/all_to_all | solution.py:29
  15.7 99.4 %all-gather.3.cloned.1.call-start = ((), (), s32[]{:S(2)}) async-start(), calls=%async_computation.2 | async-start | bytes 2064384 | tf_op jit(solution)/shard_map/all_gather | solution.py:91
  25.7 10.5 %collective-permute-start = (bf16[579,2,1,128]{3,0,1,2:T(8,128)(2,1)S(1)}, bf16[579,2,1,128]{3,0,1,2:T(8,128)(2,1)S(1)}, u32[]{:S(2)}, u32[]{:S(2)}) collective-permute-start(bf16[579,2,1,128]{3,0,1,2:T(8,128)(2,1)S(1)} %pad_maximum_fusion.1), channel_id=1, source_target_pairs={{0,32},{32,64},{64,96},{96,128},{128,160},{160,192},{192,224},{224... | collective-permute-start | bytes 889352 | tf_op jit(solution)/shard_map/ppermute | solution.py:75
  36.2 24.8 %collective-permute-start.1 = (bf16[579,2,1,128]{3,0,1,2:T(8,128)(2,1)S(1)}, bf16[579,2,1,128]{3,0,1,2:T(8,128)(2,1)S(1)}, u32[]{:S(2)}, u32[]{:S(2)}) collective-permute-start(bf16[579,2,1,128]{3,0,1,2:T(8,128)(2,1)S(1)} %collective-permute-done), channel_id=1, source_target_pairs={{0,32},{32,64},{64,96},{96,128},{128,160},{160,192},{192,224},{224... | collective-permute-start | bytes 889352 | tf_op jit(solution)/shard_map/ppermute | solution.py:78
  60.9 25.2 %collective-permute-start.2 = (bf16[579,2,1,128]{3,0,1,2:T(8,128)(2,1)S(1)}, bf16[579,2,1,128]{3,0,1,2:T(8,128)(2,1)S(1)}, u32[]{:S(2)}, u32[]{:S(2)}) collective-permute-start(bf16[579,2,1,128]{3,0,1,2:T(8,128)(2,1)S(1)} %collective-permute-done.1), channel_id=1, source_target_pairs={{0,32},{32,64},{64,96},{96,128},{128,160},{160,192},{192,224},{224... | collective-permute-start | bytes 889352 | tf_op jit(solution)/shard_map/ppermute | solution.py:78
  86.1 9.9 %collective-permute-start.3 = (bf16[579,2,1,128]{3,0,1,2:T(8,128)(2,1)S(1)}, bf16[579,2,1,128]{3,0,1,2:T(8,128)(2,1)S(1)}, u32[]{:S(2)}, u32[]{:S(2)}) collective-permute-start(bf16[579,2,1,128]{3,0,1,2:T(8,128)(2,1)S(1)} %collective-permute-done.2), channel_id=1, source_target_pairs={{0,32},{32,64},{64,96},{96,128},{128,160},{160,192},{192,224},{224... | collective-permute-start | bytes 889352 | tf_op jit(solution)/shard_map/ppermute | solution.py:78
  111.2 3.9 %collective-permute-start.4 = (bf16[576,512]{1,0:T(8,128)(2,1)S(1)}, bf16[576,512]{1,0:T(8,128)(2,1)S(1)}, u32[]{:S(2)}, u32[]{:S(2)}) collective-permute-start(bf16[576,512]{1,0:T(8,128)(2,1)S(1)} %bitcast.124), channel_id=1, source_target_pairs={{0,1},{1,0},{2,3},{3,2},{4,5},{5,4},{6,7},{7,6},{8,9},{9,8},{10,11... | collective-permute-start | bytes 1769480 | tf_op jit(solution)/shard_map/ppermute | solution.py:89
  117.6 4.6 %collective-permute-start.5 = (bf16[512,8,112]{0,2,1:T(8,128)(2,1)}, bf16[512,8,112]{0,2,1:T(8,128)(2,1)S(1)}, u32[]{:S(2)}, u32[]{:S(2)}) collective-permute-start(bf16[512,8,112]{0,2,1:T(8,128)(2,1)} %get-tuple-element.77), channel_id=1, source_target_pairs={{0,1},{1,0},{2,3},{3,2},{4,5},{5,4},{6,7},{7,6},{8,9},{9,8},{10,11... | collective-permute-start | bytes 2752520 | tf_op jit(solution)/shard_map/ppermute | solution.py:98
  125.1 11.6 %collective-permute-start.6 = (bf16[576,224]{0,1:T(8,128)(2,1)S(1)}, bf16[576,224]{0,1:T(8,128)(2,1)S(1)}, u32[]{:S(2)}, u32[]{:S(2)}) collective-permute-start(bf16[576,224]{0,1:T(8,128)(2,1)S(1)} %get-tuple-element.78), channel_id=1, source_target_pairs={{0,2},{2,4},{4,6},{6,0},{1,3},{3,5},{5,7},{7,1},{8,10},{10,12},{12... | collective-permute-start | bytes 774152 | tf_op jit(solution)/shard_map/ppermute | solution.py:113
  128.6 13.2 %collective-permute-start.7 = (bf16[576,224]{0,1:T(8,128)(2,1)S(1)}, bf16[576,224]{0,1:T(8,128)(2,1)S(1)}, u32[]{:S(2)}, u32[]{:S(2)}) collective-permute-start(bf16[576,224]{0,1:T(8,128)(2,1)S(1)} %get-tuple-element.80), channel_id=1, source_target_pairs={{0,4},{2,6},{4,0},{6,2},{1,5},{3,7},{5,1},{7,3},{8,12},{10,14},{12... | collective-permute-start | bytes 774152 | tf_op jit(solution)/shard_map/ppermute | solution.py:113
  131.5 15.2 %collective-permute-start.8 = (bf16[576,224]{0,1:T(8,128)(2,1)S(1)}, bf16[576,224]{0,1:T(8,128)(2,1)S(1)}, u32[]{:S(2)}, u32[]{:S(2)}) collective-permute-start(bf16[576,224]{0,1:T(8,128)(2,1)S(1)} %get-tuple-element.79), channel_id=1, source_target_pairs={{0,6},{2,0},{4,2},{6,4},{1,7},{3,1},{5,3},{7,5},{8,14},{10,8},{12,... | collective-permute-start | bytes 774152 | tf_op jit(solution)/shard_map/ppermute | solution.py:113
  148.0 11.7 %all-to-all-start.1 = ((bf16[8,144,112]{2,1,0:T(8,128)(2,1)}), bf16[8,144,112]{2,1,0:T(8,128)(2,1)S(1)}, u32[]{:S(2)}, u32[]{:S(2)}) async-start(bf16[8,144,112]{2,1,0:T(8,128)(2,1)} %bitcast.36), calls=%async_computation.1 | async-start | bytes 589824 | tf_op jit(solution)/shard_map/all_to_all | solution.py:117
Sparse Core Ops, SparseCore 0:
  21.4 63.0 all-gather.2

commit v10 on v8

--- a/solution.py
+++ b/solution.py
@@ -18,6 +18,7 @@
     level = NY * rows
     span = min(4, nz - 1)
     score_scale = 1.0 / math.sqrt(HD)
+    weight_cols = lax.all_gather(out_weight, "z", axis=1, tiled=True)
 
     hq = heads // NY
     packed = jnp.concatenate(
@@ -86,9 +87,10 @@
     c = lax.axis_index("c")
     swap = [(0, 1), (1, 0)]
     own_attended = lax.all_gather(attended, "y", axis=1, tiled=True)
-    weight_cols = lax.all_gather(out_weight, "z", axis=1, tiled=True)
-    weight_cols, own_attended = lax.optimization_barrier((weight_cols, own_attended))
     other_attended = lax.ppermute(own_attended, "c", swap)
+    weight_cols, own_attended, other_attended = lax.optimization_barrier(
+        (weight_cols, own_attended, other_attended)
+    )
     chunk = out_weight.shape[1]
     weight_cols = weight_cols.reshape(weight_cols.shape[0], nz // 2, 2, chunk)
     own_weight = lax.dynamic_index_in_dim(weight_cols, c, axis=2, keepdims=False)

time: 153 us -> 152 us (level)
  waiting for transfers between devices: 51.2 us -> 41.3 us
  starting transfers between devices: 53.8 us -> 62.9 us
    all_gather x1, waiting for transfers between devices: 15 us -> 2.58 us  [local(): weight_cols = lax.all_gather(out_weight, 'z', axis=1, tiled=True)]
    ppermute x1, starting transfers between devices: 2.1 us -> 10.8 us  [local(): other_attended = lax.ppermute(own_attended, 'c', swap)]
    dynamic_slice x0 -> x1, local copies, waits for them, and re-layouts: none -> 2.52 us  [local(): lax.dynamic_index_in_dim(weight_cols, c, axis=2, keepdims=False)]
    ppermute x1, waiting for transfers between devices: 0.01 us -> 2.06 us  [local(): lax.ppermute(lax.dynamic_index_in_dim(weight_cols, 1 - c, axis=2, keepdim...]
    squeeze x1 -> x0, local copies, waits for them, and re-layouts: 1.59 us -> none  [local(): lax.dynamic_index_in_dim(weight_cols, 1 - c, axis=2, keepdims=False)]
  transfers between devices with their start and end apart: 12 -> 12, of which waited for: 11 -> 12; matrix products, arithmetic and copies ran while one was open for 7% -> 6% of each run, Pallas kernels for 0% -> 0%
where the time goes in v10:
time: 152 us; the launch traced here: 150 us
  starting transfers between devices  62.9 us (41%)
  waiting for transfers between devices  41.3 us (27%)
  between operations  14.4 us (9%)
  blocking collectives  10.6 us (7%)
  local copies, waits for them, and re-layouts  9.96 us (7%)
  matrix products  7.42 us (5%)
  other arithmetic  3.68 us (2%)
    ppermute x3, starting transfers between devices, local(): arriving = lax.ppermute(block, 'z', relay)  15.2 us
    ppermute x1, starting transfers between devices, local(): other_attended = lax.ppermute(own_attended, 'c', swap)  10.8 us
    ppermute x1, starting transfers between devices, local(): lax.ppermute(lax.dynamic_index_in_dim(weight_cols, 1 - c, axis=2, keepdim...  10.7 us
    all_gather x1, blocking collectives, local(): own_attended = lax.all_gather(attended, 'y', axis=1, tiled=True)  10.6 us
    ppermute x3, starting transfers between devices, local(): part = lax.ppermute(part, 'x', [(i, (i + shift) % nx) for i in range(nx)])  10.5 us
    ppermute x3, waiting for transfers between devices, local(): arriving = lax.ppermute(block, 'z', relay)  10.3 us
    ppermute x3, waiting for transfers between devices, local(): part = lax.ppermute(part, 'x', [(i, (i + shift) % nx) for i in range(nx)])  8.99 us
    all_to_all x1, starting transfers between devices, local(): summed = lax.all_to_all(summed, ('y', 'c'), 0, 0, tiled=True)  6.17 us
  transfers between devices with their start and end apart: 12, of which 12 were waited for; matrix products, arithmetic and copies ran while one was open for 6% of the time, Pallas kernels for 0%

profile of v10, /device:TPU:1, one launch (start us, length us, event | category | flops | bytes accessed | tf_op | source)
XLA Modules:
  0.0 150.3 jit_solution(8930919923779015925)
XLA Ops:
  7.2 1.2 reshape.339
  8.3 1.0 reshape.308
  9.3 0.7 convert_element_type.67
  10.4 0.8 copy.25
  11.2 5.0 %all-to-all-start = ((bf16[145,3,4,1,128]{4,0,1,3,2:T(8,128)(2,1)}), bf16[145,3,4,1,128]{4,0,1,3,2:T(8,128)(2,1)S(1)}, u32[]{:S(2)}, u32[]{:S(2)}) async-start(bf16[145,3,4,1,128]{4,0,1,3,2:T(8,128)(2,1)} %copy.25), calls=%async_computation | async-start | bytes 933888 | tf_op jit(solution)/shard_map/all_to_all | solution.py:30
  16.2 0.7 all-gather.3.cloned.1.call-update
  17.0 5.9 %all-to-all-done = bf16[145,3,4,1,128]{4,0,1,3,2:T(8,128)(2,1)S(1)} async-done(((bf16[145,3,4,1,128]{4,0,1,3,2:T(8,128)(2,1)}), bf16[145,3,4,1,128]{4,0,1,3,2:T(8,128)(2,1)S(1)}, u32[]{:S(2)}, u32[]{:S(2)}) %all-to-all-start) | async-done | bytes 445472 | tf_op jit(solution)/shard_map/all_to_all | solution.py:30
  23.1 0.5 fusion.78
  24.0 4.6 %collective-permute-start = (bf16[579,2,1,128]{3,0,1,2:T(8,128)(2,1)S(1)}, bf16[579,2,1,128]{3,0,1,2:T(8,128)(2,1)S(1)}, u32[]{:S(2)}, u32[]{:S(2)}) collective-permute-start(bf16[579,2,1,128]{3,0,1,2:T(8,128)(2,1)S(1)} %pad_maximum_fusion.1), channel_id=1, source_target_pairs={{0,32},{32,64},{64,96},{96,128},{128,160},{160,192},{192,224},{224... | collective-permute-start | bytes 889352 | tf_op jit(solution)/shard_map/ppermute | solution.py:76
  28.6 0.6 fusion.1
  29.2 3.1 %collective-permute-done = bf16[579,2,1,128]{3,0,1,2:T(8,128)(2,1)S(1)} collective-permute-done((bf16[579,2,1,128]{3,0,1,2:T(8,128)(2,1)S(1)}, bf16[579,2,1,128]{3,0,1,2:T(8,128)(2,1)S(1)}, u32[]{:S(2)}, u32[]{:S(2)}) %collective-permute-start) | collective-permute-done | bytes 296480 | tf_op jit(solution)/shard_map/ppermute | solution.py:76
  32.3 4.1 %collective-permute-start.1 = (bf16[579,2,1,128]{3,0,1,2:T(8,128)(2,1)S(1)}, bf16[579,2,1,128]{3,0,1,2:T(8,128)(2,1)S(1)}, u32[]{:S(2)}, u32[]{:S(2)}) collective-permute-start(bf16[579,2,1,128]{3,0,1,2:T(8,128)(2,1)S(1)} %collective-permute-done), channel_id=1, source_target_pairs={{0,32},{32,64},{64,96},{96,128},{128,160},{160,192},{192,224},{224... | collective-permute-start | bytes 889352 | tf_op jit(solution)/shard_map/ppermute | solution.py:79
  36.4 0.5 fusion.79
  37.5 0.6 multiply_add_fusion.1
  38.1 1.9 %collective-permute-done.1 = bf16[579,2,1,128]{3,0,1,2:T(8,128)(2,1)S(1)} collective-permute-done((bf16[579,2,1,128]{3,0,1,2:T(8,128)(2,1)S(1)}, bf16[579,2,1,128]{3,0,1,2:T(8,128)(2,1)S(1)}, u32[]{:S(2)}, u32[]{:S(2)}) %collective-permute-start.1) | collective-permute-done | bytes 296480 | tf_op jit(solution)/shard_map/ppermute | solution.py:79
  40.0 4.1 %collective-permute-start.2 = (bf16[579,2,1,128]{3,0,1,2:T(8,128)(2,1)S(1)}, bf16[579,2,1,128]{3,0,1,2:T(8,128)(2,1)S(1)}, u32[]{:S(2)}, u32[]{:S(2)}) collective-permute-start(bf16[579,2,1,128]{3,0,1,2:T(8,128)(2,1)S(1)} %collective-permute-done.1), channel_id=1, source_target_pairs={{0,32},{32,64},{64,96},{96,128},{128,160},{160,192},{192,224},{224... | collective-permute-start | bytes 889352 | tf_op jit(solution)/shard_map/ppermute | solution.py:79
  44.2 0.5 fusion.80
  44.8 0.5 fusion.8
  45.3 0.6 multiply_add_fusion
  45.9 4.0 %collective-permute-done.2 = bf16[579,2,1,128]{3,0,1,2:T(8,128)(2,1)S(1)} collective-permute-done((bf16[579,2,1,128]{3,0,1,2:T(8,128)(2,1)S(1)}, bf16[579,2,1,128]{3,0,1,2:T(8,128)(2,1)S(1)}, u32[]{:S(2)}, u32[]{:S(2)}) %collective-permute-start.2) | collective-permute-done | bytes 296480 | tf_op jit(solution)/shard_map/ppermute | solution.py:79
  49.9 7.0 %collective-permute-start.3 = (bf16[579,2,1,128]{3,0,1,2:T(8,128)(2,1)S(1)}, bf16[579,2,1,128]{3,0,1,2:T(8,128)(2,1)S(1)}, u32[]{:S(2)}, u32[]{:S(2)}) collective-permute-start(bf16[579,2,1,128]{3,0,1,2:T(8,128)(2,1)S(1)} %collective-permute-done.2), channel_id=1, source_target_pairs={{0,32},{32,64},{64,96},{96,128},{128,160},{160,192},{192,224},{224... | collective-permute-start | bytes 889352 | tf_op jit(solution)/shard_map/ppermute | solution.py:79
  56.9 0.5 fusion.82
  57.4 4.3 %collective-permute-done.3 = bf16[579,2,1,128]{3,0,1,2:T(8,128)(2,1)S(1)} collective-permute-done((bf16[579,2,1,128]{3,0,1,2:T(8,128)(2,1)S(1)}, bf16[579,2,1,128]{3,0,1,2:T(8,128)(2,1)S(1)}, u32[]{:S(2)}, u32[]{:S(2)}) %collective-permute-start.3) | collective-permute-done | bytes 296480 | tf_op jit(solution)/shard_map/ppermute | solution.py:79
  61.8 0.5 fusion.81
  62.4 0.9 fusion.9
  63.4 0.6 convolution_bitcast_fusion.1
  64.0 0.8 fusion.4
  64.8 10.6 %all-gather = bf16[1,576,512]{2,1,0:T(8,128)(2,1)S(1)} all-gather(bf16[1,576,128]{2,1,0:T(8,128)(2,1)S(1)} %fusion.4), channel_id=2, replica_groups=mesh['z'=16,'y'=4,'x'=4,'c'=2] {'y'}, dimensions={2}, use_global_device_ids=true | all-gather | bytes 737280 | tf_op jit(solution)/shard_map/all_gather | solution.py:89
  75.4 10.8 %collective-permute-start.4 = (bf16[576,512]{1,0:T(8,128)(2,1)S(1)}, bf16[576,512]{1,0:T(8,128)(2,1)S(1)}, u32[]{:S(2)}, u32[]{:S(2)}) collective-permute-start(bf16[576,512]{1,0:T(8,128)(2,1)S(1)} %bitcast.124), channel_id=1, source_target_pairs={{0,1},{1,0},{2,3},{3,2},{4,5},{5,4},{6,7},{7,6},{8,9},{9,8},{10,11... | collective-permute-start | bytes 1769480 | tf_op jit(solution)/shard_map/ppermute | solution.py:90
  86.2 1.6 %collective-permute-done.4 = bf16[576,512]{1,0:T(8,128)(2,1)S(1)} collective-permute-done((bf16[576,512]{1,0:T(8,128)(2,1)S(1)}, bf16[576,512]{1,0:T(8,128)(2,1)S(1)}, u32[]{:S(2)}, u32[]{:S(2)}) %collective-permute-start.4) | collective-permute-done | bytes 589856 | tf_op jit(solution)/shard_map/ppermute | solution.py:90
  87.8 2.6 %all-gather.3.cloned.1.call-done = bf16[512,1792]{0,1:T(8,128)(2,1)} async-done(((bf16[512,112]{0,1:T(8,128)(2,1)}), bf16[512,1792]{0,1:T(8,128)(2,1)}) %all-gather.3.cloned.1.call-update) | async-done | bytes 1835024 | tf_op jit(solution)/shard_map/all_gather | solution.py:21
  90.4 2.5 %constant_dynamic-slice_fusion = (bf16[512,8,1,112]{0,3,2,1:T(8,128)(2,1)S(1)}, bf16[512,8,112]{0,2,1:T(8,128)(2,1)}) fusion(bf16[512,8,2,112]{0,3,2,1:T(8,128)(2,1)} %bitcast.126, s32[]{:T(128)S(6)} %select_n.86, s32[]{:T(128)S(6)} %select_n.87), kind=kLoop, calls=%fused_computation.109 | loop fusion | bytes 3670024 | tf_op jit(solution)/shard_map/jit(dynamic_index_in_dim)/dynamic_slice | solution.py:96
  92.9 10.7 %collective-permute-start.5 = (bf16[512,8,112]{0,2,1:T(8,128)(2,1)}, bf16[512,8,112]{0,2,1:T(8,128)(2,1)S(1)}, u32[]{:S(2)}, u32[]{:S(2)}) collective-permute-start(bf16[512,8,112]{0,2,1:T(8,128)(2,1)} %get-tuple-element.77), channel_id=1, source_target_pairs={{0,1},{1,0},{2,3},{3,2},{4,5},{5,4},{6,7},{7,6},{8,9},{9,8},{10,11... | collective-permute-start | bytes 2752520 | tf_op jit(solution)/shard_map/ppermute | solution.py:97
  103.7 2.1 %collective-permute-done.5 = bf16[512,8,112]{0,2,1:T(8,128)(2,1)S(1)} collective-permute-done((bf16[512,8,112]{0,2,1:T(8,128)(2,1)}, bf16[512,8,112]{0,2,1:T(8,128)(2,1)S(1)}, u32[]{:S(2)}, u32[]{:S(2)}) %collective-permute-start.5) | collective-permute-done | bytes 917536 | tf_op jit(solution)/shard_map/ppermute | solution.py:97
  105.7 0.8 fusion.83
  106.5 0.8 add_convert_fusion
  107.4 1.1 copy.33
  108.6 3.1 %collective-permute-start.6 = (bf16[576,224]{0,1:T(8,128)(2,1)S(1)}, bf16[576,224]{0,1:T(8,128)(2,1)S(1)}, u32[]{:S(2)}, u32[]{:S(2)}) collective-permute-start(bf16[576,224]{0,1:T(8,128)(2,1)S(1)} %get-tuple-element.78), channel_id=1, source_target_pairs={{0,2},{2,4},{4,6},{6,0},{1,3},{3,5},{5,7},{7,1},{8,10},{10,12},{12... | collective-permute-start | bytes 774152 | tf_op jit(solution)/shard_map/ppermute | solution.py:112
  111.7 4.6 %collective-permute-start.7 = (bf16[576,224]{0,1:T(8,128)(2,1)S(1)}, bf16[576,224]{0,1:T(8,128)(2,1)S(1)}, u32[]{:S(2)}, u32[]{:S(2)}) collective-permute-start(bf16[576,224]{0,1:T(8,128)(2,1)S(1)} %get-tuple-element.80), channel_id=1, source_target_pairs={{0,4},{2,6},{4,0},{6,2},{1,5},{3,7},{5,1},{7,3},{8,12},{10,14},{12... | collective-permute-start | bytes 774152 | tf_op jit(solution)/shard_map/ppermute | solution.py:112
  116.3 2.8 %collective-permute-start.8 = (bf16[576,224]{0,1:T(8,128)(2,1)S(1)}, bf16[576,224]{0,1:T(8,128)(2,1)S(1)}, u32[]{:S(2)}, u32[]{:S(2)}) collective-permute-start(bf16[576,224]{0,1:T(8,128)(2,1)S(1)} %get-tuple-element.79), channel_id=1, source_target_pairs={{0,6},{2,0},{4,2},{6,4},{1,7},{3,1},{5,3},{7,5},{8,14},{10,8},{12,... | collective-permute-start | bytes 774152 | tf_op jit(solution)/shard_map/ppermute | solution.py:112
  119.1 0.7 collective-permute-done.6
  119.8 7.3 %collective-permute-done.7 = bf16[576,224]{0,1:T(8,128)(2,1)S(1)} collective-permute-done((bf16[576,224]{0,1:T(8,128)(2,1)S(1)}, bf16[576,224]{0,1:T(8,128)(2,1)S(1)}, u32[]{:S(2)}, u32[]{:S(2)}) %collective-permute-start.7) | collective-permute-done | bytes 258080 | tf_op jit(solution)/shard_map/ppermute | solution.py:112
  127.1 1.1 collective-permute-done.8
  128.6 0.7 copy.35
  129.4 6.2 %all-to-all-start.1 = ((bf16[8,144,112]{2,1,0:T(8,128)(2,1)}), bf16[8,144,112]{2,1,0:T(8,128)(2,1)S(1)}, u32[]{:S(2)}, u32[]{:S(2)}) async-start(bf16[8,144,112]{2,1,0:T(8,128)(2,1)} %bitcast.36), calls=%async_computation.1 | async-start | bytes 589824 | tf_op jit(solution)/shard_map/all_to_all | solution.py:116
  135.5 0.8 copy.37
  136.3 6.1 %all-to-all-done.1 = bf16[8,144,112]{2,1,0:T(8,128)(2,1)S(1)} async-done(((bf16[8,144,112]{2,1,0:T(8,128)(2,1)}), bf16[8,144,112]{2,1,0:T(8,128)(2,1)S(1)}, u32[]{:S(2)}, u32[]{:S(2)}) %all-to-all-start.1) | async-done | bytes 258080 | tf_op jit(solution)/shard_map/all_to_all | solution.py:116
  142.5 0.9 reshape.336
  (49 shorter events, 2.5 us)
Async XLA Ops:
  11.2 11.6 %all-to-all-start = ((bf16[145,3,4,1,128]{4,0,1,3,2:T(8,128)(2,1)}), bf16[145,3,4,1,128]{4,0,1,3,2:T(8,128)(2,1)S(1)}, u32[]{:S(2)}, u32[]{:S(2)}) async-start(bf16[145,3,4,1,128]{4,0,1,3,2:T(8,128)(2,1)} %copy.25), calls=%async_computation | async-start | bytes 933888 | tf_op jit(solution)/shard_map/all_to_all | solution.py:30
  16.2 74.2 %all-gather.3.cloned.1.call-start = ((), (), s32[]{:S(2)}) async-start(), calls=%async_computation.2 | async-start | bytes 1949696 | tf_op jit(solution)/shard_map/all_gather | solution.py:21
  24.0 8.3 %collective-permute-start = (bf16[579,2,1,128]{3,0,1,2:T(8,128)(2,1)S(1)}, bf16[579,2,1,128]{3,0,1,2:T(8,128)(2,1)S(1)}, u32[]{:S(2)}, u32[]{:S(2)}) collective-permute-start(bf16[579,2,1,128]{3,0,1,2:T(8,128)(2,1)S(1)} %pad_maximum_fusion.1), channel_id=1, source_target_pairs={{0,32},{32,64},{64,96},{96,128},{128,160},{160,192},{192,224},{224... | collective-permute-start | bytes 889352 | tf_op jit(solution)/shard_map/ppermute | solution.py:76
  32.3 7.8 %collective-permute-start.1 = (bf16[579,2,1,128]{3,0,1,2:T(8,128)(2,1)S(1)}, bf16[579,2,1,128]{3,0,1,2:T(8,128)(2,1)S(1)}, u32[]{:S(2)}, u32[]{:S(2)}) collective-permute-start(bf16[579,2,1,128]{3,0,1,2:T(8,128)(2,1)S(1)} %collective-permute-done), channel_id=1, source_target_pairs={{0,32},{32,64},{64,96},{96,128},{128,160},{160,192},{192,224},{224... | collective-permute-start | bytes 889352 | tf_op jit(solution)/shard_map/ppermute | solution.py:79
  40.0 9.9 %collective-permute-start.2 = (bf16[579,2,1,128]{3,0,1,2:T(8,128)(2,1)S(1)}, bf16[579,2,1,128]{3,0,1,2:T(8,128)(2,1)S(1)}, u32[]{:S(2)}, u32[]{:S(2)}) collective-permute-start(bf16[579,2,1,128]{3,0,1,2:T(8,128)(2,1)S(1)} %collective-permute-done.1), channel_id=1, source_target_pairs={{0,32},{32,64},{64,96},{96,128},{128,160},{160,192},{192,224},{224... | collective-permute-start | bytes 889352 | tf_op jit(solution)/shard_map/ppermute | solution.py:79
  49.9 11.9 %collective-permute-start.3 = (bf16[579,2,1,128]{3,0,1,2:T(8,128)(2,1)S(1)}, bf16[579,2,1,128]{3,0,1,2:T(8,128)(2,1)S(1)}, u32[]{:S(2)}, u32[]{:S(2)}) collective-permute-start(bf16[579,2,1,128]{3,0,1,2:T(8,128)(2,1)S(1)} %collective-permute-done.2), channel_id=1, source_target_pairs={{0,32},{32,64},{64,96},{96,128},{128,160},{160,192},{192,224},{224... | collective-permute-start | bytes 889352 | tf_op jit(solution)/shard_map/ppermute | solution.py:79
  75.4 12.4 %collective-permute-start.4 = (bf16[576,512]{1,0:T(8,128)(2,1)S(1)}, bf16[576,512]{1,0:T(8,128)(2,1)S(1)}, u32[]{:S(2)}, u32[]{:S(2)}) collective-permute-start(bf16[576,512]{1,0:T(8,128)(2,1)S(1)} %bitcast.124), channel_id=1, source_target_pairs={{0,1},{1,0},{2,3},{3,2},{4,5},{5,4},{6,7},{7,6},{8,9},{9,8},{10,11... | collective-permute-start | bytes 1769480 | tf_op jit(solution)/shard_map/ppermute | solution.py:90
  92.9 12.8 %collective-permute-start.5 = (bf16[512,8,112]{0,2,1:T(8,128)(2,1)}, bf16[512,8,112]{0,2,1:T(8,128)(2,1)S(1)}, u32[]{:S(2)}, u32[]{:S(2)}) collective-permute-start(bf16[512,8,112]{0,2,1:T(8,128)(2,1)} %get-tuple-element.77), channel_id=1, source_target_pairs={{0,1},{1,0},{2,3},{3,2},{4,5},{5,4},{6,7},{7,6},{8,9},{9,8},{10,11... | collective-permute-start | bytes 2752520 | tf_op jit(solution)/shard_map/ppermute | solution.py:97
  108.6 11.2 %collective-permute-start.6 = (bf16[576,224]{0,1:T(8,128)(2,1)S(1)}, bf16[576,224]{0,1:T(8,128)(2,1)S(1)}, u32[]{:S(2)}, u32[]{:S(2)}) collective-permute-start(bf16[576,224]{0,1:T(8,128)(2,1)S(1)} %get-tuple-element.78), channel_id=1, source_target_pairs={{0,2},{2,4},{4,6},{6,0},{1,3},{3,5},{5,7},{7,1},{8,10},{10,12},{12... | collective-permute-start | bytes 774152 | tf_op jit(solution)/shard_map/ppermute | solution.py:112
  111.7 15.4 %collective-permute-start.7 = (bf16[576,224]{0,1:T(8,128)(2,1)S(1)}, bf16[576,224]{0,1:T(8,128)(2,1)S(1)}, u32[]{:S(2)}, u32[]{:S(2)}) collective-permute-start(bf16[576,224]{0,1:T(8,128)(2,1)S(1)} %get-tuple-element.80), channel_id=1, source_target_pairs={{0,4},{2,6},{4,0},{6,2},{1,5},{3,7},{5,1},{7,3},{8,12},{10,14},{12... | collective-permute-start | bytes 774152 | tf_op jit(solution)/shard_map/ppermute | solution.py:112
  116.3 11.8 %collective-permute-start.8 = (bf16[576,224]{0,1:T(8,128)(2,1)S(1)}, bf16[576,224]{0,1:T(8,128)(2,1)S(1)}, u32[]{:S(2)}, u32[]{:S(2)}) collective-permute-start(bf16[576,224]{0,1:T(8,128)(2,1)S(1)} %get-tuple-element.79), channel_id=1, source_target_pairs={{0,6},{2,0},{4,2},{6,4},{1,7},{3,1},{5,3},{7,5},{8,14},{10,8},{12,... | collective-permute-start | bytes 774152 | tf_op jit(solution)/shard_map/ppermute | solution.py:112
  129.4 13.0 %all-to-all-start.1 = ((bf16[8,144,112]{2,1,0:T(8,128)(2,1)}), bf16[8,144,112]{2,1,0:T(8,128)(2,1)S(1)}, u32[]{:S(2)}, u32[]{:S(2)}) async-start(bf16[8,144,112]{2,1,0:T(8,128)(2,1)} %bitcast.36), calls=%async_computation.1 | async-start | bytes 589824 | tf_op jit(solution)/shard_map/all_to_all | solution.py:116
Sparse Core Ops, SparseCore 0:
  19.1 71.2 all-gather.2

commit v11 on v10

--- a/solution.py
+++ b/solution.py
@@ -104,17 +104,11 @@
         other_attended, other_weight, preferred_element_type=jnp.float32
     )
     nx = lax.axis_size("x")
-    x = lax.axis_index("x")
-    quarters = partial_value.astype(jnp.bfloat16).reshape(level, nx, -1)
-    summed = lax.dynamic_index_in_dim(quarters, x, axis=1, keepdims=False).astype(jnp.float32)
-    for shift in range(1, nx):
-        part = lax.dynamic_index_in_dim(quarters, (x + shift) % nx, axis=1, keepdims=False)
-        part = lax.ppermute(part, "x", [(i, (i + shift) % nx) for i in range(nx)])
-        summed = summed + part.astype(jnp.float32)
-    summed = summed.astype(jnp.bfloat16)
-    summed = summed.reshape(NY, rows, 2, chunk).transpose(0, 2, 1, 3).reshape(2 * NY, rows, chunk)
-    summed = lax.all_to_all(summed, ("y", "c"), 0, 0, tiled=True)
-    hidden_states = summed.reshape(NY, 2, rows, chunk).transpose(2, 1, 0, 3).reshape(rows, 2 * NY * chunk)
+    pieces = partial_value.astype(jnp.bfloat16).reshape(NY, rows, nx * 2, chunk)
+    pieces = pieces.transpose(0, 2, 1, 3).reshape(NY * nx * 2, rows, chunk)
+    pieces = lax.all_to_all(pieces, ("y", "x", "c"), 0, 0, tiled=True)
+    summed = pieces.reshape(NY, nx, 2, rows, chunk).astype(jnp.float32).sum(axis=1)
+    hidden_states = summed.astype(jnp.bfloat16).transpose(2, 1, 0, 3).reshape(rows, 2 * NY * chunk)
 
     head_major = keys_values.reshape(rows, 2, heads, HD).transpose(1, 2, 0, 3)
     return (hidden_states, head_major)

time: 152 us -> 143 us (0.941)
  starting transfers between devices: 62.9 us -> 54.1 us
  waiting for transfers between devices: 41.3 us -> 43 us
    all_to_all x1, waiting for transfers between devices: 6.06 us -> 16.9 us  [local(): pieces = lax.all_to_all(pieces, ('y', 'x', 'c'), 0, 0, tiled=True)]
    ppermute x3 -> x0, starting transfers between devices: 10.5 us -> none  [local(): part = lax.ppermute(part, 'x', [(i, (i + shift) % nx) for i in range(nx)])]
    ppermute x3 -> x0, waiting for transfers between devices: 8.99 us -> none  [local(): part = lax.ppermute(part, 'x', [(i, (i + shift) % nx) for i in range(nx)])]
    reshape x2 -> x3, local copies, waits for them, and re-layouts: 1.12 us -> 3.5 us  [the longest x2 2.55 us: local(): pieces = partial_value.astype(jnp.bfloat16).reshape(NY, rows, nx * 2, chunk)]
    all_to_all x1, starting transfers between devices: 6.17 us -> 7.87 us  [local(): pieces = lax.all_to_all(pieces, ('y', 'x', 'c'), 0, 0, tiled=True)]
  transfers between devices with their start and end apart: 12 -> 9, of which waited for: 12 -> 9; matrix products, arithmetic and copies ran while one was open for 6% -> 7% of each run, Pallas kernels for 0% -> 0%
where the time goes in v11:
time: 143 us
  starting transfers between devices  54.1 us (38%)
  waiting for transfers between devices  43 us (30%)
  between operations  14.4 us (10%)
  blocking collectives  10.6 us (7%)
  local copies, waits for them, and re-layouts  9.25 us (6%)
  matrix products  7.42 us (5%)
  other arithmetic  3.8 us (3%)
    all_to_all x1, waiting for transfers between devices, local(): pieces = lax.all_to_all(pieces, ('y', 'x', 'c'), 0, 0, tiled=True)  16.9 us
    ppermute x3, starting transfers between devices, local(): arriving = lax.ppermute(block, 'z', relay)  15.2 us
    ppermute x1, starting transfers between devices, local(): other_attended = lax.ppermute(own_attended, 'c', swap)  10.8 us
    ppermute x1, starting transfers between devices, local(): lax.ppermute(lax.dynamic_index_in_dim(weight_cols, 1 - c, axis=2, keepdim...  10.7 us
    all_gather x1, blocking collectives, local(): own_attended = lax.all_gather(attended, 'y', axis=1, tiled=True)  10.6 us
    ppermute x3, waiting for transfers between devices, local(): arriving = lax.ppermute(block, 'z', relay)  10.3 us
    all_to_all x1, starting transfers between devices, local(): pieces = lax.all_to_all(pieces, ('y', 'x', 'c'), 0, 0, tiled=True)  7.87 us
    all_to_all x1, waiting for transfers between devices, local(): lax.all_to_all(packed, 'y', 2, 0, tiled=True)  5.89 us
  transfers between devices with their start and end apart: 9, of which 9 were waited for; matrix products, arithmetic and copies ran while one was open for 7% of the time, Pallas kernels for 0%

profile of v11, /device:TPU:1, one launch (start us, length us, event | category | flops | bytes accessed | tf_op | source)
XLA Modules:
  0.0 142.6 jit_solution(8503918672396820640)
XLA Ops:
  7.2 1.2 reshape.332
  8.3 1.0 reshape.303
  9.3 0.7 convert_element_type.51
  10.0 0.2 maximum_bitcast_fusion
  10.2 0.2 pad_maximum_fusion
  10.4 0.8 copy.31
  11.2 5.0 %all-to-all-start = ((bf16[145,3,4,1,128]{4,0,1,3,2:T(8,128)(2,1)}), bf16[145,3,4,1,128]{4,0,1,3,2:T(8,128)(2,1)S(1)}, u32[]{:S(2)}, u32[]{:S(2)}) async-start(bf16[145,3,4,1,128]{4,0,1,3,2:T(8,128)(2,1)} %copy.31), calls=%async_computation | async-start | bytes 933888 | tf_op jit(solution)/shard_map/all_to_all | solution.py:30
  16.2 0.7 all-gather.3.cloned.1.call-update
  17.0 5.9 %all-to-all-done = bf16[145,3,4,1,128]{4,0,1,3,2:T(8,128)(2,1)S(1)} async-done(((bf16[145,3,4,1,128]{4,0,1,3,2:T(8,128)(2,1)}), bf16[145,3,4,1,128]{4,0,1,3,2:T(8,128)(2,1)S(1)}, u32[]{:S(2)}, u32[]{:S(2)}) %all-to-all-start) | async-done | bytes 445472 | tf_op jit(solution)/shard_map/all_to_all | solution.py:30
  23.1 0.5 fusion.75
  23.6 0.3 fusion.14
  24.0 4.6 %collective-permute-start = (bf16[579,2,1,128]{3,0,1,2:T(8,128)(2,1)S(1)}, bf16[579,2,1,128]{3,0,1,2:T(8,128)(2,1)S(1)}, u32[]{:S(2)}, u32[]{:S(2)}) collective-permute-start(bf16[579,2,1,128]{3,0,1,2:T(8,128)(2,1)S(1)} %pad_maximum_fusion.1), channel_id=1, source_target_pairs={{0,32},{32,64},{64,96},{96,128},{128,160},{160,192},{192,224},{224... | collective-permute-start | bytes 889352 | tf_op jit(solution)/shard_map/ppermute | solution.py:76
  28.6 0.6 fusion.1
  29.2 3.1 %collective-permute-done = bf16[579,2,1,128]{3,0,1,2:T(8,128)(2,1)S(1)} collective-permute-done((bf16[579,2,1,128]{3,0,1,2:T(8,128)(2,1)S(1)}, bf16[579,2,1,128]{3,0,1,2:T(8,128)(2,1)S(1)}, u32[]{:S(2)}, u32[]{:S(2)}) %collective-permute-start) | collective-permute-done | bytes 296480 | tf_op jit(solution)/shard_map/ppermute | solution.py:76
  32.3 4.1 %collective-permute-start.1 = (bf16[579,2,1,128]{3,0,1,2:T(8,128)(2,1)S(1)}, bf16[579,2,1,128]{3,0,1,2:T(8,128)(2,1)S(1)}, u32[]{:S(2)}, u32[]{:S(2)}) collective-permute-start(bf16[579,2,1,128]{3,0,1,2:T(8,128)(2,1)S(1)} %collective-permute-done), channel_id=1, source_target_pairs={{0,32},{32,64},{64,96},{96,128},{128,160},{160,192},{192,224},{224... | collective-permute-start | bytes 889352 | tf_op jit(solution)/shard_map/ppermute | solution.py:79
  36.4 0.5 fusion.76
  37.0 0.5 fusion.6
  37.5 0.6 multiply_add_fusion.1
  38.1 1.9 %collective-permute-done.1 = bf16[579,2,1,128]{3,0,1,2:T(8,128)(2,1)S(1)} collective-permute-done((bf16[579,2,1,128]{3,0,1,2:T(8,128)(2,1)S(1)}, bf16[579,2,1,128]{3,0,1,2:T(8,128)(2,1)S(1)}, u32[]{:S(2)}, u32[]{:S(2)}) %collective-permute-start.1) | collective-permute-done | bytes 296480 | tf_op jit(solution)/shard_map/ppermute | solution.py:79
  40.0 4.1 %collective-permute-start.2 = (bf16[579,2,1,128]{3,0,1,2:T(8,128)(2,1)S(1)}, bf16[579,2,1,128]{3,0,1,2:T(8,128)(2,1)S(1)}, u32[]{:S(2)}, u32[]{:S(2)}) collective-permute-start(bf16[579,2,1,128]{3,0,1,2:T(8,128)(2,1)S(1)} %collective-permute-done.1), channel_id=1, source_target_pairs={{0,32},{32,64},{64,96},{96,128},{128,160},{160,192},{192,224},{224... | collective-permute-start | bytes 889352 | tf_op jit(solution)/shard_map/ppermute | solution.py:79
  44.2 0.5 fusion.77
  44.8 0.5 fusion.8
  45.3 0.6 multiply_add_fusion
  45.9 4.0 %collective-permute-done.2 = bf16[579,2,1,128]{3,0,1,2:T(8,128)(2,1)S(1)} collective-permute-done((bf16[579,2,1,128]{3,0,1,2:T(8,128)(2,1)S(1)}, bf16[579,2,1,128]{3,0,1,2:T(8,128)(2,1)S(1)}, u32[]{:S(2)}, u32[]{:S(2)}) %collective-permute-start.2) | collective-permute-done | bytes 296480 | tf_op jit(solution)/shard_map/ppermute | solution.py:79
  49.9 7.0 %collective-permute-start.3 = (bf16[579,2,1,128]{3,0,1,2:T(8,128)(2,1)S(1)}, bf16[579,2,1,128]{3,0,1,2:T(8,128)(2,1)S(1)}, u32[]{:S(2)}, u32[]{:S(2)}) collective-permute-start(bf16[579,2,1,128]{3,0,1,2:T(8,128)(2,1)S(1)} %collective-permute-done.2), channel_id=1, source_target_pairs={{0,32},{32,64},{64,96},{96,128},{128,160},{160,192},{192,224},{224... | collective-permute-start | bytes 889352 | tf_op jit(solution)/shard_map/ppermute | solution.py:79
  56.9 0.5 fusion.79
  57.4 4.3 %collective-permute-done.3 = bf16[579,2,1,128]{3,0,1,2:T(8,128)(2,1)S(1)} collective-permute-done((bf16[579,2,1,128]{3,0,1,2:T(8,128)(2,1)S(1)}, bf16[579,2,1,128]{3,0,1,2:T(8,128)(2,1)S(1)}, u32[]{:S(2)}, u32[]{:S(2)}) %collective-permute-start.3) | collective-permute-done | bytes 296480 | tf_op jit(solution)/shard_map/ppermute | solution.py:79
  61.8 0.5 fusion.78
  62.4 0.9 fusion.9
  63.4 0.6 convolution_bitcast_fusion.1
  64.0 0.8 fusion.4
  64.8 10.6 %all-gather = bf16[1,576,512]{2,1,0:T(8,128)(2,1)S(1)} all-gather(bf16[1,576,128]{2,1,0:T(8,128)(2,1)S(1)} %fusion.4), channel_id=2, replica_groups=mesh['z'=16,'y'=4,'x'=4,'c'=2] {'y'}, dimensions={2}, use_global_device_ids=true | all-gather | bytes 737280 | tf_op jit(solution)/shard_map/all_gather | solution.py:89
  75.4 10.8 %collective-permute-start.4 = (bf16[576,512]{1,0:T(8,128)(2,1)S(1)}, bf16[576,512]{1,0:T(8,128)(2,1)S(1)}, u32[]{:S(2)}, u32[]{:S(2)}) collective-permute-start(bf16[576,512]{1,0:T(8,128)(2,1)S(1)} %bitcast.113), channel_id=1, source_target_pairs={{0,1},{1,0},{2,3},{3,2},{4,5},{5,4},{6,7},{7,6},{8,9},{9,8},{10,11... | collective-permute-start | bytes 1769480 | tf_op jit(solution)/shard_map/ppermute | solution.py:90
  86.2 1.6 %collective-permute-done.4 = bf16[576,512]{1,0:T(8,128)(2,1)S(1)} collective-permute-done((bf16[576,512]{1,0:T(8,128)(2,1)S(1)}, bf16[576,512]{1,0:T(8,128)(2,1)S(1)}, u32[]{:S(2)}, u32[]{:S(2)}) %collective-permute-start.4) | collective-permute-done | bytes 589856 | tf_op jit(solution)/shard_map/ppermute | solution.py:90
  87.8 2.6 %all-gather.3.cloned.1.call-done = bf16[512,1792]{0,1:T(8,128)(2,1)} async-done(((bf16[512,112]{0,1:T(8,128)(2,1)}), bf16[512,1792]{0,1:T(8,128)(2,1)}) %all-gather.3.cloned.1.call-update) | async-done | bytes 1835024 | tf_op jit(solution)/shard_map/all_gather | solution.py:21
  90.4 1.6 %constant_dynamic-slice_fusion = (bf16[512,8,1,112]{0,3,2,1:T(8,128)(2,1)S(1)}, bf16[512,8,112]{0,2,1:T(8,128)(2,1)S(1)}) fusion(bf16[512,8,2,112]{0,3,2,1:T(8,128)(2,1)} %bitcast.115, s32[]{:T(128)S(6)} %select_n.58, s32[]{:T(128)S(6)} %select_n.59), kind=kLoop, calls=%fused_computation.104 | loop fusion | bytes 3670024 | tf_op jit(solution)/shard_map/jit(dynamic_index_in_dim)/dynamic_slice | solution.py:96
  92.0 10.7 %collective-permute-start.5 = (bf16[512,8,112]{0,2,1:T(8,128)(2,1)S(1)}, bf16[512,8,112]{0,2,1:T(8,128)(2,1)S(1)}, u32[]{:S(2)}, u32[]{:S(2)}) collective-permute-start(bf16[512,8,112]{0,2,1:T(8,128)(2,1)S(1)} %get-tuple-element.79), channel_id=1, source_target_pairs={{0,1},{1,0},{2,3},{3,2},{4,5},{5,4},{6,7},{7,6},{8,9},{9,8},{10,11... | collective-permute-start | bytes 2752520 | tf_op jit(solution)/shard_map/ppermute | solution.py:97
  102.7 1.9 %collective-permute-done.5 = bf16[512,8,112]{0,2,1:T(8,128)(2,1)S(1)} collective-permute-done((bf16[512,8,112]{0,2,1:T(8,128)(2,1)S(1)}, bf16[512,8,112]{0,2,1:T(8,128)(2,1)S(1)}, u32[]{:S(2)}, u32[]{:S(2)}) %collective-permute-start.5) | collective-permute-done | bytes 917536 | tf_op jit(solution)/shard_map/ppermute | solution.py:97
  104.6 0.8 fusion.80
  105.4 0.8 add_convert_fusion
  106.2 1.4 reshape.327
  107.6 1.2 copy.39
  108.8 7.9 %all-to-all-start.1 = ((bf16[32,144,112]{2,1,0:T(8,128)(2,1)}), bf16[32,144,112]{2,1,0:T(8,128)(2,1)S(1)}, u32[]{:S(2)}, u32[]{:S(2)}) async-start(bf16[32,144,112]{2,1,0:T(8,128)(2,1)} %bitcast.31), calls=%async_computation.1 | async-start | bytes 2359296 | tf_op jit(solution)/shard_map/all_to_all | solution.py:109
  116.7 0.8 copy.41
  117.4 16.9 %all-to-all-done.1 = bf16[32,144,112]{2,1,0:T(8,128)(2,1)S(1)} async-done(((bf16[32,144,112]{2,1,0:T(8,128)(2,1)}), bf16[32,144,112]{2,1,0:T(8,128)(2,1)S(1)}, u32[]{:S(2)}, u32[]{:S(2)}) %all-to-all-start.1) | async-done | bytes 1032224 | tf_op jit(solution)/shard_map/all_to_all | solution.py:109
  134.4 0.3 reduce_sum.77
  134.6 0.2 copy.40
  134.8 0.9 reshape.330
  (40 shorter events, 0.5 us)
Async XLA Ops:
  11.2 11.6 %all-to-all-start = ((bf16[145,3,4,1,128]{4,0,1,3,2:T(8,128)(2,1)}), bf16[145,3,4,1,128]{4,0,1,3,2:T(8,128)(2,1)S(1)}, u32[]{:S(2)}, u32[]{:S(2)}) async-start(bf16[145,3,4,1,128]{4,0,1,3,2:T(8,128)(2,1)} %copy.31), calls=%async_computation | async-start | bytes 933888 | tf_op jit(solution)/shard_map/all_to_all | solution.py:30
  16.2 74.2 %all-gather.3.cloned.1.call-start = ((), (), s32[]{:S(2)}) async-start(), calls=%async_computation.2 | async-start | bytes 1949696 | tf_op jit(solution)/shard_map/all_gather | solution.py:21
  24.0 8.3 %collective-permute-start = (bf16[579,2,1,128]{3,0,1,2:T(8,128)(2,1)S(1)}, bf16[579,2,1,128]{3,0,1,2:T(8,128)(2,1)S(1)}, u32[]{:S(2)}, u32[]{:S(2)}) collective-permute-start(bf16[579,2,1,128]{3,0,1,2:T(8,128)(2,1)S(1)} %pad_maximum_fusion.1), channel_id=1, source_target_pairs={{0,32},{32,64},{64,96},{96,128},{128,160},{160,192},{192,224},{224... | collective-permute-start | bytes 889352 | tf_op jit(solution)/shard_map/ppermute | solution.py:76
  32.3 7.8 %collective-permute-start.1 = (bf16[579,2,1,128]{3,0,1,2:T(8,128)(2,1)S(1)}, bf16[579,2,1,128]{3,0,1,2:T(8,128)(2,1)S(1)}, u32[]{:S(2)}, u32[]{:S(2)}) collective-permute-start(bf16[579,2,1,128]{3,0,1,2:T(8,128)(2,1)S(1)} %collective-permute-done), channel_id=1, source_target_pairs={{0,32},{32,64},{64,96},{96,128},{128,160},{160,192},{192,224},{224... | collective-permute-start | bytes 889352 | tf_op jit(solution)/shard_map/ppermute | solution.py:79
  40.0 9.9 %collective-permute-start.2 = (bf16[579,2,1,128]{3,0,1,2:T(8,128)(2,1)S(1)}, bf16[579,2,1,128]{3,0,1,2:T(8,128)(2,1)S(1)}, u32[]{:S(2)}, u32[]{:S(2)}) collective-permute-start(bf16[579,2,1,128]{3,0,1,2:T(8,128)(2,1)S(1)} %collective-permute-done.1), channel_id=1, source_target_pairs={{0,32},{32,64},{64,96},{96,128},{128,160},{160,192},{192,224},{224... | collective-permute-start | bytes 889352 | tf_op jit(solution)/shard_map/ppermute | solution.py:79
  49.9 11.9 %collective-permute-start.3 = (bf16[579,2,1,128]{3,0,1,2:T(8,128)(2,1)S(1)}, bf16[579,2,1,128]{3,0,1,2:T(8,128)(2,1)S(1)}, u32[]{:S(2)}, u32[]{:S(2)}) collective-permute-start(bf16[579,2,1,128]{3,0,1,2:T(8,128)(2,1)S(1)} %collective-permute-done.2), channel_id=1, source_target_pairs={{0,32},{32,64},{64,96},{96,128},{128,160},{160,192},{192,224},{224... | collective-permute-start | bytes 889352 | tf_op jit(solution)/shard_map/ppermute | solution.py:79
  75.4 12.4 %collective-permute-start.4 = (bf16[576,512]{1,0:T(8,128)(2,1)S(1)}, bf16[576,512]{1,0:T(8,128)(2,1)S(1)}, u32[]{:S(2)}, u32[]{:S(2)}) collective-permute-start(bf16[576,512]{1,0:T(8,128)(2,1)S(1)} %bitcast.113), channel_id=1, source_target_pairs={{0,1},{1,0},{2,3},{3,2},{4,5},{5,4},{6,7},{7,6},{8,9},{9,8},{10,11... | collective-permute-start | bytes 1769480 | tf_op jit(solution)/shard_map/ppermute | solution.py:90
  92.0 12.6 %collective-permute-start.5 = (bf16[512,8,112]{0,2,1:T(8,128)(2,1)S(1)}, bf16[512,8,112]{0,2,1:T(8,128)(2,1)S(1)}, u32[]{:S(2)}, u32[]{:S(2)}) collective-permute-start(bf16[512,8,112]{0,2,1:T(8,128)(2,1)S(1)} %get-tuple-element.79), channel_id=1, source_target_pairs={{0,1},{1,0},{2,3},{3,2},{4,5},{5,4},{6,7},{7,6},{8,9},{9,8},{10,11... | collective-permute-start | bytes 2752520 | tf_op jit(solution)/shard_map/ppermute | solution.py:97
  108.8 25.6 %all-to-all-start.1 = ((bf16[32,144,112]{2,1,0:T(8,128)(2,1)}), bf16[32,144,112]{2,1,0:T(8,128)(2,1)S(1)}, u32[]{:S(2)}, u32[]{:S(2)}) async-start(bf16[32,144,112]{2,1,0:T(8,128)(2,1)} %bitcast.31), calls=%async_computation.1 | async-start | bytes 2359296 | tf_op jit(solution)/shard_map/all_to_all | solution.py:109
Sparse Core Ops, SparseCore 0:
  19.1 71.2 all-gather.2

commit v12 on v11

--- a/solution.py
+++ b/solution.py
@@ -18,7 +18,14 @@
     level = NY * rows
     span = min(4, nz - 1)
     score_scale = 1.0 / math.sqrt(HD)
-    weight_cols = lax.all_gather(out_weight, "z", axis=1, tiled=True)
+    half = out_weight.shape[1] // 2
+    weight_cols = jnp.concatenate(
+        [
+            lax.all_gather(out_weight[:, :half], "z", axis=1, tiled=True).reshape(-1, nz, half),
+            lax.all_gather(out_weight[:, half:], "z", axis=1, tiled=True).reshape(-1, nz, half),
+        ],
+        axis=2,
+    ).reshape(out_weight.shape[0], nz * 2 * half)
 
     hq = heads // NY
     packed = jnp.concatenate(

time: 143 us -> 185 us (1.29)
  blocking collectives: 10.6 us -> 72.9 us
  between operations: 14.4 us -> 1.01 us
  waiting for transfers between devices: 43 us -> 36 us
    all_gather x0 -> x2, blocking collectives: none -> 63 us  [the longest x1 36.4 us: local(): lax.all_gather(out_weight[:, :half], 'z', axis=1, tiled=True)]
    ppermute x1, starting transfers between devices: 10.7 us -> 15.8 us  [local(): lax.ppermute(lax.dynamic_index_in_dim(weight_cols, 1 - c, axis=2, keepdim...]
    ppermute x3, waiting for transfers between devices: 10.3 us -> 7.41 us  [local(): arriving = lax.ppermute(block, 'z', relay)]
    ppermute x3, starting transfers between devices: 15.2 us -> 12.4 us  [local(): arriving = lax.ppermute(block, 'z', relay)]
    all_gather x1 -> x0, waiting for transfers between devices: 2.58 us -> none  [local(): weight_cols = lax.all_gather(out_weight, 'z', axis=1, tiled=True)]
  transfers between devices with their start and end apart: 9 -> 8, of which waited for: 9 -> 7; matrix products, arithmetic and copies ran while one was open for 7% -> 3% of each run, Pallas kernels for 0% -> 0%
where the time goes in v12:
time: 185 us
  blocking collectives  72.9 us (39%)
  starting transfers between devices  55.5 us (30%)
  waiting for transfers between devices  36 us (19%)
  local copies, waits for them, and re-layouts  7.84 us (4%)
  matrix products  7.4 us (4%)
  other arithmetic  3.98 us (2%)
    all_gather x1, blocking collectives, local(): lax.all_gather(out_weight[:, :half], 'z', axis=1, tiled=True)  36.4 us
    all_gather x1, blocking collectives, local(): lax.all_gather(out_weight[:, half:], 'z', axis=1, tiled=True)  26.6 us
    all_to_all x1, waiting for transfers between devices, local(): pieces = lax.all_to_all(pieces, ('y', 'x', 'c'), 0, 0, tiled=True)  16.9 us
    ppermute x1, starting transfers between devices, local(): lax.ppermute(lax.dynamic_index_in_dim(weight_cols, 1 - c, axis=2, keepdim...  15.8 us
    ppermute x3, starting transfers between devices, local(): arriving = lax.ppermute(block, 'z', relay)  12.4 us
    ppermute x1, starting transfers between devices, local(): other_attended = lax.ppermute(own_attended, 'c', swap)  10.8 us
    all_gather x1, blocking collectives, local(): own_attended = lax.all_gather(attended, 'y', axis=1, tiled=True)  9.91 us
    ppermute x3, waiting for transfers between devices, local(): arriving = lax.ppermute(block, 'z', relay)  7.41 us
  transfers between devices with their start and end apart: 8, of which 7 were waited for; matrix products, arithmetic and copies ran while one was open for 3% of the time, Pallas kernels for 0%

profile of v12, /device:TPU:1, one launch (start us, length us, event | category | flops | bytes accessed | tf_op | source)
XLA Modules:
  0.0 184.5 jit_solution(5069312250929960411)
XLA Ops:
  0.6 1.2 reshape.344
  1.8 1.0 reshape.315
  2.7 0.7 convert_element_type.51
  3.4 0.2 maximum_bitcast_fusion
  3.6 0.2 pad_maximum_fusion.1
  3.9 0.8 copy.31
  4.7 5.0 %all-to-all-start = ((bf16[145,3,4,1,128]{4,0,1,3,2:T(8,128)(2,1)}), bf16[145,3,4,1,128]{4,0,1,3,2:T(8,128)(2,1)S(1)}, u32[]{:S(2)}, u32[]{:S(2)}) async-start(bf16[145,3,4,1,128]{4,0,1,3,2:T(8,128)(2,1)} %copy.31), calls=%async_computation | async-start | bytes 933888 | tf_op jit(solution)/shard_map/all_to_all | solution.py:37
  9.7 6.6 %all-to-all-done = bf16[145,3,4,1,128]{4,0,1,3,2:T(8,128)(2,1)S(1)} async-done(((bf16[145,3,4,1,128]{4,0,1,3,2:T(8,128)(2,1)}), bf16[145,3,4,1,128]{4,0,1,3,2:T(8,128)(2,1)S(1)}, u32[]{:S(2)}, u32[]{:S(2)}) %all-to-all-start) | async-done | bytes 445472 | tf_op jit(solution)/shard_map/all_to_all | solution.py:37
  16.6 0.5 fusion.76
  17.1 0.3 fusion.14
  17.5 4.6 %collective-permute-start = (bf16[579,2,1,128]{3,0,1,2:T(8,128)(2,1)S(1)}, bf16[579,2,1,128]{3,0,1,2:T(8,128)(2,1)S(1)}, u32[]{:S(2)}, u32[]{:S(2)}) collective-permute-start(bf16[579,2,1,128]{3,0,1,2:T(8,128)(2,1)S(1)} %pad_maximum_fusion.2), channel_id=1, source_target_pairs={{0,32},{32,64},{64,96},{96,128},{128,160},{160,192},{192,224},{224... | collective-permute-start | bytes 889352 | tf_op jit(solution)/shard_map/ppermute | solution.py:83
  22.1 0.6 fusion.1
  22.6 3.1 %collective-permute-done = bf16[579,2,1,128]{3,0,1,2:T(8,128)(2,1)S(1)} collective-permute-done((bf16[579,2,1,128]{3,0,1,2:T(8,128)(2,1)S(1)}, bf16[579,2,1,128]{3,0,1,2:T(8,128)(2,1)S(1)}, u32[]{:S(2)}, u32[]{:S(2)}) %collective-permute-start) | collective-permute-done | bytes 296480 | tf_op jit(solution)/shard_map/ppermute | solution.py:83
  25.7 4.1 %collective-permute-start.1 = (bf16[579,2,1,128]{3,0,1,2:T(8,128)(2,1)S(1)}, bf16[579,2,1,128]{3,0,1,2:T(8,128)(2,1)S(1)}, u32[]{:S(2)}, u32[]{:S(2)}) collective-permute-start(bf16[579,2,1,128]{3,0,1,2:T(8,128)(2,1)S(1)} %collective-permute-done), channel_id=1, source_target_pairs={{0,32},{32,64},{64,96},{96,128},{128,160},{160,192},{192,224},{224... | collective-permute-start | bytes 889352 | tf_op jit(solution)/shard_map/ppermute | solution.py:86
  29.8 0.5 fusion.77
  30.4 0.5 fusion.6
  30.9 0.6 multiply_add_fusion.1
  31.6 1.9 %collective-permute-done.1 = bf16[579,2,1,128]{3,0,1,2:T(8,128)(2,1)S(1)} collective-permute-done((bf16[579,2,1,128]{3,0,1,2:T(8,128)(2,1)S(1)}, bf16[579,2,1,128]{3,0,1,2:T(8,128)(2,1)S(1)}, u32[]{:S(2)}, u32[]{:S(2)}) %collective-permute-start.1) | collective-permute-done | bytes 296480 | tf_op jit(solution)/shard_map/ppermute | solution.py:86
  33.5 4.1 %collective-permute-start.2 = (bf16[579,2,1,128]{3,0,1,2:T(8,128)(2,1)S(1)}, bf16[579,2,1,128]{3,0,1,2:T(8,128)(2,1)S(1)}, u32[]{:S(2)}, u32[]{:S(2)}) collective-permute-start(bf16[579,2,1,128]{3,0,1,2:T(8,128)(2,1)S(1)} %collective-permute-done.1), channel_id=1, source_target_pairs={{0,32},{32,64},{64,96},{96,128},{128,160},{160,192},{192,224},{224... | collective-permute-start | bytes 889352 | tf_op jit(solution)/shard_map/ppermute | solution.py:86
  37.6 0.5 fusion.78
  38.2 0.5 fusion.8
  38.7 0.6 multiply_add_fusion
  39.3 1.9 %collective-permute-done.2 = bf16[579,2,1,128]{3,0,1,2:T(8,128)(2,1)S(1)} collective-permute-done((bf16[579,2,1,128]{3,0,1,2:T(8,128)(2,1)S(1)}, bf16[579,2,1,128]{3,0,1,2:T(8,128)(2,1)S(1)}, u32[]{:S(2)}, u32[]{:S(2)}) %collective-permute-start.2) | collective-permute-done | bytes 296480 | tf_op jit(solution)/shard_map/ppermute | solution.py:86
  41.3 4.2 %collective-permute-start.3 = (bf16[579,2,1,128]{3,0,1,2:T(8,128)(2,1)S(1)}, bf16[579,2,1,128]{3,0,1,2:T(8,128)(2,1)S(1)}, u32[]{:S(2)}, u32[]{:S(2)}) collective-permute-start(bf16[579,2,1,128]{3,0,1,2:T(8,128)(2,1)S(1)} %collective-permute-done.2), channel_id=1, source_target_pairs={{0,32},{32,64},{64,96},{96,128},{128,160},{160,192},{192,224},{224... | collective-permute-start | bytes 889352 | tf_op jit(solution)/shard_map/ppermute | solution.py:86
  45.5 0.5 fusion.80
  46.1 3.5 %collective-permute-done.3 = bf16[579,2,1,128]{3,0,1,2:T(8,128)(2,1)S(1)} collective-permute-done((bf16[579,2,1,128]{3,0,1,2:T(8,128)(2,1)S(1)}, bf16[579,2,1,128]{3,0,1,2:T(8,128)(2,1)S(1)}, u32[]{:S(2)}, u32[]{:S(2)}) %collective-permute-start.3) | collective-permute-done | bytes 296480 | tf_op jit(solution)/shard_map/ppermute | solution.py:86
  49.6 0.5 fusion.79
  50.2 0.6 convolution_bitcast_fusion.1
  50.8 0.9 fusion.9
  51.8 0.8 fusion.4
  52.6 9.9 %all-gather = bf16[1,576,512]{2,1,0:T(8,128)(2,1)S(1)} all-gather(bf16[1,576,128]{2,1,0:T(8,128)(2,1)S(1)} %fusion.4), channel_id=2, replica_groups=mesh['z'=16,'y'=4,'x'=4,'c'=2] {'y'}, dimensions={2}, use_global_device_ids=true | all-gather | bytes 737280 | tf_op jit(solution)/shard_map/all_gather | solution.py:96
  62.5 10.8 %collective-permute-start.4 = (bf16[576,512]{1,0:T(8,128)(2,1)S(1)}, bf16[576,512]{1,0:T(8,128)(2,1)S(1)}, u32[]{:S(2)}, u32[]{:S(2)}) collective-permute-start(bf16[576,512]{1,0:T(8,128)(2,1)S(1)} %bitcast.119), channel_id=1, source_target_pairs={{0,1},{1,0},{2,3},{3,2},{4,5},{5,4},{6,7},{7,6},{8,9},{9,8},{10,11... | collective-permute-start | bytes 1769480 | tf_op jit(solution)/shard_map/ppermute | solution.py:97
  73.3 36.4 %all_gather.9 = bf16[512,896]{0,1:T(8,128)(2,1)S(1)} all-gather(bf16[512,56]{0,1:T(8,128)(2,1)S(1)} %get-tuple-element.80), channel_id=1, replica_groups=mesh['z'=16,'y'=4,'x'=4,'c'=2] {'z'}, dimensions={1}, use_global_device_ids=true | all-gather | bytes 974848 | tf_op jit(solution)/shard_map/all_gather | solution.py:24
  109.7 26.6 %all_gather.10 = bf16[512,896]{0,1:T(8,128)(2,1)S(1)} all-gather(bf16[512,56]{0,1:T(8,128)(2,1)S(1)} %get-tuple-element.81), channel_id=1, replica_groups=mesh['z'=16,'y'=4,'x'=4,'c'=2] {'z'}, dimensions={1}, use_global_device_ids=true | all-gather | bytes 974848 | tf_op jit(solution)/shard_map/all_gather | solution.py:25
  136.2 0.2 pad_maximum_fusion
  136.4 0.2 constant_dynamic-slice_fusion
  136.6 15.8 %collective-permute-start.5 = (bf16[512,8,112]{0,2,1:T(8,128)(2,1)S(1)}, bf16[512,8,112]{0,2,1:T(8,128)(2,1)S(1)}, u32[]{:S(2)}, u32[]{:S(2)}) collective-permute-start(bf16[512,8,112]{0,2,1:T(8,128)(2,1)S(1)} %get-tuple-element.79), channel_id=1, source_target_pairs={{0,1},{1,0},{2,3},{3,2},{4,5},{5,4},{6,7},{7,6},{8,9},{9,8},{10,11... | collective-permute-start | bytes 2752520 | tf_op jit(solution)/shard_map/ppermute | solution.py:104
  152.4 1.9 %collective-permute-done.5 = bf16[512,8,112]{0,2,1:T(8,128)(2,1)S(1)} collective-permute-done((bf16[512,8,112]{0,2,1:T(8,128)(2,1)S(1)}, bf16[512,8,112]{0,2,1:T(8,128)(2,1)S(1)}, u32[]{:S(2)}, u32[]{:S(2)}) %collective-permute-start.5) | collective-permute-done | bytes 917536 | tf_op jit(solution)/shard_map/ppermute | solution.py:104
  154.3 0.8 fusion.81
  155.1 0.8 add_convert_fusion
  155.9 1.4 reshape.339
  157.3 1.2 copy.39
  158.5 6.9 %all-to-all-start.1 = ((bf16[32,144,112]{2,1,0:T(8,128)(2,1)}), bf16[32,144,112]{2,1,0:T(8,128)(2,1)S(1)}, u32[]{:S(2)}, u32[]{:S(2)}) async-start(bf16[32,144,112]{2,1,0:T(8,128)(2,1)} %bitcast.34), calls=%async_computation.1 | async-start | bytes 2359296 | tf_op jit(solution)/shard_map/all_to_all | solution.py:116
  165.4 0.8 copy.41
  166.2 16.9 %all-to-all-done.1 = bf16[32,144,112]{2,1,0:T(8,128)(2,1)S(1)} async-done(((bf16[32,144,112]{2,1,0:T(8,128)(2,1)}), bf16[32,144,112]{2,1,0:T(8,128)(2,1)S(1)}, u32[]{:S(2)}, u32[]{:S(2)}) %all-to-all-start.1) | async-done | bytes 1032224 | tf_op jit(solution)/shard_map/all_to_all | solution.py:116
  183.1 0.3 reduce_sum.77
  183.4 0.2 copy.40
  183.6 0.9 reshape.342
  (43 shorter events, 0.6 us)
Async XLA Ops:
  3.6 6.1 %copy-start = (bf16[512,112]{0,1:T(8,128)(2,1)S(1)}, bf16[512,112]{0,1:T(8,128)(2,1)}, u32[]{:S(2)}) copy-start(bf16[512,112]{0,1:T(8,128)(2,1)} %param.11) | copy-start | bytes 344068
  4.7 11.6 %all-to-all-start = ((bf16[145,3,4,1,128]{4,0,1,3,2:T(8,128)(2,1)}), bf16[145,3,4,1,128]{4,0,1,3,2:T(8,128)(2,1)S(1)}, u32[]{:S(2)}, u32[]{:S(2)}) async-start(bf16[145,3,4,1,128]{4,0,1,3,2:T(8,128)(2,1)} %copy.31), calls=%async_computation | async-start | bytes 933888 | tf_op jit(solution)/shard_map/all_to_all | solution.py:37
  17.5 8.3 %collective-permute-start = (bf16[579,2,1,128]{3,0,1,2:T(8,128)(2,1)S(1)}, bf16[579,2,1,128]{3,0,1,2:T(8,128)(2,1)S(1)}, u32[]{:S(2)}, u32[]{:S(2)}) collective-permute-start(bf16[579,2,1,128]{3,0,1,2:T(8,128)(2,1)S(1)} %pad_maximum_fusion.2), channel_id=1, source_target_pairs={{0,32},{32,64},{64,96},{96,128},{128,160},{160,192},{192,224},{224... | collective-permute-start | bytes 889352 | tf_op jit(solution)/shard_map/ppermute | solution.py:83
  25.7 7.7 %collective-permute-start.1 = (bf16[579,2,1,128]{3,0,1,2:T(8,128)(2,1)S(1)}, bf16[579,2,1,128]{3,0,1,2:T(8,128)(2,1)S(1)}, u32[]{:S(2)}, u32[]{:S(2)}) collective-permute-start(bf16[579,2,1,128]{3,0,1,2:T(8,128)(2,1)S(1)} %collective-permute-done), channel_id=1, source_target_pairs={{0,32},{32,64},{64,96},{96,128},{128,160},{160,192},{192,224},{224... | collective-permute-start | bytes 889352 | tf_op jit(solution)/shard_map/ppermute | solution.py:86
  33.5 7.8 %collective-permute-start.2 = (bf16[579,2,1,128]{3,0,1,2:T(8,128)(2,1)S(1)}, bf16[579,2,1,128]{3,0,1,2:T(8,128)(2,1)S(1)}, u32[]{:S(2)}, u32[]{:S(2)}) collective-permute-start(bf16[579,2,1,128]{3,0,1,2:T(8,128)(2,1)S(1)} %collective-permute-done.1), channel_id=1, source_target_pairs={{0,32},{32,64},{64,96},{96,128},{128,160},{160,192},{192,224},{224... | collective-permute-start | bytes 889352 | tf_op jit(solution)/shard_map/ppermute | solution.py:86
  41.3 8.3 %collective-permute-start.3 = (bf16[579,2,1,128]{3,0,1,2:T(8,128)(2,1)S(1)}, bf16[579,2,1,128]{3,0,1,2:T(8,128)(2,1)S(1)}, u32[]{:S(2)}, u32[]{:S(2)}) collective-permute-start(bf16[579,2,1,128]{3,0,1,2:T(8,128)(2,1)S(1)} %collective-permute-done.2), channel_id=1, source_target_pairs={{0,32},{32,64},{64,96},{96,128},{128,160},{160,192},{192,224},{224... | collective-permute-start | bytes 889352 | tf_op jit(solution)/shard_map/ppermute | solution.py:86
  62.5 73.9 %collective-permute-start.4 = (bf16[576,512]{1,0:T(8,128)(2,1)S(1)}, bf16[576,512]{1,0:T(8,128)(2,1)S(1)}, u32[]{:S(2)}, u32[]{:S(2)}) collective-permute-start(bf16[576,512]{1,0:T(8,128)(2,1)S(1)} %bitcast.119), channel_id=1, source_target_pairs={{0,1},{1,0},{2,3},{3,2},{4,5},{5,4},{6,7},{7,6},{8,9},{9,8},{10,11... | collective-permute-start | bytes 1769480 | tf_op jit(solution)/shard_map/ppermute | solution.py:97
  136.6 17.7 %collective-permute-start.5 = (bf16[512,8,112]{0,2,1:T(8,128)(2,1)S(1)}, bf16[512,8,112]{0,2,1:T(8,128)(2,1)S(1)}, u32[]{:S(2)}, u32[]{:S(2)}) collective-permute-start(bf16[512,8,112]{0,2,1:T(8,128)(2,1)S(1)} %get-tuple-element.79), channel_id=1, source_target_pairs={{0,1},{1,0},{2,3},{3,2},{4,5},{5,4},{6,7},{7,6},{8,9},{9,8},{10,11... | collective-permute-start | bytes 2752520 | tf_op jit(solution)/shard_map/ppermute | solution.py:104
  158.5 24.6 %all-to-all-start.1 = ((bf16[32,144,112]{2,1,0:T(8,128)(2,1)}), bf16[32,144,112]{2,1,0:T(8,128)(2,1)S(1)}, u32[]{:S(2)}, u32[]{:S(2)}) async-start(bf16[32,144,112]{2,1,0:T(8,128)(2,1)} %bitcast.34), calls=%async_computation.1 | async-start | bytes 2359296 | tf_op jit(solution)/shard_map/all_to_all | solution.py:116

commit v13 on v11

--- a/solution.py
+++ b/solution.py
@@ -18,7 +18,12 @@
     level = NY * rows
     span = min(4, nz - 1)
     score_scale = 1.0 / math.sqrt(HD)
-    weight_cols = lax.all_gather(out_weight, "z", axis=1, tiled=True)
+    c = lax.axis_index("c")
+    swap = [(0, 1), (1, 0)]
+    half = out_weight.shape[1] // 2
+    slab = jnp.concatenate([out_weight, lax.ppermute(out_weight, "c", swap)], axis=0)
+    slab = lax.dynamic_slice_in_dim(slab, c * half, half, axis=1).T
+    weight_rows = lax.all_gather(slab, "z", axis=0, tiled=True)
 
     hq = heads // NY
     packed = jnp.concatenate(
@@ -84,31 +89,23 @@
     attended = (accumulated / row_total[..., None]).astype(jnp.bfloat16)
     attended = attended.transpose(1, 0, 2).reshape(level, hq * HD)
 
-    c = lax.axis_index("c")
-    swap = [(0, 1), (1, 0)]
     own_attended = lax.all_gather(attended, "y", axis=1, tiled=True)
     other_attended = lax.ppermute(own_attended, "c", swap)
-    weight_cols, own_attended, other_attended = lax.optimization_barrier(
-        (weight_cols, own_attended, other_attended)
+    weight_rows, own_attended, other_attended = lax.optimization_barrier(
+        (weight_rows, own_attended, other_attended)
     )
-    chunk = out_weight.shape[1]
-    weight_cols = weight_cols.reshape(weight_cols.shape[0], nz // 2, 2, chunk)
-    own_weight = lax.dynamic_index_in_dim(weight_cols, c, axis=2, keepdims=False)
-    other_weight = lax.ppermute(
-        lax.dynamic_index_in_dim(weight_cols, 1 - c, axis=2, keepdims=False), "c", swap
-    )
-    own_weight = own_weight.reshape(own_weight.shape[0], -1)
-    other_weight = other_weight.reshape(other_weight.shape[0], -1)
-    partial_value = jnp.dot(own_attended, own_weight, preferred_element_type=jnp.float32)
-    partial_value = partial_value + jnp.dot(
-        other_attended, other_weight, preferred_element_type=jnp.float32
+    features = own_attended.shape[1]
+    partial_value = jnp.einsum(
+        "rk,nk->rn", own_attended, weight_rows[:, :features], preferred_element_type=jnp.float32
+    ) + jnp.einsum(
+        "rk,nk->rn", other_attended, weight_rows[:, features:], preferred_element_type=jnp.float32
     )
     nx = lax.axis_size("x")
-    pieces = partial_value.astype(jnp.bfloat16).reshape(NY, rows, nx * 2, chunk)
-    pieces = pieces.transpose(0, 2, 1, 3).reshape(NY * nx * 2, rows, chunk)
+    pieces = partial_value.astype(jnp.bfloat16).reshape(NY, rows, nx * 2, 2 * half)
+    pieces = pieces.transpose(0, 2, 1, 3).reshape(NY * nx * 2, rows, 2 * half)
     pieces = lax.all_to_all(pieces, ("y", "x", "c"), 0, 0, tiled=True)
-    summed = pieces.reshape(NY, nx, 2, rows, chunk).astype(jnp.float32).sum(axis=1)
-    hidden_states = summed.astype(jnp.bfloat16).transpose(2, 1, 0, 3).reshape(rows, 2 * NY * chunk)
+    summed = pieces.reshape(NY, nx, 2, rows, 2, half).astype(jnp.float32).sum(axis=1)
+    hidden_states = summed.astype(jnp.bfloat16).transpose(2, 3, 0, 1, 4).reshape(rows, 4 * NY * half)
 
     head_major = keys_values.reshape(rows, 2, heads, HD).transpose(1, 2, 0, 3)
     return (hidden_states, head_major)

time: 143 us -> 141 us (0.986)
  waiting for transfers between devices: 43 us -> 38 us
    all_to_all x1, starting transfers between devices: 7.87 us -> 15.4 us  [local(): pieces = lax.all_to_all(pieces, ('y', 'x', 'c'), 0, 0, tiled=True)]
    all_to_all x1, waiting for transfers between devices: 5.89 us -> 0.01 us  [local(): lax.all_to_all(packed, 'y', 2, 0, tiled=True)]
    ppermute x1, starting transfers between devices: 10.7 us -> 7.3 us  [local(): lax.ppermute(out_weight, 'c', swap)]
    ppermute x3, waiting for transfers between devices: 10.3 us -> 13.3 us  [local(): arriving = lax.ppermute(block, 'z', relay)]
    ppermute x3, starting transfers between devices: 15.2 us -> 12.1 us  [local(): arriving = lax.ppermute(block, 'z', relay)]
    ppermute x1, starting transfers between devices: 4.6 us -> 2.28 us  [local(): block = lax.ppermute(pair, 'z', relay)]
    dynamic_slice x1 -> x0, local copies, waits for them, and re-layouts: 1.58 us -> none  [local(): lax.dynamic_index_in_dim(weight_cols, c, axis=2, keepdims=False)]
  transfers between devices with their start and end apart: 9 -> 9, of which waited for: 9 -> 8; matrix products, arithmetic and copies ran while one was open for 7% -> 7% of each run, Pallas kernels for 0% -> 0%
where the time goes in v13:
time: 141 us; the launch traced here: 140 us
  starting transfers between devices  54 us (38%)
  waiting for transfers between devices  38 us (27%)
  between operations  14.4 us (10%)
  blocking collectives  11.1 us (8%)
  local copies, waits for them, and re-layouts  9.24 us (7%)
  matrix products  8.74 us (6%)
  other arithmetic  4.63 us (3%)
    all_to_all x1, waiting for transfers between devices, local(): pieces = lax.all_to_all(pieces, ('y', 'x', 'c'), 0, 0, tiled=True)  16.9 us
    all_to_all x1, starting transfers between devices, local(): pieces = lax.all_to_all(pieces, ('y', 'x', 'c'), 0, 0, tiled=True)  15.4 us
    ppermute x3, waiting for transfers between devices, local(): arriving = lax.ppermute(block, 'z', relay)  13.3 us
    ppermute x3, starting transfers between devices, local(): arriving = lax.ppermute(block, 'z', relay)  12.1 us
    ppermute x1, starting transfers between devices, local(): other_attended = lax.ppermute(own_attended, 'c', swap)  11.9 us
    all_gather x1, blocking collectives, local(): own_attended = lax.all_gather(attended, 'y', axis=1, tiled=True)  11.1 us
    ppermute x1, starting transfers between devices, local(): lax.ppermute(out_weight, 'c', swap)  7.3 us
    all_to_all x1, starting transfers between devices, local(): lax.all_to_all(packed, 'y', 2, 0, tiled=True)  5.01 us
  transfers between devices with their start and end apart: 9, of which 8 were waited for; matrix products, arithmetic and copies ran while one was open for 7% of the time, Pallas kernels for 0%

profile of v13, /device:TPU:1, one launch (start us, length us, event | category | flops | bytes accessed | tf_op | source)
XLA Modules:
  0.0 140.2 jit_solution(5813686756780228452)
XLA Ops:
  7.2 1.2 reshape.319
  8.3 1.0 reshape.293
  9.3 0.7 convert_element_type.51
  10.0 0.2 maximum_bitcast_fusion
  10.2 0.2 pad_maximum_fusion
  10.4 0.8 copy.22
  11.2 5.0 %all-to-all-start = ((bf16[145,3,4,1,128]{4,0,1,3,2:T(8,128)(2,1)}), bf16[145,3,4,1,128]{4,0,1,3,2:T(8,128)(2,1)S(1)}, u32[]{:S(2)}, u32[]{:S(2)}) async-start(bf16[145,3,4,1,128]{4,0,1,3,2:T(8,128)(2,1)} %copy.22), calls=%async_computation | async-start | bytes 933888 | tf_op jit(solution)/shard_map/all_to_all | solution.py:35
  16.2 7.3 %collective-permute-start = (bf16[512,112]{0,1:T(8,128)(2,1)S(1)}, bf16[512,112]{0,1:T(8,128)(2,1)S(1)}, u32[]{:S(2)}, u32[]{:S(2)}) collective-permute-start(bf16[512,112]{0,1:T(8,128)(2,1)S(1)} %copy-done.1), channel_id=1, source_target_pairs={{0,1},{1,0},{2,3},{3,2},{4,5},{5,4},{6,7},{7,6},{8,9},{9,8},{10,11... | collective-permute-start | bytes 344072 | tf_op jit(solution)/shard_map/ppermute | solution.py:24
  23.6 0.9 collective-permute-done
  24.5 0.7 fusion.68
  25.3 0.1 slice.100
  25.4 0.5 fusion.80
  25.9 0.3 fusion.14
  26.3 2.3 %collective-permute-start.1 = (bf16[579,2,1,128]{3,0,1,2:T(8,128)(2,1)S(1)}, bf16[579,2,1,128]{3,0,1,2:T(8,128)(2,1)S(1)}, u32[]{:S(2)}, u32[]{:S(2)}) collective-permute-start(bf16[579,2,1,128]{3,0,1,2:T(8,128)(2,1)S(1)} %pad_maximum_fusion.1), channel_id=1, source_target_pairs={{0,32},{32,64},{64,96},{96,128},{128,160},{160,192},{192,224},{224... | collective-permute-start | bytes 889352 | tf_op jit(solution)/shard_map/ppermute | solution.py:81
  28.6 0.6 fusion.1
  29.2 3.1 %collective-permute-done.1 = bf16[579,2,1,128]{3,0,1,2:T(8,128)(2,1)S(1)} collective-permute-done((bf16[579,2,1,128]{3,0,1,2:T(8,128)(2,1)S(1)}, bf16[579,2,1,128]{3,0,1,2:T(8,128)(2,1)S(1)}, u32[]{:S(2)}, u32[]{:S(2)}) %collective-permute-start.1) | collective-permute-done | bytes 296480 | tf_op jit(solution)/shard_map/ppermute | solution.py:81
  32.3 4.1 %collective-permute-start.2 = (bf16[579,2,1,128]{3,0,1,2:T(8,128)(2,1)S(1)}, bf16[579,2,1,128]{3,0,1,2:T(8,128)(2,1)S(1)}, u32[]{:S(2)}, u32[]{:S(2)}) collective-permute-start(bf16[579,2,1,128]{3,0,1,2:T(8,128)(2,1)S(1)} %collective-permute-done.1), channel_id=1, source_target_pairs={{0,32},{32,64},{64,96},{96,128},{128,160},{160,192},{192,224},{224... | collective-permute-start | bytes 889352 | tf_op jit(solution)/shard_map/ppermute | solution.py:84
  36.4 0.5 fusion.81
  36.9 0.5 fusion.6
  37.5 0.6 multiply_add_fusion.1
  38.1 1.9 %collective-permute-done.2 = bf16[579,2,1,128]{3,0,1,2:T(8,128)(2,1)S(1)} collective-permute-done((bf16[579,2,1,128]{3,0,1,2:T(8,128)(2,1)S(1)}, bf16[579,2,1,128]{3,0,1,2:T(8,128)(2,1)S(1)}, u32[]{:S(2)}, u32[]{:S(2)}) %collective-permute-start.2) | collective-permute-done | bytes 296480 | tf_op jit(solution)/shard_map/ppermute | solution.py:84
  40.0 4.1 %collective-permute-start.3 = (bf16[579,2,1,128]{3,0,1,2:T(8,128)(2,1)S(1)}, bf16[579,2,1,128]{3,0,1,2:T(8,128)(2,1)S(1)}, u32[]{:S(2)}, u32[]{:S(2)}) collective-permute-start(bf16[579,2,1,128]{3,0,1,2:T(8,128)(2,1)S(1)} %collective-permute-done.2), channel_id=1, source_target_pairs={{0,32},{32,64},{64,96},{96,128},{128,160},{160,192},{192,224},{224... | collective-permute-start | bytes 889352 | tf_op jit(solution)/shard_map/ppermute | solution.py:84
  44.2 0.5 fusion.82
  44.7 0.5 fusion.8
  45.3 0.6 multiply_add_fusion
  45.9 4.0 %collective-permute-done.3 = bf16[579,2,1,128]{3,0,1,2:T(8,128)(2,1)S(1)} collective-permute-done((bf16[579,2,1,128]{3,0,1,2:T(8,128)(2,1)S(1)}, bf16[579,2,1,128]{3,0,1,2:T(8,128)(2,1)S(1)}, u32[]{:S(2)}, u32[]{:S(2)}) %collective-permute-start.3) | collective-permute-done | bytes 296480 | tf_op jit(solution)/shard_map/ppermute | solution.py:84
  50.0 4.0 %collective-permute-start.4 = (bf16[579,2,1,128]{3,0,1,2:T(8,128)(2,1)S(1)}, bf16[579,2,1,128]{3,0,1,2:T(8,128)(2,1)S(1)}, u32[]{:S(2)}, u32[]{:S(2)}) collective-permute-start(bf16[579,2,1,128]{3,0,1,2:T(8,128)(2,1)S(1)} %collective-permute-done.3), channel_id=1, source_target_pairs={{0,32},{32,64},{64,96},{96,128},{128,160},{160,192},{192,224},{224... | collective-permute-start | bytes 889352 | tf_op jit(solution)/shard_map/ppermute | solution.py:84
  54.0 0.5 fusion.84
  54.5 7.3 %collective-permute-done.4 = bf16[579,2,1,128]{3,0,1,2:T(8,128)(2,1)S(1)} collective-permute-done((bf16[579,2,1,128]{3,0,1,2:T(8,128)(2,1)S(1)}, bf16[579,2,1,128]{3,0,1,2:T(8,128)(2,1)S(1)}, u32[]{:S(2)}, u32[]{:S(2)}) %collective-permute-start.4) | collective-permute-done | bytes 296480 | tf_op jit(solution)/shard_map/ppermute | solution.py:84
  61.9 0.5 fusion.83
  62.4 0.9 fusion.9
  63.4 0.6 convolution_bitcast_fusion.1
  64.1 0.8 fusion.4
  64.8 11.1 %all-gather = bf16[1,576,512]{2,1,0:T(8,128)(2,1)S(1)} all-gather(bf16[1,576,128]{2,1,0:T(8,128)(2,1)S(1)} %fusion.4), channel_id=2, replica_groups=mesh['z'=16,'y'=4,'x'=4,'c'=2] {'y'}, dimensions={2}, use_global_device_ids=true | all-gather | bytes 737280 | tf_op jit(solution)/shard_map/all_gather | solution.py:92
  76.0 11.9 %collective-permute-start.5 = (bf16[576,512]{1,0:T(8,128)(2,1)S(1)}, bf16[576,512]{1,0:T(8,128)(2,1)S(1)}, u32[]{:S(2)}, u32[]{:S(2)}) collective-permute-start(bf16[576,512]{1,0:T(8,128)(2,1)S(1)} %bitcast.107), channel_id=1, source_target_pairs={{0,1},{1,0},{2,3},{3,2},{4,5},{5,4},{6,7},{7,6},{8,9},{9,8},{10,11... | collective-permute-start | bytes 1769480 | tf_op jit(solution)/shard_map/ppermute | solution.py:93
  87.9 1.4 %collective-permute-done.5 = bf16[576,512]{1,0:T(8,128)(2,1)S(1)} collective-permute-done((bf16[576,512]{1,0:T(8,128)(2,1)S(1)}, bf16[576,512]{1,0:T(8,128)(2,1)S(1)}, u32[]{:S(2)}, u32[]{:S(2)}) %collective-permute-start.5) | collective-permute-done | bytes 589856 | tf_op jit(solution)/shard_map/ppermute | solution.py:93
  89.3 2.3 %all-gather.3.cloned.1.call-done = bf16[896,1024]{1,0:T(8,128)(2,1)} async-done(((bf16[56,1024]{1,0:T(8,128)(2,1)}), bf16[896,1024]{1,0:T(8,128)(2,1)}) %all-gather.3.cloned.1.call-update) | async-done | bytes 1835024 | tf_op jit(solution)/shard_map/all_gather | solution.py:26
  91.6 2.1 %fusion.15 = f32[576,896]{1,0:T(8,128)S(1)} fusion(bf16[576,512]{1,0:T(8,128)(2,1)S(1)} %collective-permute-done.5, bf16[896,1024]{1,0:T(8,128)(2,1)} %all-gather.3.cloned.1.call-done), kind=kOutput, calls=%fused_computation.36 | convolution fusion | flops 528482304 | bytes 3571712 | tf_op jit(solution)/shard_map/rk,nk->rn/dot_general | solution.py:100
  93.7 0.8 add_convert_fusion
  94.5 1.4 reshape.314
  95.9 1.2 copy.30
  97.1 15.4 %all-to-all-start.1 = ((bf16[32,144,112]{2,1,0:T(8,128)(2,1)}), bf16[32,144,112]{2,1,0:T(8,128)(2,1)S(1)}, u32[]{:S(2)}, u32[]{:S(2)}) async-start(bf16[32,144,112]{2,1,0:T(8,128)(2,1)} %bitcast.28), calls=%async_computation.1 | async-start | bytes 2359296 | tf_op jit(solution)/shard_map/all_to_all | solution.py:106
  112.5 0.8 copy.33
  113.3 16.9 %all-to-all-done.1 = bf16[32,144,112]{2,1,0:T(8,128)(2,1)S(1)} async-done(((bf16[32,144,112]{2,1,0:T(8,128)(2,1)}), bf16[32,144,112]{2,1,0:T(8,128)(2,1)S(1)}, u32[]{:S(2)}, u32[]{:S(2)}) %all-to-all-start.1) | async-done | bytes 1032224 | tf_op jit(solution)/shard_map/all_to_all | solution.py:106
  130.2 0.8 copy.31
  131.0 0.4 reduce_sum.77
  131.4 0.6 copy.32
  132.0 1.3 reshape.317
  (45 shorter events, 0.5 us)
Async XLA Ops:
  10.2 6.1 %copy-start.1 = (bf16[512,112]{0,1:T(8,128)(2,1)S(1)}, bf16[512,112]{0,1:T(8,128)(2,1)}, u32[]{:S(2)}) copy-start(bf16[512,112]{0,1:T(8,128)(2,1)} %param.11) | copy-start | bytes 344068
  11.2 13.9 %all-to-all-start = ((bf16[145,3,4,1,128]{4,0,1,3,2:T(8,128)(2,1)}), bf16[145,3,4,1,128]{4,0,1,3,2:T(8,128)(2,1)S(1)}, u32[]{:S(2)}, u32[]{:S(2)}) async-start(bf16[145,3,4,1,128]{4,0,1,3,2:T(8,128)(2,1)} %copy.22), calls=%async_computation | async-start | bytes 933888 | tf_op jit(solution)/shard_map/all_to_all | solution.py:35
  16.2 75.3 %all-gather.3.cloned.1.call-start = ((), (), s32[]{:S(2)}) async-start(), calls=%async_computation.2 | async-start | bytes 1949696 | tf_op jit(solution)/shard_map/all_gather | solution.py:26
  16.2 8.3 %collective-permute-start = (bf16[512,112]{0,1:T(8,128)(2,1)S(1)}, bf16[512,112]{0,1:T(8,128)(2,1)S(1)}, u32[]{:S(2)}, u32[]{:S(2)}) collective-permute-start(bf16[512,112]{0,1:T(8,128)(2,1)S(1)} %copy-done.1), channel_id=1, source_target_pairs={{0,1},{1,0},{2,3},{3,2},{4,5},{5,4},{6,7},{7,6},{8,9},{9,8},{10,11... | collective-permute-start | bytes 344072 | tf_op jit(solution)/shard_map/ppermute | solution.py:24
  26.3 6.0 %collective-permute-start.1 = (bf16[579,2,1,128]{3,0,1,2:T(8,128)(2,1)S(1)}, bf16[579,2,1,128]{3,0,1,2:T(8,128)(2,1)S(1)}, u32[]{:S(2)}, u32[]{:S(2)}) collective-permute-start(bf16[579,2,1,128]{3,0,1,2:T(8,128)(2,1)S(1)} %pad_maximum_fusion.1), channel_id=1, source_target_pairs={{0,32},{32,64},{64,96},{96,128},{128,160},{160,192},{192,224},{224... | collective-permute-start | bytes 889352 | tf_op jit(solution)/shard_map/ppermute | solution.py:81
  32.3 7.7 %collective-permute-start.2 = (bf16[579,2,1,128]{3,0,1,2:T(8,128)(2,1)S(1)}, bf16[579,2,1,128]{3,0,1,2:T(8,128)(2,1)S(1)}, u32[]{:S(2)}, u32[]{:S(2)}) collective-permute-start(bf16[579,2,1,128]{3,0,1,2:T(8,128)(2,1)S(1)} %collective-permute-done.1), channel_id=1, source_target_pairs={{0,32},{32,64},{64,96},{96,128},{128,160},{160,192},{192,224},{224... | collective-permute-start | bytes 889352 | tf_op jit(solution)/shard_map/ppermute | solution.py:84
  40.0 9.9 %collective-permute-start.3 = (bf16[579,2,1,128]{3,0,1,2:T(8,128)(2,1)S(1)}, bf16[579,2,1,128]{3,0,1,2:T(8,128)(2,1)S(1)}, u32[]{:S(2)}, u32[]{:S(2)}) collective-permute-start(bf16[579,2,1,128]{3,0,1,2:T(8,128)(2,1)S(1)} %collective-permute-done.2), channel_id=1, source_target_pairs={{0,32},{32,64},{64,96},{96,128},{128,160},{160,192},{192,224},{224... | collective-permute-start | bytes 889352 | tf_op jit(solution)/shard_map/ppermute | solution.py:84
  50.0 11.9 %collective-permute-start.4 = (bf16[579,2,1,128]{3,0,1,2:T(8,128)(2,1)S(1)}, bf16[579,2,1,128]{3,0,1,2:T(8,128)(2,1)S(1)}, u32[]{:S(2)}, u32[]{:S(2)}) collective-permute-start(bf16[579,2,1,128]{3,0,1,2:T(8,128)(2,1)S(1)} %collective-permute-done.3), channel_id=1, source_target_pairs={{0,32},{32,64},{64,96},{96,128},{128,160},{160,192},{192,224},{224... | collective-permute-start | bytes 889352 | tf_op jit(solution)/shard_map/ppermute | solution.py:84
  76.0 13.3 %collective-permute-start.5 = (bf16[576,512]{1,0:T(8,128)(2,1)S(1)}, bf16[576,512]{1,0:T(8,128)(2,1)S(1)}, u32[]{:S(2)}, u32[]{:S(2)}) collective-permute-start(bf16[576,512]{1,0:T(8,128)(2,1)S(1)} %bitcast.107), channel_id=1, source_target_pairs={{0,1},{1,0},{2,3},{3,2},{4,5},{5,4},{6,7},{7,6},{8,9},{9,8},{10,11... | collective-permute-start | bytes 1769480 | tf_op jit(solution)/shard_map/ppermute | solution.py:93
  91.6 2.1 %copy-start = (bf16[896,1024]{1,0:T(8,128)(2,1)S(1)}, bf16[896,1024]{1,0:T(8,128)(2,1)}, u32[]{:S(2)}) copy-start(bf16[896,1024]{1,0:T(8,128)(2,1)} %all-gather.3.cloned.1.call-done) | copy-start | bytes 5505028
  97.1 33.1 %all-to-all-start.1 = ((bf16[32,144,112]{2,1,0:T(8,128)(2,1)}), bf16[32,144,112]{2,1,0:T(8,128)(2,1)S(1)}, u32[]{:S(2)}, u32[]{:S(2)}) async-start(bf16[32,144,112]{2,1,0:T(8,128)(2,1)} %bitcast.28), calls=%async_computation.1 | async-start | bytes 2359296 | tf_op jit(solution)/shard_map/all_to_all | solution.py:106
Sparse Core Ops, SparseCore 0:
  25.3 66.2 all-gather.2

commit v14 on v13

--- a/solution.py
+++ b/solution.py
@@ -23,7 +23,6 @@
     half = out_weight.shape[1] // 2
     slab = jnp.concatenate([out_weight, lax.ppermute(out_weight, "c", swap)], axis=0)
     slab = lax.dynamic_slice_in_dim(slab, c * half, half, axis=1).T
-    weight_rows = lax.all_gather(slab, "z", axis=0, tiled=True)
 
     hq = heads // NY
     packed = jnp.concatenate(
@@ -32,6 +31,8 @@
     seg_row = jnp.zeros((3 * hq * HD,), jnp.bfloat16).at[:rows].set(segment_ids.astype(jnp.bfloat16))
     seg_row = jnp.broadcast_to(seg_row.reshape(1, 3, 1, hq, HD), (1, 3, NY, hq, HD))
     packed = jnp.concatenate([packed, seg_row], axis=0)
+    packed, slab = lax.optimization_barrier((packed, slab))
+    weight_rows = lax.all_gather(slab, "z", axis=0, tiled=True)
     packed = lax.all_to_all(packed, "y", 2, 0, tiled=True).reshape(NY, rows + 1, 3, hq, HD)
     query_rows = packed[:, :rows, 0].reshape(level, hq, HD)
     pair = packed[:, :rows, 1:].reshape(level, 2, hq, HD)

time: 141 us -> 145 us (1.028)
  starting transfers between devices: 54 us -> 44.8 us
  waiting for transfers between devices: 38 us -> 45.5 us
  blocking collectives: 11.1 us -> 15.7 us
    all_to_all x1, waiting for transfers between devices: 0.01 us -> 8.25 us  [local(): lax.all_to_all(packed, 'y', 2, 0, tiled=True)]
    ppermute x1, starting transfers between devices: 11.9 us -> 6.53 us  [local(): other_attended = lax.ppermute(own_attended, 'c', swap)]
    all_to_all x1, starting transfers between devices: 15.4 us -> 10.2 us  [local(): pieces = lax.all_to_all(pieces, ('y', 'x', 'c'), 0, 0, tiled=True)]
    all_gather x1, blocking collectives: 11.1 us -> 15.7 us  [local(): own_attended = lax.all_gather(attended, 'y', axis=1, tiled=True)]
    all_gather x1, waiting for transfers between devices: 2.26 us -> 0.01 us  [local(): weight_rows = lax.all_gather(slab, 'z', axis=0, tiled=True)]
    ppermute x3, starting transfers between devices: 12.1 us -> 14.4 us  [local(): arriving = lax.ppermute(block, 'z', relay)]
    ppermute x1, waiting for transfers between devices: 3.1 us -> 5.32 us  [local(): block = lax.ppermute(pair, 'z', relay)]
    ppermute x1, starting transfers between devices: 7.3 us -> 8.92 us  [local(): lax.ppermute(out_weight, 'c', swap)]
  transfers between devices with their start and end apart: 9 -> 9, of which waited for: 8 -> 7; matrix products, arithmetic and copies ran while one was open for 7% -> 9% of each run, Pallas kernels for 0% -> 0%
where the time goes in v14:
time: 145 us; the launch traced here: 143 us
  waiting for transfers between devices  45.5 us (31%)
  starting transfers between devices  44.8 us (31%)
  blocking collectives  15.7 us (11%)
  between operations  14.4 us (10%)
  local copies, waits for them, and re-layouts  9.23 us (6%)
  matrix products  8.74 us (6%)
  other arithmetic  4.63 us (3%)
    all_to_all x1, waiting for transfers between devices, local(): pieces = lax.all_to_all(pieces, ('y', 'x', 'c'), 0, 0, tiled=True)  16.9 us
    all_gather x1, blocking collectives, local(): own_attended = lax.all_gather(attended, 'y', axis=1, tiled=True)  15.7 us
    ppermute x3, starting transfers between devices, local(): arriving = lax.ppermute(block, 'z', relay)  14.4 us
    ppermute x3, waiting for transfers between devices, local(): arriving = lax.ppermute(block, 'z', relay)  12.9 us
    all_to_all x1, starting transfers between devices, local(): pieces = lax.all_to_all(pieces, ('y', 'x', 'c'), 0, 0, tiled=True)  10.2 us
    ppermute x1, starting transfers between devices, local(): lax.ppermute(out_weight, 'c', swap)  8.92 us
    all_to_all x1, waiting for transfers between devices, local(): lax.all_to_all(packed, 'y', 2, 0, tiled=True)  8.25 us
    ppermute x1, starting transfers between devices, local(): other_attended = lax.ppermute(own_attended, 'c', swap)  6.53 us
  transfers between devices with their start and end apart: 9, of which 7 were waited for; matrix products, arithmetic and copies ran while one was open for 9% of the time, Pallas kernels for 0%

profile of v14, /device:TPU:1, one launch (start us, length us, event | category | flops | bytes accessed | tf_op | source)
XLA Modules:
  0.0 143.0 jit_solution(7453057654016407849)
XLA Ops:
  7.2 8.9 %collective-permute-start = (bf16[512,112]{0,1:T(8,128)(2,1)}, bf16[512,112]{0,1:T(8,128)(2,1)S(1)}, u32[]{:S(2)}, u32[]{:S(2)}) collective-permute-start(bf16[512,112]{0,1:T(8,128)(2,1)} %param.11), channel_id=1, source_target_pairs={{0,1},{1,0},{2,3},{3,2},{4,5},{5,4},{6,7},{7,6},{8,9},{9,8},{10,11... | collective-permute-start | bytes 344072 | tf_op jit(solution)/shard_map/ppermute | solution.py:24
  16.1 1.2 reshape.319
  17.3 1.0 reshape.293
  18.2 0.7 convert_element_type.51
  18.9 0.2 maximum_bitcast_fusion
  19.1 0.2 pad_maximum_fusion
  19.3 0.7 fusion.68
  20.0 0.8 copy.22
  20.8 3.5 %all-to-all-start = ((bf16[145,3,4,1,128]{4,0,1,3,2:T(8,128)(2,1)}), bf16[145,3,4,1,128]{4,0,1,3,2:T(8,128)(2,1)S(1)}, u32[]{:S(2)}, u32[]{:S(2)}) async-start(bf16[145,3,4,1,128]{4,0,1,3,2:T(8,128)(2,1)} %copy.22), calls=%async_computation | async-start | bytes 933888 | tf_op jit(solution)/shard_map/all_to_all | solution.py:36
  24.4 0.7 all-gather.3.cloned.1.call-update
  25.0 8.2 %all-to-all-done = bf16[145,3,4,1,128]{4,0,1,3,2:T(8,128)(2,1)S(1)} async-done(((bf16[145,3,4,1,128]{4,0,1,3,2:T(8,128)(2,1)}), bf16[145,3,4,1,128]{4,0,1,3,2:T(8,128)(2,1)S(1)}, u32[]{:S(2)}, u32[]{:S(2)}) %all-to-all-start) | async-done | bytes 445472 | tf_op jit(solution)/shard_map/all_to_all | solution.py:36
  33.4 0.1 slice.100
  33.5 0.5 fusion.80
  34.0 0.3 fusion.14
  34.4 1.3 collective-permute-start.1
  35.8 0.6 fusion.1
  36.3 5.3 %collective-permute-done.1 = bf16[579,2,1,128]{3,0,1,2:T(8,128)(2,1)S(1)} collective-permute-done((bf16[579,2,1,128]{3,0,1,2:T(8,128)(2,1)S(1)}, bf16[579,2,1,128]{3,0,1,2:T(8,128)(2,1)S(1)}, u32[]{:S(2)}, u32[]{:S(2)}) %collective-permute-start.1) | collective-permute-done | bytes 296480 | tf_op jit(solution)/shard_map/ppermute | solution.py:82
  41.7 4.1 %collective-permute-start.2 = (bf16[579,2,1,128]{3,0,1,2:T(8,128)(2,1)S(1)}, bf16[579,2,1,128]{3,0,1,2:T(8,128)(2,1)S(1)}, u32[]{:S(2)}, u32[]{:S(2)}) collective-permute-start(bf16[579,2,1,128]{3,0,1,2:T(8,128)(2,1)S(1)} %collective-permute-done.1), channel_id=1, source_target_pairs={{0,32},{32,64},{64,96},{96,128},{128,160},{160,192},{192,224},{224... | collective-permute-start | bytes 889352 | tf_op jit(solution)/shard_map/ppermute | solution.py:85
  45.8 0.5 fusion.81
  46.4 0.5 fusion.6
  46.9 0.6 multiply_add_fusion.1
  47.5 4.2 %collective-permute-done.2 = bf16[579,2,1,128]{3,0,1,2:T(8,128)(2,1)S(1)} collective-permute-done((bf16[579,2,1,128]{3,0,1,2:T(8,128)(2,1)S(1)}, bf16[579,2,1,128]{3,0,1,2:T(8,128)(2,1)S(1)}, u32[]{:S(2)}, u32[]{:S(2)}) %collective-permute-start.2) | collective-permute-done | bytes 296480 | tf_op jit(solution)/shard_map/ppermute | solution.py:85
  51.8 4.2 %collective-permute-start.3 = (bf16[579,2,1,128]{3,0,1,2:T(8,128)(2,1)S(1)}, bf16[579,2,1,128]{3,0,1,2:T(8,128)(2,1)S(1)}, u32[]{:S(2)}, u32[]{:S(2)}) collective-permute-start(bf16[579,2,1,128]{3,0,1,2:T(8,128)(2,1)S(1)} %collective-permute-done.2), channel_id=1, source_target_pairs={{0,32},{32,64},{64,96},{96,128},{128,160},{160,192},{192,224},{224... | collective-permute-start | bytes 889352 | tf_op jit(solution)/shard_map/ppermute | solution.py:85
  56.0 0.5 fusion.82
  56.6 0.5 fusion.8
  57.1 0.6 multiply_add_fusion
  57.7 3.2 %collective-permute-done.3 = bf16[579,2,1,128]{3,0,1,2:T(8,128)(2,1)S(1)} collective-permute-done((bf16[579,2,1,128]{3,0,1,2:T(8,128)(2,1)S(1)}, bf16[579,2,1,128]{3,0,1,2:T(8,128)(2,1)S(1)}, u32[]{:S(2)}, u32[]{:S(2)}) %collective-permute-start.3) | collective-permute-done | bytes 296480 | tf_op jit(solution)/shard_map/ppermute | solution.py:85
  60.9 6.0 %collective-permute-start.4 = (bf16[579,2,1,128]{3,0,1,2:T(8,128)(2,1)S(1)}, bf16[579,2,1,128]{3,0,1,2:T(8,128)(2,1)S(1)}, u32[]{:S(2)}, u32[]{:S(2)}) collective-permute-start(bf16[579,2,1,128]{3,0,1,2:T(8,128)(2,1)S(1)} %collective-permute-done.3), channel_id=1, source_target_pairs={{0,32},{32,64},{64,96},{96,128},{128,160},{160,192},{192,224},{224... | collective-permute-start | bytes 889352 | tf_op jit(solution)/shard_map/ppermute | solution.py:85
  67.0 0.5 fusion.84
  67.5 5.5 %collective-permute-done.4 = bf16[579,2,1,128]{3,0,1,2:T(8,128)(2,1)S(1)} collective-permute-done((bf16[579,2,1,128]{3,0,1,2:T(8,128)(2,1)S(1)}, bf16[579,2,1,128]{3,0,1,2:T(8,128)(2,1)S(1)}, u32[]{:S(2)}, u32[]{:S(2)}) %collective-permute-start.4) | collective-permute-done | bytes 296480 | tf_op jit(solution)/shard_map/ppermute | solution.py:85
  73.0 0.5 fusion.83
  73.6 0.9 fusion.9
  74.6 0.6 convolution_bitcast_fusion.1
  75.2 0.8 fusion.4
  76.0 15.7 %all-gather = bf16[1,576,512]{2,1,0:T(8,128)(2,1)S(1)} all-gather(bf16[1,576,128]{2,1,0:T(8,128)(2,1)S(1)} %fusion.4), channel_id=2, replica_groups=mesh['z'=16,'y'=4,'x'=4,'c'=2] {'y'}, dimensions={2}, use_global_device_ids=true | all-gather | bytes 737280 | tf_op jit(solution)/shard_map/all_gather | solution.py:93
  91.6 6.5 %collective-permute-start.5 = (bf16[576,512]{1,0:T(8,128)(2,1)S(1)}, bf16[576,512]{1,0:T(8,128)(2,1)S(1)}, u32[]{:S(2)}, u32[]{:S(2)}) collective-permute-start(bf16[576,512]{1,0:T(8,128)(2,1)S(1)} %bitcast.107), channel_id=1, source_target_pairs={{0,1},{1,0},{2,3},{3,2},{4,5},{5,4},{6,7},{7,6},{8,9},{9,8},{10,11... | collective-permute-start | bytes 1769480 | tf_op jit(solution)/shard_map/ppermute | solution.py:94
  98.2 1.4 collective-permute-done.5
  99.6 2.1 %fusion.15 = f32[576,896]{1,0:T(8,128)S(1)} fusion(bf16[576,512]{1,0:T(8,128)(2,1)S(1)} %collective-permute-done.5, bf16[896,1024]{1,0:T(8,128)(2,1)} %all-gather.3.cloned.1.call-done), kind=kOutput, calls=%fused_computation.36 | convolution fusion | flops 528482304 | bytes 3571712 | tf_op jit(solution)/shard_map/rk,nk->rn/dot_general | solution.py:101
  101.7 0.8 add_convert_fusion
  102.6 1.4 reshape.314
  104.0 1.2 copy.30
  105.1 10.2 %all-to-all-start.1 = ((bf16[32,144,112]{2,1,0:T(8,128)(2,1)}), bf16[32,144,112]{2,1,0:T(8,128)(2,1)S(1)}, u32[]{:S(2)}, u32[]{:S(2)}) async-start(bf16[32,144,112]{2,1,0:T(8,128)(2,1)} %bitcast.28), calls=%async_computation.1 | async-start | bytes 2359296 | tf_op jit(solution)/shard_map/all_to_all | solution.py:107
  115.3 0.8 copy.33
  116.1 16.9 %all-to-all-done.1 = bf16[32,144,112]{2,1,0:T(8,128)(2,1)S(1)} async-done(((bf16[32,144,112]{2,1,0:T(8,128)(2,1)}), bf16[32,144,112]{2,1,0:T(8,128)(2,1)S(1)}, u32[]{:S(2)}, u32[]{:S(2)}) %all-to-all-start.1) | async-done | bytes 1032224 | tf_op jit(solution)/shard_map/all_to_all | solution.py:107
  133.0 0.8 copy.31
  133.8 0.4 reduce_sum.77
  134.3 0.6 copy.32
  134.9 1.3 reshape.317
  (45 shorter events, 0.5 us)
Async XLA Ops:
  7.2 12.2 %copy-start.1 = (bf16[512,112]{0,1:T(8,128)(2,1)S(1)}, bf16[512,112]{0,1:T(8,128)(2,1)}, u32[]{:S(2)}) copy-start(bf16[512,112]{0,1:T(8,128)(2,1)} %param.11) | copy-start | bytes 344068
  7.2 12.1 %collective-permute-start = (bf16[512,112]{0,1:T(8,128)(2,1)}, bf16[512,112]{0,1:T(8,128)(2,1)S(1)}, u32[]{:S(2)}, u32[]{:S(2)}) collective-permute-start(bf16[512,112]{0,1:T(8,128)(2,1)} %param.11), channel_id=1, source_target_pairs={{0,1},{1,0},{2,3},{3,2},{4,5},{5,4},{6,7},{7,6},{8,9},{9,8},{10,11... | collective-permute-start | bytes 344072 | tf_op jit(solution)/shard_map/ppermute | solution.py:24
  20.8 12.5 %all-to-all-start = ((bf16[145,3,4,1,128]{4,0,1,3,2:T(8,128)(2,1)}), bf16[145,3,4,1,128]{4,0,1,3,2:T(8,128)(2,1)S(1)}, u32[]{:S(2)}, u32[]{:S(2)}) async-start(bf16[145,3,4,1,128]{4,0,1,3,2:T(8,128)(2,1)} %copy.22), calls=%async_computation | async-start | bytes 933888 | tf_op jit(solution)/shard_map/all_to_all | solution.py:36
  24.3 75.3 %all-gather.3.cloned.1.call-start = ((), (), s32[]{:S(2)}) async-start(), calls=%async_computation.2 | async-start | bytes 1949696 | tf_op jit(solution)/shard_map/all_gather | solution.py:35
  34.4 7.2 %collective-permute-start.1 = (bf16[579,2,1,128]{3,0,1,2:T(8,128)(2,1)S(1)}, bf16[579,2,1,128]{3,0,1,2:T(8,128)(2,1)S(1)}, u32[]{:S(2)}, u32[]{:S(2)}) collective-permute-start(bf16[579,2,1,128]{3,0,1,2:T(8,128)(2,1)S(1)} %pad_maximum_fusion.1), channel_id=1, source_target_pairs={{0,32},{32,64},{64,96},{96,128},{128,160},{160,192},{192,224},{224... | collective-permute-start | bytes 889352 | tf_op jit(solution)/shard_map/ppermute | solution.py:82
  41.7 10.1 %collective-permute-start.2 = (bf16[579,2,1,128]{3,0,1,2:T(8,128)(2,1)S(1)}, bf16[579,2,1,128]{3,0,1,2:T(8,128)(2,1)S(1)}, u32[]{:S(2)}, u32[]{:S(2)}) collective-permute-start(bf16[579,2,1,128]{3,0,1,2:T(8,128)(2,1)S(1)} %collective-permute-done.1), channel_id=1, source_target_pairs={{0,32},{32,64},{64,96},{96,128},{128,160},{160,192},{192,224},{224... | collective-permute-start | bytes 889352 | tf_op jit(solution)/shard_map/ppermute | solution.py:85
  51.8 9.1 %collective-permute-start.3 = (bf16[579,2,1,128]{3,0,1,2:T(8,128)(2,1)S(1)}, bf16[579,2,1,128]{3,0,1,2:T(8,128)(2,1)S(1)}, u32[]{:S(2)}, u32[]{:S(2)}) collective-permute-start(bf16[579,2,1,128]{3,0,1,2:T(8,128)(2,1)S(1)} %collective-permute-done.2), channel_id=1, source_target_pairs={{0,32},{32,64},{64,96},{96,128},{128,160},{160,192},{192,224},{224... | collective-permute-start | bytes 889352 | tf_op jit(solution)/shard_map/ppermute | solution.py:85
  60.9 12.1 %collective-permute-start.4 = (bf16[579,2,1,128]{3,0,1,2:T(8,128)(2,1)S(1)}, bf16[579,2,1,128]{3,0,1,2:T(8,128)(2,1)S(1)}, u32[]{:S(2)}, u32[]{:S(2)}) collective-permute-start(bf16[579,2,1,128]{3,0,1,2:T(8,128)(2,1)S(1)} %collective-permute-done.3), channel_id=1, source_target_pairs={{0,32},{32,64},{64,96},{96,128},{128,160},{160,192},{192,224},{224... | collective-permute-start | bytes 889352 | tf_op jit(solution)/shard_map/ppermute | solution.py:85
  91.6 8.0 %collective-permute-start.5 = (bf16[576,512]{1,0:T(8,128)(2,1)S(1)}, bf16[576,512]{1,0:T(8,128)(2,1)S(1)}, u32[]{:S(2)}, u32[]{:S(2)}) collective-permute-start(bf16[576,512]{1,0:T(8,128)(2,1)S(1)} %bitcast.107), channel_id=1, source_target_pairs={{0,1},{1,0},{2,3},{3,2},{4,5},{5,4},{6,7},{7,6},{8,9},{9,8},{10,11... | collective-permute-start | bytes 1769480 | tf_op jit(solution)/shard_map/ppermute | solution.py:94
  99.6 2.1 %copy-start = (bf16[896,1024]{1,0:T(8,128)(2,1)S(1)}, bf16[896,1024]{1,0:T(8,128)(2,1)}, u32[]{:S(2)}) copy-start(bf16[896,1024]{1,0:T(8,128)(2,1)} %all-gather.3.cloned.1.call-done) | copy-start | bytes 5505028
  105.1 27.9 %all-to-all-start.1 = ((bf16[32,144,112]{2,1,0:T(8,128)(2,1)}), bf16[32,144,112]{2,1,0:T(8,128)(2,1)S(1)}, u32[]{:S(2)}, u32[]{:S(2)}) async-start(bf16[32,144,112]{2,1,0:T(8,128)(2,1)} %bitcast.28), calls=%async_computation.1 | async-start | bytes 2359296 | tf_op jit(solution)/shard_map/all_to_all | solution.py:107
Sparse Core Ops, SparseCore 0:
  27.8 66.0 all-gather.2

commit v15 on v13

--- a/solution.py
+++ b/solution.py
@@ -8,6 +8,7 @@
 
 HD = 128
 NY = 4
+MOST = 2161
 
 
 def local(queries, keys_values, segment_ids, out_weight):
@@ -46,9 +47,11 @@
     def attend(carried, block, distance):
         run_max, row_total, accumulated = carried
         source = z - distance
-        key_seg = block[level:].reshape(-1)[:level].astype(jnp.int32)
-        key_rows = block[:level, 0]
-        value_rows = block[:level, 1]
+        keys = block.shape[0] - extra
+        skipped = level - keys
+        key_seg = block[keys:].reshape(-1)[skipped:level].astype(jnp.int32)
+        key_rows = block[:keys, 0]
+        value_rows = block[:keys, 1]
         scores = (
             jnp.einsum("qhd,khd->hqk", query_rows, key_rows, preferred_element_type=jnp.float32)
             * score_scale
@@ -79,9 +82,13 @@
     relay = [(i, i + 1) for i in range(nz - 1)]
     carried = attend(carried, pair, 0)
     block = lax.ppermute(pair, "z", relay)
+    skip = min(max(0, span * level - (MOST - 1)), level) // 16 * 16
     for distance in range(2, span + 1):
         block, carried = lax.optimization_barrier((block, carried))
-        arriving = lax.ppermute(block, "z", relay)
+        outgoing = block
+        if distance == span:
+            outgoing = jnp.concatenate([block[skip:level], block[level:]], axis=0)
+        arriving = lax.ppermute(outgoing, "z", relay)
         carried = attend(carried, block, distance - 1)
         block = arriving
     carried = attend(carried, block, span)

time: 141 us -> 141 us (level)
    all_gather x1, waiting for transfers between devices: 2.26 us -> 3.87 us  [local(): weight_rows = lax.all_gather(slab, 'z', axis=0, tiled=True)]
where the time goes in v15:
time: 141 us; the launch traced here: 140 us
  starting transfers between devices  53.5 us (38%)
  waiting for transfers between devices  38.7 us (27%)
  between operations  14.4 us (10%)
  blocking collectives  11 us (8%)
  local copies, waits for them, and re-layouts  9.25 us (7%)
  matrix products  8.55 us (6%)
  other arithmetic  4.61 us (3%)
    all_to_all x1, waiting for transfers between devices, local(): pieces = lax.all_to_all(pieces, ('y', 'x', 'c'), 0, 0, tiled=True)  16.9 us
    all_to_all x1, starting transfers between devices, local(): pieces = lax.all_to_all(pieces, ('y', 'x', 'c'), 0, 0, tiled=True)  15.3 us
    ppermute x3, waiting for transfers between devices, local(): arriving = lax.ppermute(outgoing, 'z', relay)  12.2 us
    ppermute x3, starting transfers between devices, local(): arriving = lax.ppermute(outgoing, 'z', relay)  12.1 us
    ppermute x1, starting transfers between devices, local(): other_attended = lax.ppermute(own_attended, 'c', swap)  11.5 us
    all_gather x1, blocking collectives, local(): own_attended = lax.all_gather(attended, 'y', axis=1, tiled=True)  11 us
    ppermute x1, starting transfers between devices, local(): lax.ppermute(out_weight, 'c', swap)  7.3 us
    all_to_all x1, starting transfers between devices, local(): lax.all_to_all(packed, 'y', 2, 0, tiled=True)  5.01 us
  transfers between devices with their start and end apart: 9, of which 8 were waited for; matrix products, arithmetic and copies ran while one was open for 7% of the time, Pallas kernels for 0%

profile of v15, /device:TPU:1, one launch (start us, length us, event | category | flops | bytes accessed | tf_op | source)
XLA Modules:
  0.0 140.0 jit_solution(12885980168812555498)
XLA Ops:
  7.2 1.2 reshape.319
  8.3 1.0 reshape.293
  9.3 0.7 convert_element_type.51
  10.0 0.2 maximum_bitcast_fusion
  10.2 0.2 pad_maximum_fusion
  10.4 0.8 copy.22
  11.2 5.0 %all-to-all-start = ((bf16[145,3,4,1,128]{4,0,1,3,2:T(8,128)(2,1)}), bf16[145,3,4,1,128]{4,0,1,3,2:T(8,128)(2,1)S(1)}, u32[]{:S(2)}, u32[]{:S(2)}) async-start(bf16[145,3,4,1,128]{4,0,1,3,2:T(8,128)(2,1)} %copy.22), calls=%async_computation | async-start | bytes 933888 | tf_op jit(solution)/shard_map/all_to_all | solution.py:36
  16.2 7.3 %collective-permute-start = (bf16[512,112]{0,1:T(8,128)(2,1)S(1)}, bf16[512,112]{0,1:T(8,128)(2,1)S(1)}, u32[]{:S(2)}, u32[]{:S(2)}) collective-permute-start(bf16[512,112]{0,1:T(8,128)(2,1)S(1)} %copy-done.1), channel_id=1, source_target_pairs={{0,1},{1,0},{2,3},{3,2},{4,5},{5,4},{6,7},{7,6},{8,9},{9,8},{10,11... | collective-permute-start | bytes 344072 | tf_op jit(solution)/shard_map/ppermute | solution.py:25
  23.6 0.9 collective-permute-done
  24.5 0.7 fusion.69
  25.4 0.5 fusion.81
  25.9 0.3 fusion.13
  26.3 2.3 %collective-permute-start.1 = (bf16[579,2,1,128]{3,0,1,2:T(8,128)(2,1)S(1)}, bf16[579,2,1,128]{3,0,1,2:T(8,128)(2,1)S(1)}, u32[]{:S(2)}, u32[]{:S(2)}) collective-permute-start(bf16[579,2,1,128]{3,0,1,2:T(8,128)(2,1)S(1)} %pad_maximum_fusion.1), channel_id=1, source_target_pairs={{0,32},{32,64},{64,96},{96,128},{128,160},{160,192},{192,224},{224... | collective-permute-start | bytes 889352 | tf_op jit(solution)/shard_map/ppermute | solution.py:84
  28.6 0.6 fusion.2
  29.2 3.1 %collective-permute-done.1 = bf16[579,2,1,128]{3,0,1,2:T(8,128)(2,1)S(1)} collective-permute-done((bf16[579,2,1,128]{3,0,1,2:T(8,128)(2,1)S(1)}, bf16[579,2,1,128]{3,0,1,2:T(8,128)(2,1)S(1)}, u32[]{:S(2)}, u32[]{:S(2)}) %collective-permute-start.1) | collective-permute-done | bytes 296480 | tf_op jit(solution)/shard_map/ppermute | solution.py:84
  32.3 4.1 %collective-permute-start.2 = (bf16[579,2,1,128]{3,0,1,2:T(8,128)(2,1)S(1)}, bf16[579,2,1,128]{3,0,1,2:T(8,128)(2,1)S(1)}, u32[]{:S(2)}, u32[]{:S(2)}) collective-permute-start(bf16[579,2,1,128]{3,0,1,2:T(8,128)(2,1)S(1)} %collective-permute-done.1), channel_id=1, source_target_pairs={{0,32},{32,64},{64,96},{96,128},{128,160},{160,192},{192,224},{224... | collective-permute-start | bytes 889352 | tf_op jit(solution)/shard_map/ppermute | solution.py:91
  36.4 0.5 fusion.82
  37.0 0.5 fusion.7
  37.5 0.6 multiply_add_fusion.1
  38.1 1.9 %collective-permute-done.2 = bf16[579,2,1,128]{3,0,1,2:T(8,128)(2,1)S(1)} collective-permute-done((bf16[579,2,1,128]{3,0,1,2:T(8,128)(2,1)S(1)}, bf16[579,2,1,128]{3,0,1,2:T(8,128)(2,1)S(1)}, u32[]{:S(2)}, u32[]{:S(2)}) %collective-permute-start.2) | collective-permute-done | bytes 296480 | tf_op jit(solution)/shard_map/ppermute | solution.py:91
  40.0 4.1 %collective-permute-start.3 = (bf16[579,2,1,128]{3,0,1,2:T(8,128)(2,1)S(1)}, bf16[579,2,1,128]{3,0,1,2:T(8,128)(2,1)S(1)}, u32[]{:S(2)}, u32[]{:S(2)}) collective-permute-start(bf16[579,2,1,128]{3,0,1,2:T(8,128)(2,1)S(1)} %collective-permute-done.2), channel_id=1, source_target_pairs={{0,32},{32,64},{64,96},{96,128},{128,160},{160,192},{192,224},{224... | collective-permute-start | bytes 889352 | tf_op jit(solution)/shard_map/ppermute | solution.py:91
  44.2 0.5 fusion.83
  44.8 0.5 fusion.9
  45.3 0.6 multiply_add_fusion
  45.9 4.0 %collective-permute-done.3 = bf16[579,2,1,128]{3,0,1,2:T(8,128)(2,1)S(1)} collective-permute-done((bf16[579,2,1,128]{3,0,1,2:T(8,128)(2,1)S(1)}, bf16[579,2,1,128]{3,0,1,2:T(8,128)(2,1)S(1)}, u32[]{:S(2)}, u32[]{:S(2)}) %collective-permute-start.3) | collective-permute-done | bytes 296480 | tf_op jit(solution)/shard_map/ppermute | solution.py:91
  50.0 4.0 %collective-permute-start.4 = (bf16[435,2,1,128]{3,0,1,2:T(8,128)(2,1)S(1)}, bf16[435,2,1,128]{3,0,1,2:T(8,128)(2,1)S(1)}, u32[]{:S(2)}, u32[]{:S(2)}) collective-permute-start(bf16[435,2,1,128]{3,0,1,2:T(8,128)(2,1)S(1)} %concatenate.23), channel_id=1, source_target_pairs={{0,32},{32,64},{64,96},{96,128},{128,160},{160,192},{192,224},{224... | collective-permute-start | bytes 668168 | tf_op jit(solution)/shard_map/ppermute | solution.py:91
  54.0 0.5 fusion.85
  54.5 6.2 %collective-permute-done.4 = bf16[435,2,1,128]{3,0,1,2:T(8,128)(2,1)S(1)} collective-permute-done((bf16[435,2,1,128]{3,0,1,2:T(8,128)(2,1)S(1)}, bf16[435,2,1,128]{3,0,1,2:T(8,128)(2,1)S(1)}, u32[]{:S(2)}, u32[]{:S(2)}) %collective-permute-start.4) | collective-permute-done | bytes 222752 | tf_op jit(solution)/shard_map/ppermute | solution.py:91
  60.9 0.4 fusion.84
  61.3 0.4 fusion.17
  61.7 0.5 fusion.10
  62.2 0.6 convolution_bitcast_fusion.1
  62.9 0.7 fusion.5
  63.5 11.0 %all-gather = bf16[1,576,512]{2,1,0:T(8,128)(2,1)S(1)} all-gather(bf16[1,576,128]{2,1,0:T(8,128)(2,1)S(1)} %fusion.5), channel_id=2, replica_groups=mesh['z'=16,'y'=4,'x'=4,'c'=2] {'y'}, dimensions={2}, use_global_device_ids=true | all-gather | bytes 737280 | tf_op jit(solution)/shard_map/all_gather | solution.py:99
  74.6 11.5 %collective-permute-start.5 = (bf16[576,512]{1,0:T(8,128)(2,1)S(1)}, bf16[576,512]{1,0:T(8,128)(2,1)S(1)}, u32[]{:S(2)}, u32[]{:S(2)}) collective-permute-start(bf16[576,512]{1,0:T(8,128)(2,1)S(1)} %bitcast.107), channel_id=1, source_target_pairs={{0,1},{1,0},{2,3},{3,2},{4,5},{5,4},{6,7},{7,6},{8,9},{9,8},{10,11... | collective-permute-start | bytes 1769480 | tf_op jit(solution)/shard_map/ppermute | solution.py:100
  86.1 1.6 %collective-permute-done.5 = bf16[576,512]{1,0:T(8,128)(2,1)S(1)} collective-permute-done((bf16[576,512]{1,0:T(8,128)(2,1)S(1)}, bf16[576,512]{1,0:T(8,128)(2,1)S(1)}, u32[]{:S(2)}, u32[]{:S(2)}) %collective-permute-start.5) | collective-permute-done | bytes 589856 | tf_op jit(solution)/shard_map/ppermute | solution.py:100
  87.7 3.9 %all-gather.3.cloned.1.call-done = bf16[896,1024]{1,0:T(8,128)(2,1)} async-done(((bf16[56,1024]{1,0:T(8,128)(2,1)}), bf16[896,1024]{1,0:T(8,128)(2,1)}) %all-gather.3.cloned.1.call-update) | async-done | bytes 1835024 | tf_op jit(solution)/shard_map/all_gather | solution.py:27
  91.5 2.1 %fusion.14 = f32[576,896]{1,0:T(8,128)S(1)} fusion(bf16[576,512]{1,0:T(8,128)(2,1)S(1)} %collective-permute-done.5, bf16[896,1024]{1,0:T(8,128)(2,1)} %all-gather.3.cloned.1.call-done), kind=kOutput, calls=%fused_computation.35 | convolution fusion | flops 528482304 | bytes 3571712 | tf_op jit(solution)/shard_map/rk,nk->rn/dot_general | solution.py:107
  93.7 0.8 add_convert_fusion
  94.5 1.4 reshape.314
  95.9 1.2 copy.30
  97.1 15.3 %all-to-all-start.1 = ((bf16[32,144,112]{2,1,0:T(8,128)(2,1)}), bf16[32,144,112]{2,1,0:T(8,128)(2,1)S(1)}, u32[]{:S(2)}, u32[]{:S(2)}) async-start(bf16[32,144,112]{2,1,0:T(8,128)(2,1)} %bitcast.28), calls=%async_computation.1 | async-start | bytes 2359296 | tf_op jit(solution)/shard_map/all_to_all | solution.py:113
  112.4 0.8 copy.33
  113.1 16.9 %all-to-all-done.1 = bf16[32,144,112]{2,1,0:T(8,128)(2,1)S(1)} async-done(((bf16[32,144,112]{2,1,0:T(8,128)(2,1)}), bf16[32,144,112]{2,1,0:T(8,128)(2,1)S(1)}, u32[]{:S(2)}, u32[]{:S(2)}) %all-to-all-start.1) | async-done | bytes 1032224 | tf_op jit(solution)/shard_map/all_to_all | solution.py:113
  130.0 0.8 copy.31
  130.8 0.4 reduce_sum.77
  131.3 0.6 copy.32
  131.9 1.3 reshape.317
  (47 shorter events, 0.7 us)
Async XLA Ops:
  10.2 6.1 %copy-start.1 = (bf16[512,112]{0,1:T(8,128)(2,1)S(1)}, bf16[512,112]{0,1:T(8,128)(2,1)}, u32[]{:S(2)}) copy-start(bf16[512,112]{0,1:T(8,128)(2,1)} %param.11) | copy-start | bytes 344068
  11.2 13.9 %all-to-all-start = ((bf16[145,3,4,1,128]{4,0,1,3,2:T(8,128)(2,1)}), bf16[145,3,4,1,128]{4,0,1,3,2:T(8,128)(2,1)S(1)}, u32[]{:S(2)}, u32[]{:S(2)}) async-start(bf16[145,3,4,1,128]{4,0,1,3,2:T(8,128)(2,1)} %copy.22), calls=%async_computation | async-start | bytes 933888 | tf_op jit(solution)/shard_map/all_to_all | solution.py:36
  16.2 75.3 %all-gather.3.cloned.1.call-start = ((), (), s32[]{:S(2)}) async-start(), calls=%async_computation.2 | async-start | bytes 1949696 | tf_op jit(solution)/shard_map/all_gather | solution.py:27
  16.2 8.3 %collective-permute-start = (bf16[512,112]{0,1:T(8,128)(2,1)S(1)}, bf16[512,112]{0,1:T(8,128)(2,1)S(1)}, u32[]{:S(2)}, u32[]{:S(2)}) collective-permute-start(bf16[512,112]{0,1:T(8,128)(2,1)S(1)} %copy-done.1), channel_id=1, source_target_pairs={{0,1},{1,0},{2,3},{3,2},{4,5},{5,4},{6,7},{7,6},{8,9},{9,8},{10,11... | collective-permute-start | bytes 344072 | tf_op jit(solution)/shard_map/ppermute | solution.py:25
  26.3 5.9 %collective-permute-start.1 = (bf16[579,2,1,128]{3,0,1,2:T(8,128)(2,1)S(1)}, bf16[579,2,1,128]{3,0,1,2:T(8,128)(2,1)S(1)}, u32[]{:S(2)}, u32[]{:S(2)}) collective-permute-start(bf16[579,2,1,128]{3,0,1,2:T(8,128)(2,1)S(1)} %pad_maximum_fusion.1), channel_id=1, source_target_pairs={{0,32},{32,64},{64,96},{96,128},{128,160},{160,192},{192,224},{224... | collective-permute-start | bytes 889352 | tf_op jit(solution)/shard_map/ppermute | solution.py:84
  32.3 7.8 %collective-permute-start.2 = (bf16[579,2,1,128]{3,0,1,2:T(8,128)(2,1)S(1)}, bf16[579,2,1,128]{3,0,1,2:T(8,128)(2,1)S(1)}, u32[]{:S(2)}, u32[]{:S(2)}) collective-permute-start(bf16[579,2,1,128]{3,0,1,2:T(8,128)(2,1)S(1)} %collective-permute-done.1), channel_id=1, source_target_pairs={{0,32},{32,64},{64,96},{96,128},{128,160},{160,192},{192,224},{224... | collective-permute-start | bytes 889352 | tf_op jit(solution)/shard_map/ppermute | solution.py:91
  40.0 9.9 %collective-permute-start.3 = (bf16[579,2,1,128]{3,0,1,2:T(8,128)(2,1)S(1)}, bf16[579,2,1,128]{3,0,1,2:T(8,128)(2,1)S(1)}, u32[]{:S(2)}, u32[]{:S(2)}) collective-permute-start(bf16[579,2,1,128]{3,0,1,2:T(8,128)(2,1)S(1)} %collective-permute-done.2), channel_id=1, source_target_pairs={{0,32},{32,64},{64,96},{96,128},{128,160},{160,192},{192,224},{224... | collective-permute-start | bytes 889352 | tf_op jit(solution)/shard_map/ppermute | solution.py:91
  50.0 10.8 %collective-permute-start.4 = (bf16[435,2,1,128]{3,0,1,2:T(8,128)(2,1)S(1)}, bf16[435,2,1,128]{3,0,1,2:T(8,128)(2,1)S(1)}, u32[]{:S(2)}, u32[]{:S(2)}) collective-permute-start(bf16[435,2,1,128]{3,0,1,2:T(8,128)(2,1)S(1)} %concatenate.23), channel_id=1, source_target_pairs={{0,32},{32,64},{64,96},{96,128},{128,160},{160,192},{192,224},{224... | collective-permute-start | bytes 668168 | tf_op jit(solution)/shard_map/ppermute | solution.py:91
  74.6 13.1 %collective-permute-start.5 = (bf16[576,512]{1,0:T(8,128)(2,1)S(1)}, bf16[576,512]{1,0:T(8,128)(2,1)S(1)}, u32[]{:S(2)}, u32[]{:S(2)}) collective-permute-start(bf16[576,512]{1,0:T(8,128)(2,1)S(1)} %bitcast.107), channel_id=1, source_target_pairs={{0,1},{1,0},{2,3},{3,2},{4,5},{5,4},{6,7},{7,6},{8,9},{9,8},{10,11... | collective-permute-start | bytes 1769480 | tf_op jit(solution)/shard_map/ppermute | solution.py:100
  91.5 2.1 %copy-start = (bf16[896,1024]{1,0:T(8,128)(2,1)S(1)}, bf16[896,1024]{1,0:T(8,128)(2,1)}, u32[]{:S(2)}) copy-start(bf16[896,1024]{1,0:T(8,128)(2,1)} %all-gather.3.cloned.1.call-done) | copy-start | bytes 5505028
  97.1 33.0 %all-to-all-start.1 = ((bf16[32,144,112]{2,1,0:T(8,128)(2,1)}), bf16[32,144,112]{2,1,0:T(8,128)(2,1)S(1)}, u32[]{:S(2)}, u32[]{:S(2)}) async-start(bf16[32,144,112]{2,1,0:T(8,128)(2,1)} %bitcast.28), calls=%async_computation.1 | async-start | bytes 2359296 | tf_op jit(solution)/shard_map/all_to_all | solution.py:113
Sparse Core Ops, SparseCore 0:
  25.3 66.1 all-gather.2

commit v16 on v13

--- a/solution.py
+++ b/solution.py
@@ -91,14 +91,10 @@
 
     own_attended = lax.all_gather(attended, "y", axis=1, tiled=True)
     other_attended = lax.ppermute(own_attended, "c", swap)
-    weight_rows, own_attended, other_attended = lax.optimization_barrier(
-        (weight_rows, own_attended, other_attended)
-    )
-    features = own_attended.shape[1]
+    chip_attended = jnp.concatenate([own_attended, other_attended], axis=1)
+    weight_rows, chip_attended = lax.optimization_barrier((weight_rows, chip_attended))
     partial_value = jnp.einsum(
-        "rk,nk->rn", own_attended, weight_rows[:, :features], preferred_element_type=jnp.float32
-    ) + jnp.einsum(
-        "rk,nk->rn", other_attended, weight_rows[:, features:], preferred_element_type=jnp.float32
+        "rk,nk->rn", chip_attended, weight_rows, preferred_element_type=jnp.float32
     )
     nx = lax.axis_size("x")
     pieces = partial_value.astype(jnp.bfloat16).reshape(NY, rows, nx * 2, 2 * half)

time: 141 us -> 141 us (level)
    dot_general x2 -> x1, matrix products: 2.96 us -> 2.91 us  [local(): jnp.einsum('rk,nk->rn', chip_attended, weight_rows, preferred_element_typ...]
where the time goes in v16:
time: 141 us; the launch traced here: 140 us
  starting transfers between devices  54.5 us (39%)
  waiting for transfers between devices  37.6 us (27%)
  between operations  14.4 us (10%)
  blocking collectives  10.9 us (8%)
  local copies, waits for them, and re-layouts  9.24 us (7%)
  matrix products  8.69 us (6%)
  other arithmetic  4.76 us (3%)
    all_to_all x1, waiting for transfers between devices, local(): pieces = lax.all_to_all(pieces, ('y', 'x', 'c'), 0, 0, tiled=True)  16.9 us
    all_to_all x1, starting transfers between devices, local(): pieces = lax.all_to_all(pieces, ('y', 'x', 'c'), 0, 0, tiled=True)  15.7 us
    ppermute x3, waiting for transfers between devices, local(): arriving = lax.ppermute(block, 'z', relay)  13.3 us
    ppermute x3, starting transfers between devices, local(): arriving = lax.ppermute(block, 'z', relay)  12.2 us
    ppermute x1, starting transfers between devices, local(): other_attended = lax.ppermute(own_attended, 'c', swap)  12.1 us
    all_gather x1, blocking collectives, local(): own_attended = lax.all_gather(attended, 'y', axis=1, tiled=True)  10.9 us
    ppermute x1, starting transfers between devices, local(): lax.ppermute(out_weight, 'c', swap)  7.3 us
    all_to_all x1, starting transfers between devices, local(): lax.all_to_all(packed, 'y', 2, 0, tiled=True)  5.01 us
  transfers between devices with their start and end apart: 9, of which 8 were waited for; matrix products, arithmetic and copies ran while one was open for 7% of the time, Pallas kernels for 0%

profile of v16, /device:TPU:1, one launch (start us, length us, event | category | flops | bytes accessed | tf_op | source)
XLA Modules:
  0.0 140.1 jit_solution(9419913038925949511)
XLA Ops:
  7.2 1.2 reshape.319
  8.3 1.0 reshape.293
  9.3 0.7 convert_element_type.51
  10.0 0.2 maximum_bitcast_fusion
  10.2 0.2 pad_maximum_fusion.1
  10.4 0.8 copy.22
  11.2 5.0 %all-to-all-start = ((bf16[145,3,4,1,128]{4,0,1,3,2:T(8,128)(2,1)}), bf16[145,3,4,1,128]{4,0,1,3,2:T(8,128)(2,1)S(1)}, u32[]{:S(2)}, u32[]{:S(2)}) async-start(bf16[145,3,4,1,128]{4,0,1,3,2:T(8,128)(2,1)} %copy.22), calls=%async_computation | async-start | bytes 933888 | tf_op jit(solution)/shard_map/all_to_all | solution.py:35
  16.2 7.3 %collective-permute-start = (bf16[512,112]{0,1:T(8,128)(2,1)S(1)}, bf16[512,112]{0,1:T(8,128)(2,1)S(1)}, u32[]{:S(2)}, u32[]{:S(2)}) collective-permute-start(bf16[512,112]{0,1:T(8,128)(2,1)S(1)} %copy-done), channel_id=1, source_target_pairs={{0,1},{1,0},{2,3},{3,2},{4,5},{5,4},{6,7},{7,6},{8,9},{9,8},{10,11... | collective-permute-start | bytes 344072 | tf_op jit(solution)/shard_map/ppermute | solution.py:24
  23.6 0.9 collective-permute-done
  24.5 0.7 fusion.65
  25.3 0.1 slice.94
  25.4 0.5 fusion.77
  25.9 0.3 fusion.14
  26.3 2.3 %collective-permute-start.1 = (bf16[579,2,1,128]{3,0,1,2:T(8,128)(2,1)S(1)}, bf16[579,2,1,128]{3,0,1,2:T(8,128)(2,1)S(1)}, u32[]{:S(2)}, u32[]{:S(2)}) collective-permute-start(bf16[579,2,1,128]{3,0,1,2:T(8,128)(2,1)S(1)} %pad_maximum_fusion.2), channel_id=1, source_target_pairs={{0,32},{32,64},{64,96},{96,128},{128,160},{160,192},{192,224},{224... | collective-permute-start | bytes 889352 | tf_op jit(solution)/shard_map/ppermute | solution.py:81
  28.6 0.6 fusion.1
  29.2 3.1 %collective-permute-done.1 = bf16[579,2,1,128]{3,0,1,2:T(8,128)(2,1)S(1)} collective-permute-done((bf16[579,2,1,128]{3,0,1,2:T(8,128)(2,1)S(1)}, bf16[579,2,1,128]{3,0,1,2:T(8,128)(2,1)S(1)}, u32[]{:S(2)}, u32[]{:S(2)}) %collective-permute-start.1) | collective-permute-done | bytes 296480 | tf_op jit(solution)/shard_map/ppermute | solution.py:81
  32.3 4.1 %collective-permute-start.2 = (bf16[579,2,1,128]{3,0,1,2:T(8,128)(2,1)S(1)}, bf16[579,2,1,128]{3,0,1,2:T(8,128)(2,1)S(1)}, u32[]{:S(2)}, u32[]{:S(2)}) collective-permute-start(bf16[579,2,1,128]{3,0,1,2:T(8,128)(2,1)S(1)} %collective-permute-done.1), channel_id=1, source_target_pairs={{0,32},{32,64},{64,96},{96,128},{128,160},{160,192},{192,224},{224... | collective-permute-start | bytes 889352 | tf_op jit(solution)/shard_map/ppermute | solution.py:84
  36.4 0.5 fusion.78
  37.0 0.5 fusion.6
  37.5 0.6 multiply_add_fusion.1
  38.1 1.9 %collective-permute-done.2 = bf16[579,2,1,128]{3,0,1,2:T(8,128)(2,1)S(1)} collective-permute-done((bf16[579,2,1,128]{3,0,1,2:T(8,128)(2,1)S(1)}, bf16[579,2,1,128]{3,0,1,2:T(8,128)(2,1)S(1)}, u32[]{:S(2)}, u32[]{:S(2)}) %collective-permute-start.2) | collective-permute-done | bytes 296480 | tf_op jit(solution)/shard_map/ppermute | solution.py:84
  40.1 4.1 %collective-permute-start.3 = (bf16[579,2,1,128]{3,0,1,2:T(8,128)(2,1)S(1)}, bf16[579,2,1,128]{3,0,1,2:T(8,128)(2,1)S(1)}, u32[]{:S(2)}, u32[]{:S(2)}) collective-permute-start(bf16[579,2,1,128]{3,0,1,2:T(8,128)(2,1)S(1)} %collective-permute-done.2), channel_id=1, source_target_pairs={{0,32},{32,64},{64,96},{96,128},{128,160},{160,192},{192,224},{224... | collective-permute-start | bytes 889352 | tf_op jit(solution)/shard_map/ppermute | solution.py:84
  44.2 0.5 fusion.79
  44.8 0.5 fusion.8
  45.3 0.6 multiply_add_fusion
  45.9 4.0 %collective-permute-done.3 = bf16[579,2,1,128]{3,0,1,2:T(8,128)(2,1)S(1)} collective-permute-done((bf16[579,2,1,128]{3,0,1,2:T(8,128)(2,1)S(1)}, bf16[579,2,1,128]{3,0,1,2:T(8,128)(2,1)S(1)}, u32[]{:S(2)}, u32[]{:S(2)}) %collective-permute-start.3) | collective-permute-done | bytes 296480 | tf_op jit(solution)/shard_map/ppermute | solution.py:84
  49.9 4.0 %collective-permute-start.4 = (bf16[579,2,1,128]{3,0,1,2:T(8,128)(2,1)S(1)}, bf16[579,2,1,128]{3,0,1,2:T(8,128)(2,1)S(1)}, u32[]{:S(2)}, u32[]{:S(2)}) collective-permute-start(bf16[579,2,1,128]{3,0,1,2:T(8,128)(2,1)S(1)} %collective-permute-done.3), channel_id=1, source_target_pairs={{0,32},{32,64},{64,96},{96,128},{128,160},{160,192},{192,224},{224... | collective-permute-start | bytes 889352 | tf_op jit(solution)/shard_map/ppermute | solution.py:84
  54.0 0.5 fusion.81
  54.5 7.4 %collective-permute-done.4 = bf16[579,2,1,128]{3,0,1,2:T(8,128)(2,1)S(1)} collective-permute-done((bf16[579,2,1,128]{3,0,1,2:T(8,128)(2,1)S(1)}, bf16[579,2,1,128]{3,0,1,2:T(8,128)(2,1)S(1)}, u32[]{:S(2)}, u32[]{:S(2)}) %collective-permute-start.4) | collective-permute-done | bytes 296480 | tf_op jit(solution)/shard_map/ppermute | solution.py:84
  61.9 0.5 fusion.80
  62.4 0.9 fusion.9
  63.4 0.6 convolution_bitcast_fusion.1
  64.1 0.8 fusion.4
  64.8 10.9 %all-gather = bf16[1,576,512]{2,1,0:T(8,128)(2,1)S(1)} all-gather(bf16[1,576,128]{2,1,0:T(8,128)(2,1)S(1)} %fusion.4), channel_id=2, replica_groups=mesh['z'=16,'y'=4,'x'=4,'c'=2] {'y'}, dimensions={2}, use_global_device_ids=true | all-gather | bytes 737280 | tf_op jit(solution)/shard_map/all_gather | solution.py:92
  75.8 12.1 %collective-permute-start.5 = (bf16[576,512]{1,0:T(8,128)(2,1)S(1)}, bf16[576,512]{1,0:T(8,128)(2,1)S(1)}, u32[]{:S(2)}, u32[]{:S(2)}) collective-permute-start(bf16[576,512]{1,0:T(8,128)(2,1)S(1)} %bitcast.107), channel_id=1, source_target_pairs={{0,1},{1,0},{2,3},{3,2},{4,5},{5,4},{6,7},{7,6},{8,9},{9,8},{10,11... | collective-permute-start | bytes 1769480 | tf_op jit(solution)/shard_map/ppermute | solution.py:93
  87.9 1.4 %collective-permute-done.5 = bf16[576,512]{1,0:T(8,128)(2,1)S(1)} collective-permute-done((bf16[576,512]{1,0:T(8,128)(2,1)S(1)}, bf16[576,512]{1,0:T(8,128)(2,1)S(1)}, u32[]{:S(2)}, u32[]{:S(2)}) %collective-permute-start.5) | collective-permute-done | bytes 589856 | tf_op jit(solution)/shard_map/ppermute | solution.py:93
  89.3 0.1 pad_maximum_fusion
  89.4 1.9 %all-gather.3.cloned.1.call-done = bf16[896,1024]{1,0:T(8,128)(2,1)} async-done(((bf16[56,1024]{1,0:T(8,128)(2,1)}), bf16[896,1024]{1,0:T(8,128)(2,1)}) %all-gather.3.cloned.1.call-update) | async-done | bytes 1835024 | tf_op jit(solution)/shard_map/all_gather | solution.py:26
  91.3 2.9 %convolution_convert_fusion = bf16[576,896]{1,0:T(8,128)(2,1)S(1)} fusion(bf16[576,1024]{1,0:T(8,128)(2,1)S(1)} %pad_maximum_fusion, bf16[896,1024]{1,0:T(8,128)(2,1)} %all-gather.3.cloned.1.call-done), kind=kOutput, calls=%fused_computation | convolution fusion | flops 1057480704 | bytes 4046848 | tf_op jit(solution)/shard_map/rk,nk->rn/dot_general | solution.py:96
  94.2 1.4 reshape.314
  95.6 1.2 copy.30
  96.8 15.7 %all-to-all-start.1 = ((bf16[32,144,112]{2,1,0:T(8,128)(2,1)}), bf16[32,144,112]{2,1,0:T(8,128)(2,1)S(1)}, u32[]{:S(2)}, u32[]{:S(2)}) async-start(bf16[32,144,112]{2,1,0:T(8,128)(2,1)} %bitcast.28), calls=%async_computation.1 | async-start | bytes 2359296 | tf_op jit(solution)/shard_map/all_to_all | solution.py:102
  112.4 0.8 copy.33
  113.2 16.9 %all-to-all-done.1 = bf16[32,144,112]{2,1,0:T(8,128)(2,1)S(1)} async-done(((bf16[32,144,112]{2,1,0:T(8,128)(2,1)}), bf16[32,144,112]{2,1,0:T(8,128)(2,1)S(1)}, u32[]{:S(2)}, u32[]{:S(2)}) %all-to-all-start.1) | async-done | bytes 1032224 | tf_op jit(solution)/shard_map/all_to_all | solution.py:102
  130.1 0.8 copy.31
  130.9 0.4 reduce_sum.77
  131.4 0.6 copy.32
  132.0 1.3 reshape.317
  (43 shorter events, 0.5 us)
Async XLA Ops:
  10.2 6.1 %copy-start = (bf16[512,112]{0,1:T(8,128)(2,1)S(1)}, bf16[512,112]{0,1:T(8,128)(2,1)}, u32[]{:S(2)}) copy-start(bf16[512,112]{0,1:T(8,128)(2,1)} %param.11) | copy-start | bytes 344068
  11.2 13.9 %all-to-all-start = ((bf16[145,3,4,1,128]{4,0,1,3,2:T(8,128)(2,1)}), bf16[145,3,4,1,128]{4,0,1,3,2:T(8,128)(2,1)S(1)}, u32[]{:S(2)}, u32[]{:S(2)}) async-start(bf16[145,3,4,1,128]{4,0,1,3,2:T(8,128)(2,1)} %copy.22), calls=%async_computation | async-start | bytes 933888 | tf_op jit(solution)/shard_map/all_to_all | solution.py:35
  16.2 75.0 %all-gather.3.cloned.1.call-start = ((), (), s32[]{:S(2)}) async-start(), calls=%async_computation.2 | async-start | bytes 1949696 | tf_op jit(solution)/shard_map/all_gather | solution.py:26
  16.2 8.3 %collective-permute-start = (bf16[512,112]{0,1:T(8,128)(2,1)S(1)}, bf16[512,112]{0,1:T(8,128)(2,1)S(1)}, u32[]{:S(2)}, u32[]{:S(2)}) collective-permute-start(bf16[512,112]{0,1:T(8,128)(2,1)S(1)} %copy-done), channel_id=1, source_target_pairs={{0,1},{1,0},{2,3},{3,2},{4,5},{5,4},{6,7},{7,6},{8,9},{9,8},{10,11... | collective-permute-start | bytes 344072 | tf_op jit(solution)/shard_map/ppermute | solution.py:24
  26.3 6.0 %collective-permute-start.1 = (bf16[579,2,1,128]{3,0,1,2:T(8,128)(2,1)S(1)}, bf16[579,2,1,128]{3,0,1,2:T(8,128)(2,1)S(1)}, u32[]{:S(2)}, u32[]{:S(2)}) collective-permute-start(bf16[579,2,1,128]{3,0,1,2:T(8,128)(2,1)S(1)} %pad_maximum_fusion.2), channel_id=1, source_target_pairs={{0,32},{32,64},{64,96},{96,128},{128,160},{160,192},{192,224},{224... | collective-permute-start | bytes 889352 | tf_op jit(solution)/shard_map/ppermute | solution.py:81
  32.3 7.8 %collective-permute-start.2 = (bf16[579,2,1,128]{3,0,1,2:T(8,128)(2,1)S(1)}, bf16[579,2,1,128]{3,0,1,2:T(8,128)(2,1)S(1)}, u32[]{:S(2)}, u32[]{:S(2)}) collective-permute-start(bf16[579,2,1,128]{3,0,1,2:T(8,128)(2,1)S(1)} %collective-permute-done.1), channel_id=1, source_target_pairs={{0,32},{32,64},{64,96},{96,128},{128,160},{160,192},{192,224},{224... | collective-permute-start | bytes 889352 | tf_op jit(solution)/shard_map/ppermute | solution.py:84
  40.1 9.9 %collective-permute-start.3 = (bf16[579,2,1,128]{3,0,1,2:T(8,128)(2,1)S(1)}, bf16[579,2,1,128]{3,0,1,2:T(8,128)(2,1)S(1)}, u32[]{:S(2)}, u32[]{:S(2)}) collective-permute-start(bf16[579,2,1,128]{3,0,1,2:T(8,128)(2,1)S(1)} %collective-permute-done.2), channel_id=1, source_target_pairs={{0,32},{32,64},{64,96},{96,128},{128,160},{160,192},{192,224},{224... | collective-permute-start | bytes 889352 | tf_op jit(solution)/shard_map/ppermute | solution.py:84
  49.9 11.9 %collective-permute-start.4 = (bf16[579,2,1,128]{3,0,1,2:T(8,128)(2,1)S(1)}, bf16[579,2,1,128]{3,0,1,2:T(8,128)(2,1)S(1)}, u32[]{:S(2)}, u32[]{:S(2)}) collective-permute-start(bf16[579,2,1,128]{3,0,1,2:T(8,128)(2,1)S(1)} %collective-permute-done.3), channel_id=1, source_target_pairs={{0,32},{32,64},{64,96},{96,128},{128,160},{160,192},{192,224},{224... | collective-permute-start | bytes 889352 | tf_op jit(solution)/shard_map/ppermute | solution.py:84
  75.8 13.5 %collective-permute-start.5 = (bf16[576,512]{1,0:T(8,128)(2,1)S(1)}, bf16[576,512]{1,0:T(8,128)(2,1)S(1)}, u32[]{:S(2)}, u32[]{:S(2)}) collective-permute-start(bf16[576,512]{1,0:T(8,128)(2,1)S(1)} %bitcast.107), channel_id=1, source_target_pairs={{0,1},{1,0},{2,3},{3,2},{4,5},{5,4},{6,7},{7,6},{8,9},{9,8},{10,11... | collective-permute-start | bytes 1769480 | tf_op jit(solution)/shard_map/ppermute | solution.py:93
  96.8 33.4 %all-to-all-start.1 = ((bf16[32,144,112]{2,1,0:T(8,128)(2,1)}), bf16[32,144,112]{2,1,0:T(8,128)(2,1)S(1)}, u32[]{:S(2)}, u32[]{:S(2)}) async-start(bf16[32,144,112]{2,1,0:T(8,128)(2,1)} %bitcast.28), calls=%async_computation.1 | async-start | bytes 2359296 | tf_op jit(solution)/shard_map/all_to_all | solution.py:102
Sparse Core Ops, SparseCore 0:
  25.3 65.9 all-gather.2
